TPU v7x, 32 devices: a whole 2x2x4 slice. The times are simulated.
32 devices in a mesh: site: 4 (over y, x), sector: 4 (over z), chan: 2 (over core).
Axes of the slice: x: 2, y: 2, z: 4, core: 2. Of those that a mesh axis runs over, the one named last changes fastest.
Arguments:
- environment: bfloat16 [4, 18, 4, 256, 256], P('site', 'chan', 'sector'), may hold values from -6 to 6
- ket_tensor: bfloat16 [4, 4, 4, 256, 256], P('site', 'sector'), may hold values from -0.375 to 0.375
- bra_tensor: bfloat16 [4, 4, 4, 256, 256], P('site', 'sector'), may hold values from -0.375 to 0.375
- mpo_tensor: bfloat16 [4, 18, 18, 4], P('site', None, 'chan'), may hold values from -1.5 to 1.5
- block_length: int32 [4], P('sector'), may hold values from 64 to 256, as said below
Outputs:
- advanced: bfloat16 [4, 18, 4, 256, 256], P('site', 'chan', 'sector')
Inputs may be any that keep to these rules, and one draw needn't show every extreme that they name: `block_length`: rows and columns of a sector's block at or past its length are padding: environment's entries there are taken as zero and advanced's entries there are zero; some sector has exactly 256.
All inputs are finite; a program needn't handle non-finite values.
Results may differ from a plain program's by a relative error of at most 0.009.
Values may be sent and summed in bfloat16 or wider, within the bound.
No kernel may reach another device: no remote copies, remote signals or barrier semaphores. Data moves between devices by JAX's collectives and lax.ppermute only.
A program may use at most 64 MiB of HBM per device.

v0:
```python
import jax
import jax.numpy as jnp
from jax import lax
from jax.sharding import PartitionSpec as P

STEPS = 2


def passed_along(value, axis, steps):
    count = lax.axis_size(axis)
    pairs = [(source, (source + steps) % count) for source in range(count)]
    return lax.ppermute(value, axis, pairs)


def shards(environment, ket_tensor, bra_tensor, mpo_tensor, block_length):
    stride = lax.axis_size("sector") // 2
    width = environment.shape[-1]
    index = jnp.arange(width, dtype=jnp.int32)
    alive = index < block_length[0]
    live_both = alive[:, None] & alive[None, :]
    live_mask = live_both.astype(jnp.float32)
    ket_blocks = ket_tensor[0, 0]
    bra_blocks = bra_tensor[0, 0]
    mpo_local = mpo_tensor[0]
    current = jnp.where(live_both, environment, jnp.zeros((), jnp.bfloat16))
    for step in range(STEPS):
        gathered = lax.all_gather(current, "chan", axis=1, tiled=True)
        mixed = jnp.einsum(
            "wvp,wba->pvba", mpo_local, gathered[0, :, 0], preferred_element_type=jnp.float32
        ).astype(jnp.bfloat16)
        rotated = jnp.einsum(
            "pvba,pac->pvbc", mixed, ket_blocks, preferred_element_type=jnp.float32
        ).astype(jnp.bfloat16)
        projected = jnp.einsum(
            "pbd,pvbc->pvdc", bra_blocks, rotated, preferred_element_type=jnp.float32
        ).astype(jnp.bfloat16)
        first = passed_along(projected[1], "sector", 1)
        second = passed_along(projected[2], "sector", stride)
        third = passed_along(projected[3], "sector", stride + 1)
        total = projected[0].astype(jnp.float32) + first.astype(jnp.float32)
        total = total + second.astype(jnp.float32) + third.astype(jnp.float32)
        updated = (total * live_mask[None]).astype(jnp.bfloat16)
        current = passed_along(updated[None, :, None], "site", 1)
    return current


def solution(mesh):
    return jax.shard_map(
        shards,
        mesh=mesh,
        in_specs=(
            P("site", "chan", "sector", None, None),
            P("site", "sector", None, None, None),
            P("site", "sector", None, None, None),
            P("site", None, "chan", None),
            P("sector"),
        ),
        out_specs=P("site", "chan", "sector", None, None),
        check_vma=False,
    )
```

profile of v0, /device:TPU:0, one launch (start us, length us, event | category | flops | bytes accessed | tf_op | source)
XLA Modules:
  0.0 360.0 jit_solution(18138028591745550052)
XLA Ops:
  7.6 2.4 bitcast_select_fusion
  10.0 13.8 %all-gather.3.cloned.1.call-done = bf16[1,18,1,256,256]{4,3,2,0,1:T(8,128)(2,1)} async-done(((bf16[1,9,1,256,256]{4,3,2,0,1:T(8,128)(2,1)}), bf16[1,18,1,256,256]{4,3,2,0,1:T(8,128)(2,1)}) %all-gather.3.cloned.1.call-update) | async-done | bytes 2359312 | tf_op jit(solution)/shard_map/all_gather | solution.py:27
  23.8 7.3 %convert_bitcast_fusion.1 = bf16[4,9,256,256]{3,1,0,2:T(8,128)(2,1)} fusion(bf16[1,18,1,256,256]{4,3,2,0,1:T(8,128)(2,1)} %all-gather.3.cloned.1.call-done, bf16[18,9,4]{0,2,1:T(4,128)(2,1)S(1)} %bitcast.79), kind=kOutput, calls=%fused_computation.1 | convolution fusion | flops 87293952 | bytes 7079184 | tf_op jit(solution)/shard_map/wvp,wba->pvba/dot_general | solution.py:28
  31.1 12.4 %convert_bitcast_fusion.3 = bf16[4,9,256,256]{2,3,1,0:T(8,128)(2,1)} fusion(bf16[4,9,256,256]{3,1,0,2:T(8,128)(2,1)} %convert_bitcast_fusion.1, bf16[1,1,4,256,256]{4,3,2,1,0:T(8,128)(2,1)S(1)} %copy-done, bf16[1,1,4,256,256]{4,3,2,1,0:T(8,128)(2,1)S(1)} %copy-done.2), kind=kOutput, calls=%fused_computation.9 | convolution fusion | flops 2420637696 | bytes 10485760 | tf_op jit(solution)/shard_map/pbd,pvbc->pvdc/dot_general | solution.py:34
  43.5 2.2 slice_bitcast_fusion.6
  45.7 1.8 collective-permute-start
  47.5 2.1 collective-permute-start.2
  50.4 25.9 %collective-permute-done = bf16[9,256,256]{1,2,0:T(8,128)(2,1)S(1)} collective-permute-done((bf16[9,256,256]{1,2,0:T(8,128)(2,1)S(1)}, bf16[9,256,256]{1,2,0:T(8,128)(2,1)S(1)}, u32[]{:S(2)}, u32[]{:S(2)}) %collective-permute-start) | collective-permute-done | bytes 1179680 | tf_op jit(solution)/shard_map/ppermute | solution.py:12
  76.4 24.3 %collective-permute-done.2 = bf16[9,256,256]{1,2,0:T(8,128)(2,1)S(1)} collective-permute-done((bf16[9,256,256]{1,2,0:T(8,128)(2,1)S(1)}, bf16[9,256,256]{1,2,0:T(8,128)(2,1)S(1)}, u32[]{:S(2)}, u32[]{:S(2)}) %collective-permute-start.2) | collective-permute-done | bytes 1179680 | tf_op jit(solution)/shard_map/ppermute | solution.py:12
  100.6 51.0 %collective-permute-done.1 = bf16[9,256,256]{1,2,0:T(8,128)(2,1)S(1)} collective-permute-done((bf16[9,256,256]{1,2,0:T(8,128)(2,1)S(1)}, bf16[9,256,256]{1,2,0:T(8,128)(2,1)S(1)}, u32[]{:S(2)}, u32[]{:S(2)}) %collective-permute-start.1) | collective-permute-done | bytes 1179680 | tf_op jit(solution)/shard_map/ppermute | solution.py:12
  151.6 2.0 fusion.36
  153.6 1.9 collective-permute-start.3
  155.5 27.1 %collective-permute-done.3 = bf16[1,9,1,256,256]{3,4,1,2,0:T(8,128)(2,1)S(1)} collective-permute-done((bf16[1,9,1,256,256]{3,4,1,2,0:T(8,128)(2,1)S(1)}, bf16[1,9,1,256,256]{3,4,1,2,0:T(8,128)(2,1)S(1)}, u32[]{:S(2)}, u32[]{:S(2)}) %collective-permute-start.3) | collective-permute-done | bytes 1179680 | tf_op jit(solution)/shard_map/ppermute | solution.py:12
  184.1 9.0 %all-gather.5.cloned.1.call-done = bf16[1,18,1,256,256]{4,3,2,0,1:T(8,128)(2,1)} async-done(((bf16[1,9,1,256,256]{4,3,2,0,1:T(8,128)(2,1)}), bf16[1,18,1,256,256]{4,3,2,0,1:T(8,128)(2,1)}) %all-gather.5.cloned.1.call-update) | async-done | bytes 2359312 | tf_op jit(solution)/shard_map/all_gather | solution.py:27
  193.1 7.2 %convert_bitcast_fusion = bf16[4,9,256,256]{3,1,0,2:T(8,128)(2,1)} fusion(bf16[1,18,1,256,256]{4,3,2,0,1:T(8,128)(2,1)} %all-gather.5.cloned.1.call-done, bf16[18,9,4]{0,2,1:T(4,128)(2,1)S(1)} %bitcast.80), kind=kOutput, calls=%fused_computation | convolution fusion | flops 87293952 | bytes 7079184 | tf_op jit(solution)/shard_map/wvp,wba->pvba/dot_general | solution.py:28
  200.3 12.4 %convert_bitcast_fusion.2 = bf16[4,9,256,256]{2,3,1,0:T(8,128)(2,1)} fusion(bf16[4,9,256,256]{3,1,0,2:T(8,128)(2,1)} %convert_bitcast_fusion, bf16[1,1,4,256,256]{4,3,2,1,0:T(8,128)(2,1)S(1)} %copy-done, bf16[1,1,4,256,256]{4,3,2,1,0:T(8,128)(2,1)S(1)} %copy-done.2), kind=kOutput, calls=%fused_computation.6 | convolution fusion | flops 2420637696 | bytes 10485760 | tf_op jit(solution)/shard_map/pbd,pvbc->pvdc/dot_general | solution.py:34
  212.7 2.2 slice_bitcast_fusion.2
  214.9 1.8 collective-permute-start.4
  216.7 2.1 collective-permute-start.6
  219.7 25.9 %collective-permute-done.4 = bf16[9,256,256]{1,2,0:T(8,128)(2,1)S(1)} collective-permute-done((bf16[9,256,256]{1,2,0:T(8,128)(2,1)S(1)}, bf16[9,256,256]{1,2,0:T(8,128)(2,1)S(1)}, u32[]{:S(2)}, u32[]{:S(2)}) %collective-permute-start.4) | collective-permute-done | bytes 1179680 | tf_op jit(solution)/shard_map/ppermute | solution.py:12
  245.6 24.3 %collective-permute-done.6 = bf16[9,256,256]{1,2,0:T(8,128)(2,1)S(1)} collective-permute-done((bf16[9,256,256]{1,2,0:T(8,128)(2,1)S(1)}, bf16[9,256,256]{1,2,0:T(8,128)(2,1)S(1)}, u32[]{:S(2)}, u32[]{:S(2)}) %collective-permute-start.6) | collective-permute-done | bytes 1179680 | tf_op jit(solution)/shard_map/ppermute | solution.py:12
  269.9 50.9 %collective-permute-done.5 = bf16[9,256,256]{1,2,0:T(8,128)(2,1)S(1)} collective-permute-done((bf16[9,256,256]{1,2,0:T(8,128)(2,1)S(1)}, bf16[9,256,256]{1,2,0:T(8,128)(2,1)S(1)}, u32[]{:S(2)}, u32[]{:S(2)}) %collective-permute-start.5) | collective-permute-done | bytes 1179680 | tf_op jit(solution)/shard_map/ppermute | solution.py:12
  320.8 2.0 fusion.37
  324.5 27.1 %collective-permute-done.7 = bf16[1,9,1,256,256]{3,4,1,2,0:T(8,128)(2,1)S(1)} collective-permute-done((bf16[1,9,1,256,256]{3,4,1,2,0:T(8,128)(2,1)S(1)}, bf16[1,9,1,256,256]{3,4,1,2,0:T(8,128)(2,1)S(1)}, u32[]{:S(2)}, u32[]{:S(2)}) %collective-permute-start.7) | collective-permute-done | bytes 1179680 | tf_op jit(solution)/shard_map/ppermute | solution.py:12
  (18 shorter events, 6.9 us)
Async XLA Ops:
  6.5 24.6 %copy-start = (bf16[1,1,4,256,256]{4,3,2,1,0:T(8,128)(2,1)S(1)}, bf16[1,1,4,256,256]{4,3,2,1,0:T(8,128)(2,1)}, u32[]{:S(2)}) copy-start(bf16[1,1,4,256,256]{4,3,2,1,0:T(8,128)(2,1)} %param.7) | copy-start | bytes 1572868
  6.5 17.2 %copy-start.1 = (bf16[1,18,9,4]{1,3,2,0:T(4,128)(2,1)S(1)}, bf16[1,18,9,4]{1,3,2,0:T(4,128)(2,1)}, u32[]{:S(2)}) copy-start(bf16[1,18,9,4]{1,3,2,0:T(4,128)(2,1)} %param.8) | copy-start | bytes 3892
  6.5 17.2 %all-gather.3.cloned.1.call-start = ((), (), s32[]{:S(2)}) async-start(), calls=%async_computation | async-start | bytes 3538944 | tf_op jit(solution)/shard_map/all_gather | solution.py:27
  10.0 183.2 %all-gather.5.cloned.1.call-start = ((), (), s32[]{:S(2)}) async-start(), calls=%async_computation.1 | async-start | bytes 3538944 | tf_op jit(solution)/shard_map/all_gather | solution.py:27
  23.8 7.3 %copy-start.2 = (bf16[1,1,4,256,256]{4,3,2,1,0:T(8,128)(2,1)S(1)}, bf16[1,1,4,256,256]{4,3,2,1,0:T(8,128)(2,1)}, u32[]{:S(2)}) copy-start(bf16[1,1,4,256,256]{4,3,2,1,0:T(8,128)(2,1)} %param.6) | copy-start | bytes 1572868
  45.7 30.7 %collective-permute-start = (bf16[9,256,256]{1,2,0:T(8,128)(2,1)S(1)}, bf16[9,256,256]{1,2,0:T(8,128)(2,1)S(1)}, u32[]{:S(2)}, u32[]{:S(2)}) collective-permute-start(bf16[9,256,256]{1,2,0:T(8,128)(2,1)S(1)} %get-tuple-element.8), channel_id=1, source_target_pairs={{0,2},{2,4},{4,6},{6,0},{1,3},{3,5},{5,7},{7,1},{8,10},{10,12},{12... | collective-permute-start | bytes 3538952 | tf_op jit(solution)/shard_map/ppermute | solution.py:12
  47.5 53.2 %collective-permute-start.2 = (bf16[9,256,256]{1,2,0:T(8,128)(2,1)S(1)}, bf16[9,256,256]{1,2,0:T(8,128)(2,1)S(1)}, u32[]{:S(2)}, u32[]{:S(2)}) collective-permute-start(bf16[9,256,256]{1,2,0:T(8,128)(2,1)S(1)} %get-tuple-element.9), channel_id=1, source_target_pairs={{0,6},{2,0},{4,2},{6,4},{1,7},{3,1},{5,3},{7,5},{8,14},{10,8},{12,... | collective-permute-start | bytes 3538952 | tf_op jit(solution)/shard_map/ppermute | solution.py:12
  49.6 102.0 %collective-permute-start.1 = (bf16[9,256,256]{1,2,0:T(8,128)(2,1)S(1)}, bf16[9,256,256]{1,2,0:T(8,128)(2,1)S(1)}, u32[]{:S(2)}, u32[]{:S(2)}) collective-permute-start(bf16[9,256,256]{1,2,0:T(8,128)(2,1)S(1)} %get-tuple-element.10), channel_id=1, source_target_pairs={{0,4},{2,6},{4,0},{6,2},{1,5},{3,7},{5,1},{7,3},{8,12},{10,14},{12... | collective-permute-start | bytes 3538952 | tf_op jit(solution)/shard_map/ppermute | solution.py:12
  153.6 29.0 %collective-permute-start.3 = (bf16[1,9,1,256,256]{3,4,1,2,0:T(8,128)(2,1)S(1)}, bf16[1,9,1,256,256]{3,4,1,2,0:T(8,128)(2,1)S(1)}, u32[]{:S(2)}, u32[]{:S(2)}) collective-permute-start(bf16[1,9,1,256,256]{3,4,1,2,0:T(8,128)(2,1)S(1)} %fusion.36), channel_id=1, source_target_pairs={{0,8},{8,16},{16,24},{24,0},{1,9},{9,17},{17,25},{25,1},{2,10},{10... | collective-permute-start | bytes 3538952 | tf_op jit(solution)/shard_map/ppermute | solution.py:12
  214.9 30.7 %collective-permute-start.4 = (bf16[9,256,256]{1,2,0:T(8,128)(2,1)S(1)}, bf16[9,256,256]{1,2,0:T(8,128)(2,1)S(1)}, u32[]{:S(2)}, u32[]{:S(2)}) collective-permute-start(bf16[9,256,256]{1,2,0:T(8,128)(2,1)S(1)} %get-tuple-element.5), channel_id=1, source_target_pairs={{0,2},{2,4},{4,6},{6,0},{1,3},{3,5},{5,7},{7,1},{8,10},{10,12},{12... | collective-permute-start | bytes 3538952 | tf_op jit(solution)/shard_map/ppermute | solution.py:12
  216.7 53.2 %collective-permute-start.6 = (bf16[9,256,256]{1,2,0:T(8,128)(2,1)S(1)}, bf16[9,256,256]{1,2,0:T(8,128)(2,1)S(1)}, u32[]{:S(2)}, u32[]{:S(2)}) collective-permute-start(bf16[9,256,256]{1,2,0:T(8,128)(2,1)S(1)} %get-tuple-element.6), channel_id=1, source_target_pairs={{0,6},{2,0},{4,2},{6,4},{1,7},{3,1},{5,3},{7,5},{8,14},{10,8},{12,... | collective-permute-start | bytes 3538952 | tf_op jit(solution)/shard_map/ppermute | solution.py:12
  218.8 102.0 %collective-permute-start.5 = (bf16[9,256,256]{1,2,0:T(8,128)(2,1)S(1)}, bf16[9,256,256]{1,2,0:T(8,128)(2,1)S(1)}, u32[]{:S(2)}, u32[]{:S(2)}) collective-permute-start(bf16[9,256,256]{1,2,0:T(8,128)(2,1)S(1)} %get-tuple-element.7), channel_id=1, source_target_pairs={{0,4},{2,6},{4,0},{6,2},{1,5},{3,7},{5,1},{7,3},{8,12},{10,14},{12... | collective-permute-start | bytes 3538952 | tf_op jit(solution)/shard_map/ppermute | solution.py:12
  322.8 28.8 %collective-permute-start.7 = (bf16[1,9,1,256,256]{3,4,1,2,0:T(8,128)(2,1)S(1)}, bf16[1,9,1,256,256]{3,4,1,2,0:T(8,128)(2,1)S(1)}, u32[]{:S(2)}, u32[]{:S(2)}) collective-permute-start(bf16[1,9,1,256,256]{3,4,1,2,0:T(8,128)(2,1)S(1)} %fusion.37), channel_id=1, source_target_pairs={{0,8},{8,16},{16,24},{24,0},{1,9},{9,17},{17,25},{25,1},{2,10},{10... | collective-permute-start | bytes 3538952 | tf_op jit(solution)/shard_map/ppermute | solution.py:12
Sparse Core Ops, SparseCore 0:
  10.1 13.6 all-gather.2
  184.2 8.8 all-gather.4
where the time goes:
time: 360 us
  waiting for transfers between devices  279 us (78%)
  matrix products  39.3 us (11%)
  between operations  14.2 us (4%)
  starting transfers between devices  13.2 us (4%)
  local copies, waits for them, and re-layouts  7.65 us (2%)
  other arithmetic  6.41 us (2%)
    ppermute x8, waiting for transfers between devices, passed_along(): return lax.ppermute(value, axis, pairs)  257 us
    dot_general x2, matrix products, shards(): jnp.einsum('pbd,pvbc->pvdc', bra_blocks, rotated, preferred_element_type=...  24.7 us
    all_gather x2, waiting for transfers between devices, shards(): gathered = lax.all_gather(current, 'chan', axis=1, tiled=True)  22.8 us
    dot_general x2, matrix products, shards(): jnp.einsum('wvp,wba->pvba', mpo_local, gathered[0, :, 0], preferred_eleme...  14.5 us
    ppermute x8, starting transfers between devices, passed_along(): return lax.ppermute(value, axis, pairs)  13.1 us
  transfers between devices with their start and end apart: 10, of which 10 were waited for; matrix products, arithmetic and copies ran while one was open for 0% of the time, Pallas kernels for 0%

commit v1 on v0

v1 whole, which is shorter than its diff:
```python
import jax
import jax.numpy as jnp
from jax import lax
from jax.sharding import PartitionSpec as P

STEPS = 2

LINE_P = ((3, 1, 3, 1), (2, 3, 1, 2), (1, 2, 2, 3))
RIGHT = ((0, 1), (1, 2), (2, 3))
LEFT = ((3, 2), (2, 1), (1, 0))
MIDDLE = ((0, 2), (3, 1))
LAST = ((0, 1), (1, 3), (3, 2), (2, 0))


def shifted(value, axis, steps):
    count = lax.axis_size(axis)
    pairs = [(source, (source + steps) % count) for source in range(count)]
    return lax.ppermute(value, axis, pairs)


def term(gathered, ket_p, bra_p, mpo_p):
    mixed = jnp.einsum(
        "wv,wba->vba", mpo_p, gathered, preferred_element_type=jnp.float32
    ).astype(jnp.bfloat16)
    rotated = jnp.einsum(
        "vba,ac->vbc", mixed, ket_p, preferred_element_type=jnp.float32
    ).astype(jnp.bfloat16)
    return jnp.einsum(
        "bd,vbc->vdc", bra_p, rotated, preferred_element_type=jnp.float32
    ).astype(jnp.bfloat16)


def pick(table, sector, ket, bra, mpo):
    p = jnp.asarray(table, jnp.int32)[sector]
    return (
        lax.dynamic_index_in_dim(ket, p, 0, keepdims=False),
        lax.dynamic_index_in_dim(bra, p, 0, keepdims=False),
        lax.dynamic_index_in_dim(mpo, p, 2, keepdims=False),
    )


def advance_line(current, ket, bra, mpo, live_mask, sector):
    gathered = lax.all_gather(current, "chan", axis=0, tiled=True)
    f32 = jnp.float32
    one = jnp.ones((), f32)
    zero = jnp.zeros((), f32)
    slots = [term(gathered, *pick(t, sector, ket, bra, mpo)) for t in LINE_P[:2]]
    got_right = lax.ppermute(
        jnp.where(sector == 2, slots[1], slots[0]), "sector", RIGHT
    )
    got_left = lax.ppermute(
        jnp.where(sector == 1, slots[1], slots[0]), "sector", LEFT
    )
    got_middle = lax.ppermute(slots[1], "sector", MIDDLE)
    third = term(gathered, *pick(LINE_P[2], sector, ket, bra, mpo))
    keep_right = jnp.where(sector == 1, zero, one)
    keep_left = jnp.where(sector == 2, zero, one)
    send = third.astype(f32) + (1 - keep_right) * got_right.astype(f32)
    send = send + (1 - keep_left) * got_left.astype(f32)
    got_last = lax.ppermute(send.astype(jnp.bfloat16), "sector", LAST)
    own = term(gathered, ket[0], bra[0], mpo[:, :, 0])
    total = own.astype(f32) + keep_right * got_right.astype(f32)
    total = total + keep_left * got_left.astype(f32)
    total = total + got_middle.astype(f32) + got_last.astype(f32)
    return (total * live_mask[None]).astype(jnp.bfloat16)


def advance_direct(current, ket, bra, mpo, live_mask):
    stride = lax.axis_size("sector") // 2
    gathered = lax.all_gather(current, "chan", axis=0, tiled=True)
    f32 = jnp.float32
    total = term(gathered, ket[0], bra[0], mpo[:, :, 0]).astype(f32)
    for p, steps in ((1, 1), (2, stride), (3, stride + 1)):
        part = term(gathered, ket[p], bra[p], mpo[:, :, p])
        total = total + shifted(part, "sector", steps).astype(f32)
    return (total * live_mask[None]).astype(jnp.bfloat16)


def shards(environment, ket_tensor, bra_tensor, mpo_tensor, block_length):
    width = environment.shape[-1]
    index = jnp.arange(width, dtype=jnp.int32)
    alive = index < block_length[0]
    live_both = alive[:, None] & alive[None, :]
    live_mask = live_both.astype(jnp.float32)
    sector = lax.axis_index("sector")
    line = lax.axis_size("sector") == 4
    tensors = [(ket_tensor[0, 0], bra_tensor[0, 0], mpo_tensor[0])]
    for _ in range(1, STEPS):
        ket, bra, mpo = tensors[-1]
        tensors.append(tuple(shifted(t, "site", -1) for t in (ket, bra, mpo)))
    current = jnp.where(live_both, environment[0, :, 0], jnp.zeros((), jnp.bfloat16))
    for ket, bra, mpo in tensors:
        if line:
            current = advance_line(current, ket, bra, mpo, live_mask, sector)
        else:
            current = advance_direct(current, ket, bra, mpo, live_mask)
    return shifted(current[None, :, None], "site", STEPS)


def solution(mesh):
    return jax.shard_map(
        shards,
        mesh=mesh,
        in_specs=(
            P("site", "chan", "sector", None, None),
            P("site", "sector", None, None, None),
            P("site", "sector", None, None, None),
            P("site", None, "chan", None),
            P("sector"),
        ),
        out_specs=P("site", "chan", "sector", None, None),
        check_vma=False,
    )
```

time: 360 us -> 291 us (0.81)
  waiting for transfers between devices: 279 us -> 146 us
  starting transfers between devices: 13.2 us -> 48.3 us
  matrix products: 39.3 us -> 64.4 us
  between operations: 14.2 us -> 19.7 us
    ppermute x8 -> x12, waiting for transfers between devices: 257 us -> 132 us  [the longest x2 50.2 us: advance_line(): got_last = lax.ppermute(send.astype(jnp.bfloat16), 'sector', LAST)]
    ppermute x8 -> x12, starting transfers between devices: 13.1 us -> 48.3 us  [the longest x2 22.8 us: advance_line(): got_last = lax.ppermute(send.astype(jnp.bfloat16), 'sector', LAST)]
    dot_general x4 -> x16, matrix products: 39.3 us -> 64.4 us  [the longest x8 35.3 us: term(): jnp.einsum('bd,vbc->vdc', bra_p, rotated, preferred_element_type=jnp.floa...]
    all_gather x2, waiting for transfers between devices: 22.8 us -> 14.1 us  [advance_line(): gathered = lax.all_gather(current, 'chan', axis=0, tiled=True)]
    squeeze x2 -> x0, local copies, waits for them, and re-layouts: 4.42 us -> none  [shards(): first = passed_along(projected[1], 'sector', 1)]
    broadcast_in_dim x2 -> x0, other arithmetic: 3.93 us -> none  [shards(): current = passed_along(updated[None, :, None], 'site', 1)]
  transfers between devices with their start and end apart: 10 -> 14, of which waited for: 10 -> 11; matrix products, arithmetic and copies ran while one was open for 0% -> 12% of each run, Pallas kernels for 0% -> 0%
where the time goes in v1:
time: 291 us; the launch traced here: 290 us
  waiting for transfers between devices  146 us (50%)
  matrix products  64.4 us (22%)
  starting transfers between devices  48.3 us (17%)
  between operations  19.7 us (7%)
  other arithmetic  6.16 us (2%)
  local copies, waits for them, and re-layouts  5.73 us (2%)
    ppermute x2, waiting for transfers between devices, advance_line(): got_last = lax.ppermute(send.astype(jnp.bfloat16), 'sector', LAST)  50.2 us
    ppermute x4, waiting for transfers between devices, shifted(): return lax.ppermute(value, axis, pairs)  36.6 us
    dot_general x8, matrix products, term(): jnp.einsum('bd,vbc->vdc', bra_p, rotated, preferred_element_type=jnp.floa...  35.3 us
    dot_general x8, matrix products, term(): jnp.einsum('wv,wba->vba', mpo_p, gathered, preferred_element_type=jnp.flo...  29.1 us
    ppermute x2, waiting for transfers between devices, advance_line(): lax.ppermute(jnp.where(sector == 2, slots[1], slots[0]), 'sector', RIGHT)  28.1 us
    ppermute x2, starting transfers between devices, advance_line(): got_last = lax.ppermute(send.astype(jnp.bfloat16), 'sector', LAST)  22.8 us
    all_gather x2, waiting for transfers between devices, advance_line(): gathered = lax.all_gather(current, 'chan', axis=0, tiled=True)  14.1 us
    ppermute x2, starting transfers between devices, advance_line(): got_middle = lax.ppermute(slots[1], 'sector', MIDDLE)  11.5 us
  transfers between devices with their start and end apart: 14, of which 11 were waited for; matrix products, arithmetic and copies ran while one was open for 12% of the time, Pallas kernels for 0%

profile of v1, /device:TPU:0, one launch (start us, length us, event | category | flops | bytes accessed | tf_op | source)
XLA Modules:
  0.0 290.1 jit_solution(6067562432771504465)
XLA Ops:
  15.2 9.2 %all-gather.3.cloned.1.call-done = bf16[18,256,256]{2,1,0:T(8,128)(2,1)} async-done(((bf16[9,256,256]{2,1,0:T(8,128)(2,1)}), bf16[18,256,256]{2,1,0:T(8,128)(2,1)}) %all-gather.3.cloned.1.call-update) | async-done | bytes 2359312 | tf_op jit(solution)/shard_map/all_gather | solution.py:43
  24.4 4.9 %fusion.39 = bf16[9,256,256]{2,0,1:T(8,128)(2,1)} fusion(bf16[18,256,256]{2,1,0:T(8,128)(2,1)} %all-gather.3.cloned.1.call-done, bf16[1,18,9,4]{1,2,3,0:T(8,128)(2,1)S(1)} %copy.121, s32[]{:T(128)S(6)} %select_n.80), kind=kOutput, calls=%fused_computation.45 | convolution fusion | flops 21823488 | bytes 3543044 | tf_op jit(solution)/shard_map/wv,wba->vba/dot_general | solution.py:22
  29.4 4.2 %fusion.58 = bf16[9,256,256]{1,2,0:T(8,128)(2,1)} fusion(bf16[9,256,256]{2,0,1:T(8,128)(2,1)} %fusion.39, bf16[1,1,4,256,256]{4,3,2,1,0:T(8,128)(2,1)} %param.13, s32[]{:T(128)S(6)} %select_n.80, bf16[1,1,4,256,256]{4,3,2,1,0:T(8,128)(2,1)S(1)} %copy-done.4), kind=kOutput, calls=%fused_computation.68 | convolution fusion | flops 605159424 | bytes 3539968 | tf_op jit(solution)/shard_map/bd,vbc->vdc/dot_general | solution.py:28
  33.5 3.3 %fusion.36 = bf16[9,256,256]{2,0,1:T(8,128)(2,1)} fusion(bf16[18,256,256]{2,1,0:T(8,128)(2,1)S(1)} %copy-done, bf16[1,18,9,4]{1,2,3,0:T(8,128)(2,1)S(1)} %copy.121, s32[]{:T(128)S(6)} %select_n.79), kind=kOutput, calls=%fused_computation.44 | convolution fusion | flops 21823488 | bytes 3543044 | tf_op jit(solution)/shard_map/wv,wba->vba/dot_general | solution.py:22
  36.8 5.2 %broadcast_select_fusion.1 = (bf16[9,256,256]{1,2,0:T(8,128)(2,1)}, bf16[9,256,256]{1,2,0:T(8,128)(2,1)}, bf16[9,256,256]{1,2,0:T(8,128)(2,1)}) fusion(bf16[9,256,256]{1,2,0:T(8,128)(2,1)} %fusion.58, pred[]{:T(512)S(6)} %eq.4, pred[]{:T(512)S(6)} %eq.5, bf16[1,1,4,256,256]{4,3,2,1,0:T(8,128)(2,1)} %param.13, s32[]{:T(128)S(6)} %select_n.79, ...), kind=kOutput, calls=%fused_computation.81 | convolution fusion | flops 606339072 | bytes 7079936 | tf_op jit(solution)/shard_map/bd,vbc->vdc/dot_general | solution.py:28
  42.1 3.7 %collective-permute-start = (bf16[9,256,256]{1,2,0:T(8,128)(2,1)}, bf16[9,256,256]{1,2,0:T(8,128)(2,1)S(1)}, u32[]{:S(2)}, u32[]{:S(2)}) collective-permute-start(bf16[9,256,256]{1,2,0:T(8,128)(2,1)} %get-tuple-element.8), channel_id=1, source_target_pairs={{0,2},{2,4},{4,6},{1,3},{3,5},{5,7},{8,10},{10,12},{12,14},{9,11},... | collective-permute-start | bytes 3538952 | tf_op jit(solution)/shard_map/ppermute | solution.py:48
  50.5 6.5 %collective-permute-start.2 = (bf16[9,256,256]{1,2,0:T(8,128)(2,1)}, bf16[9,256,256]{1,2,0:T(8,128)(2,1)}, u32[]{:S(2)}, u32[]{:S(2)}) collective-permute-start(bf16[9,256,256]{1,2,0:T(8,128)(2,1)} %get-tuple-element.13), channel_id=1, source_target_pairs={{0,4},{6,2},{1,5},{7,3},{8,12},{14,10},{9,13},{15,11},{16,20},{22,... | collective-permute-start | bytes 3538952 | tf_op jit(solution)/shard_map/ppermute | solution.py:54
  60.3 12.0 %collective-permute-done = bf16[9,256,256]{1,2,0:T(8,128)(2,1)S(1)} collective-permute-done((bf16[9,256,256]{1,2,0:T(8,128)(2,1)}, bf16[9,256,256]{1,2,0:T(8,128)(2,1)S(1)}, u32[]{:S(2)}, u32[]{:S(2)}) %collective-permute-start) | collective-permute-done | bytes 1179680 | tf_op jit(solution)/shard_map/ppermute | solution.py:48
  72.3 3.6 %collective-permute-done.1 = bf16[9,256,256]{1,2,0:T(8,128)(2,1)} collective-permute-done((bf16[9,256,256]{1,2,0:T(8,128)(2,1)}, bf16[9,256,256]{1,2,0:T(8,128)(2,1)}, u32[]{:S(2)}, u32[]{:S(2)}) %collective-permute-start.1) | collective-permute-done | bytes 1179680 | tf_op jit(solution)/shard_map/ppermute | solution.py:51
  75.9 4.4 %fusion.24 = bf16[9,256,256]{1,2,0:T(8,128)(2,1)} fusion(bf16[9,256,256]{1,2,0:T(8,128)(2,1)S(1)} %collective-permute-done, bf16[9,256,256]{1,2,0:T(8,128)(2,1)} %collective-permute-done.1, bf16[9,256,256]{2,0,1:T(8,128)(2,1)} %fusion.42, f32[]{:T(128)S(6)} %sub.9, f32[]{:T(128)S(6)} %sub.8, bf16[1,1,4,256,256]{4,3,2,1,0:T(8,128)(2,1)} %param.13, ...), kind=kOutput, calls=%fused_computation.32 | convolution fusion | flops 609878016 | bytes 5900288 | tf_op jit(solution)/shard_map/bd,vbc->vdc/dot_general | solution.py:28
  87.7 9.9 %collective-permute-done.2 = bf16[9,256,256]{1,2,0:T(8,128)(2,1)} collective-permute-done((bf16[9,256,256]{1,2,0:T(8,128)(2,1)}, bf16[9,256,256]{1,2,0:T(8,128)(2,1)}, u32[]{:S(2)}, u32[]{:S(2)}) %collective-permute-start.2) | collective-permute-done | bytes 1179680 | tf_op jit(solution)/shard_map/ppermute | solution.py:54
  97.7 30.6 %collective-permute-done.3 = bf16[9,256,256]{1,2,0:T(8,128)(2,1)} collective-permute-done((bf16[9,256,256]{1,2,0:T(8,128)(2,1)}, bf16[9,256,256]{1,2,0:T(8,128)(2,1)}, u32[]{:S(2)}, u32[]{:S(2)}) %collective-permute-start.3) | collective-permute-done | bytes 1179680 | tf_op jit(solution)/shard_map/ppermute | solution.py:60
  137.2 4.9 %all-gather.5.cloned.1.call-done = bf16[18,256,256]{2,1,0:T(8,128)(2,1)} async-done(((bf16[9,256,256]{2,1,0:T(8,128)(2,1)}), bf16[18,256,256]{2,1,0:T(8,128)(2,1)}) %all-gather.5.cloned.1.call-update) | async-done | bytes 2359312 | tf_op jit(solution)/shard_map/all_gather | solution.py:43
  142.1 5.1 %fusion.47 = bf16[9,256,256]{2,0,1:T(8,128)(2,1)} fusion(bf16[18,256,256]{2,1,0:T(8,128)(2,1)} %all-gather.5.cloned.1.call-done, bf16[18,9,4]{0,1,2:T(8,128)(2,1)S(1)} %collective-permute-done.4, s32[]{:T(128)S(6)} %select_n.79), kind=kOutput, calls=%fused_computation.47 | convolution fusion | flops 21823488 | bytes 3543044 | tf_op jit(solution)/shard_map/wv,wba->vba/dot_general | solution.py:22
  150.5 9.6 %collective-permute-done.6 = bf16[4,256,256]{2,1,0:T(8,128)(2,1)} collective-permute-done((bf16[4,256,256]{2,1,0:T(8,128)(2,1)}, bf16[4,256,256]{2,1,0:T(8,128)(2,1)}, u32[]{:S(2)}, u32[]{:S(2)}) %collective-permute-start.6) | collective-permute-done | bytes 524320 | tf_op jit(solution)/shard_map/ppermute | solution.py:18
  160.1 4.1 %fusion.59 = bf16[9,256,256]{1,2,0:T(8,128)(2,1)} fusion(bf16[9,256,256]{2,0,1:T(8,128)(2,1)} %fusion.47, bf16[4,256,256]{2,1,0:T(8,128)(2,1)} %collective-permute-done.6, s32[]{:T(128)S(6)} %select_n.79, bf16[4,256,256]{2,1,0:T(8,128)(2,1)} %collective-permute-done.5), kind=kOutput, calls=%fused_computation.69 | convolution fusion | flops 605159424 | bytes 3539968 | tf_op jit(solution)/shard_map/bd,vbc->vdc/dot_general | solution.py:28
  164.2 4.8 %broadcast_select_fusion = (bf16[9,256,256]{1,2,0:T(8,128)(2,1)}, bf16[9,256,256]{1,2,0:T(8,128)(2,1)}) fusion(bf16[9,256,256]{1,2,0:T(8,128)(2,1)} %fusion.59, pred[]{:T(512)S(6)} %eq.4, pred[]{:T(512)S(6)} %eq.5, bf16[4,256,256]{2,1,0:T(8,128)(2,1)} %collective-permute-done.6, s32[]{:T(128)S(6)} %select_n.80, bf16[9,256,256]{2,0,1:T(8,128)(2,1)} %fusion.50, ...), kind=kOutput, calls=%fused_computation.80 | convolution fusion | flops 606339072 | bytes 5900288 | tf_op jit(solution)/shard_map/bd,vbc->vdc/dot_general | solution.py:28
  172.6 5.0 %collective-permute-start.9 = (bf16[9,256,256]{1,2,0:T(8,128)(2,1)}, bf16[9,256,256]{1,2,0:T(8,128)(2,1)}, u32[]{:S(2)}, u32[]{:S(2)}) collective-permute-start(bf16[9,256,256]{1,2,0:T(8,128)(2,1)} %fusion.59), channel_id=1, source_target_pairs={{0,4},{6,2},{1,5},{7,3},{8,12},{14,10},{9,13},{15,11},{16,20},{22,... | collective-permute-start | bytes 3538952 | tf_op jit(solution)/shard_map/ppermute | solution.py:54
  181.0 16.1 %collective-permute-done.7 = bf16[9,256,256]{1,2,0:T(8,128)(2,1)} collective-permute-done((bf16[9,256,256]{1,2,0:T(8,128)(2,1)}, bf16[9,256,256]{1,2,0:T(8,128)(2,1)}, u32[]{:S(2)}, u32[]{:S(2)}) %collective-permute-start.7) | collective-permute-done | bytes 1179680 | tf_op jit(solution)/shard_map/ppermute | solution.py:48
  200.3 4.8 %fusion.33 = bf16[9,256,256]{1,2,0:T(8,128)(2,1)} fusion(bf16[9,256,256]{1,2,0:T(8,128)(2,1)} %collective-permute-done.7, bf16[9,256,256]{1,2,0:T(8,128)(2,1)} %collective-permute-done.8, bf16[9,256,256]{2,0,1:T(8,128)(2,1)} %fusion.53, f32[]{:T(128)S(6)} %sub.9, f32[]{:T(128)S(6)} %sub.8, bf16[4,256,256]{2,1,0:T(8,128)(2,1)} %collective-permute-done.6, ...), kind=kOutput, calls=%fused_computation.41 | convolution fusion | flops 609878016 | bytes 5900288 | tf_op jit(solution)/shard_map/bd,vbc->vdc/dot_general | solution.py:28
  205.1 21.4 %collective-permute-start.10 = (bf16[9,256,256]{1,2,0:T(8,128)(2,1)}, bf16[9,256,256]{1,2,0:T(8,128)(2,1)}, u32[]{:S(2)}, u32[]{:S(2)}) collective-permute-start(bf16[9,256,256]{1,2,0:T(8,128)(2,1)} %fusion.33), channel_id=1, source_target_pairs={{0,2},{2,6},{6,4},{4,0},{1,3},{3,7},{7,5},{5,1},{8,10},{10,14},{14... | collective-permute-start | bytes 3538952 | tf_op jit(solution)/shard_map/ppermute | solution.py:60
  229.4 19.6 %collective-permute-done.10 = bf16[9,256,256]{1,2,0:T(8,128)(2,1)} collective-permute-done((bf16[9,256,256]{1,2,0:T(8,128)(2,1)}, bf16[9,256,256]{1,2,0:T(8,128)(2,1)}, u32[]{:S(2)}, u32[]{:S(2)}) %collective-permute-start.10) | collective-permute-done | bytes 1179680 | tf_op jit(solution)/shard_map/ppermute | solution.py:60
  249.0 4.7 %fusion.56 = bf16[1,9,1,256,256]{3,4,1,2,0:T(8,128)(2,1)S(1)} fusion(bf16[9,256,256]{1,2,0:T(8,128)(2,1)} %collective-permute-done.10, bf16[9,256,256]{1,2,0:T(8,128)(2,1)} %collective-permute-done.9, bf16[9,256,256]{1,2,0:T(8,128)(2,1)} %collective-permute-done.8, bf16[9,256,256]{1,2,0:T(8,128)(2,1)} %collective-permute-done.7, ...), kind=kOutput, calls=%fused_computation.66 | convolution fusion | flops 612827136 | bytes 8519688 | tf_op jit(solution)/shard_map/bd,vbc->vdc/dot_general | solution.py:28
  254.7 27.0 %collective-permute-done.11 = bf16[1,9,1,256,256]{3,4,1,2,0:T(8,128)(2,1)S(1)} collective-permute-done((bf16[1,9,1,256,256]{3,4,1,2,0:T(8,128)(2,1)S(1)}, bf16[1,9,1,256,256]{3,4,1,2,0:T(8,128)(2,1)S(1)}, u32[]{:S(2)}, u32[]{:S(2)}) %collective-permute-start.11) | collective-permute-done | bytes 1179680 | tf_op jit(solution)/shard_map/ppermute | solution.py:18
  (49 shorter events, 45.7 us)
Async XLA Ops:
  6.5 4.1 %copy-start.7 = (s32[4]{0:T(128)S(1)}, s32[4]{0:T(128)}, u32[]{:S(2)}) copy-start(s32[4]{0:T(128)} %constant.75.clone) | copy-start | bytes 52
  6.5 5.9 %copy-start.6 = (s32[4]{0:T(128)S(1)}, s32[4]{0:T(128)}, u32[]{:S(2)}) copy-start(s32[4]{0:T(128)} %constant.76.clone) | copy-start | bytes 52
  6.5 7.5 %copy-start.3 = (bf16[1,18,9,4]{1,3,2,0:T(4,128)(2,1)S(1)}, bf16[1,18,9,4]{1,3,2,0:T(4,128)(2,1)}, u32[]{:S(2)}) copy-start(bf16[1,18,9,4]{1,3,2,0:T(4,128)(2,1)} %param.14) | copy-start | bytes 3892
  6.5 17.9 %all-gather.3.cloned.1.call-start = ((), (), s32[]{:S(2)}) async-start(), calls=%async_computation | async-start | bytes 3538944 | tf_op jit(solution)/shard_map/all_gather | solution.py:43
  10.6 131.5 %all-gather.5.cloned.1.call-start = ((), (), s32[]{:S(2)}) async-start(), calls=%async_computation.1 | async-start | bytes 3538944 | tf_op jit(solution)/shard_map/all_gather | solution.py:43
  15.2 14.2 %copy-start.4 = (bf16[1,1,4,256,256]{4,3,2,1,0:T(8,128)(2,1)S(1)}, bf16[1,1,4,256,256]{4,3,2,1,0:T(8,128)(2,1)}, u32[]{:S(2)}) copy-start(bf16[1,1,4,256,256]{4,3,2,1,0:T(8,128)(2,1)} %param.12) | copy-start | bytes 1572868
  29.4 4.2 %copy-start = (bf16[18,256,256]{2,1,0:T(8,128)(2,1)S(1)}, bf16[18,256,256]{2,1,0:T(8,128)(2,1)}, u32[]{:S(2)}) copy-start(bf16[18,256,256]{2,1,0:T(8,128)(2,1)} %all-gather.3.cloned.1.call-done) | copy-start | bytes 7077892
  42.1 30.3 %collective-permute-start = (bf16[9,256,256]{1,2,0:T(8,128)(2,1)}, bf16[9,256,256]{1,2,0:T(8,128)(2,1)S(1)}, u32[]{:S(2)}, u32[]{:S(2)}) collective-permute-start(bf16[9,256,256]{1,2,0:T(8,128)(2,1)} %get-tuple-element.8), channel_id=1, source_target_pairs={{0,2},{2,4},{4,6},{1,3},{3,5},{5,7},{8,10},{10,12},{12,14},{9,11},... | collective-permute-start | bytes 3538952 | tf_op jit(solution)/shard_map/ppermute | solution.py:48
  45.8 30.1 %collective-permute-start.1 = (bf16[9,256,256]{1,2,0:T(8,128)(2,1)}, bf16[9,256,256]{1,2,0:T(8,128)(2,1)}, u32[]{:S(2)}, u32[]{:S(2)}) collective-permute-start(bf16[9,256,256]{1,2,0:T(8,128)(2,1)} %get-tuple-element.7), channel_id=1, source_target_pairs={{6,4},{4,2},{2,0},{7,5},{5,3},{3,1},{14,12},{12,10},{10,8},{15,13}... | collective-permute-start | bytes 3538952 | tf_op jit(solution)/shard_map/ppermute | solution.py:51
  50.5 47.1 %collective-permute-start.2 = (bf16[9,256,256]{1,2,0:T(8,128)(2,1)}, bf16[9,256,256]{1,2,0:T(8,128)(2,1)}, u32[]{:S(2)}, u32[]{:S(2)}) collective-permute-start(bf16[9,256,256]{1,2,0:T(8,128)(2,1)} %get-tuple-element.13), channel_id=1, source_target_pairs={{0,4},{6,2},{1,5},{7,3},{8,12},{14,10},{9,13},{15,11},{16,20},{22,... | collective-permute-start | bytes 3538952 | tf_op jit(solution)/shard_map/ppermute | solution.py:54
  80.3 47.9 %collective-permute-start.3 = (bf16[9,256,256]{1,2,0:T(8,128)(2,1)}, bf16[9,256,256]{1,2,0:T(8,128)(2,1)}, u32[]{:S(2)}, u32[]{:S(2)}) collective-permute-start(bf16[9,256,256]{1,2,0:T(8,128)(2,1)} %fusion.24), channel_id=1, source_target_pairs={{0,2},{2,6},{6,4},{4,0},{1,3},{3,7},{7,5},{5,1},{8,10},{10,14},{14... | collective-permute-start | bytes 3538952 | tf_op jit(solution)/shard_map/ppermute | solution.py:60
  131.2 4.0 %copy-start.5 = (bf16[1,1,4,256,256]{4,3,2,1,0:T(8,128)(2,1)S(1)}, bf16[1,1,4,256,256]{4,3,2,1,0:T(8,128)(2,1)}, u32[]{:S(2)}) copy-start(bf16[1,1,4,256,256]{4,3,2,1,0:T(8,128)(2,1)} %param.12) | copy-start | bytes 1572868
  132.8 4.5 %collective-permute-start.4 = (bf16[18,9,4]{0,1,2:T(8,128)(2,1)S(1)}, bf16[18,9,4]{0,1,2:T(8,128)(2,1)S(1)}, u32[]{:S(2)}, u32[]{:S(2)}) collective-permute-start(bf16[18,9,4]{0,1,2:T(8,128)(2,1)S(1)} %bitcast.145), channel_id=1, source_target_pairs={{0,24},{8,0},{16,8},{24,16},{1,25},{9,1},{17,9},{25,17},{2,26},{10... | collective-permute-start | bytes 3896 | tf_op jit(solution)/shard_map/ppermute | solution.py:18
  135.2 15.3 %collective-permute-start.5 = (bf16[4,256,256]{2,1,0:T(8,128)(2,1)S(1)}, bf16[4,256,256]{2,1,0:T(8,128)(2,1)}, u32[]{:S(2)}, u32[]{:S(2)}) collective-permute-start(bf16[4,256,256]{2,1,0:T(8,128)(2,1)S(1)} %bitcast.146), channel_id=1, source_target_pairs={{0,24},{8,0},{16,8},{24,16},{1,25},{9,1},{17,9},{25,17},{2,26},{10... | collective-permute-start | bytes 1572872 | tf_op jit(solution)/shard_map/ppermute | solution.py:18
  135.8 24.3 %collective-permute-start.6 = (bf16[4,256,256]{2,1,0:T(8,128)(2,1)}, bf16[4,256,256]{2,1,0:T(8,128)(2,1)}, u32[]{:S(2)}, u32[]{:S(2)}) collective-permute-start(bf16[4,256,256]{2,1,0:T(8,128)(2,1)} %bitcast.39), channel_id=1, source_target_pairs={{0,24},{8,0},{16,8},{24,16},{1,25},{9,1},{17,9},{25,17},{2,26},{10... | collective-permute-start | bytes 1572872 | tf_op jit(solution)/shard_map/ppermute | solution.py:18
  142.1 5.1 %copy-start.1 = (bf16[18,256,256]{2,1,0:T(8,128)(2,1)S(1)}, bf16[18,256,256]{2,1,0:T(8,128)(2,1)}, u32[]{:S(2)}) copy-start(bf16[18,256,256]{2,1,0:T(8,128)(2,1)} %all-gather.5.cloned.1.call-done) | copy-start | bytes 7077892
  169.0 28.0 %collective-permute-start.7 = (bf16[9,256,256]{1,2,0:T(8,128)(2,1)}, bf16[9,256,256]{1,2,0:T(8,128)(2,1)}, u32[]{:S(2)}, u32[]{:S(2)}) collective-permute-start(bf16[9,256,256]{1,2,0:T(8,128)(2,1)} %get-tuple-element.6), channel_id=1, source_target_pairs={{0,2},{2,4},{4,6},{1,3},{3,5},{5,7},{8,10},{10,12},{12,14},{9,11},... | collective-permute-start | bytes 3538952 | tf_op jit(solution)/shard_map/ppermute | solution.py:48
  171.4 28.9 %collective-permute-start.8 = (bf16[9,256,256]{1,2,0:T(8,128)(2,1)}, bf16[9,256,256]{1,2,0:T(8,128)(2,1)}, u32[]{:S(2)}, u32[]{:S(2)}) collective-permute-start(bf16[9,256,256]{1,2,0:T(8,128)(2,1)} %get-tuple-element.5), channel_id=1, source_target_pairs={{6,4},{4,2},{2,0},{7,5},{5,3},{3,1},{14,12},{12,10},{10,8},{15,13}... | collective-permute-start | bytes 3538952 | tf_op jit(solution)/shard_map/ppermute | solution.py:51
  172.6 56.8 %collective-permute-start.9 = (bf16[9,256,256]{1,2,0:T(8,128)(2,1)}, bf16[9,256,256]{1,2,0:T(8,128)(2,1)}, u32[]{:S(2)}, u32[]{:S(2)}) collective-permute-start(bf16[9,256,256]{1,2,0:T(8,128)(2,1)} %fusion.59), channel_id=1, source_target_pairs={{0,4},{6,2},{1,5},{7,3},{8,12},{14,10},{9,13},{15,11},{16,20},{22,... | collective-permute-start | bytes 3538952 | tf_op jit(solution)/shard_map/ppermute | solution.py:54
  205.1 44.0 %copy-start.2 = (f32[256,256]{0,1:T(8,128)S(1)}, f32[256,256]{0,1:T(8,128)}, u32[]{:S(2)}) copy-start(f32[256,256]{0,1:T(8,128)} %get-tuple-element.11) | copy-start | bytes 786436
  205.1 43.9 %collective-permute-start.10 = (bf16[9,256,256]{1,2,0:T(8,128)(2,1)}, bf16[9,256,256]{1,2,0:T(8,128)(2,1)}, u32[]{:S(2)}, u32[]{:S(2)}) collective-permute-start(bf16[9,256,256]{1,2,0:T(8,128)(2,1)} %fusion.33), channel_id=1, source_target_pairs={{0,2},{2,6},{6,4},{4,0},{1,3},{3,7},{7,5},{5,1},{8,10},{10,14},{14... | collective-permute-start | bytes 3538952 | tf_op jit(solution)/shard_map/ppermute | solution.py:60
  253.8 27.9 %collective-permute-start.11 = (bf16[1,9,1,256,256]{3,4,1,2,0:T(8,128)(2,1)S(1)}, bf16[1,9,1,256,256]{3,4,1,2,0:T(8,128)(2,1)S(1)}, u32[]{:S(2)}, u32[]{:S(2)}) collective-permute-start(bf16[1,9,1,256,256]{3,4,1,2,0:T(8,128)(2,1)S(1)} %fusion.56), channel_id=1, source_target_pairs={{0,16},{8,24},{16,0},{24,8},{1,17},{9,25},{17,1},{25,9},{2,18},{10... | collective-permute-start | bytes 3538952 | tf_op jit(solution)/shard_map/ppermute | solution.py:18
Sparse Core Ops, SparseCore 0:
  10.7 13.6 all-gather.2
  132.9 9.1 all-gather.4

commit v2 on v1

--- a/solution.py
+++ b/solution.py
@@ -5,10 +5,11 @@
 
 STEPS = 2
 
-LINE_P = ((3, 1, 3, 1), (2, 3, 1, 2), (1, 2, 2, 3))
+SLOT_A = (3, 1, 1, 2)
+SLOT_B = (2, 3, 3, 1)
+LAST_P = (1, 2, 2, 3)
 RIGHT = ((0, 1), (1, 2), (2, 3))
 LEFT = ((3, 2), (2, 1), (1, 0))
-MIDDLE = ((0, 2), (3, 1))
 LAST = ((0, 1), (1, 3), (3, 2), (2, 0))
 
 
@@ -39,20 +40,19 @@
     )
 
 
-def advance_line(current, ket, bra, mpo, live_mask, sector):
+def advance_line(current, ket, bra, mpo, live_mask, sector, held):
     gathered = lax.all_gather(current, "chan", axis=0, tiled=True)
     f32 = jnp.float32
     one = jnp.ones((), f32)
     zero = jnp.zeros((), f32)
-    slots = [term(gathered, *pick(t, sector, ket, bra, mpo)) for t in LINE_P[:2]]
-    got_right = lax.ppermute(
-        jnp.where(sector == 2, slots[1], slots[0]), "sector", RIGHT
-    )
-    got_left = lax.ppermute(
-        jnp.where(sector == 1, slots[1], slots[0]), "sector", LEFT
-    )
-    got_middle = lax.ppermute(slots[1], "sector", MIDDLE)
-    third = term(gathered, *pick(LINE_P[2], sector, ket, bra, mpo))
+    slot_a = term(gathered, *pick(SLOT_A, sector, ket, bra, mpo))
+    slot_b = term(gathered, *pick(SLOT_B, sector, ket, bra, mpo))
+    got_right = lax.ppermute(slot_a, "sector", RIGHT)
+    got_left = lax.ppermute(slot_b, "sector", LEFT)
+    got_middle = lax.ppermute(slot_b, "sector", ((0, 2),))
+    got_middle = got_middle + lax.ppermute(slot_a, "sector", ((3, 1),))
+    got_right, held = lax.optimization_barrier((got_right, held))
+    third = term(gathered, *pick(LAST_P, sector, ket, bra, mpo))
     keep_right = jnp.where(sector == 1, zero, one)
     keep_left = jnp.where(sector == 2, zero, one)
     send = third.astype(f32) + (1 - keep_right) * got_right.astype(f32)
@@ -62,7 +62,7 @@
     total = own.astype(f32) + keep_right * got_right.astype(f32)
     total = total + keep_left * got_left.astype(f32)
     total = total + got_middle.astype(f32) + got_last.astype(f32)
-    return (total * live_mask[None]).astype(jnp.bfloat16)
+    return (total * live_mask[None]).astype(jnp.bfloat16), held
 
 
 def advance_direct(current, ket, bra, mpo, live_mask):
@@ -89,9 +89,12 @@
         ket, bra, mpo = tensors[-1]
         tensors.append(tuple(shifted(t, "site", -1) for t in (ket, bra, mpo)))
     current = jnp.where(live_both, environment[0, :, 0], jnp.zeros((), jnp.bfloat16))
-    for ket, bra, mpo in tensors:
+    for step in range(STEPS):
+        ket, bra, mpo = tensors[step]
         if line:
-            current = advance_line(current, ket, bra, mpo, live_mask, sector)
+            current, tensors[step + 1 :] = advance_line(
+                current, ket, bra, mpo, live_mask, sector, tensors[step + 1 :]
+            )
         else:
             current = advance_direct(current, ket, bra, mpo, live_mask)
     return shifted(current[None, :, None], "site", STEPS)

time: 291 us -> 289 us (level)
  starting transfers between devices: 48.3 us -> 32.5 us
  waiting for transfers between devices: 146 us -> 159 us
  other arithmetic: 6.16 us -> 10.2 us
    ppermute x2, starting transfers between devices: 22.8 us -> 0.51 us  [advance_line(): got_last = lax.ppermute(send.astype(jnp.bfloat16), 'sector', LAST)]
    ppermute x2, waiting for transfers between devices: 50.2 us -> 65.7 us  [advance_line(): got_last = lax.ppermute(send.astype(jnp.bfloat16), 'sector', LAST)]
    ppermute x6 -> x8, waiting for transfers between devices: 44.8 us -> 33.3 us  [the longest x2 15 us: advance_line(): got_middle = lax.ppermute(slot_b, 'sector', ((0, 2),))]
    ppermute x6 -> x8, starting transfers between devices: 20.1 us -> 26 us  [the longest x2 10.8 us: advance_line(): got_middle = lax.ppermute(slot_b, 'sector', ((0, 2),))]
    ppermute x4, waiting for transfers between devices: 36.6 us -> 41.4 us  [shifted(): return lax.ppermute(value, axis, pairs)]
    all_gather x2, waiting for transfers between devices: 14.1 us -> 18.5 us  [advance_line(): gathered = lax.all_gather(current, 'chan', axis=0, tiled=True)]
    broadcast_in_dim x0 -> x1, other arithmetic: none -> 3.85 us  [shards(): return shifted(current[None, :, None], 'site', STEPS)]
    dot_general x8, matrix products: 35.3 us -> 32.3 us  [term(): jnp.einsum('bd,vbc->vdc', bra_p, rotated, preferred_element_type=jnp.floa...]
  transfers between devices with their start and end apart: 14 -> 16, of which waited for: 11 -> 10; matrix products, arithmetic and copies ran while one was open for 12% -> 16% of each run, Pallas kernels for 0% -> 0%
where the time goes in v2:
time: 289 us
  waiting for transfers between devices  159 us (55%)
  matrix products  61.5 us (21%)
  starting transfers between devices  32.5 us (11%)
  between operations  20.4 us (7%)
  other arithmetic  10.2 us (4%)
  local copies, waits for them, and re-layouts  5.24 us (2%)
    ppermute x2, waiting for transfers between devices, advance_line(): got_last = lax.ppermute(send.astype(jnp.bfloat16), 'sector', LAST)  65.7 us
    ppermute x4, waiting for transfers between devices, shifted(): return lax.ppermute(value, axis, pairs)  41.4 us
    dot_general x8, matrix products, term(): jnp.einsum('bd,vbc->vdc', bra_p, rotated, preferred_element_type=jnp.floa...  32.3 us
    dot_general x8, matrix products, term(): jnp.einsum('wv,wba->vba', mpo_p, gathered, preferred_element_type=jnp.flo...  29.3 us
    all_gather x2, waiting for transfers between devices, advance_line(): gathered = lax.all_gather(current, 'chan', axis=0, tiled=True)  18.5 us
    ppermute x2, waiting for transfers between devices, advance_line(): got_middle = lax.ppermute(slot_b, 'sector', ((0, 2),))  15 us
    ppermute x2, waiting for transfers between devices, advance_line(): got_left = lax.ppermute(slot_b, 'sector', LEFT)  11.9 us
    ppermute x2, starting transfers between devices, advance_line(): got_middle = lax.ppermute(slot_b, 'sector', ((0, 2),))  10.8 us
  transfers between devices with their start and end apart: 16, of which 10 were waited for; matrix products, arithmetic and copies ran while one was open for 16% of the time, Pallas kernels for 0%

profile of v2, /device:TPU:0, one launch (start us, length us, event | category | flops | bytes accessed | tf_op | source)
XLA Modules:
  0.0 288.9 jit_solution(10075397105479395774)
XLA Ops:
  15.5 8.3 %all-gather.3.cloned.1.call-done = bf16[18,256,256]{2,1,0:T(8,128)(2,1)} async-done(((bf16[9,256,256]{2,1,0:T(8,128)(2,1)}), bf16[18,256,256]{2,1,0:T(8,128)(2,1)}) %all-gather.3.cloned.1.call-update) | async-done | bytes 2359312 | tf_op jit(solution)/shard_map/all_gather | solution.py:44
  23.8 4.9 %fusion.34 = bf16[9,256,256]{2,0,1:T(8,128)(2,1)} fusion(bf16[18,256,256]{2,1,0:T(8,128)(2,1)} %all-gather.3.cloned.1.call-done, bf16[1,18,9,4]{1,2,3,0:T(8,128)(2,1)S(1)} %copy.117, s32[]{:T(128)S(6)} %select_n.54), kind=kOutput, calls=%fused_computation.43 | convolution fusion | flops 21823488 | bytes 3543044 | tf_op jit(solution)/shard_map/wv,wba->vba/dot_general | solution.py:23
  28.7 4.1 %fusion.57 = bf16[9,256,256]{1,2,0:T(8,128)(2,1)} fusion(bf16[9,256,256]{2,0,1:T(8,128)(2,1)} %fusion.34, bf16[1,1,4,256,256]{4,3,2,1,0:T(8,128)(2,1)S(1)} %copy-done.3, s32[]{:T(128)S(6)} %select_n.54, bf16[1,1,4,256,256]{4,3,2,1,0:T(8,128)(2,1)} %param.12), kind=kOutput, calls=%fused_computation.66 | convolution fusion | flops 605159424 | bytes 3539968 | tf_op jit(solution)/shard_map/bd,vbc->vdc/dot_general | solution.py:29
  32.8 4.6 %collective-permute-start = (bf16[9,256,256]{1,2,0:T(8,128)(2,1)}, bf16[9,256,256]{1,2,0:T(8,128)(2,1)}, u32[]{:S(2)}, u32[]{:S(2)}) collective-permute-start(bf16[9,256,256]{1,2,0:T(8,128)(2,1)} %fusion.57), channel_id=1, source_target_pairs={{0,2},{2,4},{4,6},{1,3},{3,5},{5,7},{8,10},{10,12},{12,14},{9,11},... | collective-permute-start | bytes 3538952 | tf_op jit(solution)/shard_map/ppermute | solution.py:50
  37.5 3.3 %fusion.39 = bf16[9,256,256]{2,0,1:T(8,128)(2,1)} fusion(bf16[18,256,256]{2,1,0:T(8,128)(2,1)S(1)} %copy-done, bf16[1,18,9,4]{1,2,3,0:T(8,128)(2,1)S(1)} %copy.117, s32[]{:T(128)S(6)} %select_n.58), kind=kOutput, calls=%fused_computation.44 | convolution fusion | flops 21823488 | bytes 3543044 | tf_op jit(solution)/shard_map/wv,wba->vba/dot_general | solution.py:23
  40.8 4.0 %fusion.58 = bf16[9,256,256]{1,2,0:T(8,128)(2,1)} fusion(bf16[9,256,256]{2,0,1:T(8,128)(2,1)} %fusion.39, bf16[1,1,4,256,256]{4,3,2,1,0:T(8,128)(2,1)S(1)} %copy-done.3, s32[]{:T(128)S(6)} %select_n.58, bf16[1,1,4,256,256]{4,3,2,1,0:T(8,128)(2,1)} %param.12), kind=kOutput, calls=%fused_computation.67 | convolution fusion | flops 605159424 | bytes 3539968 | tf_op jit(solution)/shard_map/bd,vbc->vdc/dot_general | solution.py:29
  56.6 15.0 %collective-permute-done.3 = bf16[18,9,4]{0,1,2:T(8,128)(2,1)S(1)} collective-permute-done((bf16[18,9,4]{0,1,2:T(8,128)(2,1)S(1)}, bf16[18,9,4]{0,1,2:T(8,128)(2,1)S(1)}, u32[]{:S(2)}, u32[]{:S(2)}) %collective-permute-start.3) | collective-permute-done | bytes 1328 | tf_op jit(solution)/shard_map/ppermute | solution.py:19
  71.6 5.2 %collective-permute-start.5 = (bf16[9,256,256]{1,2,0:T(8,128)(2,1)}, bf16[9,256,256]{1,2,0:T(8,128)(2,1)}, u32[]{:S(2)}, u32[]{:S(2)}) collective-permute-start(bf16[9,256,256]{1,2,0:T(8,128)(2,1)} %fusion.58), channel_id=1, source_target_pairs={{0,4},{1,5},{8,12},{9,13},{16,20},{17,21},{24,28},{25,29}} | collective-permute-start | bytes 3538952 | tf_op jit(solution)/shard_map/ppermute | solution.py:52
  78.6 4.9 %fusion.24 = bf16[9,256,256]{1,2,0:T(8,128)(2,1)} fusion(bf16[9,256,256]{1,2,0:T(8,128)(2,1)} %collective-permute-done, bf16[9,256,256]{1,2,0:T(8,128)(2,1)} %collective-permute-done.4, bf16[9,256,256]{2,0,1:T(8,128)(2,1)} %fusion.42, f32[]{:T(128)S(6)} %sub.9, f32[]{:T(128)S(6)} %sub.8, bf16[1,1,4,256,256]{4,3,2,1,0:T(8,128)(2,1)S(1)} %copy-done.3, ...), kind=kOutput, calls=%fused_computation.32 | convolution fusion | flops 609878016 | bytes 5900288 | tf_op jit(solution)/shard_map/bd,vbc->vdc/dot_general | solution.py:29
  89.3 13.3 %collective-permute-done.5 = bf16[9,256,256]{1,2,0:T(8,128)(2,1)} collective-permute-done((bf16[9,256,256]{1,2,0:T(8,128)(2,1)}, bf16[9,256,256]{1,2,0:T(8,128)(2,1)}, u32[]{:S(2)}, u32[]{:S(2)}) %collective-permute-start.5) | collective-permute-done | bytes 1179680 | tf_op jit(solution)/shard_map/ppermute | solution.py:52
  102.6 27.7 %collective-permute-done.7 = bf16[9,256,256]{1,2,0:T(8,128)(2,1)} collective-permute-done((bf16[9,256,256]{1,2,0:T(8,128)(2,1)}, bf16[9,256,256]{1,2,0:T(8,128)(2,1)}, u32[]{:S(2)}, u32[]{:S(2)}) %collective-permute-start.7) | collective-permute-done | bytes 1179680 | tf_op jit(solution)/shard_map/ppermute | solution.py:60
  130.3 3.9 %fusion.21 = bf16[9,256,256]{1,2,0:T(8,128)(2,1)S(1)} fusion(bf16[9,256,256]{1,2,0:T(8,128)(2,1)} %collective-permute-done, bf16[9,256,256]{1,2,0:T(8,128)(2,1)} %collective-permute-done.4, bf16[9,256,256]{2,1,0:T(8,128)(2,1)S(1)} %convolution_convert_fusion.12, bf16[9,256,256]{1,2,0:T(8,128)(2,1)} %collective-permute-done.7, ...), kind=kLoop, calls=%fused_computation.29 | loop fusion | flops 8257536 | bytes 8519688 | tf_op jit(solution)/shard_map/convert_element_type | solution.py:65
  135.7 10.2 %all-gather.5.cloned.1.call-done = bf16[18,256,256]{2,1,0:T(8,128)(2,1)} async-done(((bf16[9,256,256]{2,1,0:T(8,128)(2,1)}), bf16[18,256,256]{2,1,0:T(8,128)(2,1)}) %all-gather.5.cloned.1.call-update) | async-done | bytes 2359312 | tf_op jit(solution)/shard_map/all_gather | solution.py:44
  146.0 5.0 %fusion.48 = bf16[9,256,256]{2,0,1:T(8,128)(2,1)} fusion(bf16[18,256,256]{2,1,0:T(8,128)(2,1)} %all-gather.5.cloned.1.call-done, bf16[18,9,4]{0,1,2:T(8,128)(2,1)S(1)} %collective-permute-done.3, s32[]{:T(128)S(6)} %select_n.54), kind=kOutput, calls=%fused_computation.47 | convolution fusion | flops 21823488 | bytes 3543044 | tf_op jit(solution)/shard_map/wv,wba->vba/dot_general | solution.py:23
  150.9 4.2 %fusion.59 = bf16[9,256,256]{1,2,0:T(8,128)(2,1)} fusion(bf16[9,256,256]{2,0,1:T(8,128)(2,1)} %fusion.48, bf16[4,256,256]{2,1,0:T(8,128)(2,1)} %collective-permute-done.2, s32[]{:T(128)S(6)} %select_n.54, bf16[4,256,256]{2,1,0:T(8,128)(2,1)} %collective-permute-done.1), kind=kOutput, calls=%fused_computation.68 | convolution fusion | flops 605159424 | bytes 3539968 | tf_op jit(solution)/shard_map/bd,vbc->vdc/dot_general | solution.py:29
  155.1 4.6 %collective-permute-start.8 = (bf16[9,256,256]{1,2,0:T(8,128)(2,1)}, bf16[9,256,256]{1,2,0:T(8,128)(2,1)}, u32[]{:S(2)}, u32[]{:S(2)}) collective-permute-start(bf16[9,256,256]{1,2,0:T(8,128)(2,1)} %fusion.59), channel_id=1, source_target_pairs={{0,2},{2,4},{4,6},{1,3},{3,5},{5,7},{8,10},{10,12},{12,14},{9,11},... | collective-permute-start | bytes 3538952 | tf_op jit(solution)/shard_map/ppermute | solution.py:50
  163.1 4.1 %fusion.60 = bf16[9,256,256]{1,2,0:T(8,128)(2,1)} fusion(bf16[9,256,256]{2,0,1:T(8,128)(2,1)} %fusion.51, bf16[4,256,256]{2,1,0:T(8,128)(2,1)} %collective-permute-done.2, s32[]{:T(128)S(6)} %select_n.58, bf16[4,256,256]{2,1,0:T(8,128)(2,1)} %collective-permute-done.1), kind=kOutput, calls=%fused_computation.69 | convolution fusion | flops 605159424 | bytes 3539968 | tf_op jit(solution)/shard_map/bd,vbc->vdc/dot_general | solution.py:29
  170.2 5.5 %collective-permute-start.10 = (bf16[9,256,256]{1,2,0:T(8,128)(2,1)}, bf16[9,256,256]{1,2,0:T(8,128)(2,1)}, u32[]{:S(2)}, u32[]{:S(2)}) collective-permute-start(bf16[9,256,256]{1,2,0:T(8,128)(2,1)} %fusion.60), channel_id=1, source_target_pairs={{0,4},{1,5},{8,12},{9,13},{16,20},{17,21},{24,28},{25,29}} | collective-permute-start | bytes 3538952 | tf_op jit(solution)/shard_map/ppermute | solution.py:52
  179.0 6.4 %collective-permute-done.8 = bf16[9,256,256]{1,2,0:T(8,128)(2,1)} collective-permute-done((bf16[9,256,256]{1,2,0:T(8,128)(2,1)}, bf16[9,256,256]{1,2,0:T(8,128)(2,1)}, u32[]{:S(2)}, u32[]{:S(2)}) %collective-permute-start.8) | collective-permute-done | bytes 1179680 | tf_op jit(solution)/shard_map/ppermute | solution.py:50
  185.4 11.9 %collective-permute-done.9 = bf16[9,256,256]{1,2,0:T(8,128)(2,1)} collective-permute-done((bf16[9,256,256]{1,2,0:T(8,128)(2,1)}, bf16[9,256,256]{1,2,0:T(8,128)(2,1)}, u32[]{:S(2)}, u32[]{:S(2)}) %collective-permute-start.9) | collective-permute-done | bytes 1179680 | tf_op jit(solution)/shard_map/ppermute | solution.py:51
  197.3 4.9 %fusion.33 = bf16[9,256,256]{1,2,0:T(8,128)(2,1)} fusion(bf16[9,256,256]{1,2,0:T(8,128)(2,1)} %collective-permute-done.8, bf16[9,256,256]{1,2,0:T(8,128)(2,1)} %collective-permute-done.9, bf16[9,256,256]{2,0,1:T(8,128)(2,1)} %fusion.54, f32[]{:T(128)S(6)} %sub.9, f32[]{:T(128)S(6)} %sub.8, bf16[4,256,256]{2,1,0:T(8,128)(2,1)} %collective-permute-done.2, ...), kind=kOutput, calls=%fused_computation.41 | convolution fusion | flops 609878016 | bytes 5900288 | tf_op jit(solution)/shard_map/bd,vbc->vdc/dot_general | solution.py:29
  210.7 38.0 %collective-permute-done.12 = bf16[9,256,256]{1,2,0:T(8,128)(2,1)} collective-permute-done((bf16[9,256,256]{1,2,0:T(8,128)(2,1)}, bf16[9,256,256]{1,2,0:T(8,128)(2,1)}, u32[]{:S(2)}, u32[]{:S(2)}) %collective-permute-start.12) | collective-permute-done | bytes 1179680 | tf_op jit(solution)/shard_map/ppermute | solution.py:60
  248.7 3.9 %fusion.61 = bf16[1,9,1,256,256]{3,4,1,2,0:T(8,128)(2,1)S(1)} fusion(bf16[9,256,256]{1,2,0:T(8,128)(2,1)} %collective-permute-done.12, bf16[9,256,256]{1,2,0:T(8,128)(2,1)} %collective-permute-done.9, bf16[9,256,256]{1,2,0:T(8,128)(2,1)} %collective-permute-done.8, bf16[9,256,256]{2,1,0:T(8,128)(2,1)S(1)} %convolution_convert_fusion.6, ...), kind=kLoop, calls=%fused_computation.70 | loop fusion | flops 8257536 | bytes 8519688 | tf_op jit(solution)/shard_map/broadcast_in_dim | solution.py:100
  254.1 26.4 %collective-permute-done.13 = bf16[1,9,1,256,256]{3,4,1,2,0:T(8,128)(2,1)S(1)} collective-permute-done((bf16[1,9,1,256,256]{3,4,1,2,0:T(8,128)(2,1)S(1)}, bf16[1,9,1,256,256]{3,4,1,2,0:T(8,128)(2,1)S(1)}, u32[]{:S(2)}, u32[]{:S(2)}) %collective-permute-start.13) | collective-permute-done | bytes 1179680 | tf_op jit(solution)/shard_map/ppermute | solution.py:19
  (52 shorter events, 44.0 us)
Async XLA Ops:
  6.5 3.5 %copy-start.6 = (s32[4]{0:T(128)S(1)}, s32[4]{0:T(128)}, u32[]{:S(2)}) copy-start(s32[4]{0:T(128)} %constant.76.clone) | copy-start | bytes 52
  6.5 5.5 %copy-start.5 = (s32[4]{0:T(128)S(1)}, s32[4]{0:T(128)}, u32[]{:S(2)}) copy-start(s32[4]{0:T(128)} %constant.75.clone) | copy-start | bytes 52
  6.5 7.5 %copy-start.2 = (bf16[1,18,9,4]{1,3,2,0:T(4,128)(2,1)S(1)}, bf16[1,18,9,4]{1,3,2,0:T(4,128)(2,1)}, u32[]{:S(2)}) copy-start(bf16[1,18,9,4]{1,3,2,0:T(4,128)(2,1)} %param.14) | copy-start | bytes 3892
  6.5 17.2 %all-gather.3.cloned.1.call-start = ((), (), s32[]{:S(2)}) async-start(), calls=%async_computation | async-start | bytes 3538944 | tf_op jit(solution)/shard_map/all_gather | solution.py:44
  9.9 136.0 %all-gather.5.cloned.1.call-start = ((), (), s32[]{:S(2)}) async-start(), calls=%async_computation.1 | async-start | bytes 3538944 | tf_op jit(solution)/shard_map/all_gather | solution.py:44
  15.4 13.2 %copy-start.3 = (bf16[1,1,4,256,256]{4,3,2,1,0:T(8,128)(2,1)S(1)}, bf16[1,1,4,256,256]{4,3,2,1,0:T(8,128)(2,1)}, u32[]{:S(2)}) copy-start(bf16[1,1,4,256,256]{4,3,2,1,0:T(8,128)(2,1)} %param.13) | copy-start | bytes 1572868
  28.7 8.8 %copy-start = (bf16[18,256,256]{2,1,0:T(8,128)(2,1)S(1)}, bf16[18,256,256]{2,1,0:T(8,128)(2,1)}, u32[]{:S(2)}) copy-start(bf16[18,256,256]{2,1,0:T(8,128)(2,1)} %all-gather.3.cloned.1.call-done) | copy-start | bytes 7077892
  32.8 45.7 %collective-permute-start = (bf16[9,256,256]{1,2,0:T(8,128)(2,1)}, bf16[9,256,256]{1,2,0:T(8,128)(2,1)}, u32[]{:S(2)}, u32[]{:S(2)}) collective-permute-start(bf16[9,256,256]{1,2,0:T(8,128)(2,1)} %fusion.57), channel_id=1, source_target_pairs={{0,2},{2,4},{4,6},{1,3},{3,5},{5,7},{8,10},{10,12},{12,14},{9,11},... | collective-permute-start | bytes 3538952 | tf_op jit(solution)/shard_map/ppermute | solution.py:50
  40.8 9.8 %copy-start.4 = (s32[4]{0:T(128)S(1)}, s32[4]{0:T(128)}, u32[]{:S(2)}) copy-start(s32[4]{0:T(128)} %constant.77.clone) | copy-start | bytes 52
  44.9 33.7 %collective-permute-start.4 = (bf16[9,256,256]{1,2,0:T(8,128)(2,1)}, bf16[9,256,256]{1,2,0:T(8,128)(2,1)}, u32[]{:S(2)}, u32[]{:S(2)}) collective-permute-start(bf16[9,256,256]{1,2,0:T(8,128)(2,1)} %fusion.58), channel_id=1, source_target_pairs={{6,4},{4,2},{2,0},{7,5},{5,3},{3,1},{14,12},{12,10},{10,8},{15,13}... | collective-permute-start | bytes 3538952 | tf_op jit(solution)/shard_map/ppermute | solution.py:51
  46.1 30.7 %collective-permute-start.2 = (bf16[4,256,256]{2,1,0:T(8,128)(2,1)S(1)}, bf16[4,256,256]{2,1,0:T(8,128)(2,1)}, u32[]{:S(2)}, u32[]{:S(2)}) collective-permute-start(bf16[4,256,256]{2,1,0:T(8,128)(2,1)S(1)} %bitcast.136), channel_id=1, source_target_pairs={{0,24},{8,0},{16,8},{24,16},{1,25},{9,1},{17,9},{25,17},{2,26},{10... | collective-permute-start | bytes 1572872 | tf_op jit(solution)/shard_map/ppermute | solution.py:19
  48.6 30.0 %collective-permute-start.1 = (bf16[4,256,256]{2,1,0:T(8,128)(2,1)}, bf16[4,256,256]{2,1,0:T(8,128)(2,1)}, u32[]{:S(2)}, u32[]{:S(2)}) collective-permute-start(bf16[4,256,256]{2,1,0:T(8,128)(2,1)} %bitcast.137), channel_id=1, source_target_pairs={{0,24},{8,0},{16,8},{24,16},{1,25},{9,1},{17,9},{25,17},{2,26},{10... | collective-permute-start | bytes 1572872 | tf_op jit(solution)/shard_map/ppermute | solution.py:19
  49.1 22.5 %collective-permute-start.3 = (bf16[18,9,4]{0,1,2:T(8,128)(2,1)S(1)}, bf16[18,9,4]{0,1,2:T(8,128)(2,1)S(1)}, u32[]{:S(2)}, u32[]{:S(2)}) collective-permute-start(bf16[18,9,4]{0,1,2:T(8,128)(2,1)S(1)} %bitcast.134), channel_id=1, source_target_pairs={{0,24},{8,0},{16,8},{24,16},{1,25},{9,1},{17,9},{25,17},{2,26},{10... | collective-permute-start | bytes 3896 | tf_op jit(solution)/shard_map/ppermute | solution.py:19
  71.6 31.0 %collective-permute-start.5 = (bf16[9,256,256]{1,2,0:T(8,128)(2,1)}, bf16[9,256,256]{1,2,0:T(8,128)(2,1)}, u32[]{:S(2)}, u32[]{:S(2)}) collective-permute-start(bf16[9,256,256]{1,2,0:T(8,128)(2,1)} %fusion.58), channel_id=1, source_target_pairs={{0,4},{1,5},{8,12},{9,13},{16,20},{17,21},{24,28},{25,29}} | collective-permute-start | bytes 3538952 | tf_op jit(solution)/shard_map/ppermute | solution.py:52
  76.9 25.7 %collective-permute-start.6 = (bf16[9,256,256]{1,2,0:T(8,128)(2,1)}, bf16[9,256,256]{1,2,0:T(8,128)(2,1)}, u32[]{:S(2)}, u32[]{:S(2)}) collective-permute-start(bf16[9,256,256]{1,2,0:T(8,128)(2,1)} %fusion.57), channel_id=1, source_target_pairs={{6,2},{7,3},{14,10},{15,11},{22,18},{23,19},{30,26},{31,27}} | collective-permute-start | bytes 3538952 | tf_op jit(solution)/shard_map/ppermute | solution.py:53
  83.4 46.9 %collective-permute-start.7 = (bf16[9,256,256]{1,2,0:T(8,128)(2,1)}, bf16[9,256,256]{1,2,0:T(8,128)(2,1)}, u32[]{:S(2)}, u32[]{:S(2)}) collective-permute-start(bf16[9,256,256]{1,2,0:T(8,128)(2,1)} %fusion.24), channel_id=1, source_target_pairs={{0,2},{2,6},{6,4},{4,0},{1,3},{3,7},{7,5},{5,1},{8,10},{10,14},{14... | collective-permute-start | bytes 3538952 | tf_op jit(solution)/shard_map/ppermute | solution.py:60
  150.9 8.9 %copy-start.1 = (bf16[18,256,256]{2,1,0:T(8,128)(2,1)S(1)}, bf16[18,256,256]{2,1,0:T(8,128)(2,1)}, u32[]{:S(2)}) copy-start(bf16[18,256,256]{2,1,0:T(8,128)(2,1)} %all-gather.5.cloned.1.call-done) | copy-start | bytes 7077892
  155.1 30.3 %collective-permute-start.8 = (bf16[9,256,256]{1,2,0:T(8,128)(2,1)}, bf16[9,256,256]{1,2,0:T(8,128)(2,1)}, u32[]{:S(2)}, u32[]{:S(2)}) collective-permute-start(bf16[9,256,256]{1,2,0:T(8,128)(2,1)} %fusion.59), channel_id=1, source_target_pairs={{0,2},{2,4},{4,6},{1,3},{3,5},{5,7},{8,10},{10,12},{12,14},{9,11},... | collective-permute-start | bytes 3538952 | tf_op jit(solution)/shard_map/ppermute | solution.py:50
  167.2 30.1 %collective-permute-start.9 = (bf16[9,256,256]{1,2,0:T(8,128)(2,1)}, bf16[9,256,256]{1,2,0:T(8,128)(2,1)}, u32[]{:S(2)}, u32[]{:S(2)}) collective-permute-start(bf16[9,256,256]{1,2,0:T(8,128)(2,1)} %fusion.60), channel_id=1, source_target_pairs={{6,4},{4,2},{2,0},{7,5},{5,3},{3,1},{14,12},{12,10},{10,8},{15,13}... | collective-permute-start | bytes 3538952 | tf_op jit(solution)/shard_map/ppermute | solution.py:51
  168.5 40.5 %collective-permute-start.11 = (bf16[9,256,256]{1,2,0:T(8,128)(2,1)}, bf16[9,256,256]{1,2,0:T(8,128)(2,1)}, u32[]{:S(2)}, u32[]{:S(2)}) collective-permute-start(bf16[9,256,256]{1,2,0:T(8,128)(2,1)} %fusion.59), channel_id=1, source_target_pairs={{6,2},{7,3},{14,10},{15,11},{22,18},{23,19},{30,26},{31,27}} | collective-permute-start | bytes 3538952 | tf_op jit(solution)/shard_map/ppermute | solution.py:53
  170.2 40.5 %collective-permute-start.10 = (bf16[9,256,256]{1,2,0:T(8,128)(2,1)}, bf16[9,256,256]{1,2,0:T(8,128)(2,1)}, u32[]{:S(2)}, u32[]{:S(2)}) collective-permute-start(bf16[9,256,256]{1,2,0:T(8,128)(2,1)} %fusion.60), channel_id=1, source_target_pairs={{0,4},{1,5},{8,12},{9,13},{16,20},{17,21},{24,28},{25,29}} | collective-permute-start | bytes 3538952 | tf_op jit(solution)/shard_map/ppermute | solution.py:52
  202.2 46.5 %collective-permute-start.12 = (bf16[9,256,256]{1,2,0:T(8,128)(2,1)}, bf16[9,256,256]{1,2,0:T(8,128)(2,1)}, u32[]{:S(2)}, u32[]{:S(2)}) collective-permute-start(bf16[9,256,256]{1,2,0:T(8,128)(2,1)} %fusion.33), channel_id=1, source_target_pairs={{0,2},{2,6},{6,4},{4,0},{1,3},{3,7},{7,5},{5,1},{8,10},{10,14},{14... | collective-permute-start | bytes 3538952 | tf_op jit(solution)/shard_map/ppermute | solution.py:60
  252.6 28.0 %collective-permute-start.13 = (bf16[1,9,1,256,256]{3,4,1,2,0:T(8,128)(2,1)S(1)}, bf16[1,9,1,256,256]{3,4,1,2,0:T(8,128)(2,1)S(1)}, u32[]{:S(2)}, u32[]{:S(2)}) collective-permute-start(bf16[1,9,1,256,256]{3,4,1,2,0:T(8,128)(2,1)S(1)} %fusion.61), channel_id=1, source_target_pairs={{0,16},{8,24},{16,0},{24,8},{1,17},{9,25},{17,1},{25,9},{2,18},{10... | collective-permute-start | bytes 3538952 | tf_op jit(solution)/shard_map/ppermute | solution.py:19
Sparse Core Ops, SparseCore 0:
  10.1 13.6 all-gather.2
  135.9 10.0 all-gather.4

commit v3 on v2

--- a/solution.py
+++ b/solution.py
@@ -47,11 +47,14 @@
     zero = jnp.zeros((), f32)
     slot_a = term(gathered, *pick(SLOT_A, sector, ket, bra, mpo))
     slot_b = term(gathered, *pick(SLOT_B, sector, ket, bra, mpo))
+    held, slot_a, slot_b = lax.optimization_barrier((held, slot_a, slot_b))
+    middle_right = lax.ppermute(slot_b, "sector", ((0, 2),))
+    middle_left = lax.ppermute(slot_a, "sector", ((3, 1),))
     got_right = lax.ppermute(slot_a, "sector", RIGHT)
     got_left = lax.ppermute(slot_b, "sector", LEFT)
-    got_middle = lax.ppermute(slot_b, "sector", ((0, 2),))
-    got_middle = got_middle + lax.ppermute(slot_a, "sector", ((3, 1),))
-    got_right, held = lax.optimization_barrier((got_right, held))
+    got = lax.optimization_barrier((got_right, got_left, middle_right, middle_left))
+    got_right, got_left, middle_right, middle_left = got
+    got_middle = middle_right + middle_left
     third = term(gathered, *pick(LAST_P, sector, ket, bra, mpo))
     keep_right = jnp.where(sector == 1, zero, one)
     keep_left = jnp.where(sector == 2, zero, one)

time: 289 us -> 293 us (1.014)
  starting transfers between devices: 32.5 us -> 39.4 us
  waiting for transfers between devices: 159 us -> 156 us
    ppermute x4, waiting for transfers between devices: 15 us -> 49.4 us  [the longest x2 49.4 us: advance_line(): middle_right = lax.ppermute(slot_b, 'sector', ((0, 2),))]
    ppermute x2, waiting for transfers between devices: 65.7 us -> 42.3 us  [advance_line(): got_last = lax.ppermute(send.astype(jnp.bfloat16), 'sector', LAST)]
    ppermute x2, waiting for transfers between devices: 6.4 us -> 25.9 us  [advance_line(): got_right = lax.ppermute(slot_a, 'sector', RIGHT)]
    ppermute x4, waiting for transfers between devices: 41.4 us -> 24.9 us  [shifted(): return lax.ppermute(value, axis, pairs)]
    ppermute x2, waiting for transfers between devices: 11.9 us -> 0.01 us  [advance_line(): got_left = lax.ppermute(slot_b, 'sector', LEFT)]
    all_gather x2, waiting for transfers between devices: 18.5 us -> 13.5 us  [advance_line(): gathered = lax.all_gather(current, 'chan', axis=0, tiled=True)]
    ppermute x2, starting transfers between devices: 0.51 us -> 4.06 us  [advance_line(): got_last = lax.ppermute(send.astype(jnp.bfloat16), 'sector', LAST)]
  transfers between devices with their start and end apart: 16 -> 16, of which waited for: 10 -> 9; matrix products, arithmetic and copies ran while one was open for 16% -> 13% of each run, Pallas kernels for 0% -> 0%
where the time goes in v3:
time: 293 us; the launch traced here: 292 us
  waiting for transfers between devices  156 us (53%)
  matrix products  61.4 us (21%)
  starting transfers between devices  39.4 us (13%)
  between operations  19.9 us (7%)
  other arithmetic  10.2 us (3%)
  local copies, waits for them, and re-layouts  5.11 us (2%)
    ppermute x2, waiting for transfers between devices, advance_line(): middle_right = lax.ppermute(slot_b, 'sector', ((0, 2),))  49.4 us
    ppermute x2, waiting for transfers between devices, advance_line(): got_last = lax.ppermute(send.astype(jnp.bfloat16), 'sector', LAST)  42.3 us
    dot_general x8, matrix products, term(): jnp.einsum('bd,vbc->vdc', bra_p, rotated, preferred_element_type=jnp.floa...  31.9 us
    dot_general x8, matrix products, term(): jnp.einsum('wv,wba->vba', mpo_p, gathered, preferred_element_type=jnp.flo...  29.4 us
    ppermute x2, waiting for transfers between devices, advance_line(): got_right = lax.ppermute(slot_a, 'sector', RIGHT)  25.9 us
    ppermute x4, waiting for transfers between devices, shifted(): return lax.ppermute(value, axis, pairs)  24.9 us
    all_gather x2, waiting for transfers between devices, advance_line(): gathered = lax.all_gather(current, 'chan', axis=0, tiled=True)  13.5 us
    ppermute x2, starting transfers between devices, advance_line(): middle_right = lax.ppermute(slot_b, 'sector', ((0, 2),))  13.1 us
  transfers between devices with their start and end apart: 16, of which 9 were waited for; matrix products, arithmetic and copies ran while one was open for 13% of the time, Pallas kernels for 0%

profile of v3, /device:TPU:0, one launch (start us, length us, event | category | flops | bytes accessed | tf_op | source)
XLA Modules:
  0.0 292.0 jit_solution(17849878971171603143)
XLA Ops:
  10.1 3.9 %collective-permute-start.2 = (bf16[18,9,4]{0,1,2:T(8,128)(2,1)S(1)}, bf16[18,9,4]{0,1,2:T(8,128)(2,1)S(1)}, u32[]{:S(2)}, u32[]{:S(2)}) collective-permute-start(bf16[18,9,4]{0,1,2:T(8,128)(2,1)S(1)} %bitcast.133), channel_id=1, source_target_pairs={{0,24},{8,0},{16,8},{24,16},{1,25},{9,1},{17,9},{25,17},{2,26},{10... | collective-permute-start | bytes 3896 | tf_op jit(solution)/shard_map/ppermute | solution.py:19
  23.8 5.1 %fusion.37 = bf16[9,256,256]{2,0,1:T(8,128)(2,1)} fusion(bf16[18,256,256]{2,1,0:T(8,128)(2,1)} %all-gather.3.cloned.1.call-done, bf16[1,18,9,4]{1,2,3,0:T(8,128)(2,1)S(1)} %copy.117, s32[]{:T(128)S(6)} %select_n.56), kind=kOutput, calls=%fused_computation.44 | convolution fusion | flops 21823488 | bytes 3543044 | tf_op jit(solution)/shard_map/wv,wba->vba/dot_general | solution.py:23
  32.2 4.0 %fusion.58 = bf16[9,256,256]{1,2,0:T(8,128)(2,1)} fusion(bf16[9,256,256]{2,0,1:T(8,128)(2,1)} %fusion.37, bf16[1,1,4,256,256]{4,3,2,1,0:T(8,128)(2,1)S(1)} %copy-done.3, s32[]{:T(128)S(6)} %select_n.56, bf16[1,1,4,256,256]{4,3,2,1,0:T(8,128)(2,1)} %param.12), kind=kOutput, calls=%fused_computation.67 | convolution fusion | flops 605159424 | bytes 3539968 | tf_op jit(solution)/shard_map/bd,vbc->vdc/dot_general | solution.py:29
  36.2 4.0 %fusion.57 = bf16[9,256,256]{1,2,0:T(8,128)(2,1)} fusion(bf16[9,256,256]{2,0,1:T(8,128)(2,1)} %fusion.34, bf16[1,1,4,256,256]{4,3,2,1,0:T(8,128)(2,1)S(1)} %copy-done.3, s32[]{:T(128)S(6)} %select_n.54, bf16[1,1,4,256,256]{4,3,2,1,0:T(8,128)(2,1)} %param.12), kind=kOutput, calls=%fused_computation.66 | convolution fusion | flops 605159424 | bytes 3539968 | tf_op jit(solution)/shard_map/bd,vbc->vdc/dot_general | solution.py:29
  42.0 4.3 %collective-permute-start.3 = (bf16[9,256,256]{1,2,0:T(8,128)(2,1)}, bf16[9,256,256]{1,2,0:T(8,128)(2,1)}, u32[]{:S(2)}, u32[]{:S(2)}) collective-permute-start(bf16[9,256,256]{1,2,0:T(8,128)(2,1)} %fusion.57), channel_id=1, source_target_pairs={{0,2},{2,4},{4,6},{1,3},{3,5},{5,7},{8,10},{10,12},{12,14},{9,11},... | collective-permute-start | bytes 3538952 | tf_op jit(solution)/shard_map/ppermute | solution.py:53
  46.2 6.5 %collective-permute-start.5 = (bf16[9,256,256]{1,2,0:T(8,128)(2,1)}, bf16[9,256,256]{1,2,0:T(8,128)(2,1)}, u32[]{:S(2)}, u32[]{:S(2)}) collective-permute-start(bf16[9,256,256]{1,2,0:T(8,128)(2,1)} %fusion.58), channel_id=1, source_target_pairs={{0,4},{1,5},{8,12},{9,13},{16,20},{17,21},{24,28},{25,29}} | collective-permute-start | bytes 3538952 | tf_op jit(solution)/shard_map/ppermute | solution.py:51
  60.1 11.7 %collective-permute-done.3 = bf16[9,256,256]{1,2,0:T(8,128)(2,1)} collective-permute-done((bf16[9,256,256]{1,2,0:T(8,128)(2,1)}, bf16[9,256,256]{1,2,0:T(8,128)(2,1)}, u32[]{:S(2)}, u32[]{:S(2)}) %collective-permute-start.3) | collective-permute-done | bytes 1179680 | tf_op jit(solution)/shard_map/ppermute | solution.py:53
  71.8 24.7 %collective-permute-done.5 = bf16[9,256,256]{1,2,0:T(8,128)(2,1)} collective-permute-done((bf16[9,256,256]{1,2,0:T(8,128)(2,1)}, bf16[9,256,256]{1,2,0:T(8,128)(2,1)}, u32[]{:S(2)}, u32[]{:S(2)}) %collective-permute-start.5) | collective-permute-done | bytes 1179680 | tf_op jit(solution)/shard_map/ppermute | solution.py:51
  96.5 4.8 %fusion.24 = bf16[9,256,256]{1,2,0:T(8,128)(2,1)} fusion(bf16[9,256,256]{1,2,0:T(8,128)(2,1)} %collective-permute-done.3, bf16[9,256,256]{1,2,0:T(8,128)(2,1)} %collective-permute-done.4, bf16[9,256,256]{2,0,1:T(8,128)(2,1)} %fusion.42, f32[]{:T(128)S(6)} %sub.9, f32[]{:T(128)S(6)} %sub.8, bf16[1,1,4,256,256]{4,3,2,1,0:T(8,128)(2,1)S(1)} %copy-done.3, ...), kind=kOutput, calls=%fused_computation.32 | convolution fusion | flops 609878016 | bytes 5900288 | tf_op jit(solution)/shard_map/bd,vbc->vdc/dot_general | solution.py:29
  109.2 21.4 %collective-permute-done.7 = bf16[9,256,256]{1,2,0:T(8,128)(2,1)} collective-permute-done((bf16[9,256,256]{1,2,0:T(8,128)(2,1)}, bf16[9,256,256]{1,2,0:T(8,128)(2,1)}, u32[]{:S(2)}, u32[]{:S(2)}) %collective-permute-start.7) | collective-permute-done | bytes 1179680 | tf_op jit(solution)/shard_map/ppermute | solution.py:63
  130.6 3.9 %fusion.21 = bf16[9,256,256]{1,2,0:T(8,128)(2,1)S(1)} fusion(bf16[9,256,256]{1,2,0:T(8,128)(2,1)} %collective-permute-done.3, bf16[9,256,256]{1,2,0:T(8,128)(2,1)} %collective-permute-done.4, bf16[9,256,256]{2,1,0:T(8,128)(2,1)S(1)} %convolution_convert_fusion.10, bf16[9,256,256]{1,2,0:T(8,128)(2,1)} %collective-permute-done.7, ...), kind=kLoop, calls=%fused_computation.29 | loop fusion | flops 8257536 | bytes 8519688 | tf_op jit(solution)/shard_map/convert_element_type | solution.py:68
  136.0 10.4 %all-gather.5.cloned.1.call-done = bf16[18,256,256]{2,1,0:T(8,128)(2,1)} async-done(((bf16[9,256,256]{2,1,0:T(8,128)(2,1)}), bf16[18,256,256]{2,1,0:T(8,128)(2,1)}) %all-gather.5.cloned.1.call-update) | async-done | bytes 2359312 | tf_op jit(solution)/shard_map/all_gather | solution.py:44
  146.4 4.9 %fusion.48 = bf16[9,256,256]{2,0,1:T(8,128)(2,1)} fusion(bf16[18,256,256]{2,1,0:T(8,128)(2,1)} %all-gather.5.cloned.1.call-done, bf16[18,9,4]{0,1,2:T(8,128)(2,1)S(1)} %collective-permute-done.2, s32[]{:T(128)S(6)} %select_n.54), kind=kOutput, calls=%fused_computation.47 | convolution fusion | flops 21823488 | bytes 3543044 | tf_op jit(solution)/shard_map/wv,wba->vba/dot_general | solution.py:23
  151.4 4.2 %fusion.59 = bf16[9,256,256]{1,2,0:T(8,128)(2,1)} fusion(bf16[9,256,256]{2,0,1:T(8,128)(2,1)} %fusion.48, bf16[4,256,256]{2,1,0:T(8,128)(2,1)} %collective-permute-done.1, s32[]{:T(128)S(6)} %select_n.54, bf16[4,256,256]{2,1,0:T(8,128)(2,1)} %collective-permute-done), kind=kOutput, calls=%fused_computation.68 | convolution fusion | flops 605159424 | bytes 3539968 | tf_op jit(solution)/shard_map/bd,vbc->vdc/dot_general | solution.py:29
  158.9 4.1 %fusion.60 = bf16[9,256,256]{1,2,0:T(8,128)(2,1)} fusion(bf16[9,256,256]{2,0,1:T(8,128)(2,1)} %fusion.51, bf16[4,256,256]{2,1,0:T(8,128)(2,1)} %collective-permute-done.1, s32[]{:T(128)S(6)} %select_n.56, bf16[4,256,256]{2,1,0:T(8,128)(2,1)} %collective-permute-done), kind=kOutput, calls=%fused_computation.69 | convolution fusion | flops 605159424 | bytes 3539968 | tf_op jit(solution)/shard_map/bd,vbc->vdc/dot_general | solution.py:29
  164.7 4.3 %collective-permute-start.8 = (bf16[9,256,256]{1,2,0:T(8,128)(2,1)}, bf16[9,256,256]{1,2,0:T(8,128)(2,1)}, u32[]{:S(2)}, u32[]{:S(2)}) collective-permute-start(bf16[9,256,256]{1,2,0:T(8,128)(2,1)} %fusion.59), channel_id=1, source_target_pairs={{0,2},{2,4},{4,6},{1,3},{3,5},{5,7},{8,10},{10,12},{12,14},{9,11},... | collective-permute-start | bytes 3538952 | tf_op jit(solution)/shard_map/ppermute | solution.py:53
  169.0 6.5 %collective-permute-start.10 = (bf16[9,256,256]{1,2,0:T(8,128)(2,1)}, bf16[9,256,256]{1,2,0:T(8,128)(2,1)}, u32[]{:S(2)}, u32[]{:S(2)}) collective-permute-start(bf16[9,256,256]{1,2,0:T(8,128)(2,1)} %fusion.60), channel_id=1, source_target_pairs={{0,4},{1,5},{8,12},{9,13},{16,20},{17,21},{24,28},{25,29}} | collective-permute-start | bytes 3538952 | tf_op jit(solution)/shard_map/ppermute | solution.py:51
  177.0 3.3 %fusion.54 = bf16[9,256,256]{2,0,1:T(8,128)(2,1)} fusion(bf16[18,256,256]{2,1,0:T(8,128)(2,1)S(1)} %copy-done.1, bf16[18,9,4]{0,1,2:T(8,128)(2,1)S(1)} %collective-permute-done.2, s32[]{:T(128)S(6)} %select_n.59), kind=kOutput, calls=%fused_computation.49 | convolution fusion | flops 21823488 | bytes 3543044 | tf_op jit(solution)/shard_map/wv,wba->vba/dot_general | solution.py:23
  180.3 14.2 %collective-permute-done.8 = bf16[9,256,256]{1,2,0:T(8,128)(2,1)} collective-permute-done((bf16[9,256,256]{1,2,0:T(8,128)(2,1)}, bf16[9,256,256]{1,2,0:T(8,128)(2,1)}, u32[]{:S(2)}, u32[]{:S(2)}) %collective-permute-start.8) | collective-permute-done | bytes 1179680 | tf_op jit(solution)/shard_map/ppermute | solution.py:53
  194.6 24.7 %collective-permute-done.10 = bf16[9,256,256]{1,2,0:T(8,128)(2,1)} collective-permute-done((bf16[9,256,256]{1,2,0:T(8,128)(2,1)}, bf16[9,256,256]{1,2,0:T(8,128)(2,1)}, u32[]{:S(2)}, u32[]{:S(2)}) %collective-permute-start.10) | collective-permute-done | bytes 1179680 | tf_op jit(solution)/shard_map/ppermute | solution.py:51
  219.3 4.8 %fusion.33 = bf16[9,256,256]{1,2,0:T(8,128)(2,1)} fusion(bf16[9,256,256]{1,2,0:T(8,128)(2,1)} %collective-permute-done.8, bf16[9,256,256]{1,2,0:T(8,128)(2,1)} %collective-permute-done.9, bf16[9,256,256]{2,0,1:T(8,128)(2,1)} %fusion.54, f32[]{:T(128)S(6)} %sub.9, f32[]{:T(128)S(6)} %sub.8, bf16[4,256,256]{2,1,0:T(8,128)(2,1)} %collective-permute-done.1, ...), kind=kOutput, calls=%fused_computation.41 | convolution fusion | flops 609878016 | bytes 5900288 | tf_op jit(solution)/shard_map/bd,vbc->vdc/dot_general | solution.py:29
  232.5 20.9 %collective-permute-done.12 = bf16[9,256,256]{1,2,0:T(8,128)(2,1)} collective-permute-done((bf16[9,256,256]{1,2,0:T(8,128)(2,1)}, bf16[9,256,256]{1,2,0:T(8,128)(2,1)}, u32[]{:S(2)}, u32[]{:S(2)}) %collective-permute-start.12) | collective-permute-done | bytes 1179680 | tf_op jit(solution)/shard_map/ppermute | solution.py:63
  253.4 3.9 %fusion.61 = bf16[1,9,1,256,256]{3,4,1,2,0:T(8,128)(2,1)S(1)} fusion(bf16[9,256,256]{1,2,0:T(8,128)(2,1)} %collective-permute-done.12, bf16[9,256,256]{1,2,0:T(8,128)(2,1)} %collective-permute-done.9, bf16[9,256,256]{1,2,0:T(8,128)(2,1)} %collective-permute-done.8, bf16[9,256,256]{2,1,0:T(8,128)(2,1)S(1)} %convolution_convert_fusion.6, ...), kind=kLoop, calls=%fused_computation.70 | loop fusion | flops 8257536 | bytes 8519688 | tf_op jit(solution)/shard_map/broadcast_in_dim | solution.py:103
  258.8 24.8 %collective-permute-done.13 = bf16[1,9,1,256,256]{3,4,1,2,0:T(8,128)(2,1)S(1)} collective-permute-done((bf16[1,9,1,256,256]{3,4,1,2,0:T(8,128)(2,1)S(1)}, bf16[1,9,1,256,256]{3,4,1,2,0:T(8,128)(2,1)S(1)}, u32[]{:S(2)}, u32[]{:S(2)}) %collective-permute-start.13) | collective-permute-done | bytes 1179680 | tf_op jit(solution)/shard_map/ppermute | solution.py:19
  (52 shorter events, 46.7 us)
Async XLA Ops:
  6.5 9.4 %copy-start.6 = (s32[4]{0:T(128)S(1)}, s32[4]{0:T(128)}, u32[]{:S(2)}) copy-start(s32[4]{0:T(128)} %constant.76.clone) | copy-start | bytes 52
  6.5 11.2 %copy-start.5 = (s32[4]{0:T(128)S(1)}, s32[4]{0:T(128)}, u32[]{:S(2)}) copy-start(s32[4]{0:T(128)} %constant.75.clone) | copy-start | bytes 52
  6.5 3.5 %copy-start.2 = (bf16[1,18,9,4]{1,3,2,0:T(4,128)(2,1)S(1)}, bf16[1,18,9,4]{1,3,2,0:T(4,128)(2,1)}, u32[]{:S(2)}) copy-start(bf16[1,18,9,4]{1,3,2,0:T(4,128)(2,1)} %param.14) | copy-start | bytes 3892
  6.5 7.5 %copy-start.3 = (bf16[1,1,4,256,256]{4,3,2,1,0:T(8,128)(2,1)S(1)}, bf16[1,1,4,256,256]{4,3,2,1,0:T(8,128)(2,1)}, u32[]{:S(2)}) copy-start(bf16[1,1,4,256,256]{4,3,2,1,0:T(8,128)(2,1)} %param.13) | copy-start | bytes 1572868
  6.5 17.3 %all-gather.3.cloned.1.call-start = ((), (), s32[]{:S(2)}) async-start(), calls=%async_computation | async-start | bytes 3538944 | tf_op jit(solution)/shard_map/all_gather | solution.py:44
  10.0 136.5 %all-gather.5.cloned.1.call-start = ((), (), s32[]{:S(2)}) async-start(), calls=%async_computation.1 | async-start | bytes 3538944 | tf_op jit(solution)/shard_map/all_gather | solution.py:44
  10.1 30.2 %collective-permute-start.2 = (bf16[18,9,4]{0,1,2:T(8,128)(2,1)S(1)}, bf16[18,9,4]{0,1,2:T(8,128)(2,1)S(1)}, u32[]{:S(2)}, u32[]{:S(2)}) collective-permute-start(bf16[18,9,4]{0,1,2:T(8,128)(2,1)S(1)} %bitcast.133), channel_id=1, source_target_pairs={{0,24},{8,0},{16,8},{24,16},{1,25},{9,1},{17,9},{25,17},{2,26},{10... | collective-permute-start | bytes 3896 | tf_op jit(solution)/shard_map/ppermute | solution.py:19
  14.0 26.2 %collective-permute-start.1 = (bf16[4,256,256]{2,1,0:T(8,128)(2,1)S(1)}, bf16[4,256,256]{2,1,0:T(8,128)(2,1)}, u32[]{:S(2)}, u32[]{:S(2)}) collective-permute-start(bf16[4,256,256]{2,1,0:T(8,128)(2,1)S(1)} %bitcast.135), channel_id=1, source_target_pairs={{0,24},{8,0},{16,8},{24,16},{1,25},{9,1},{17,9},{25,17},{2,26},{10... | collective-permute-start | bytes 1572872 | tf_op jit(solution)/shard_map/ppermute | solution.py:19
  14.5 25.7 %collective-permute-start = (bf16[4,256,256]{2,1,0:T(8,128)(2,1)}, bf16[4,256,256]{2,1,0:T(8,128)(2,1)}, u32[]{:S(2)}, u32[]{:S(2)}) collective-permute-start(bf16[4,256,256]{2,1,0:T(8,128)(2,1)} %bitcast), channel_id=1, source_target_pairs={{0,24},{8,0},{16,8},{24,16},{1,25},{9,1},{17,9},{25,17},{2,26},{10... | collective-permute-start | bytes 1572872 | tf_op jit(solution)/shard_map/ppermute | solution.py:19
  23.8 5.1 %copy-start = (bf16[18,256,256]{2,1,0:T(8,128)(2,1)S(1)}, bf16[18,256,256]{2,1,0:T(8,128)(2,1)}, u32[]{:S(2)}) copy-start(bf16[18,256,256]{2,1,0:T(8,128)(2,1)} %all-gather.3.cloned.1.call-done) | copy-start | bytes 7077892
  36.2 17.8 %copy-start.4 = (s32[4]{0:T(128)S(1)}, s32[4]{0:T(128)}, u32[]{:S(2)}) copy-start(s32[4]{0:T(128)} %constant.77.clone) | copy-start | bytes 52
  40.3 19.8 %collective-permute-start.6 = (bf16[9,256,256]{1,2,0:T(8,128)(2,1)}, bf16[9,256,256]{1,2,0:T(8,128)(2,1)}, u32[]{:S(2)}, u32[]{:S(2)}) collective-permute-start(bf16[9,256,256]{1,2,0:T(8,128)(2,1)} %fusion.57), channel_id=1, source_target_pairs={{6,2},{7,3},{14,10},{15,11},{22,18},{23,19},{30,26},{31,27}} | collective-permute-start | bytes 3538952 | tf_op jit(solution)/shard_map/ppermute | solution.py:52
  42.0 29.8 %collective-permute-start.3 = (bf16[9,256,256]{1,2,0:T(8,128)(2,1)}, bf16[9,256,256]{1,2,0:T(8,128)(2,1)}, u32[]{:S(2)}, u32[]{:S(2)}) collective-permute-start(bf16[9,256,256]{1,2,0:T(8,128)(2,1)} %fusion.57), channel_id=1, source_target_pairs={{0,2},{2,4},{4,6},{1,3},{3,5},{5,7},{8,10},{10,12},{12,14},{9,11},... | collective-permute-start | bytes 3538952 | tf_op jit(solution)/shard_map/ppermute | solution.py:53
  46.2 50.3 %collective-permute-start.5 = (bf16[9,256,256]{1,2,0:T(8,128)(2,1)}, bf16[9,256,256]{1,2,0:T(8,128)(2,1)}, u32[]{:S(2)}, u32[]{:S(2)}) collective-permute-start(bf16[9,256,256]{1,2,0:T(8,128)(2,1)} %fusion.58), channel_id=1, source_target_pairs={{0,4},{1,5},{8,12},{9,13},{16,20},{17,21},{24,28},{25,29}} | collective-permute-start | bytes 3538952 | tf_op jit(solution)/shard_map/ppermute | solution.py:51
  52.8 43.7 %collective-permute-start.4 = (bf16[9,256,256]{1,2,0:T(8,128)(2,1)}, bf16[9,256,256]{1,2,0:T(8,128)(2,1)}, u32[]{:S(2)}, u32[]{:S(2)}) collective-permute-start(bf16[9,256,256]{1,2,0:T(8,128)(2,1)} %fusion.58), channel_id=1, source_target_pairs={{6,4},{4,2},{2,0},{7,5},{5,3},{3,1},{14,12},{12,10},{10,8},{15,13}... | collective-permute-start | bytes 3538952 | tf_op jit(solution)/shard_map/ppermute | solution.py:54
  101.3 29.3 %collective-permute-start.7 = (bf16[9,256,256]{1,2,0:T(8,128)(2,1)}, bf16[9,256,256]{1,2,0:T(8,128)(2,1)}, u32[]{:S(2)}, u32[]{:S(2)}) collective-permute-start(bf16[9,256,256]{1,2,0:T(8,128)(2,1)} %fusion.24), channel_id=1, source_target_pairs={{0,2},{2,6},{6,4},{4,0},{1,3},{3,7},{7,5},{5,1},{8,10},{10,14},{14... | collective-permute-start | bytes 3538952 | tf_op jit(solution)/shard_map/ppermute | solution.py:63
  151.4 4.2 %copy-start.1 = (bf16[18,256,256]{2,1,0:T(8,128)(2,1)S(1)}, bf16[18,256,256]{2,1,0:T(8,128)(2,1)}, u32[]{:S(2)}) copy-start(bf16[18,256,256]{2,1,0:T(8,128)(2,1)} %all-gather.5.cloned.1.call-done) | copy-start | bytes 7077892
  163.0 17.3 %collective-permute-start.11 = (bf16[9,256,256]{1,2,0:T(8,128)(2,1)}, bf16[9,256,256]{1,2,0:T(8,128)(2,1)}, u32[]{:S(2)}, u32[]{:S(2)}) collective-permute-start(bf16[9,256,256]{1,2,0:T(8,128)(2,1)} %fusion.59), channel_id=1, source_target_pairs={{6,2},{7,3},{14,10},{15,11},{22,18},{23,19},{30,26},{31,27}} | collective-permute-start | bytes 3538952 | tf_op jit(solution)/shard_map/ppermute | solution.py:52
  164.7 29.8 %collective-permute-start.8 = (bf16[9,256,256]{1,2,0:T(8,128)(2,1)}, bf16[9,256,256]{1,2,0:T(8,128)(2,1)}, u32[]{:S(2)}, u32[]{:S(2)}) collective-permute-start(bf16[9,256,256]{1,2,0:T(8,128)(2,1)} %fusion.59), channel_id=1, source_target_pairs={{0,2},{2,4},{4,6},{1,3},{3,5},{5,7},{8,10},{10,12},{12,14},{9,11},... | collective-permute-start | bytes 3538952 | tf_op jit(solution)/shard_map/ppermute | solution.py:53
  169.0 50.3 %collective-permute-start.10 = (bf16[9,256,256]{1,2,0:T(8,128)(2,1)}, bf16[9,256,256]{1,2,0:T(8,128)(2,1)}, u32[]{:S(2)}, u32[]{:S(2)}) collective-permute-start(bf16[9,256,256]{1,2,0:T(8,128)(2,1)} %fusion.60), channel_id=1, source_target_pairs={{0,4},{1,5},{8,12},{9,13},{16,20},{17,21},{24,28},{25,29}} | collective-permute-start | bytes 3538952 | tf_op jit(solution)/shard_map/ppermute | solution.py:51
  175.5 43.7 %collective-permute-start.9 = (bf16[9,256,256]{1,2,0:T(8,128)(2,1)}, bf16[9,256,256]{1,2,0:T(8,128)(2,1)}, u32[]{:S(2)}, u32[]{:S(2)}) collective-permute-start(bf16[9,256,256]{1,2,0:T(8,128)(2,1)} %fusion.60), channel_id=1, source_target_pairs={{6,4},{4,2},{2,0},{7,5},{5,3},{3,1},{14,12},{12,10},{10,8},{15,13}... | collective-permute-start | bytes 3538952 | tf_op jit(solution)/shard_map/ppermute | solution.py:54
  224.0 29.3 %collective-permute-start.12 = (bf16[9,256,256]{1,2,0:T(8,128)(2,1)}, bf16[9,256,256]{1,2,0:T(8,128)(2,1)}, u32[]{:S(2)}, u32[]{:S(2)}) collective-permute-start(bf16[9,256,256]{1,2,0:T(8,128)(2,1)} %fusion.33), channel_id=1, source_target_pairs={{0,2},{2,6},{6,4},{4,0},{1,3},{3,7},{7,5},{5,1},{8,10},{10,14},{14... | collective-permute-start | bytes 3538952 | tf_op jit(solution)/shard_map/ppermute | solution.py:63
  257.2 26.4 %collective-permute-start.13 = (bf16[1,9,1,256,256]{3,4,1,2,0:T(8,128)(2,1)S(1)}, bf16[1,9,1,256,256]{3,4,1,2,0:T(8,128)(2,1)S(1)}, u32[]{:S(2)}, u32[]{:S(2)}) collective-permute-start(bf16[1,9,1,256,256]{3,4,1,2,0:T(8,128)(2,1)S(1)} %fusion.61), channel_id=1, source_target_pairs={{0,16},{8,24},{16,0},{24,8},{1,17},{9,25},{17,1},{25,9},{2,18},{10... | collective-permute-start | bytes 3538952 | tf_op jit(solution)/shard_map/ppermute | solution.py:19
Sparse Core Ops, SparseCore 0:
  10.1 13.6 all-gather.2
  136.1 10.2 all-gather.4

commit v4 on v3

--- a/solution.py
+++ b/solution.py
@@ -31,6 +31,16 @@
     ).astype(jnp.bfloat16)
 
 
+def chan_gathered(current, mpo):
+    count = lax.axis_size("chan")
+    me = lax.axis_index("chan")
+    width = current.shape[0]
+    held = [current] + [shifted(current, "chan", k) for k in range(1, count)]
+    rows = [(me - k) % count for k in range(count)]
+    order = jnp.concatenate([jnp.arange(width) + r * width for r in rows])
+    return jnp.concatenate(held, axis=0), jnp.take(mpo, order, axis=0)
+
+
 def pick(table, sector, ket, bra, mpo):
     p = jnp.asarray(table, jnp.int32)[sector]
     return (
@@ -41,7 +51,7 @@
 
 
 def advance_line(current, ket, bra, mpo, live_mask, sector, held):
-    gathered = lax.all_gather(current, "chan", axis=0, tiled=True)
+    gathered, mpo = chan_gathered(current, mpo)
     f32 = jnp.float32
     one = jnp.ones((), f32)
     zero = jnp.zeros((), f32)
@@ -70,7 +80,7 @@
 
 def advance_direct(current, ket, bra, mpo, live_mask):
     stride = lax.axis_size("sector") // 2
-    gathered = lax.all_gather(current, "chan", axis=0, tiled=True)
+    gathered, mpo = chan_gathered(current, mpo)
     f32 = jnp.float32
     total = term(gathered, ket[0], bra[0], mpo[:, :, 0]).astype(f32)
     for p, steps in ((1, 1), (2, stride), (3, stride + 1)):

time: 293 us -> 270 us (0.922)
  waiting for transfers between devices: 156 us -> 141 us
  between operations: 19.9 us -> 6.56 us
  matrix products: 61.4 us -> 51.8 us
  local copies, waits for them, and re-layouts: 5.11 us -> 11.3 us
  starting transfers between devices: 39.4 us -> 45.1 us
  other arithmetic: 10.2 us -> 13.3 us
    all_gather x2 -> x0, waiting for transfers between devices: 13.5 us -> none  [advance_line(): gathered = lax.all_gather(current, 'chan', axis=0, tiled=True)]
    ppermute x2, waiting for transfers between devices: 49.4 us -> 41.3 us  [advance_line(): middle_right = lax.ppermute(slot_b, 'sector', ((0, 2),))]
    ppermute x2, starting transfers between devices: 4.06 us -> 12 us  [advance_line(): got_last = lax.ppermute(send.astype(jnp.bfloat16), 'sector', LAST)]
    ppermute x2, waiting for transfers between devices: 0.01 us -> 7.16 us  [advance_line(): got_left = lax.ppermute(slot_b, 'sector', LEFT)]
    dot_general x8, matrix products: 29.4 us -> 22.3 us  [term(): jnp.einsum('wv,wba->vba', mpo_p, gathered, preferred_element_type=jnp.flo...]
    ppermute x2, waiting for transfers between devices: 42.3 us -> 37.1 us  [advance_line(): got_last = lax.ppermute(send.astype(jnp.bfloat16), 'sector', LAST)]
    concatenate x0 -> x1, local copies, waits for them, and re-layouts: none -> 3.68 us  [chan_gathered(): return (jnp.concatenate(held, axis=0), jnp.take(mpo, order, axis=0))]
    ppermute x2, waiting for transfers between devices: 25.9 us -> 29.6 us  [advance_line(): got_right = lax.ppermute(slot_a, 'sector', RIGHT)]
  transfers between devices with their start and end apart: 16 -> 16, of which waited for: 9 -> 10; matrix products, arithmetic and copies ran while one was open for 13% -> 15% of each run, Pallas kernels for 0% -> 0%
where the time goes in v4:
time: 270 us; the launch traced here: 269 us
  waiting for transfers between devices  141 us (52%)
  matrix products  51.8 us (19%)
  starting transfers between devices  45.1 us (17%)
  other arithmetic  13.3 us (5%)
  local copies, waits for them, and re-layouts  11.3 us (4%)
  between operations  6.56 us (2%)
    ppermute x2, waiting for transfers between devices, advance_line(): middle_right = lax.ppermute(slot_b, 'sector', ((0, 2),))  41.3 us
    ppermute x2, waiting for transfers between devices, advance_line(): got_last = lax.ppermute(send.astype(jnp.bfloat16), 'sector', LAST)  37.1 us
    ppermute x2, waiting for transfers between devices, advance_line(): got_right = lax.ppermute(slot_a, 'sector', RIGHT)  29.6 us
    dot_general x8, matrix products, term(): jnp.einsum('bd,vbc->vdc', bra_p, rotated, preferred_element_type=jnp.floa...  29.4 us
    ppermute x6, waiting for transfers between devices, shifted(): return lax.ppermute(value, axis, pairs)  25.8 us
    dot_general x8, matrix products, term(): jnp.einsum('wv,wba->vba', mpo_p, gathered, preferred_element_type=jnp.flo...  22.3 us
    ppermute x2, starting transfers between devices, advance_line(): got_last = lax.ppermute(send.astype(jnp.bfloat16), 'sector', LAST)  12 us
    ppermute x2, starting transfers between devices, advance_line(): middle_right = lax.ppermute(slot_b, 'sector', ((0, 2),))  10.6 us
  transfers between devices with their start and end apart: 16, of which 10 were waited for; matrix products, arithmetic and copies ran while one was open for 15% of the time, Pallas kernels for 0%

profile of v4, /device:TPU:0, one launch (start us, length us, event | category | flops | bytes accessed | tf_op | source)
XLA Modules:
  0.0 268.9 jit_solution(13022396803708674595)
XLA Ops:
  27.6 3.6 %fusion.27 = bf16[9,256,256]{1,2,0:T(8,128)(2,1)} fusion(bf16[9,256,256]{2,0,1:T(8,128)(2,1)} %fusion.4, bf16[1,1,4,256,256]{4,3,2,1,0:T(8,128)(2,1)} %param.15, s32[]{:T(128)S(6)} %select_n.80, bf16[1,1,4,256,256]{4,3,2,1,0:T(8,128)(2,1)} %param.14), kind=kOutput, calls=%fused_computation.63 | convolution fusion | flops 605159424 | bytes 3539968 | tf_op jit(solution)/shard_map/bd,vbc->vdc/dot_general | solution.py:29
  31.3 3.6 %fusion.26 = bf16[9,256,256]{1,2,0:T(8,128)(2,1)} fusion(bf16[9,256,256]{2,0,1:T(8,128)(2,1)} %fusion.6, bf16[1,1,4,256,256]{4,3,2,1,0:T(8,128)(2,1)} %param.15, s32[]{:T(128)S(6)} %select_n.78, bf16[1,1,4,256,256]{4,3,2,1,0:T(8,128)(2,1)} %param.14), kind=kOutput, calls=%fused_computation.62 | convolution fusion | flops 605159424 | bytes 3539968 | tf_op jit(solution)/shard_map/bd,vbc->vdc/dot_general | solution.py:29
  39.8 6.5 %collective-permute-start.6 = (bf16[9,256,256]{1,2,0:T(8,128)(2,1)}, bf16[9,256,256]{1,2,0:T(8,128)(2,1)}, u32[]{:S(2)}, u32[]{:S(2)}) collective-permute-start(bf16[9,256,256]{1,2,0:T(8,128)(2,1)} %fusion.27), channel_id=1, source_target_pairs={{0,4},{1,5},{8,12},{9,13},{16,20},{17,21},{24,28},{25,29}} | collective-permute-start | bytes 3538952 | tf_op jit(solution)/shard_map/ppermute | solution.py:61
  48.0 4.0 %fusion = bf16[9,256,256]{2,0,1:T(8,128)(2,1)} fusion(bf16[18,256,256]{2,1,0:T(8,128)(2,1)S(1)} %pad_maximum_fusion, bf16[18,9,1]{1,2,0:T(2,128)(2,1)} %get-tuple-element.42), kind=kOutput, calls=%fused_computation.2 | convolution fusion | flops 21233664 | bytes 3539268 | tf_op jit(solution)/shard_map/wv,wba->vba/dot_general | solution.py:23
  52.0 13.1 %collective-permute-done.4 = bf16[9,256,256]{1,2,0:T(8,128)(2,1)S(1)} collective-permute-done((bf16[9,256,256]{1,2,0:T(8,128)(2,1)}, bf16[9,256,256]{1,2,0:T(8,128)(2,1)S(1)}, u32[]{:S(2)}, u32[]{:S(2)}) %collective-permute-start.4) | collective-permute-done | bytes 1179680 | tf_op jit(solution)/shard_map/ppermute | solution.py:63
  67.9 21.1 %collective-permute-done.6 = bf16[9,256,256]{1,2,0:T(8,128)(2,1)} collective-permute-done((bf16[9,256,256]{1,2,0:T(8,128)(2,1)}, bf16[9,256,256]{1,2,0:T(8,128)(2,1)}, u32[]{:S(2)}, u32[]{:S(2)}) %collective-permute-start.6) | collective-permute-done | bytes 1179680 | tf_op jit(solution)/shard_map/ppermute | solution.py:61
  89.1 4.2 %fusion.16 = bf16[9,256,256]{1,2,0:T(8,128)(2,1)} fusion(bf16[9,256,256]{1,2,0:T(8,128)(2,1)S(1)} %collective-permute-done.4, bf16[9,256,256]{1,2,0:T(8,128)(2,1)} %collective-permute-done.5, bf16[9,256,256]{2,0,1:T(8,128)(2,1)} %fusion, f32[]{:T(128)S(6)} %sub.14, f32[]{:T(128)S(6)} %sub.13, bf16[1,1,4,256,256]{4,3,2,1,0:T(8,128)(2,1)} %param.15, ...), kind=kOutput, calls=%fused_computation.26 | convolution fusion | flops 609878016 | bytes 5900288 | tf_op jit(solution)/shard_map/bd,vbc->vdc/dot_general | solution.py:29
  93.3 6.7 %collective-permute-start.8 = (bf16[9,256,256]{1,2,0:T(8,128)(2,1)}, bf16[9,256,256]{1,2,0:T(8,128)(2,1)}, u32[]{:S(2)}, u32[]{:S(2)}) collective-permute-start(bf16[9,256,256]{1,2,0:T(8,128)(2,1)} %fusion.16), channel_id=1, source_target_pairs={{0,2},{2,6},{6,4},{4,0},{1,3},{3,7},{7,5},{5,1},{8,10},{10,14},{14... | collective-permute-start | bytes 3538952 | tf_op jit(solution)/shard_map/ppermute | solution.py:73
  103.3 3.7 %convolution_convert_fusion.10 = bf16[9,256,256]{2,1,0:T(8,128)(2,1)} fusion(bf16[9,256,256]{2,0,1:T(8,128)(2,1)} %fusion.2, bf16[1,1,4,256,256]{4,3,2,1,0:T(8,128)(2,1)} %param.15, bf16[1,1,4,256,256]{4,3,2,1,0:T(8,128)(2,1)} %param.14), kind=kOutput, calls=%fused_computation.56 | convolution fusion | flops 605159424 | bytes 3538944 | tf_op jit(solution)/shard_map/bd,vbc->vdc/dot_general | solution.py:29
  107.0 17.1 %collective-permute-done.8 = bf16[9,256,256]{1,2,0:T(8,128)(2,1)} collective-permute-done((bf16[9,256,256]{1,2,0:T(8,128)(2,1)}, bf16[9,256,256]{1,2,0:T(8,128)(2,1)}, u32[]{:S(2)}, u32[]{:S(2)}) %collective-permute-start.8) | collective-permute-done | bytes 1179680 | tf_op jit(solution)/shard_map/ppermute | solution.py:73
  124.1 3.9 %fusion.13 = bf16[9,256,256]{1,2,0:T(8,128)(2,1)S(1)} fusion(bf16[9,256,256]{1,2,0:T(8,128)(2,1)S(1)} %copy-done.2, bf16[9,256,256]{1,2,0:T(8,128)(2,1)} %collective-permute-done.5, bf16[9,256,256]{2,1,0:T(8,128)(2,1)} %convolution_convert_fusion.10, bf16[9,256,256]{1,2,0:T(8,128)(2,1)} %collective-permute-done.8, f32[256,256]{0,1:T(8,128)S(1)} %copy-done, ...), kind=kLoop, calls=%fused_computation.23 | loop fusion | flops 8257536 | bytes 8519688 | tf_op jit(solution)/shard_map/convert_element_type | solution.py:78
  132.5 3.7 %copy.30 = bf16[18,256,256]{2,0,1:T(8,128)(2,1)S(1)} copy(bf16[18,256,256]{1,2,0:T(8,128)(2,1)} %pad_maximum_fusion.1) | data formatting | bytes 4718592 | tf_op jit(solution)/shard_map/concatenate | solution.py:41
  140.3 3.6 %fusion.29 = bf16[9,256,256]{1,2,0:T(8,128)(2,1)} fusion(bf16[9,256,256]{2,0,1:T(8,128)(2,1)} %fusion.81, bf16[4,256,256]{2,1,0:T(8,128)(2,1)} %collective-permute-done.1, s32[]{:T(128)S(6)} %select_n.80, bf16[4,256,256]{2,1,0:T(8,128)(2,1)} %collective-permute-done), kind=kOutput, calls=%fused_computation.65 | convolution fusion | flops 605159424 | bytes 3539968 | tf_op jit(solution)/shard_map/bd,vbc->vdc/dot_general | solution.py:29
  144.0 3.6 %fusion.28 = bf16[9,256,256]{1,2,0:T(8,128)(2,1)} fusion(bf16[9,256,256]{2,0,1:T(8,128)(2,1)} %fusion.83, bf16[4,256,256]{2,1,0:T(8,128)(2,1)} %collective-permute-done.1, s32[]{:T(128)S(6)} %select_n.78, bf16[4,256,256]{2,1,0:T(8,128)(2,1)} %collective-permute-done), kind=kOutput, calls=%fused_computation.64 | convolution fusion | flops 605159424 | bytes 3539968 | tf_op jit(solution)/shard_map/bd,vbc->vdc/dot_general | solution.py:29
  147.6 5.4 %collective-permute-start.10 = (bf16[9,256,256]{1,2,0:T(8,128)(2,1)}, bf16[9,256,256]{1,2,0:T(8,128)(2,1)}, u32[]{:S(2)}, u32[]{:S(2)}) collective-permute-start(bf16[9,256,256]{1,2,0:T(8,128)(2,1)} %fusion.28), channel_id=1, source_target_pairs={{0,2},{2,4},{4,6},{1,3},{3,5},{5,7},{8,10},{10,12},{12,14},{9,11},... | collective-permute-start | bytes 3538952 | tf_op jit(solution)/shard_map/ppermute | solution.py:63
  154.3 4.0 %collective-permute-start.12 = (bf16[9,256,256]{1,2,0:T(8,128)(2,1)}, bf16[9,256,256]{1,2,0:T(8,128)(2,1)}, u32[]{:S(2)}, u32[]{:S(2)}) collective-permute-start(bf16[9,256,256]{1,2,0:T(8,128)(2,1)} %fusion.29), channel_id=1, source_target_pairs={{0,4},{1,5},{8,12},{9,13},{16,20},{17,21},{24,28},{25,29}} | collective-permute-start | bytes 3538952 | tf_op jit(solution)/shard_map/ppermute | solution.py:61
  162.1 16.5 %collective-permute-done.10 = bf16[9,256,256]{1,2,0:T(8,128)(2,1)} collective-permute-done((bf16[9,256,256]{1,2,0:T(8,128)(2,1)}, bf16[9,256,256]{1,2,0:T(8,128)(2,1)}, u32[]{:S(2)}, u32[]{:S(2)}) %collective-permute-start.10) | collective-permute-done | bytes 1179680 | tf_op jit(solution)/shard_map/ppermute | solution.py:63
  178.6 4.3 %collective-permute-done.11 = bf16[9,256,256]{1,2,0:T(8,128)(2,1)} collective-permute-done((bf16[9,256,256]{1,2,0:T(8,128)(2,1)}, bf16[9,256,256]{1,2,0:T(8,128)(2,1)}, u32[]{:S(2)}, u32[]{:S(2)}) %collective-permute-start.11) | collective-permute-done | bytes 1179680 | tf_op jit(solution)/shard_map/ppermute | solution.py:64
  182.9 20.1 %collective-permute-done.12 = bf16[9,256,256]{1,2,0:T(8,128)(2,1)} collective-permute-done((bf16[9,256,256]{1,2,0:T(8,128)(2,1)}, bf16[9,256,256]{1,2,0:T(8,128)(2,1)}, u32[]{:S(2)}, u32[]{:S(2)}) %collective-permute-start.12) | collective-permute-done | bytes 1179680 | tf_op jit(solution)/shard_map/ppermute | solution.py:61
  203.0 4.5 %fusion.25 = bf16[9,256,256]{1,2,0:T(8,128)(2,1)} fusion(bf16[9,256,256]{1,2,0:T(8,128)(2,1)} %collective-permute-done.10, bf16[9,256,256]{1,2,0:T(8,128)(2,1)} %collective-permute-done.11, bf16[9,256,256]{2,0,1:T(8,128)(2,1)} %fusion.79, f32[]{:T(128)S(6)} %sub.14, f32[]{:T(128)S(6)} %sub.13, bf16[4,256,256]{2,1,0:T(8,128)(2,1)} %collective-permute-done.1, ...), kind=kOutput, calls=%fused_computation.35 | convolution fusion | flops 609878016 | bytes 5900288 | tf_op jit(solution)/shard_map/bd,vbc->vdc/dot_general | solution.py:29
  207.5 5.3 %collective-permute-start.14 = (bf16[9,256,256]{1,2,0:T(8,128)(2,1)}, bf16[9,256,256]{1,2,0:T(8,128)(2,1)}, u32[]{:S(2)}, u32[]{:S(2)}) collective-permute-start(bf16[9,256,256]{1,2,0:T(8,128)(2,1)} %fusion.25), channel_id=1, source_target_pairs={{0,2},{2,6},{6,4},{4,0},{1,3},{3,7},{7,5},{5,1},{8,10},{10,14},{14... | collective-permute-start | bytes 3538952 | tf_op jit(solution)/shard_map/ppermute | solution.py:73
  217.5 20.0 %collective-permute-done.14 = bf16[9,256,256]{1,2,0:T(8,128)(2,1)} collective-permute-done((bf16[9,256,256]{1,2,0:T(8,128)(2,1)}, bf16[9,256,256]{1,2,0:T(8,128)(2,1)}, u32[]{:S(2)}, u32[]{:S(2)}) %collective-permute-start.14) | collective-permute-done | bytes 1179680 | tf_op jit(solution)/shard_map/ppermute | solution.py:73
  237.5 3.8 %fusion.30 = bf16[1,9,1,256,256]{3,4,1,2,0:T(8,128)(2,1)S(1)} fusion(bf16[9,256,256]{1,2,0:T(8,128)(2,1)} %collective-permute-done.14, bf16[9,256,256]{1,2,0:T(8,128)(2,1)} %collective-permute-done.11, bf16[9,256,256]{1,2,0:T(8,128)(2,1)} %collective-permute-done.10, bf16[9,256,256]{2,1,0:T(8,128)(2,1)S(1)} %convolution_convert_fusion.6, ...), kind=kLoop, calls=%fused_computation.66 | loop fusion | flops 8257536 | bytes 8519688 | tf_op jit(solution)/shard_map/broadcast_in_dim | solution.py:113
  242.9 24.4 %collective-permute-done.15 = bf16[1,9,1,256,256]{3,4,1,2,0:T(8,128)(2,1)S(1)} collective-permute-done((bf16[1,9,1,256,256]{3,4,1,2,0:T(8,128)(2,1)S(1)}, bf16[1,9,1,256,256]{3,4,1,2,0:T(8,128)(2,1)S(1)}, u32[]{:S(2)}, u32[]{:S(2)}) %collective-permute-start.15) | collective-permute-done | bytes 1179680 | tf_op jit(solution)/shard_map/ppermute | solution.py:19
  (65 shorter events, 55.5 us)
Async XLA Ops:
  0.0 9.7 %copy-start.8 = (s32[4]{0:T(128)S(1)}, s32[4]{0:T(128)}, u32[]{:S(2)}) copy-start(s32[4]{0:T(128)} %constant.105.clone) | copy-start | bytes 52
  0.0 11.7 %copy-start.7 = (s32[4]{0:T(128)S(1)}, s32[4]{0:T(128)}, u32[]{:S(2)}) copy-start(s32[4]{0:T(128)} %constant.106.clone) | copy-start | bytes 52
  0.0 13.5 %copy-start.6 = (s32[4]{0:T(128)S(1)}, s32[4]{0:T(128)}, u32[]{:S(2)}) copy-start(s32[4]{0:T(128)} %constant.107.clone) | copy-start | bytes 52
  3.0 16.4 %collective-permute-start.3 = (bf16[9,256,256]{2,1,0:T(8,128)(2,1)S(1)}, bf16[9,256,256]{2,1,0:T(8,128)(2,1)}, u32[]{:S(2)}, u32[]{:S(2)}) collective-permute-start(bf16[9,256,256]{2,1,0:T(8,128)(2,1)S(1)} %bitcast_select_fusion), channel_id=1, source_target_pairs={{0,1},{1,0},{2,3},{3,2},{4,5},{5,4},{6,7},{7,6},{8,9},{9,8},{10,11... | collective-permute-start | bytes 3538952 | tf_op jit(solution)/shard_map/ppermute | solution.py:19
  4.3 30.6 %collective-permute-start.2 = (bf16[18,9,4]{1,2,0:T(4,128)(2,1)}, bf16[18,9,4]{1,2,0:T(4,128)(2,1)}, u32[]{:S(2)}, u32[]{:S(2)}) collective-permute-start(bf16[18,9,4]{1,2,0:T(4,128)(2,1)} %bitcast.2), channel_id=1, source_target_pairs={{0,24},{8,0},{16,8},{24,16},{1,25},{9,1},{17,9},{25,17},{2,26},{10... | collective-permute-start | bytes 3896 | tf_op jit(solution)/shard_map/ppermute | solution.py:19
  7.8 27.1 %collective-permute-start = (bf16[4,256,256]{2,1,0:T(8,128)(2,1)}, bf16[4,256,256]{2,1,0:T(8,128)(2,1)}, u32[]{:S(2)}, u32[]{:S(2)}) collective-permute-start(bf16[4,256,256]{2,1,0:T(8,128)(2,1)} %bitcast), channel_id=1, source_target_pairs={{0,24},{8,0},{16,8},{24,16},{1,25},{9,1},{17,9},{25,17},{2,26},{10... | collective-permute-start | bytes 1572872 | tf_op jit(solution)/shard_map/ppermute | solution.py:19
  8.3 26.6 %collective-permute-start.1 = (bf16[4,256,256]{2,1,0:T(8,128)(2,1)}, bf16[4,256,256]{2,1,0:T(8,128)(2,1)}, u32[]{:S(2)}, u32[]{:S(2)}) collective-permute-start(bf16[4,256,256]{2,1,0:T(8,128)(2,1)} %bitcast.1), channel_id=1, source_target_pairs={{0,24},{8,0},{16,8},{24,16},{1,25},{9,1},{17,9},{25,17},{2,26},{10... | collective-permute-start | bytes 1572872 | tf_op jit(solution)/shard_map/ppermute | solution.py:19
  15.5 4.0 %copy-start.4 = (pred[18]{0:T(512)(128)(4,1)}, pred[18]{0:T(512)(128)(4,1)S(1)}, u32[]{:S(2)}) copy-start(pred[18]{0:T(512)(128)(4,1)S(1)} %get-tuple-element.36) | copy-start | bytes 58
  34.9 30.2 %collective-permute-start.4 = (bf16[9,256,256]{1,2,0:T(8,128)(2,1)}, bf16[9,256,256]{1,2,0:T(8,128)(2,1)S(1)}, u32[]{:S(2)}, u32[]{:S(2)}) collective-permute-start(bf16[9,256,256]{1,2,0:T(8,128)(2,1)} %fusion.26), channel_id=1, source_target_pairs={{0,2},{2,4},{4,6},{1,3},{3,5},{5,7},{8,10},{10,12},{12,14},{9,11},... | collective-permute-start | bytes 3538952 | tf_op jit(solution)/shard_map/ppermute | solution.py:63
  38.5 29.4 %collective-permute-start.5 = (bf16[9,256,256]{1,2,0:T(8,128)(2,1)}, bf16[9,256,256]{1,2,0:T(8,128)(2,1)}, u32[]{:S(2)}, u32[]{:S(2)}) collective-permute-start(bf16[9,256,256]{1,2,0:T(8,128)(2,1)} %fusion.27), channel_id=1, source_target_pairs={{6,4},{4,2},{2,0},{7,5},{5,3},{3,1},{14,12},{12,10},{10,8},{15,13}... | collective-permute-start | bytes 3538952 | tf_op jit(solution)/shard_map/ppermute | solution.py:64
  39.8 49.3 %collective-permute-start.6 = (bf16[9,256,256]{1,2,0:T(8,128)(2,1)}, bf16[9,256,256]{1,2,0:T(8,128)(2,1)}, u32[]{:S(2)}, u32[]{:S(2)}) collective-permute-start(bf16[9,256,256]{1,2,0:T(8,128)(2,1)} %fusion.27), channel_id=1, source_target_pairs={{0,4},{1,5},{8,12},{9,13},{16,20},{17,21},{24,28},{25,29}} | collective-permute-start | bytes 3538952 | tf_op jit(solution)/shard_map/ppermute | solution.py:61
  46.3 42.8 %collective-permute-start.7 = (bf16[9,256,256]{1,2,0:T(8,128)(2,1)}, bf16[9,256,256]{1,2,0:T(8,128)(2,1)}, u32[]{:S(2)}, u32[]{:S(2)}) collective-permute-start(bf16[9,256,256]{1,2,0:T(8,128)(2,1)} %fusion.26), channel_id=1, source_target_pairs={{6,2},{7,3},{14,10},{15,11},{22,18},{23,19},{30,26},{31,27}} | collective-permute-start | bytes 3538952 | tf_op jit(solution)/shard_map/ppermute | solution.py:62
  65.1 28.2 %copy-start.1 = (bf16[9,256,256]{1,2,0:T(8,128)(2,1)}, bf16[9,256,256]{1,2,0:T(8,128)(2,1)S(1)}, u32[]{:S(2)}) copy-start(bf16[9,256,256]{1,2,0:T(8,128)(2,1)S(1)} %collective-permute-done.4) | copy-start | bytes 3538948
  93.3 30.8 %collective-permute-start.8 = (bf16[9,256,256]{1,2,0:T(8,128)(2,1)}, bf16[9,256,256]{1,2,0:T(8,128)(2,1)}, u32[]{:S(2)}, u32[]{:S(2)}) collective-permute-start(bf16[9,256,256]{1,2,0:T(8,128)(2,1)} %fusion.16), channel_id=1, source_target_pairs={{0,2},{2,6},{6,4},{4,0},{1,3},{3,7},{7,5},{5,1},{8,10},{10,14},{14... | collective-permute-start | bytes 3538952 | tf_op jit(solution)/shard_map/ppermute | solution.py:73
  103.3 20.8 %copy-start = (f32[256,256]{0,1:T(8,128)S(1)}, f32[256,256]{0,1:T(8,128)}, u32[]{:S(2)}) copy-start(f32[256,256]{0,1:T(8,128)} %get-tuple-element.46) | copy-start | bytes 786436
  103.3 20.8 %copy-start.2 = (bf16[9,256,256]{1,2,0:T(8,128)(2,1)S(1)}, bf16[9,256,256]{1,2,0:T(8,128)(2,1)}, u32[]{:S(2)}) copy-start(bf16[9,256,256]{1,2,0:T(8,128)(2,1)} %copy-done.1) | copy-start | bytes 3538948
  124.1 5.2 %copy-start.5 = (pred[18]{0:T(512)(128)(4,1)S(1)}, pred[18]{0:T(512)(128)(4,1)}, u32[]{:S(2)}) copy-start(pred[18]{0:T(512)(128)(4,1)} %copy-done.4) | copy-start | bytes 58
  127.9 2.9 %collective-permute-start.9 = (bf16[9,256,256]{1,2,0:T(8,128)(2,1)S(1)}, bf16[9,256,256]{1,2,0:T(8,128)(2,1)S(1)}, u32[]{:S(2)}, u32[]{:S(2)}) collective-permute-start(bf16[9,256,256]{1,2,0:T(8,128)(2,1)S(1)} %fusion.13), channel_id=1, source_target_pairs={{0,1},{1,0},{2,3},{3,2},{4,5},{5,4},{6,7},{7,6},{8,9},{9,8},{10,11... | collective-permute-start | bytes 3538952 | tf_op jit(solution)/shard_map/ppermute | solution.py:19
  147.6 31.0 %collective-permute-start.10 = (bf16[9,256,256]{1,2,0:T(8,128)(2,1)}, bf16[9,256,256]{1,2,0:T(8,128)(2,1)}, u32[]{:S(2)}, u32[]{:S(2)}) collective-permute-start(bf16[9,256,256]{1,2,0:T(8,128)(2,1)} %fusion.28), channel_id=1, source_target_pairs={{0,2},{2,4},{4,6},{1,3},{3,5},{5,7},{8,10},{10,12},{12,14},{9,11},... | collective-permute-start | bytes 3538952 | tf_op jit(solution)/shard_map/ppermute | solution.py:63
  153.0 29.9 %collective-permute-start.11 = (bf16[9,256,256]{1,2,0:T(8,128)(2,1)}, bf16[9,256,256]{1,2,0:T(8,128)(2,1)}, u32[]{:S(2)}, u32[]{:S(2)}) collective-permute-start(bf16[9,256,256]{1,2,0:T(8,128)(2,1)} %fusion.29), channel_id=1, source_target_pairs={{6,4},{4,2},{2,0},{7,5},{5,3},{3,1},{14,12},{12,10},{10,8},{15,13}... | collective-permute-start | bytes 3538952 | tf_op jit(solution)/shard_map/ppermute | solution.py:64
  154.3 48.8 %collective-permute-start.12 = (bf16[9,256,256]{1,2,0:T(8,128)(2,1)}, bf16[9,256,256]{1,2,0:T(8,128)(2,1)}, u32[]{:S(2)}, u32[]{:S(2)}) collective-permute-start(bf16[9,256,256]{1,2,0:T(8,128)(2,1)} %fusion.29), channel_id=1, source_target_pairs={{0,4},{1,5},{8,12},{9,13},{16,20},{17,21},{24,28},{25,29}} | collective-permute-start | bytes 3538952 | tf_op jit(solution)/shard_map/ppermute | solution.py:61
  158.3 44.7 %collective-permute-start.13 = (bf16[9,256,256]{1,2,0:T(8,128)(2,1)}, bf16[9,256,256]{1,2,0:T(8,128)(2,1)}, u32[]{:S(2)}, u32[]{:S(2)}) collective-permute-start(bf16[9,256,256]{1,2,0:T(8,128)(2,1)} %fusion.28), channel_id=1, source_target_pairs={{6,2},{7,3},{14,10},{15,11},{22,18},{23,19},{30,26},{31,27}} | collective-permute-start | bytes 3538952 | tf_op jit(solution)/shard_map/ppermute | solution.py:62
  207.5 30.0 %collective-permute-start.14 = (bf16[9,256,256]{1,2,0:T(8,128)(2,1)}, bf16[9,256,256]{1,2,0:T(8,128)(2,1)}, u32[]{:S(2)}, u32[]{:S(2)}) collective-permute-start(bf16[9,256,256]{1,2,0:T(8,128)(2,1)} %fusion.25), channel_id=1, source_target_pairs={{0,2},{2,6},{6,4},{4,0},{1,3},{3,7},{7,5},{5,1},{8,10},{10,14},{14... | collective-permute-start | bytes 3538952 | tf_op jit(solution)/shard_map/ppermute | solution.py:73
  241.3 26.0 %collective-permute-start.15 = (bf16[1,9,1,256,256]{3,4,1,2,0:T(8,128)(2,1)S(1)}, bf16[1,9,1,256,256]{3,4,1,2,0:T(8,128)(2,1)S(1)}, u32[]{:S(2)}, u32[]{:S(2)}) collective-permute-start(bf16[1,9,1,256,256]{3,4,1,2,0:T(8,128)(2,1)S(1)} %fusion.30), channel_id=1, source_target_pairs={{0,16},{8,24},{16,0},{24,8},{1,17},{9,25},{17,1},{25,9},{2,18},{10... | collective-permute-start | bytes 3538952 | tf_op jit(solution)/shard_map/ppermute | solution.py:19
  (1 other events, 3.6 us)

commit v5 on v4

--- a/solution.py
+++ b/solution.py
@@ -50,7 +50,7 @@
     )
 
 
-def advance_line(current, ket, bra, mpo, live_mask, sector, held):
+def advance_line(current, ket, bra, mpo, live_mask, sector, held, pieces, finish):
     gathered, mpo = chan_gathered(current, mpo)
     f32 = jnp.float32
     one = jnp.ones((), f32)
@@ -70,12 +70,26 @@
     keep_left = jnp.where(sector == 2, zero, one)
     send = third.astype(f32) + (1 - keep_right) * got_right.astype(f32)
     send = send + (1 - keep_left) * got_left.astype(f32)
-    got_last = lax.ppermute(send.astype(jnp.bfloat16), "sector", LAST)
+    send = send.astype(jnp.bfloat16)
     own = term(gathered, ket[0], bra[0], mpo[:, :, 0])
     total = own.astype(f32) + keep_right * got_right.astype(f32)
-    total = total + keep_left * got_left.astype(f32)
-    total = total + got_middle.astype(f32) + got_last.astype(f32)
-    return (total * live_mask[None]).astype(jnp.bfloat16), held
+    total = total + keep_left * got_left.astype(f32) + got_middle.astype(f32)
+    width = send.shape[0]
+    bounds = [width * k // pieces for k in range(pieces + 1)]
+    results = []
+    piece = None
+    for low, high in zip(bounds[:-1], bounds[1:]):
+        if results:
+            piece, send = lax.optimization_barrier((piece, send))
+            results[-1] = finish(piece)
+        got_last = lax.ppermute(send[low:high], "sector", LAST)
+        if results:
+            results[-1], got_last = lax.optimization_barrier((results[-1], got_last))
+        piece = total[low:high] + got_last.astype(f32)
+        piece = (piece * live_mask[None]).astype(jnp.bfloat16)
+        results.append(None)
+    results[-1] = finish(piece)
+    return results, held
 
 
 def advance_direct(current, ket, bra, mpo, live_mask):
@@ -102,15 +116,23 @@
         ket, bra, mpo = tensors[-1]
         tensors.append(tuple(shifted(t, "site", -1) for t in (ket, bra, mpo)))
     current = jnp.where(live_both, environment[0, :, 0], jnp.zeros((), jnp.bfloat16))
+    def onward(part):
+        return shifted(part[None, :, None], "site", STEPS)
+
     for step in range(STEPS):
         ket, bra, mpo = tensors[step]
+        last = step == STEPS - 1
         if line:
-            current, tensors[step + 1 :] = advance_line(
-                current, ket, bra, mpo, live_mask, sector, tensors[step + 1 :]
+            parts, tensors[step + 1 :] = advance_line(
+                current, ket, bra, mpo, live_mask, sector, tensors[step + 1 :],
+                2 if last else 1, onward if last else (lambda part: part),
             )
         else:
-            current = advance_direct(current, ket, bra, mpo, live_mask)
-    return shifted(current[None, :, None], "site", STEPS)
+            parts = [advance_direct(current, ket, bra, mpo, live_mask)]
+            parts = [onward(parts[0])] if last else parts
+        if not last:
+            current = jnp.concatenate(parts, axis=0)
+    return jnp.concatenate(parts, axis=1)
 
 
 def solution(mesh):

time: 270 us -> 259 us (0.959)
  waiting for transfers between devices: 141 us -> 133 us
  starting transfers between devices: 45.1 us -> 40.8 us
    ppermute x2 -> x3, waiting for transfers between devices: 37.1 us -> 28.2 us  [advance_line(): got_last = lax.ppermute(send[low:high], 'sector', LAST)]
    ppermute x2, waiting for transfers between devices: 7.16 us -> 0.01 us  [advance_line(): got_left = lax.ppermute(slot_b, 'sector', LEFT)]
    ppermute x2, waiting for transfers between devices: 41.3 us -> 48.4 us  [advance_line(): middle_right = lax.ppermute(slot_b, 'sector', ((0, 2),))]
    ppermute x2 -> x3, starting transfers between devices: 12 us -> 5.36 us  [advance_line(): got_last = lax.ppermute(send[low:high], 'sector', LAST)]
    broadcast_in_dim x1, other arithmetic: 3.85 us -> 0.21 us  [onward(): return shifted(part[None, :, None], 'site', STEPS)]
    ppermute x6 -> x7, starting transfers between devices: 7.61 us -> 9.13 us  [shifted(): return lax.ppermute(value, axis, pairs)]
    ppermute x6 -> x7, waiting for transfers between devices: 25.8 us -> 25.4 us  [shifted(): return lax.ppermute(value, axis, pairs)]
  transfers between devices with their start and end apart: 16 -> 18, of which waited for: 10 -> 10; matrix products, arithmetic and copies ran while one was open for 15% -> 16% of each run, Pallas kernels for 0% -> 0%
where the time goes in v5:
time: 259 us
  waiting for transfers between devices  133 us (51%)
  matrix products  54.1 us (21%)
  starting transfers between devices  40.8 us (16%)
  local copies, waits for them, and re-layouts  13.2 us (5%)
  other arithmetic  10.9 us (4%)
  between operations  6.9 us (3%)
    ppermute x2, waiting for transfers between devices, advance_line(): middle_right = lax.ppermute(slot_b, 'sector', ((0, 2),))  48.4 us
    dot_general x8, matrix products, term(): jnp.einsum('bd,vbc->vdc', bra_p, rotated, preferred_element_type=jnp.floa...  31.6 us
    ppermute x2, waiting for transfers between devices, advance_line(): got_right = lax.ppermute(slot_a, 'sector', RIGHT)  30.5 us
    ppermute x3, waiting for transfers between devices, advance_line(): got_last = lax.ppermute(send[low:high], 'sector', LAST)  28.2 us
    ppermute x7, waiting for transfers between devices, shifted(): return lax.ppermute(value, axis, pairs)  25.4 us
    dot_general x8, matrix products, term(): jnp.einsum('wv,wba->vba', mpo_p, gathered, preferred_element_type=jnp.flo...  22.5 us
    ppermute x2, starting transfers between devices, advance_line(): middle_right = lax.ppermute(slot_b, 'sector', ((0, 2),))  12 us
    ppermute x2, starting transfers between devices, advance_line(): got_right = lax.ppermute(slot_a, 'sector', RIGHT)  9.3 us
  transfers between devices with their start and end apart: 18, of which 10 were waited for; matrix products, arithmetic and copies ran while one was open for 16% of the time, Pallas kernels for 0%

profile of v5, /device:TPU:0, one launch (start us, length us, event | category | flops | bytes accessed | tf_op | source)
XLA Modules:
  0.0 258.6 jit_solution(8039543377570455470)
XLA Ops:
  4.3 3.5 %collective-permute-start.2 = (bf16[18,9,4]{1,2,0:T(4,128)(2,1)}, bf16[18,9,4]{1,2,0:T(4,128)(2,1)}, u32[]{:S(2)}, u32[]{:S(2)}) collective-permute-start(bf16[18,9,4]{1,2,0:T(4,128)(2,1)} %bitcast.2), channel_id=1, source_target_pairs={{0,24},{8,0},{16,8},{24,16},{1,25},{9,1},{17,9},{25,17},{2,26},{10... | collective-permute-start | bytes 3896 | tf_op jit(solution)/shard_map/ppermute | solution.py:19
  28.0 3.6 %fusion.24 = bf16[9,256,256]{1,2,0:T(8,128)(2,1)} fusion(bf16[9,256,256]{2,0,1:T(8,128)(2,1)} %fusion.4, bf16[1,1,4,256,256]{4,3,2,1,0:T(8,128)(2,1)} %param.15, s32[]{:T(128)S(6)} %select_n.80, bf16[1,1,4,256,256]{4,3,2,1,0:T(8,128)(2,1)} %param.14), kind=kOutput, calls=%fused_computation.60 | convolution fusion | flops 605159424 | bytes 3539968 | tf_op jit(solution)/shard_map/bd,vbc->vdc/dot_general | solution.py:29
  31.7 3.6 %fusion.23 = bf16[9,256,256]{1,2,0:T(8,128)(2,1)} fusion(bf16[9,256,256]{2,0,1:T(8,128)(2,1)} %fusion.6, bf16[1,1,4,256,256]{4,3,2,1,0:T(8,128)(2,1)} %param.15, s32[]{:T(128)S(6)} %select_n.78, bf16[1,1,4,256,256]{4,3,2,1,0:T(8,128)(2,1)} %param.14), kind=kOutput, calls=%fused_computation.59 | convolution fusion | flops 605159424 | bytes 3539968 | tf_op jit(solution)/shard_map/bd,vbc->vdc/dot_general | solution.py:29
  36.0 5.1 %collective-permute-start.4 = (bf16[9,256,256]{1,2,0:T(8,128)(2,1)}, bf16[9,256,256]{1,2,0:T(8,128)(2,1)}, u32[]{:S(2)}, u32[]{:S(2)}) collective-permute-start(bf16[9,256,256]{1,2,0:T(8,128)(2,1)} %fusion.23), channel_id=1, source_target_pairs={{0,2},{2,4},{4,6},{1,3},{3,5},{5,7},{8,10},{10,12},{12,14},{9,11},... | collective-permute-start | bytes 3538952 | tf_op jit(solution)/shard_map/ppermute | solution.py:63
  41.1 5.5 %collective-permute-start.6 = (bf16[9,256,256]{1,2,0:T(8,128)(2,1)}, bf16[9,256,256]{1,2,0:T(8,128)(2,1)}, u32[]{:S(2)}, u32[]{:S(2)}) collective-permute-start(bf16[9,256,256]{1,2,0:T(8,128)(2,1)} %fusion.24), channel_id=1, source_target_pairs={{0,4},{1,5},{8,12},{9,13},{16,20},{17,21},{24,28},{25,29}} | collective-permute-start | bytes 3538952 | tf_op jit(solution)/shard_map/ppermute | solution.py:61
  47.9 4.0 %fusion = bf16[9,256,256]{2,0,1:T(8,128)(2,1)} fusion(bf16[18,256,256]{2,1,0:T(8,128)(2,1)S(1)} %pad_maximum_fusion, bf16[18,9,1]{1,2,0:T(2,128)(2,1)} %get-tuple-element.50), kind=kOutput, calls=%fused_computation.2 | convolution fusion | flops 21233664 | bytes 3539268 | tf_op jit(solution)/shard_map/wv,wba->vba/dot_general | solution.py:23
  52.0 14.8 %collective-permute-done.4 = bf16[9,256,256]{1,2,0:T(8,128)(2,1)} collective-permute-done((bf16[9,256,256]{1,2,0:T(8,128)(2,1)}, bf16[9,256,256]{1,2,0:T(8,128)(2,1)}, u32[]{:S(2)}, u32[]{:S(2)}) %collective-permute-start.4) | collective-permute-done | bytes 1179680 | tf_op jit(solution)/shard_map/ppermute | solution.py:63
  66.8 23.9 %collective-permute-done.6 = bf16[9,256,256]{1,2,0:T(8,128)(2,1)} collective-permute-done((bf16[9,256,256]{1,2,0:T(8,128)(2,1)}, bf16[9,256,256]{1,2,0:T(8,128)(2,1)}, u32[]{:S(2)}, u32[]{:S(2)}) %collective-permute-start.6) | collective-permute-done | bytes 1179680 | tf_op jit(solution)/shard_map/ppermute | solution.py:61
  90.7 4.5 %fusion.16 = bf16[9,256,256]{1,2,0:T(8,128)(2,1)} fusion(bf16[9,256,256]{1,2,0:T(8,128)(2,1)} %collective-permute-done.4, bf16[9,256,256]{1,2,0:T(8,128)(2,1)} %collective-permute-done.5, bf16[9,256,256]{2,0,1:T(8,128)(2,1)} %fusion, f32[]{:T(128)S(6)} %sub.14, f32[]{:T(128)S(6)} %sub.13, bf16[1,1,4,256,256]{4,3,2,1,0:T(8,128)(2,1)} %param.15, ...), kind=kOutput, calls=%fused_computation.26 | convolution fusion | flops 609878016 | bytes 5900288 | tf_op jit(solution)/shard_map/bd,vbc->vdc/dot_general | solution.py:29
  100.7 3.7 %convolution_convert_fusion.10 = bf16[9,256,256]{2,1,0:T(8,128)(2,1)} fusion(bf16[9,256,256]{2,0,1:T(8,128)(2,1)} %fusion.2, bf16[1,1,4,256,256]{4,3,2,1,0:T(8,128)(2,1)} %param.15, bf16[1,1,4,256,256]{4,3,2,1,0:T(8,128)(2,1)} %param.14), kind=kOutput, calls=%fused_computation.53 | convolution fusion | flops 605159424 | bytes 3538944 | tf_op jit(solution)/shard_map/bd,vbc->vdc/dot_general | solution.py:29
  104.4 19.4 %collective-permute-done.8 = bf16[9,256,256]{1,2,0:T(8,128)(2,1)} collective-permute-done((bf16[9,256,256]{1,2,0:T(8,128)(2,1)}, bf16[9,256,256]{1,2,0:T(8,128)(2,1)}, u32[]{:S(2)}, u32[]{:S(2)}) %collective-permute-start.8) | collective-permute-done | bytes 1179680 | tf_op jit(solution)/shard_map/ppermute | solution.py:85
  123.8 3.9 %fusion.13 = bf16[9,256,256]{1,2,0:T(8,128)(2,1)S(1)} fusion(bf16[9,256,256]{1,2,0:T(8,128)(2,1)} %collective-permute-done.4, bf16[9,256,256]{1,2,0:T(8,128)(2,1)} %collective-permute-done.5, bf16[9,256,256]{2,1,0:T(8,128)(2,1)} %convolution_convert_fusion.10, bf16[9,256,256]{1,2,0:T(8,128)(2,1)} %collective-permute-done.8, f32[256,256]{0,1:T(8,128)S(1)} %copy-done, ...), kind=kLoop, calls=%fused_computation.23 | loop fusion | flops 8257536 | bytes 8519688 | tf_op jit(solution)/shard_map/convert_element_type | solution.py:89
  132.2 3.7 %copy.30 = bf16[18,256,256]{2,0,1:T(8,128)(2,1)S(1)} copy(bf16[18,256,256]{1,2,0:T(8,128)(2,1)} %pad_maximum_fusion.1) | data formatting | bytes 4718592 | tf_op jit(solution)/shard_map/concatenate | solution.py:41
  140.1 3.6 %fusion.26 = bf16[9,256,256]{1,2,0:T(8,128)(2,1)} fusion(bf16[9,256,256]{2,0,1:T(8,128)(2,1)} %fusion.84, bf16[4,256,256]{2,1,0:T(8,128)(2,1)} %collective-permute-done.1, s32[]{:T(128)S(6)} %select_n.80, bf16[4,256,256]{2,1,0:T(8,128)(2,1)} %collective-permute-done), kind=kOutput, calls=%fused_computation.62 | convolution fusion | flops 605159424 | bytes 3539968 | tf_op jit(solution)/shard_map/bd,vbc->vdc/dot_general | solution.py:29
  143.7 3.6 %fusion.25 = bf16[9,256,256]{1,2,0:T(8,128)(2,1)} fusion(bf16[9,256,256]{2,0,1:T(8,128)(2,1)} %fusion.86, bf16[4,256,256]{2,1,0:T(8,128)(2,1)} %collective-permute-done.1, s32[]{:T(128)S(6)} %select_n.78, bf16[4,256,256]{2,1,0:T(8,128)(2,1)} %collective-permute-done), kind=kOutput, calls=%fused_computation.61 | convolution fusion | flops 605159424 | bytes 3539968 | tf_op jit(solution)/shard_map/bd,vbc->vdc/dot_general | solution.py:29
  149.0 4.2 %collective-permute-start.10 = (bf16[9,256,256]{1,2,0:T(8,128)(2,1)}, bf16[9,256,256]{1,2,0:T(8,128)(2,1)}, u32[]{:S(2)}, u32[]{:S(2)}) collective-permute-start(bf16[9,256,256]{1,2,0:T(8,128)(2,1)} %fusion.25), channel_id=1, source_target_pairs={{0,2},{2,4},{4,6},{1,3},{3,5},{5,7},{8,10},{10,12},{12,14},{9,11},... | collective-permute-start | bytes 3538952 | tf_op jit(solution)/shard_map/ppermute | solution.py:63
  153.3 6.5 %collective-permute-start.12 = (bf16[9,256,256]{1,2,0:T(8,128)(2,1)}, bf16[9,256,256]{1,2,0:T(8,128)(2,1)}, u32[]{:S(2)}, u32[]{:S(2)}) collective-permute-start(bf16[9,256,256]{1,2,0:T(8,128)(2,1)} %fusion.26), channel_id=1, source_target_pairs={{0,4},{1,5},{8,12},{9,13},{16,20},{17,21},{24,28},{25,29}} | collective-permute-start | bytes 3538952 | tf_op jit(solution)/shard_map/ppermute | solution.py:61
  163.2 15.7 %collective-permute-done.10 = bf16[9,256,256]{1,2,0:T(8,128)(2,1)} collective-permute-done((bf16[9,256,256]{1,2,0:T(8,128)(2,1)}, bf16[9,256,256]{1,2,0:T(8,128)(2,1)}, u32[]{:S(2)}, u32[]{:S(2)}) %collective-permute-start.10) | collective-permute-done | bytes 1179680 | tf_op jit(solution)/shard_map/ppermute | solution.py:63
  178.9 24.5 %collective-permute-done.12 = bf16[9,256,256]{1,2,0:T(8,128)(2,1)} collective-permute-done((bf16[9,256,256]{1,2,0:T(8,128)(2,1)}, bf16[9,256,256]{1,2,0:T(8,128)(2,1)}, u32[]{:S(2)}, u32[]{:S(2)}) %collective-permute-start.12) | collective-permute-done | bytes 1179680 | tf_op jit(solution)/shard_map/ppermute | solution.py:61
  203.4 4.5 %fusion.22 = bf16[9,256,256]{1,2,0:T(8,128)(2,1)} fusion(bf16[9,256,256]{1,2,0:T(8,128)(2,1)} %collective-permute-done.10, bf16[9,256,256]{1,2,0:T(8,128)(2,1)} %collective-permute-done.11, bf16[9,256,256]{2,0,1:T(8,128)(2,1)} %fusion.82, f32[]{:T(128)S(6)} %sub.14, f32[]{:T(128)S(6)} %sub.13, bf16[4,256,256]{2,1,0:T(8,128)(2,1)} %collective-permute-done.1, ...), kind=kOutput, calls=%fused_computation.32 | convolution fusion | flops 609878016 | bytes 5900288 | tf_op jit(solution)/shard_map/bd,vbc->vdc/dot_general | solution.py:29
  213.9 4.4 %fusion.19 = f32[9,256,256]{1,2,0:T(8,128)S(1)} fusion(bf16[9,256,256]{1,2,0:T(8,128)(2,1)} %collective-permute-done.10, bf16[9,256,256]{1,2,0:T(8,128)(2,1)} %collective-permute-done.11, bf16[9,256,256]{1,2,0:T(8,128)(2,1)} %collective-permute-done.12, bf16[9,256,256]{1,2,0:T(8,128)(2,1)} %collective-permute-done.13, f32[]{:T(128)S(6)} %select_n.82, ...), kind=kOutput, calls=%fused_computation.29 | convolution fusion | flops 612237312 | bytes 9437192 | tf_op jit(solution)/shard_map/bd,vbc->vdc/dot_general | solution.py:29
  218.3 6.5 %collective-permute-done.14 = bf16[4,256,256]{1,2,0:T(8,128)(2,1)} collective-permute-done((bf16[4,256,256]{1,2,0:T(8,128)(2,1)}, bf16[4,256,256]{1,2,0:T(8,128)(2,1)}, u32[]{:S(2)}, u32[]{:S(2)}) %collective-permute-start.14) | collective-permute-done | bytes 524320 | tf_op jit(solution)/shard_map/ppermute | solution.py:85
  228.7 11.2 %collective-permute-done.15 = bf16[1,4,1,256,256]{3,4,1,2,0:T(8,128)(2,1)S(1)} collective-permute-done((bf16[1,4,1,256,256]{3,4,1,2,0:T(8,128)(2,1)S(1)}, bf16[1,4,1,256,256]{3,4,1,2,0:T(8,128)(2,1)S(1)}, u32[]{:S(2)}, u32[]{:S(2)}) %collective-permute-start.15) | collective-permute-done | bytes 524320 | tf_op jit(solution)/shard_map/ppermute | solution.py:19
  244.1 12.9 %collective-permute-done.17 = bf16[1,5,1,256,256]{3,4,1,2,0:T(8,128)(2,1)S(1)} collective-permute-done((bf16[1,5,1,256,256]{3,4,1,2,0:T(8,128)(2,1)S(1)}, bf16[1,5,1,256,256]{3,4,1,2,0:T(8,128)(2,1)S(1)}, u32[]{:S(2)}, u32[]{:S(2)}) %collective-permute-start.17) | collective-permute-done | bytes 655392 | tf_op jit(solution)/shard_map/ppermute | solution.py:19
  (75 shorter events, 54.9 us)
Async XLA Ops:
  0.0 9.7 %copy-start.9 = (s32[4]{0:T(128)S(1)}, s32[4]{0:T(128)}, u32[]{:S(2)}) copy-start(s32[4]{0:T(128)} %constant.107.clone) | copy-start | bytes 52
  0.0 11.6 %copy-start.8 = (s32[4]{0:T(128)S(1)}, s32[4]{0:T(128)}, u32[]{:S(2)}) copy-start(s32[4]{0:T(128)} %constant.106.clone) | copy-start | bytes 52
  0.0 13.7 %copy-start.7 = (s32[4]{0:T(128)S(1)}, s32[4]{0:T(128)}, u32[]{:S(2)}) copy-start(s32[4]{0:T(128)} %constant.105.clone) | copy-start | bytes 52
  3.1 16.8 %collective-permute-start.3 = (bf16[9,256,256]{2,1,0:T(8,128)(2,1)S(1)}, bf16[9,256,256]{2,1,0:T(8,128)(2,1)}, u32[]{:S(2)}, u32[]{:S(2)}) collective-permute-start(bf16[9,256,256]{2,1,0:T(8,128)(2,1)S(1)} %bitcast_select_fusion), channel_id=1, source_target_pairs={{0,1},{1,0},{2,3},{3,2},{4,5},{5,4},{6,7},{7,6},{8,9},{9,8},{10,11... | collective-permute-start | bytes 3538952 | tf_op jit(solution)/shard_map/ppermute | solution.py:19
  4.3 31.0 %collective-permute-start.2 = (bf16[18,9,4]{1,2,0:T(4,128)(2,1)}, bf16[18,9,4]{1,2,0:T(4,128)(2,1)}, u32[]{:S(2)}, u32[]{:S(2)}) collective-permute-start(bf16[18,9,4]{1,2,0:T(4,128)(2,1)} %bitcast.2), channel_id=1, source_target_pairs={{0,24},{8,0},{16,8},{24,16},{1,25},{9,1},{17,9},{25,17},{2,26},{10... | collective-permute-start | bytes 3896 | tf_op jit(solution)/shard_map/ppermute | solution.py:19
  7.8 27.5 %collective-permute-start.1 = (bf16[4,256,256]{2,1,0:T(8,128)(2,1)}, bf16[4,256,256]{2,1,0:T(8,128)(2,1)}, u32[]{:S(2)}, u32[]{:S(2)}) collective-permute-start(bf16[4,256,256]{2,1,0:T(8,128)(2,1)} %bitcast.1), channel_id=1, source_target_pairs={{0,24},{8,0},{16,8},{24,16},{1,25},{9,1},{17,9},{25,17},{2,26},{10... | collective-permute-start | bytes 1572872 | tf_op jit(solution)/shard_map/ppermute | solution.py:19
  8.3 27.0 %collective-permute-start = (bf16[4,256,256]{2,1,0:T(8,128)(2,1)}, bf16[4,256,256]{2,1,0:T(8,128)(2,1)}, u32[]{:S(2)}, u32[]{:S(2)}) collective-permute-start(bf16[4,256,256]{2,1,0:T(8,128)(2,1)} %bitcast), channel_id=1, source_target_pairs={{0,24},{8,0},{16,8},{24,16},{1,25},{9,1},{17,9},{25,17},{2,26},{10... | collective-permute-start | bytes 1572872 | tf_op jit(solution)/shard_map/ppermute | solution.py:19
  35.3 16.7 %collective-permute-start.7 = (bf16[9,256,256]{1,2,0:T(8,128)(2,1)}, bf16[9,256,256]{1,2,0:T(8,128)(2,1)S(1)}, u32[]{:S(2)}, u32[]{:S(2)}) collective-permute-start(bf16[9,256,256]{1,2,0:T(8,128)(2,1)} %fusion.23), channel_id=1, source_target_pairs={{6,2},{7,3},{14,10},{15,11},{22,18},{23,19},{30,26},{31,27}} | collective-permute-start | bytes 3538952 | tf_op jit(solution)/shard_map/ppermute | solution.py:62
  36.0 30.7 %collective-permute-start.4 = (bf16[9,256,256]{1,2,0:T(8,128)(2,1)}, bf16[9,256,256]{1,2,0:T(8,128)(2,1)}, u32[]{:S(2)}, u32[]{:S(2)}) collective-permute-start(bf16[9,256,256]{1,2,0:T(8,128)(2,1)} %fusion.23), channel_id=1, source_target_pairs={{0,2},{2,4},{4,6},{1,3},{3,5},{5,7},{8,10},{10,12},{12,14},{9,11},... | collective-permute-start | bytes 3538952 | tf_op jit(solution)/shard_map/ppermute | solution.py:63
  41.1 49.6 %collective-permute-start.6 = (bf16[9,256,256]{1,2,0:T(8,128)(2,1)}, bf16[9,256,256]{1,2,0:T(8,128)(2,1)}, u32[]{:S(2)}, u32[]{:S(2)}) collective-permute-start(bf16[9,256,256]{1,2,0:T(8,128)(2,1)} %fusion.24), channel_id=1, source_target_pairs={{0,4},{1,5},{8,12},{9,13},{16,20},{17,21},{24,28},{25,29}} | collective-permute-start | bytes 3538952 | tf_op jit(solution)/shard_map/ppermute | solution.py:61
  46.6 44.1 %collective-permute-start.5 = (bf16[9,256,256]{1,2,0:T(8,128)(2,1)}, bf16[9,256,256]{1,2,0:T(8,128)(2,1)}, u32[]{:S(2)}, u32[]{:S(2)}) collective-permute-start(bf16[9,256,256]{1,2,0:T(8,128)(2,1)} %fusion.24), channel_id=1, source_target_pairs={{6,4},{4,2},{2,0},{7,5},{5,3},{3,1},{14,12},{12,10},{10,8},{15,13}... | collective-permute-start | bytes 3538952 | tf_op jit(solution)/shard_map/ppermute | solution.py:64
  52.0 43.3 %copy-start.1 = (bf16[9,256,256]{1,2,0:T(8,128)(2,1)}, bf16[9,256,256]{1,2,0:T(8,128)(2,1)S(1)}, u32[]{:S(2)}) copy-start(bf16[9,256,256]{1,2,0:T(8,128)(2,1)S(1)} %collective-permute-done.7) | copy-start | bytes 3538948
  95.3 28.6 %collective-permute-start.8 = (bf16[9,256,256]{1,2,0:T(8,128)(2,1)}, bf16[9,256,256]{1,2,0:T(8,128)(2,1)}, u32[]{:S(2)}, u32[]{:S(2)}) collective-permute-start(bf16[9,256,256]{1,2,0:T(8,128)(2,1)} %fusion.16), channel_id=1, source_target_pairs={{0,2},{2,6},{6,4},{4,0},{1,3},{3,7},{7,5},{5,1},{8,10},{10,14},{14... | collective-permute-start | bytes 3538952 | tf_op jit(solution)/shard_map/ppermute | solution.py:85
  100.7 23.1 %copy-start = (f32[256,256]{0,1:T(8,128)S(1)}, f32[256,256]{0,1:T(8,128)}, u32[]{:S(2)}) copy-start(f32[256,256]{0,1:T(8,128)} %get-tuple-element.54) | copy-start | bytes 786436
  100.7 23.1 %copy-start.2 = (bf16[9,256,256]{1,2,0:T(8,128)(2,1)S(1)}, bf16[9,256,256]{1,2,0:T(8,128)(2,1)}, u32[]{:S(2)}) copy-start(bf16[9,256,256]{1,2,0:T(8,128)(2,1)} %copy-done.1) | copy-start | bytes 3538948
  127.7 2.9 %collective-permute-start.9 = (bf16[9,256,256]{1,2,0:T(8,128)(2,1)S(1)}, bf16[9,256,256]{1,2,0:T(8,128)(2,1)S(1)}, u32[]{:S(2)}, u32[]{:S(2)}) collective-permute-start(bf16[9,256,256]{1,2,0:T(8,128)(2,1)S(1)} %fusion.13), channel_id=1, source_target_pairs={{0,1},{1,0},{2,3},{3,2},{4,5},{5,4},{6,7},{7,6},{8,9},{9,8},{10,11... | collective-permute-start | bytes 3538952 | tf_op jit(solution)/shard_map/ppermute | solution.py:19
  147.3 15.8 %collective-permute-start.13 = (bf16[9,256,256]{1,2,0:T(8,128)(2,1)}, bf16[9,256,256]{1,2,0:T(8,128)(2,1)}, u32[]{:S(2)}, u32[]{:S(2)}) collective-permute-start(bf16[9,256,256]{1,2,0:T(8,128)(2,1)} %fusion.25), channel_id=1, source_target_pairs={{6,2},{7,3},{14,10},{15,11},{22,18},{23,19},{30,26},{31,27}} | collective-permute-start | bytes 3538952 | tf_op jit(solution)/shard_map/ppermute | solution.py:62
  149.0 29.8 %collective-permute-start.10 = (bf16[9,256,256]{1,2,0:T(8,128)(2,1)}, bf16[9,256,256]{1,2,0:T(8,128)(2,1)}, u32[]{:S(2)}, u32[]{:S(2)}) collective-permute-start(bf16[9,256,256]{1,2,0:T(8,128)(2,1)} %fusion.25), channel_id=1, source_target_pairs={{0,2},{2,4},{4,6},{1,3},{3,5},{5,7},{8,10},{10,12},{12,14},{9,11},... | collective-permute-start | bytes 3538952 | tf_op jit(solution)/shard_map/ppermute | solution.py:63
  153.3 50.1 %collective-permute-start.12 = (bf16[9,256,256]{1,2,0:T(8,128)(2,1)}, bf16[9,256,256]{1,2,0:T(8,128)(2,1)}, u32[]{:S(2)}, u32[]{:S(2)}) collective-permute-start(bf16[9,256,256]{1,2,0:T(8,128)(2,1)} %fusion.26), channel_id=1, source_target_pairs={{0,4},{1,5},{8,12},{9,13},{16,20},{17,21},{24,28},{25,29}} | collective-permute-start | bytes 3538952 | tf_op jit(solution)/shard_map/ppermute | solution.py:61
  159.8 43.6 %collective-permute-start.11 = (bf16[9,256,256]{1,2,0:T(8,128)(2,1)}, bf16[9,256,256]{1,2,0:T(8,128)(2,1)}, u32[]{:S(2)}, u32[]{:S(2)}) collective-permute-start(bf16[9,256,256]{1,2,0:T(8,128)(2,1)} %fusion.26), channel_id=1, source_target_pairs={{6,4},{4,2},{2,0},{7,5},{5,3},{3,1},{14,12},{12,10},{10,8},{15,13}... | collective-permute-start | bytes 3538952 | tf_op jit(solution)/shard_map/ppermute | solution.py:64
  209.7 15.1 %collective-permute-start.14 = (bf16[4,256,256]{1,2,0:T(8,128)(2,1)}, bf16[4,256,256]{1,2,0:T(8,128)(2,1)}, u32[]{:S(2)}, u32[]{:S(2)}) collective-permute-start(bf16[4,256,256]{1,2,0:T(8,128)(2,1)} %slice.49), channel_id=1, source_target_pairs={{0,2},{2,6},{6,4},{4,0},{1,3},{3,7},{7,5},{5,1},{8,10},{10,14},{14... | collective-permute-start | bytes 1572872 | tf_op jit(solution)/shard_map/ppermute | solution.py:85
  226.0 16.3 %collective-permute-start.16 = (bf16[5,256,256]{1,2,0:T(8,128)(2,1)S(1)}, bf16[5,256,256]{1,2,0:T(8,128)(2,1)S(1)}, u32[]{:S(2)}, u32[]{:S(2)}) collective-permute-start(bf16[5,256,256]{1,2,0:T(8,128)(2,1)S(1)} %slice.40), channel_id=1, source_target_pairs={{0,2},{2,6},{6,4},{4,0},{1,3},{3,7},{7,5},{5,1},{8,10},{10,14},{14... | collective-permute-start | bytes 1966088 | tf_op jit(solution)/shard_map/ppermute | solution.py:85
  227.2 12.7 %collective-permute-start.15 = (bf16[1,4,1,256,256]{3,4,1,2,0:T(8,128)(2,1)S(1)}, bf16[1,4,1,256,256]{3,4,1,2,0:T(8,128)(2,1)S(1)}, u32[]{:S(2)}, u32[]{:S(2)}) collective-permute-start(bf16[1,4,1,256,256]{3,4,1,2,0:T(8,128)(2,1)S(1)} %bitcast.123), channel_id=1, source_target_pairs={{0,16},{8,24},{16,0},{24,8},{1,17},{9,25},{17,1},{25,9},{2,18},{10... | collective-permute-start | bytes 1572872 | tf_op jit(solution)/shard_map/ppermute | solution.py:19
  242.5 14.4 %collective-permute-start.17 = (bf16[1,5,1,256,256]{3,4,1,2,0:T(8,128)(2,1)S(1)}, bf16[1,5,1,256,256]{3,4,1,2,0:T(8,128)(2,1)S(1)}, u32[]{:S(2)}, u32[]{:S(2)}) collective-permute-start(bf16[1,5,1,256,256]{3,4,1,2,0:T(8,128)(2,1)S(1)} %fusion.31), channel_id=1, source_target_pairs={{0,16},{8,24},{16,0},{24,8},{1,17},{9,25},{17,1},{25,9},{2,18},{10... | collective-permute-start | bytes 1966088 | tf_op jit(solution)/shard_map/ppermute | solution.py:19
  (4 other events, 20.6 us)

commit v6 on v5

--- a/solution.py
+++ b/solution.py
@@ -56,12 +56,12 @@
     one = jnp.ones((), f32)
     zero = jnp.zeros((), f32)
     slot_a = term(gathered, *pick(SLOT_A, sector, ket, bra, mpo))
+    held, slot_a = lax.optimization_barrier((held, slot_a))
+    got_right = lax.ppermute(slot_a, "sector", RIGHT)
+    middle_left = lax.ppermute(slot_a, "sector", ((3, 1),))
     slot_b = term(gathered, *pick(SLOT_B, sector, ket, bra, mpo))
-    held, slot_a, slot_b = lax.optimization_barrier((held, slot_a, slot_b))
+    got_left = lax.ppermute(slot_b, "sector", LEFT)
     middle_right = lax.ppermute(slot_b, "sector", ((0, 2),))
-    middle_left = lax.ppermute(slot_a, "sector", ((3, 1),))
-    got_right = lax.ppermute(slot_a, "sector", RIGHT)
-    got_left = lax.ppermute(slot_b, "sector", LEFT)
     got = lax.optimization_barrier((got_right, got_left, middle_right, middle_left))
     got_right, got_left, middle_right, middle_left = got
     got_middle = middle_right + middle_left

time: 259 us -> 253 us (0.977)
  starting transfers between devices: 40.8 us -> 36.8 us
  waiting for transfers between devices: 133 us -> 129 us
    ppermute x2, waiting for transfers between devices: 48.4 us -> 6.04 us  [advance_line(): middle_right = lax.ppermute(slot_b, 'sector', ((0, 2),))]
    ppermute x2, waiting for transfers between devices: 0.01 us -> 17.8 us  [advance_line(): got_left = lax.ppermute(slot_b, 'sector', LEFT)]
    ppermute x2, waiting for transfers between devices: 30.5 us -> 48.1 us  [advance_line(): got_right = lax.ppermute(slot_a, 'sector', RIGHT)]
    ppermute x2, starting transfers between devices: 9.3 us -> 4.65 us  [advance_line(): got_right = lax.ppermute(slot_a, 'sector', RIGHT)]
  transfers between devices with their start and end apart: 18 -> 18, of which waited for: 10 -> 12; matrix products, arithmetic and copies ran while one was open for 16% -> 19% of each run, Pallas kernels for 0% -> 0%
where the time goes in v6:
time: 253 us; the launch traced here: 252 us
  waiting for transfers between devices  129 us (51%)
  matrix products  54.4 us (22%)
  starting transfers between devices  36.8 us (15%)
  local copies, waits for them, and re-layouts  13.3 us (5%)
  other arithmetic  10.9 us (4%)
  between operations  6.89 us (3%)
    ppermute x2, waiting for transfers between devices, advance_line(): got_right = lax.ppermute(slot_a, 'sector', RIGHT)  48.1 us
    dot_general x8, matrix products, term(): jnp.einsum('bd,vbc->vdc', bra_p, rotated, preferred_element_type=jnp.floa...  31.2 us
    ppermute x3, waiting for transfers between devices, advance_line(): got_last = lax.ppermute(send[low:high], 'sector', LAST)  30.6 us
    ppermute x7, waiting for transfers between devices, shifted(): return lax.ppermute(value, axis, pairs)  26.8 us
    dot_general x8, matrix products, term(): jnp.einsum('wv,wba->vba', mpo_p, gathered, preferred_element_type=jnp.flo...  23.2 us
    ppermute x2, waiting for transfers between devices, advance_line(): got_left = lax.ppermute(slot_b, 'sector', LEFT)  17.8 us
    ppermute x2, starting transfers between devices, advance_line(): middle_right = lax.ppermute(slot_b, 'sector', ((0, 2),))  11.9 us
    ppermute x7, starting transfers between devices, shifted(): return lax.ppermute(value, axis, pairs)  9.13 us
  transfers between devices with their start and end apart: 18, of which 12 were waited for; matrix products, arithmetic and copies ran while one was open for 19% of the time, Pallas kernels for 0%

profile of v6, /device:TPU:0, one launch (start us, length us, event | category | flops | bytes accessed | tf_op | source)
XLA Modules:
  0.0 251.7 jit_solution(13283891783500716680)
XLA Ops:
  24.7 3.6 %fusion.24 = bf16[9,256,256]{1,2,0:T(8,128)(2,1)} fusion(bf16[9,256,256]{2,0,1:T(8,128)(2,1)} %fusion.2, bf16[1,1,4,256,256]{4,3,2,1,0:T(8,128)(2,1)} %param.15, s32[]{:T(128)S(6)} %select_n.81, bf16[1,1,4,256,256]{4,3,2,1,0:T(8,128)(2,1)} %param.14), kind=kOutput, calls=%fused_computation.60 | convolution fusion | flops 605159424 | bytes 3539968 | tf_op jit(solution)/shard_map/bd,vbc->vdc/dot_general | solution.py:29
  29.6 6.6 %collective-permute-start.6 = (bf16[9,256,256]{1,2,0:T(8,128)(2,1)}, bf16[9,256,256]{1,2,0:T(8,128)(2,1)}, u32[]{:S(2)}, u32[]{:S(2)}) collective-permute-start(bf16[9,256,256]{1,2,0:T(8,128)(2,1)} %fusion.24), channel_id=1, source_target_pairs={{0,4},{1,5},{8,12},{9,13},{16,20},{17,21},{24,28},{25,29}} | collective-permute-start | bytes 3538952 | tf_op jit(solution)/shard_map/ppermute | solution.py:64
  36.2 4.0 %fusion.6 = bf16[9,256,256]{2,0,1:T(8,128)(2,1)} fusion(bf16[18,256,256]{2,1,0:T(8,128)(2,1)S(1)} %pad_maximum_fusion, bf16[18,9,1]{1,2,0:T(2,128)(2,1)} %get-tuple-element.47), kind=kOutput, calls=%fused_computation.8 | convolution fusion | flops 21233664 | bytes 3539268 | tf_op jit(solution)/shard_map/wv,wba->vba/dot_general | solution.py:23
  40.2 3.6 %fusion.23 = bf16[9,256,256]{1,2,0:T(8,128)(2,1)} fusion(bf16[9,256,256]{2,0,1:T(8,128)(2,1)} %fusion.6, bf16[1,1,4,256,256]{4,3,2,1,0:T(8,128)(2,1)} %param.15, s32[]{:T(128)S(6)} %select_n.78, bf16[1,1,4,256,256]{4,3,2,1,0:T(8,128)(2,1)} %param.14), kind=kOutput, calls=%fused_computation.59 | convolution fusion | flops 605159424 | bytes 3539968 | tf_op jit(solution)/shard_map/bd,vbc->vdc/dot_general | solution.py:29
  47.9 4.0 %fusion = bf16[9,256,256]{2,0,1:T(8,128)(2,1)} fusion(bf16[18,256,256]{2,1,0:T(8,128)(2,1)S(1)} %pad_maximum_fusion, bf16[18,9,1]{1,2,0:T(2,128)(2,1)} %get-tuple-element.44), kind=kOutput, calls=%fused_computation.2 | convolution fusion | flops 21233664 | bytes 3539268 | tf_op jit(solution)/shard_map/wv,wba->vba/dot_general | solution.py:23
  51.9 6.1 %collective-permute-done.5 = bf16[9,256,256]{1,2,0:T(8,128)(2,1)S(1)} collective-permute-done((bf16[9,256,256]{1,2,0:T(8,128)(2,1)}, bf16[9,256,256]{1,2,0:T(8,128)(2,1)S(1)}, u32[]{:S(2)}, u32[]{:S(2)}) %collective-permute-start.5) | collective-permute-done | bytes 1179680 | tf_op jit(solution)/shard_map/ppermute | solution.py:63
  58.0 4.0 %collective-permute-done.6 = bf16[9,256,256]{1,2,0:T(8,128)(2,1)} collective-permute-done((bf16[9,256,256]{1,2,0:T(8,128)(2,1)}, bf16[9,256,256]{1,2,0:T(8,128)(2,1)}, u32[]{:S(2)}, u32[]{:S(2)}) %collective-permute-start.6) | collective-permute-done | bytes 1179680 | tf_op jit(solution)/shard_map/ppermute | solution.py:64
  62.0 23.6 %collective-permute-done.4 = bf16[9,256,256]{1,2,0:T(8,128)(2,1)} collective-permute-done((bf16[9,256,256]{1,2,0:T(8,128)(2,1)}, bf16[9,256,256]{1,2,0:T(8,128)(2,1)}, u32[]{:S(2)}, u32[]{:S(2)}) %collective-permute-start.4) | collective-permute-done | bytes 1179680 | tf_op jit(solution)/shard_map/ppermute | solution.py:60
  85.6 4.2 %fusion.16 = bf16[9,256,256]{1,2,0:T(8,128)(2,1)} fusion(bf16[9,256,256]{1,2,0:T(8,128)(2,1)} %collective-permute-done.4, bf16[9,256,256]{1,2,0:T(8,128)(2,1)S(1)} %collective-permute-done.5, bf16[9,256,256]{2,0,1:T(8,128)(2,1)} %fusion, f32[]{:T(128)S(6)} %sub.14, f32[]{:T(128)S(6)} %sub.13, bf16[1,1,4,256,256]{4,3,2,1,0:T(8,128)(2,1)} %param.15, ...), kind=kOutput, calls=%fused_computation.26 | convolution fusion | flops 609878016 | bytes 5900288 | tf_op jit(solution)/shard_map/bd,vbc->vdc/dot_general | solution.py:29
  95.6 3.7 %convolution_convert_fusion.12 = bf16[9,256,256]{2,1,0:T(8,128)(2,1)} fusion(bf16[9,256,256]{2,0,1:T(8,128)(2,1)} %fusion.4, bf16[1,1,4,256,256]{4,3,2,1,0:T(8,128)(2,1)} %param.15, bf16[1,1,4,256,256]{4,3,2,1,0:T(8,128)(2,1)} %param.14), kind=kOutput, calls=%fused_computation.55 | convolution fusion | flops 605159424 | bytes 3538944 | tf_op jit(solution)/shard_map/bd,vbc->vdc/dot_general | solution.py:29
  99.3 20.2 %collective-permute-done.8 = bf16[9,256,256]{1,2,0:T(8,128)(2,1)} collective-permute-done((bf16[9,256,256]{1,2,0:T(8,128)(2,1)}, bf16[9,256,256]{1,2,0:T(8,128)(2,1)}, u32[]{:S(2)}, u32[]{:S(2)}) %collective-permute-start.8) | collective-permute-done | bytes 1179680 | tf_op jit(solution)/shard_map/ppermute | solution.py:85
  119.6 3.9 %fusion.13 = bf16[9,256,256]{1,2,0:T(8,128)(2,1)S(1)} fusion(bf16[9,256,256]{1,2,0:T(8,128)(2,1)} %collective-permute-done.4, bf16[9,256,256]{1,2,0:T(8,128)(2,1)S(1)} %copy-done.2, bf16[9,256,256]{2,1,0:T(8,128)(2,1)} %convolution_convert_fusion.12, bf16[9,256,256]{1,2,0:T(8,128)(2,1)} %collective-permute-done.8, f32[256,256]{0,1:T(8,128)S(1)} %copy-done, ...), kind=kLoop, calls=%fused_computation.23 | loop fusion | flops 8257536 | bytes 8519688 | tf_op jit(solution)/shard_map/convert_element_type | solution.py:89
  128.0 3.7 %copy.30 = bf16[18,256,256]{2,0,1:T(8,128)(2,1)S(1)} copy(bf16[18,256,256]{1,2,0:T(8,128)(2,1)} %pad_maximum_fusion.1) | data formatting | bytes 4718592 | tf_op jit(solution)/shard_map/concatenate | solution.py:41
  133.8 3.6 %fusion.26 = bf16[9,256,256]{1,2,0:T(8,128)(2,1)} fusion(bf16[9,256,256]{2,0,1:T(8,128)(2,1)} %fusion.84, bf16[4,256,256]{2,1,0:T(8,128)(2,1)} %collective-permute-done.1, s32[]{:T(128)S(6)} %select_n.81, bf16[4,256,256]{2,1,0:T(8,128)(2,1)} %collective-permute-done), kind=kOutput, calls=%fused_computation.62 | convolution fusion | flops 605159424 | bytes 3539968 | tf_op jit(solution)/shard_map/bd,vbc->vdc/dot_general | solution.py:29
  138.7 5.3 %collective-permute-start.12 = (bf16[9,256,256]{1,2,0:T(8,128)(2,1)}, bf16[9,256,256]{1,2,0:T(8,128)(2,1)}, u32[]{:S(2)}, u32[]{:S(2)}) collective-permute-start(bf16[9,256,256]{1,2,0:T(8,128)(2,1)} %fusion.26), channel_id=1, source_target_pairs={{0,4},{1,5},{8,12},{9,13},{16,20},{17,21},{24,28},{25,29}} | collective-permute-start | bytes 3538952 | tf_op jit(solution)/shard_map/ppermute | solution.py:64
  146.1 3.6 %fusion.25 = bf16[9,256,256]{1,2,0:T(8,128)(2,1)} fusion(bf16[9,256,256]{2,0,1:T(8,128)(2,1)} %fusion.86, bf16[4,256,256]{2,1,0:T(8,128)(2,1)} %collective-permute-done.1, s32[]{:T(128)S(6)} %select_n.78, bf16[4,256,256]{2,1,0:T(8,128)(2,1)} %collective-permute-done), kind=kOutput, calls=%fused_computation.61 | convolution fusion | flops 605159424 | bytes 3539968 | tf_op jit(solution)/shard_map/bd,vbc->vdc/dot_general | solution.py:29
  155.9 11.7 %collective-permute-done.11 = bf16[9,256,256]{1,2,0:T(8,128)(2,1)} collective-permute-done((bf16[9,256,256]{1,2,0:T(8,128)(2,1)}, bf16[9,256,256]{1,2,0:T(8,128)(2,1)}, u32[]{:S(2)}, u32[]{:S(2)}) %collective-permute-start.11) | collective-permute-done | bytes 1179680 | tf_op jit(solution)/shard_map/ppermute | solution.py:63
  169.7 24.5 %collective-permute-done.10 = bf16[9,256,256]{1,2,0:T(8,128)(2,1)} collective-permute-done((bf16[9,256,256]{1,2,0:T(8,128)(2,1)}, bf16[9,256,256]{1,2,0:T(8,128)(2,1)}, u32[]{:S(2)}, u32[]{:S(2)}) %collective-permute-start.10) | collective-permute-done | bytes 1179680 | tf_op jit(solution)/shard_map/ppermute | solution.py:60
  194.1 4.5 %fusion.22 = bf16[9,256,256]{1,2,0:T(8,128)(2,1)} fusion(bf16[9,256,256]{1,2,0:T(8,128)(2,1)} %collective-permute-done.10, bf16[9,256,256]{1,2,0:T(8,128)(2,1)} %collective-permute-done.11, bf16[9,256,256]{2,0,1:T(8,128)(2,1)} %fusion.82, f32[]{:T(128)S(6)} %sub.14, f32[]{:T(128)S(6)} %sub.13, bf16[4,256,256]{2,1,0:T(8,128)(2,1)} %collective-permute-done.1, ...), kind=kOutput, calls=%fused_computation.32 | convolution fusion | flops 609878016 | bytes 5900288 | tf_op jit(solution)/shard_map/bd,vbc->vdc/dot_general | solution.py:29
  205.1 4.4 %fusion.19 = f32[9,256,256]{1,2,0:T(8,128)S(1)} fusion(bf16[9,256,256]{1,2,0:T(8,128)(2,1)} %collective-permute-done.10, bf16[9,256,256]{1,2,0:T(8,128)(2,1)} %collective-permute-done.11, bf16[9,256,256]{1,2,0:T(8,128)(2,1)} %collective-permute-done.12, bf16[9,256,256]{1,2,0:T(8,128)(2,1)} %collective-permute-done.13, f32[]{:T(128)S(6)} %select_n.82, ...), kind=kOutput, calls=%fused_computation.29 | convolution fusion | flops 612237312 | bytes 9437192 | tf_op jit(solution)/shard_map/bd,vbc->vdc/dot_general | solution.py:29
  209.5 6.8 %collective-permute-done.14 = bf16[4,256,256]{1,2,0:T(8,128)(2,1)} collective-permute-done((bf16[4,256,256]{1,2,0:T(8,128)(2,1)}, bf16[4,256,256]{1,2,0:T(8,128)(2,1)}, u32[]{:S(2)}, u32[]{:S(2)}) %collective-permute-start.14) | collective-permute-done | bytes 524320 | tf_op jit(solution)/shard_map/ppermute | solution.py:85
  219.2 11.7 %collective-permute-done.15 = bf16[1,4,1,256,256]{3,4,1,2,0:T(8,128)(2,1)S(1)} collective-permute-done((bf16[1,4,1,256,256]{3,4,1,2,0:T(8,128)(2,1)S(1)}, bf16[1,4,1,256,256]{3,4,1,2,0:T(8,128)(2,1)S(1)}, u32[]{:S(2)}, u32[]{:S(2)}) %collective-permute-start.15) | collective-permute-done | bytes 524320 | tf_op jit(solution)/shard_map/ppermute | solution.py:19
  230.9 3.6 %collective-permute-done.16 = bf16[5,256,256]{1,2,0:T(8,128)(2,1)S(1)} collective-permute-done((bf16[5,256,256]{1,2,0:T(8,128)(2,1)S(1)}, bf16[5,256,256]{1,2,0:T(8,128)(2,1)S(1)}, u32[]{:S(2)}, u32[]{:S(2)}) %collective-permute-start.16) | collective-permute-done | bytes 655392 | tf_op jit(solution)/shard_map/ppermute | solution.py:85
  236.4 13.7 %collective-permute-done.17 = bf16[1,5,1,256,256]{3,4,1,2,0:T(8,128)(2,1)S(1)} collective-permute-done((bf16[1,5,1,256,256]{3,4,1,2,0:T(8,128)(2,1)S(1)}, bf16[1,5,1,256,256]{3,4,1,2,0:T(8,128)(2,1)S(1)}, u32[]{:S(2)}, u32[]{:S(2)}) %collective-permute-start.17) | collective-permute-done | bytes 655392 | tf_op jit(solution)/shard_map/ppermute | solution.py:19
  (75 shorter events, 60.2 us)
Async XLA Ops:
  0.0 9.8 %copy-start.9 = (s32[4]{0:T(128)S(1)}, s32[4]{0:T(128)}, u32[]{:S(2)}) copy-start(s32[4]{0:T(128)} %constant.105.clone) | copy-start | bytes 52
  0.0 11.8 %copy-start.8 = (s32[4]{0:T(128)S(1)}, s32[4]{0:T(128)}, u32[]{:S(2)}) copy-start(s32[4]{0:T(128)} %constant.106.clone) | copy-start | bytes 52
  0.0 13.8 %copy-start.7 = (s32[4]{0:T(128)S(1)}, s32[4]{0:T(128)}, u32[]{:S(2)}) copy-start(s32[4]{0:T(128)} %constant.107.clone) | copy-start | bytes 52
  3.1 16.8 %collective-permute-start.3 = (bf16[9,256,256]{2,1,0:T(8,128)(2,1)S(1)}, bf16[9,256,256]{2,1,0:T(8,128)(2,1)}, u32[]{:S(2)}, u32[]{:S(2)}) collective-permute-start(bf16[9,256,256]{2,1,0:T(8,128)(2,1)S(1)} %bitcast_select_fusion), channel_id=1, source_target_pairs={{0,1},{1,0},{2,3},{3,2},{4,5},{5,4},{6,7},{7,6},{8,9},{9,8},{10,11... | collective-permute-start | bytes 3538952 | tf_op jit(solution)/shard_map/ppermute | solution.py:19
  4.3 39.5 %collective-permute-start.2 = (bf16[18,9,4]{1,2,0:T(4,128)(2,1)}, bf16[18,9,4]{1,2,0:T(4,128)(2,1)}, u32[]{:S(2)}, u32[]{:S(2)}) collective-permute-start(bf16[18,9,4]{1,2,0:T(4,128)(2,1)} %bitcast.2), channel_id=1, source_target_pairs={{0,24},{8,0},{16,8},{24,16},{1,25},{9,1},{17,9},{25,17},{2,26},{10... | collective-permute-start | bytes 3896 | tf_op jit(solution)/shard_map/ppermute | solution.py:19
  7.8 36.1 %collective-permute-start = (bf16[4,256,256]{2,1,0:T(8,128)(2,1)}, bf16[4,256,256]{2,1,0:T(8,128)(2,1)}, u32[]{:S(2)}, u32[]{:S(2)}) collective-permute-start(bf16[4,256,256]{2,1,0:T(8,128)(2,1)} %bitcast), channel_id=1, source_target_pairs={{0,24},{8,0},{16,8},{24,16},{1,25},{9,1},{17,9},{25,17},{2,26},{10... | collective-permute-start | bytes 1572872 | tf_op jit(solution)/shard_map/ppermute | solution.py:19
  8.3 35.5 %collective-permute-start.1 = (bf16[4,256,256]{2,1,0:T(8,128)(2,1)}, bf16[4,256,256]{2,1,0:T(8,128)(2,1)}, u32[]{:S(2)}, u32[]{:S(2)}) collective-permute-start(bf16[4,256,256]{2,1,0:T(8,128)(2,1)} %bitcast.1), channel_id=1, source_target_pairs={{0,24},{8,0},{16,8},{24,16},{1,25},{9,1},{17,9},{25,17},{2,26},{10... | collective-permute-start | bytes 1572872 | tf_op jit(solution)/shard_map/ppermute | solution.py:19
  28.4 29.6 %collective-permute-start.5 = (bf16[9,256,256]{1,2,0:T(8,128)(2,1)}, bf16[9,256,256]{1,2,0:T(8,128)(2,1)S(1)}, u32[]{:S(2)}, u32[]{:S(2)}) collective-permute-start(bf16[9,256,256]{1,2,0:T(8,128)(2,1)} %fusion.24), channel_id=1, source_target_pairs={{6,4},{4,2},{2,0},{7,5},{5,3},{3,1},{14,12},{12,10},{10,8},{15,13}... | collective-permute-start | bytes 3538952 | tf_op jit(solution)/shard_map/ppermute | solution.py:63
  29.6 32.3 %collective-permute-start.6 = (bf16[9,256,256]{1,2,0:T(8,128)(2,1)}, bf16[9,256,256]{1,2,0:T(8,128)(2,1)}, u32[]{:S(2)}, u32[]{:S(2)}) collective-permute-start(bf16[9,256,256]{1,2,0:T(8,128)(2,1)} %fusion.24), channel_id=1, source_target_pairs={{0,4},{1,5},{8,12},{9,13},{16,20},{17,21},{24,28},{25,29}} | collective-permute-start | bytes 3538952 | tf_op jit(solution)/shard_map/ppermute | solution.py:64
  43.9 41.7 %collective-permute-start.4 = (bf16[9,256,256]{1,2,0:T(8,128)(2,1)}, bf16[9,256,256]{1,2,0:T(8,128)(2,1)}, u32[]{:S(2)}, u32[]{:S(2)}) collective-permute-start(bf16[9,256,256]{1,2,0:T(8,128)(2,1)} %fusion.23), channel_id=1, source_target_pairs={{0,2},{2,4},{4,6},{1,3},{3,5},{5,7},{8,10},{10,12},{12,14},{9,11},... | collective-permute-start | bytes 3538952 | tf_op jit(solution)/shard_map/ppermute | solution.py:60
  46.2 39.4 %collective-permute-start.7 = (bf16[9,256,256]{1,2,0:T(8,128)(2,1)}, bf16[9,256,256]{1,2,0:T(8,128)(2,1)}, u32[]{:S(2)}, u32[]{:S(2)}) collective-permute-start(bf16[9,256,256]{1,2,0:T(8,128)(2,1)} %fusion.23), channel_id=1, source_target_pairs={{6,2},{7,3},{14,10},{15,11},{22,18},{23,19},{30,26},{31,27}} | collective-permute-start | bytes 3538952 | tf_op jit(solution)/shard_map/ppermute | solution.py:61
  58.0 31.8 %copy-start.1 = (bf16[9,256,256]{1,2,0:T(8,128)(2,1)}, bf16[9,256,256]{1,2,0:T(8,128)(2,1)S(1)}, u32[]{:S(2)}) copy-start(bf16[9,256,256]{1,2,0:T(8,128)(2,1)S(1)} %collective-permute-done.5) | copy-start | bytes 3538948
  89.8 29.8 %collective-permute-start.8 = (bf16[9,256,256]{1,2,0:T(8,128)(2,1)}, bf16[9,256,256]{1,2,0:T(8,128)(2,1)}, u32[]{:S(2)}, u32[]{:S(2)}) collective-permute-start(bf16[9,256,256]{1,2,0:T(8,128)(2,1)} %fusion.16), channel_id=1, source_target_pairs={{0,2},{2,6},{6,4},{4,0},{1,3},{3,7},{7,5},{5,1},{8,10},{10,14},{14... | collective-permute-start | bytes 3538952 | tf_op jit(solution)/shard_map/ppermute | solution.py:85
  95.6 23.9 %copy-start = (f32[256,256]{0,1:T(8,128)S(1)}, f32[256,256]{0,1:T(8,128)}, u32[]{:S(2)}) copy-start(f32[256,256]{0,1:T(8,128)} %get-tuple-element.48) | copy-start | bytes 786436
  95.6 23.9 %copy-start.2 = (bf16[9,256,256]{1,2,0:T(8,128)(2,1)S(1)}, bf16[9,256,256]{1,2,0:T(8,128)(2,1)}, u32[]{:S(2)}) copy-start(bf16[9,256,256]{1,2,0:T(8,128)(2,1)} %copy-done.1) | copy-start | bytes 3538948
  123.4 2.9 %collective-permute-start.9 = (bf16[9,256,256]{1,2,0:T(8,128)(2,1)S(1)}, bf16[9,256,256]{1,2,0:T(8,128)(2,1)S(1)}, u32[]{:S(2)}, u32[]{:S(2)}) collective-permute-start(bf16[9,256,256]{1,2,0:T(8,128)(2,1)S(1)} %fusion.13), channel_id=1, source_target_pairs={{0,1},{1,0},{2,3},{3,2},{4,5},{5,4},{6,7},{7,6},{8,9},{9,8},{10,11... | collective-permute-start | bytes 3538952 | tf_op jit(solution)/shard_map/ppermute | solution.py:19
  137.4 30.2 %collective-permute-start.11 = (bf16[9,256,256]{1,2,0:T(8,128)(2,1)}, bf16[9,256,256]{1,2,0:T(8,128)(2,1)}, u32[]{:S(2)}, u32[]{:S(2)}) collective-permute-start(bf16[9,256,256]{1,2,0:T(8,128)(2,1)} %fusion.26), channel_id=1, source_target_pairs={{6,4},{4,2},{2,0},{7,5},{5,3},{3,1},{14,12},{12,10},{10,8},{15,13}... | collective-permute-start | bytes 3538952 | tf_op jit(solution)/shard_map/ppermute | solution.py:63
  138.7 31.0 %collective-permute-start.12 = (bf16[9,256,256]{1,2,0:T(8,128)(2,1)}, bf16[9,256,256]{1,2,0:T(8,128)(2,1)}, u32[]{:S(2)}, u32[]{:S(2)}) collective-permute-start(bf16[9,256,256]{1,2,0:T(8,128)(2,1)} %fusion.26), channel_id=1, source_target_pairs={{0,4},{1,5},{8,12},{9,13},{16,20},{17,21},{24,28},{25,29}} | collective-permute-start | bytes 3538952 | tf_op jit(solution)/shard_map/ppermute | solution.py:64
  149.7 44.4 %collective-permute-start.10 = (bf16[9,256,256]{1,2,0:T(8,128)(2,1)}, bf16[9,256,256]{1,2,0:T(8,128)(2,1)}, u32[]{:S(2)}, u32[]{:S(2)}) collective-permute-start(bf16[9,256,256]{1,2,0:T(8,128)(2,1)} %fusion.25), channel_id=1, source_target_pairs={{0,2},{2,4},{4,6},{1,3},{3,5},{5,7},{8,10},{10,12},{12,14},{9,11},... | collective-permute-start | bytes 3538952 | tf_op jit(solution)/shard_map/ppermute | solution.py:60
  152.1 42.1 %collective-permute-start.13 = (bf16[9,256,256]{1,2,0:T(8,128)(2,1)}, bf16[9,256,256]{1,2,0:T(8,128)(2,1)}, u32[]{:S(2)}, u32[]{:S(2)}) collective-permute-start(bf16[9,256,256]{1,2,0:T(8,128)(2,1)} %fusion.25), channel_id=1, source_target_pairs={{6,2},{7,3},{14,10},{15,11},{22,18},{23,19},{30,26},{31,27}} | collective-permute-start | bytes 3538952 | tf_op jit(solution)/shard_map/ppermute | solution.py:61
  200.5 15.8 %collective-permute-start.14 = (bf16[4,256,256]{1,2,0:T(8,128)(2,1)}, bf16[4,256,256]{1,2,0:T(8,128)(2,1)}, u32[]{:S(2)}, u32[]{:S(2)}) collective-permute-start(bf16[4,256,256]{1,2,0:T(8,128)(2,1)} %slice.49), channel_id=1, source_target_pairs={{0,2},{2,6},{6,4},{4,0},{1,3},{3,7},{7,5},{5,1},{8,10},{10,14},{14... | collective-permute-start | bytes 1572872 | tf_op jit(solution)/shard_map/ppermute | solution.py:85
  217.5 17.1 %collective-permute-start.16 = (bf16[5,256,256]{1,2,0:T(8,128)(2,1)S(1)}, bf16[5,256,256]{1,2,0:T(8,128)(2,1)S(1)}, u32[]{:S(2)}, u32[]{:S(2)}) collective-permute-start(bf16[5,256,256]{1,2,0:T(8,128)(2,1)S(1)} %slice.40), channel_id=1, source_target_pairs={{0,2},{2,6},{6,4},{4,0},{1,3},{3,7},{7,5},{5,1},{8,10},{10,14},{14... | collective-permute-start | bytes 1966088 | tf_op jit(solution)/shard_map/ppermute | solution.py:85
  217.7 13.3 %collective-permute-start.15 = (bf16[1,4,1,256,256]{3,4,1,2,0:T(8,128)(2,1)S(1)}, bf16[1,4,1,256,256]{3,4,1,2,0:T(8,128)(2,1)S(1)}, u32[]{:S(2)}, u32[]{:S(2)}) collective-permute-start(bf16[1,4,1,256,256]{3,4,1,2,0:T(8,128)(2,1)S(1)} %bitcast.123), channel_id=1, source_target_pairs={{0,16},{8,24},{16,0},{24,8},{1,17},{9,25},{17,1},{25,9},{2,18},{10... | collective-permute-start | bytes 1572872 | tf_op jit(solution)/shard_map/ppermute | solution.py:19
  234.8 15.3 %collective-permute-start.17 = (bf16[1,5,1,256,256]{3,4,1,2,0:T(8,128)(2,1)S(1)}, bf16[1,5,1,256,256]{3,4,1,2,0:T(8,128)(2,1)S(1)}, u32[]{:S(2)}, u32[]{:S(2)}) collective-permute-start(bf16[1,5,1,256,256]{3,4,1,2,0:T(8,128)(2,1)S(1)} %fusion.31), channel_id=1, source_target_pairs={{0,16},{8,24},{16,0},{24,8},{1,17},{9,25},{17,1},{25,9},{2,18},{10... | collective-permute-start | bytes 1966088 | tf_op jit(solution)/shard_map/ppermute | solution.py:19
  (4 other events, 20.9 us)

commit v7 on v6

--- a/solution.py
+++ b/solution.py
@@ -62,10 +62,10 @@
     slot_b = term(gathered, *pick(SLOT_B, sector, ket, bra, mpo))
     got_left = lax.ppermute(slot_b, "sector", LEFT)
     middle_right = lax.ppermute(slot_b, "sector", ((0, 2),))
-    got = lax.optimization_barrier((got_right, got_left, middle_right, middle_left))
-    got_right, got_left, middle_right, middle_left = got
+    third = term(gathered, *pick(LAST_P, sector, ket, bra, mpo))
+    got = (got_right, got_left, middle_right, middle_left, third)
+    got_right, got_left, middle_right, middle_left, third = lax.optimization_barrier(got)
     got_middle = middle_right + middle_left
-    third = term(gathered, *pick(LAST_P, sector, ket, bra, mpo))
     keep_right = jnp.where(sector == 1, zero, one)
     keep_left = jnp.where(sector == 2, zero, one)
     send = third.astype(f32) + (1 - keep_right) * got_right.astype(f32)

time: 253 us -> 245 us (0.968)
  waiting for transfers between devices: 129 us -> 110 us
  starting transfers between devices: 36.8 us -> 44.6 us
  other arithmetic: 10.9 us -> 16.7 us
    ppermute x2, waiting for transfers between devices: 17.8 us -> 7.89 us  [advance_line(): got_left = lax.ppermute(slot_b, 'sector', LEFT)]
    ppermute x2, waiting for transfers between devices: 48.1 us -> 40.5 us  [advance_line(): got_right = lax.ppermute(slot_a, 'sector', RIGHT)]
    convert_element_type x0 -> x2, other arithmetic: none -> 5.82 us  [advance_line(): send = send.astype(jnp.bfloat16)]
    ppermute x2, starting transfers between devices: 4.65 us -> 10.4 us  [advance_line(): got_right = lax.ppermute(slot_a, 'sector', RIGHT)]
    ppermute x3, starting transfers between devices: 5.18 us -> 8.97 us  [advance_line(): got_last = lax.ppermute(send[low:high], 'sector', LAST)]
  transfers between devices with their start and end apart: 18 -> 18, of which waited for: 12 -> 12; matrix products, arithmetic and copies ran while one was open for 19% -> 23% of each run, Pallas kernels for 0% -> 0%
where the time goes in v7:
time: 245 us; the launch traced here: 244 us
  waiting for transfers between devices  110 us (45%)
  matrix products  53.1 us (22%)
  starting transfers between devices  44.6 us (18%)
  other arithmetic  16.7 us (7%)
  local copies, waits for them, and re-layouts  12.2 us (5%)
  between operations  6.6 us (3%)
    ppermute x2, waiting for transfers between devices, advance_line(): got_right = lax.ppermute(slot_a, 'sector', RIGHT)  40.5 us
    dot_general x8, matrix products, term(): jnp.einsum('bd,vbc->vdc', bra_p, rotated, preferred_element_type=jnp.floa...  29.9 us
    ppermute x3, waiting for transfers between devices, advance_line(): got_last = lax.ppermute(send[low:high], 'sector', LAST)  28.1 us
    ppermute x7, waiting for transfers between devices, shifted(): return lax.ppermute(value, axis, pairs)  25.5 us
    dot_general x8, matrix products, term(): jnp.einsum('wv,wba->vba', mpo_p, gathered, preferred_element_type=jnp.flo...  23.2 us
    ppermute x2, starting transfers between devices, advance_line(): got_right = lax.ppermute(slot_a, 'sector', RIGHT)  10.4 us
    ppermute x2, starting transfers between devices, advance_line(): middle_right = lax.ppermute(slot_b, 'sector', ((0, 2),))  10.2 us
    ppermute x7, starting transfers between devices, shifted(): return lax.ppermute(value, axis, pairs)  9.13 us
  transfers between devices with their start and end apart: 18, of which 12 were waited for; matrix products, arithmetic and copies ran while one was open for 23% of the time, Pallas kernels for 0%

profile of v7, /device:TPU:0, one launch (start us, length us, event | category | flops | bytes accessed | tf_op | source)
XLA Modules:
  0.0 243.5 jit_solution(6962547920069253761)
XLA Ops:
  24.4 3.6 %fusion.24 = bf16[9,256,256]{1,2,0:T(8,128)(2,1)} fusion(bf16[9,256,256]{2,0,1:T(8,128)(2,1)} %fusion.2, bf16[1,1,4,256,256]{4,3,2,1,0:T(8,128)(2,1)} %param.15, s32[]{:T(128)S(6)} %select_n.81, bf16[1,1,4,256,256]{4,3,2,1,0:T(8,128)(2,1)} %param.14), kind=kOutput, calls=%fused_computation.60 | convolution fusion | flops 605159424 | bytes 3539968 | tf_op jit(solution)/shard_map/bd,vbc->vdc/dot_general | solution.py:29
  28.0 5.5 %collective-permute-start.6 = (bf16[9,256,256]{1,2,0:T(8,128)(2,1)}, bf16[9,256,256]{1,2,0:T(8,128)(2,1)}, u32[]{:S(2)}, u32[]{:S(2)}) collective-permute-start(bf16[9,256,256]{1,2,0:T(8,128)(2,1)} %fusion.24), channel_id=1, source_target_pairs={{0,4},{1,5},{8,12},{9,13},{16,20},{17,21},{24,28},{25,29}} | collective-permute-start | bytes 3538952 | tf_op jit(solution)/shard_map/ppermute | solution.py:64
  34.8 4.0 %fusion.6 = bf16[9,256,256]{2,0,1:T(8,128)(2,1)} fusion(bf16[18,256,256]{2,1,0:T(8,128)(2,1)S(1)} %pad_maximum_fusion, bf16[18,9,1]{1,2,0:T(2,128)(2,1)} %get-tuple-element.51), kind=kOutput, calls=%fused_computation.8 | convolution fusion | flops 21233664 | bytes 3539268 | tf_op jit(solution)/shard_map/wv,wba->vba/dot_general | solution.py:23
  44.1 5.2 %collective-permute-start.4 = (bf16[9,256,256]{1,2,0:T(8,128)(2,1)}, bf16[9,256,256]{1,2,0:T(8,128)(2,1)}, u32[]{:S(2)}, u32[]{:S(2)}) collective-permute-start(bf16[9,256,256]{1,2,0:T(8,128)(2,1)} %fusion.23), channel_id=1, source_target_pairs={{0,2},{2,4},{4,6},{1,3},{3,5},{5,7},{8,10},{10,12},{12,14},{9,11},... | collective-permute-start | bytes 3538952 | tf_op jit(solution)/shard_map/ppermute | solution.py:60
  49.3 4.0 %fusion = bf16[9,256,256]{2,0,1:T(8,128)(2,1)} fusion(bf16[18,256,256]{2,1,0:T(8,128)(2,1)S(1)} %pad_maximum_fusion, bf16[18,9,1]{1,2,0:T(2,128)(2,1)} %get-tuple-element.49), kind=kOutput, calls=%fused_computation.2 | convolution fusion | flops 21233664 | bytes 3539268 | tf_op jit(solution)/shard_map/wv,wba->vba/dot_general | solution.py:23
  53.3 3.6 %fusion.25 = bf16[9,256,256]{1,2,0:T(8,128)(2,1)} fusion(bf16[9,256,256]{2,0,1:T(8,128)(2,1)} %fusion, bf16[1,1,4,256,256]{4,3,2,1,0:T(8,128)(2,1)} %param.15, s32[]{:T(128)S(6)} %select_n.82, bf16[1,1,4,256,256]{4,3,2,1,0:T(8,128)(2,1)} %param.14), kind=kOutput, calls=%fused_computation.61 | convolution fusion | flops 605159424 | bytes 3539968 | tf_op jit(solution)/shard_map/bd,vbc->vdc/dot_general | solution.py:29
  62.8 20.3 %collective-permute-done.4 = bf16[9,256,256]{1,2,0:T(8,128)(2,1)} collective-permute-done((bf16[9,256,256]{1,2,0:T(8,128)(2,1)}, bf16[9,256,256]{1,2,0:T(8,128)(2,1)}, u32[]{:S(2)}, u32[]{:S(2)}) %collective-permute-start.4) | collective-permute-done | bytes 1179680 | tf_op jit(solution)/shard_map/ppermute | solution.py:60
  86.4 3.7 %collective-permute-start.8 = (bf16[9,256,256]{1,2,0:T(8,128)(2,1)}, bf16[9,256,256]{1,2,0:T(8,128)(2,1)}, u32[]{:S(2)}, u32[]{:S(2)}) collective-permute-start(bf16[9,256,256]{1,2,0:T(8,128)(2,1)} %fusion.16), channel_id=1, source_target_pairs={{0,2},{2,6},{6,4},{4,0},{1,3},{3,7},{7,5},{5,1},{8,10},{10,14},{14... | collective-permute-start | bytes 3538952 | tf_op jit(solution)/shard_map/ppermute | solution.py:85
  93.5 3.6 %convolution_convert_fusion.12 = bf16[9,256,256]{2,1,0:T(8,128)(2,1)} fusion(bf16[9,256,256]{2,0,1:T(8,128)(2,1)} %fusion.4, bf16[1,1,4,256,256]{4,3,2,1,0:T(8,128)(2,1)} %param.15, bf16[1,1,4,256,256]{4,3,2,1,0:T(8,128)(2,1)} %param.14), kind=kOutput, calls=%fused_computation.55 | convolution fusion | flops 605159424 | bytes 3538944 | tf_op jit(solution)/shard_map/bd,vbc->vdc/dot_general | solution.py:29
  97.2 19.0 %collective-permute-done.8 = bf16[9,256,256]{1,2,0:T(8,128)(2,1)} collective-permute-done((bf16[9,256,256]{1,2,0:T(8,128)(2,1)}, bf16[9,256,256]{1,2,0:T(8,128)(2,1)}, u32[]{:S(2)}, u32[]{:S(2)}) %collective-permute-start.8) | collective-permute-done | bytes 1179680 | tf_op jit(solution)/shard_map/ppermute | solution.py:85
  116.2 3.9 %fusion.13 = bf16[9,256,256]{1,2,0:T(8,128)(2,1)S(1)} fusion(bf16[9,256,256]{1,2,0:T(8,128)(2,1)} %collective-permute-done.4, bf16[9,256,256]{1,2,0:T(8,128)(2,1)S(1)} %collective-permute-done.5, bf16[9,256,256]{2,1,0:T(8,128)(2,1)} %convolution_convert_fusion.12, bf16[9,256,256]{1,2,0:T(8,128)(2,1)} %collective-permute-done.8, f32[256,256]{0,1:T(8,128)S(1)} %copy-done.2, ...), kind=kLoop, calls=%fused_computation.23 | loop fusion | flops 8257536 | bytes 8519688 | tf_op jit(solution)/shard_map/convert_element_type | solution.py:89
  124.6 3.7 %copy.30 = bf16[18,256,256]{2,0,1:T(8,128)(2,1)S(1)} copy(bf16[18,256,256]{1,2,0:T(8,128)(2,1)} %pad_maximum_fusion.1) | data formatting | bytes 4718592 | tf_op jit(solution)/shard_map/concatenate | solution.py:41
  130.4 3.6 %fusion.27 = bf16[9,256,256]{1,2,0:T(8,128)(2,1)} fusion(bf16[9,256,256]{2,0,1:T(8,128)(2,1)} %fusion.86, bf16[4,256,256]{2,1,0:T(8,128)(2,1)} %collective-permute-done.1, s32[]{:T(128)S(6)} %select_n.81, bf16[4,256,256]{2,1,0:T(8,128)(2,1)} %collective-permute-done), kind=kOutput, calls=%fused_computation.63 | convolution fusion | flops 605159424 | bytes 3539968 | tf_op jit(solution)/shard_map/bd,vbc->vdc/dot_general | solution.py:29
  134.0 4.7 %collective-permute-start.12 = (bf16[9,256,256]{1,2,0:T(8,128)(2,1)}, bf16[9,256,256]{1,2,0:T(8,128)(2,1)}, u32[]{:S(2)}, u32[]{:S(2)}) collective-permute-start(bf16[9,256,256]{1,2,0:T(8,128)(2,1)} %fusion.27), channel_id=1, source_target_pairs={{0,4},{1,5},{8,12},{9,13},{16,20},{17,21},{24,28},{25,29}} | collective-permute-start | bytes 3538952 | tf_op jit(solution)/shard_map/ppermute | solution.py:64
  147.4 5.2 %collective-permute-start.10 = (bf16[9,256,256]{1,2,0:T(8,128)(2,1)}, bf16[9,256,256]{1,2,0:T(8,128)(2,1)}, u32[]{:S(2)}, u32[]{:S(2)}) collective-permute-start(bf16[9,256,256]{1,2,0:T(8,128)(2,1)} %fusion.26), channel_id=1, source_target_pairs={{0,2},{2,4},{4,6},{1,3},{3,5},{5,7},{8,10},{10,12},{12,14},{9,11},... | collective-permute-start | bytes 3538952 | tf_op jit(solution)/shard_map/ppermute | solution.py:60
  154.7 3.7 %fusion.28 = bf16[9,256,256]{1,2,0:T(8,128)(2,1)} fusion(bf16[9,256,256]{2,0,1:T(8,128)(2,1)} %fusion.84, bf16[4,256,256]{2,1,0:T(8,128)(2,1)} %collective-permute-done.1, s32[]{:T(128)S(6)} %select_n.82, bf16[4,256,256]{2,1,0:T(8,128)(2,1)} %collective-permute-done), kind=kOutput, calls=%fused_computation.64 | convolution fusion | flops 605159424 | bytes 3539968 | tf_op jit(solution)/shard_map/bd,vbc->vdc/dot_general | solution.py:29
  158.4 6.0 %collective-permute-done.12 = bf16[9,256,256]{1,2,0:T(8,128)(2,1)} collective-permute-done((bf16[9,256,256]{1,2,0:T(8,128)(2,1)}, bf16[9,256,256]{1,2,0:T(8,128)(2,1)}, u32[]{:S(2)}, u32[]{:S(2)}) %collective-permute-start.12) | collective-permute-done | bytes 1179680 | tf_op jit(solution)/shard_map/ppermute | solution.py:64
  164.3 4.3 %collective-permute-done.11 = bf16[9,256,256]{1,2,0:T(8,128)(2,1)} collective-permute-done((bf16[9,256,256]{1,2,0:T(8,128)(2,1)}, bf16[9,256,256]{1,2,0:T(8,128)(2,1)}, u32[]{:S(2)}, u32[]{:S(2)}) %collective-permute-start.11) | collective-permute-done | bytes 1179680 | tf_op jit(solution)/shard_map/ppermute | solution.py:63
  168.6 20.2 %collective-permute-done.10 = bf16[9,256,256]{1,2,0:T(8,128)(2,1)} collective-permute-done((bf16[9,256,256]{1,2,0:T(8,128)(2,1)}, bf16[9,256,256]{1,2,0:T(8,128)(2,1)}, u32[]{:S(2)}, u32[]{:S(2)}) %collective-permute-start.10) | collective-permute-done | bytes 1179680 | tf_op jit(solution)/shard_map/ppermute | solution.py:60
  192.3 3.7 %collective-permute-start.14 = (bf16[4,256,256]{1,2,0:T(8,128)(2,1)}, bf16[4,256,256]{1,2,0:T(8,128)(2,1)}, u32[]{:S(2)}, u32[]{:S(2)}) collective-permute-start(bf16[4,256,256]{1,2,0:T(8,128)(2,1)} %slice.49), channel_id=1, source_target_pairs={{0,2},{2,6},{6,4},{4,0},{1,3},{3,7},{7,5},{5,1},{8,10},{10,14},{14... | collective-permute-start | bytes 1572872 | tf_op jit(solution)/shard_map/ppermute | solution.py:85
  198.2 4.4 %fusion.19 = f32[9,256,256]{1,2,0:T(8,128)S(1)} fusion(bf16[9,256,256]{1,2,0:T(8,128)(2,1)} %collective-permute-done.10, bf16[9,256,256]{1,2,0:T(8,128)(2,1)} %collective-permute-done.11, bf16[9,256,256]{1,2,0:T(8,128)(2,1)} %collective-permute-done.12, bf16[9,256,256]{1,2,0:T(8,128)(2,1)} %collective-permute-done.13, f32[]{:T(128)S(6)} %select_n.83, ...), kind=kOutput, calls=%fused_computation.29 | convolution fusion | flops 612237312 | bytes 9437192 | tf_op jit(solution)/shard_map/bd,vbc->vdc/dot_general | solution.py:29
  202.6 5.4 %collective-permute-done.14 = bf16[4,256,256]{1,2,0:T(8,128)(2,1)} collective-permute-done((bf16[4,256,256]{1,2,0:T(8,128)(2,1)}, bf16[4,256,256]{1,2,0:T(8,128)(2,1)}, u32[]{:S(2)}, u32[]{:S(2)}) %collective-permute-start.14) | collective-permute-done | bytes 524320 | tf_op jit(solution)/shard_map/ppermute | solution.py:85
  212.3 10.4 %collective-permute-done.15 = bf16[1,4,1,256,256]{3,4,1,2,0:T(8,128)(2,1)S(1)} collective-permute-done((bf16[1,4,1,256,256]{3,4,1,2,0:T(8,128)(2,1)S(1)}, bf16[1,4,1,256,256]{3,4,1,2,0:T(8,128)(2,1)S(1)}, u32[]{:S(2)}, u32[]{:S(2)}) %collective-permute-start.15) | collective-permute-done | bytes 524320 | tf_op jit(solution)/shard_map/ppermute | solution.py:19
  228.2 13.7 %collective-permute-done.17 = bf16[1,5,1,256,256]{3,4,1,2,0:T(8,128)(2,1)S(1)} collective-permute-done((bf16[1,5,1,256,256]{3,4,1,2,0:T(8,128)(2,1)S(1)}, bf16[1,5,1,256,256]{3,4,1,2,0:T(8,128)(2,1)S(1)}, u32[]{:S(2)}, u32[]{:S(2)}) %collective-permute-start.17) | collective-permute-done | bytes 655392 | tf_op jit(solution)/shard_map/ppermute | solution.py:19
  (77 shorter events, 71.3 us)
Async XLA Ops:
  0.0 9.8 %copy-start.9 = (s32[4]{0:T(128)S(1)}, s32[4]{0:T(128)}, u32[]{:S(2)}) copy-start(s32[4]{0:T(128)} %constant.107.clone) | copy-start | bytes 52
  0.0 11.6 %copy-start.8 = (s32[4]{0:T(128)S(1)}, s32[4]{0:T(128)}, u32[]{:S(2)}) copy-start(s32[4]{0:T(128)} %constant.106.clone) | copy-start | bytes 52
  0.0 13.7 %copy-start.7 = (s32[4]{0:T(128)S(1)}, s32[4]{0:T(128)}, u32[]{:S(2)}) copy-start(s32[4]{0:T(128)} %constant.105.clone) | copy-start | bytes 52
  3.1 16.4 %collective-permute-start.3 = (bf16[9,256,256]{2,1,0:T(8,128)(2,1)S(1)}, bf16[9,256,256]{2,1,0:T(8,128)(2,1)}, u32[]{:S(2)}, u32[]{:S(2)}) collective-permute-start(bf16[9,256,256]{2,1,0:T(8,128)(2,1)S(1)} %bitcast_select_fusion), channel_id=1, source_target_pairs={{0,1},{1,0},{2,3},{3,2},{4,5},{5,4},{6,7},{7,6},{8,9},{9,8},{10,11... | collective-permute-start | bytes 3538952 | tf_op jit(solution)/shard_map/ppermute | solution.py:19
  4.3 38.1 %collective-permute-start.2 = (bf16[18,9,4]{1,2,0:T(4,128)(2,1)}, bf16[18,9,4]{1,2,0:T(4,128)(2,1)}, u32[]{:S(2)}, u32[]{:S(2)}) collective-permute-start(bf16[18,9,4]{1,2,0:T(4,128)(2,1)} %bitcast.2), channel_id=1, source_target_pairs={{0,24},{8,0},{16,8},{24,16},{1,25},{9,1},{17,9},{25,17},{2,26},{10... | collective-permute-start | bytes 3896 | tf_op jit(solution)/shard_map/ppermute | solution.py:19
  7.8 34.6 %collective-permute-start.1 = (bf16[4,256,256]{2,1,0:T(8,128)(2,1)}, bf16[4,256,256]{2,1,0:T(8,128)(2,1)}, u32[]{:S(2)}, u32[]{:S(2)}) collective-permute-start(bf16[4,256,256]{2,1,0:T(8,128)(2,1)} %bitcast.1), channel_id=1, source_target_pairs={{0,24},{8,0},{16,8},{24,16},{1,25},{9,1},{17,9},{25,17},{2,26},{10... | collective-permute-start | bytes 1572872 | tf_op jit(solution)/shard_map/ppermute | solution.py:19
  8.3 34.1 %collective-permute-start = (bf16[4,256,256]{2,1,0:T(8,128)(2,1)}, bf16[4,256,256]{2,1,0:T(8,128)(2,1)}, u32[]{:S(2)}, u32[]{:S(2)}) collective-permute-start(bf16[4,256,256]{2,1,0:T(8,128)(2,1)} %bitcast), channel_id=1, source_target_pairs={{0,24},{8,0},{16,8},{24,16},{1,25},{9,1},{17,9},{25,17},{2,26},{10... | collective-permute-start | bytes 1572872 | tf_op jit(solution)/shard_map/ppermute | solution.py:19
  28.0 31.2 %collective-permute-start.6 = (bf16[9,256,256]{1,2,0:T(8,128)(2,1)}, bf16[9,256,256]{1,2,0:T(8,128)(2,1)}, u32[]{:S(2)}, u32[]{:S(2)}) collective-permute-start(bf16[9,256,256]{1,2,0:T(8,128)(2,1)} %fusion.24), channel_id=1, source_target_pairs={{0,4},{1,5},{8,12},{9,13},{16,20},{17,21},{24,28},{25,29}} | collective-permute-start | bytes 3538952 | tf_op jit(solution)/shard_map/ppermute | solution.py:64
  33.5 29.3 %collective-permute-start.5 = (bf16[9,256,256]{1,2,0:T(8,128)(2,1)}, bf16[9,256,256]{1,2,0:T(8,128)(2,1)S(1)}, u32[]{:S(2)}, u32[]{:S(2)}) collective-permute-start(bf16[9,256,256]{1,2,0:T(8,128)(2,1)} %fusion.24), channel_id=1, source_target_pairs={{6,4},{4,2},{2,0},{7,5},{5,3},{3,1},{14,12},{12,10},{10,8},{15,13}... | collective-permute-start | bytes 3538952 | tf_op jit(solution)/shard_map/ppermute | solution.py:63
  42.4 20.4 %collective-permute-start.7 = (bf16[9,256,256]{1,2,0:T(8,128)(2,1)}, bf16[9,256,256]{1,2,0:T(8,128)(2,1)}, u32[]{:S(2)}, u32[]{:S(2)}) collective-permute-start(bf16[9,256,256]{1,2,0:T(8,128)(2,1)} %fusion.23), channel_id=1, source_target_pairs={{6,2},{7,3},{14,10},{15,11},{22,18},{23,19},{30,26},{31,27}} | collective-permute-start | bytes 3538952 | tf_op jit(solution)/shard_map/ppermute | solution.py:61
  44.1 39.0 %collective-permute-start.4 = (bf16[9,256,256]{1,2,0:T(8,128)(2,1)}, bf16[9,256,256]{1,2,0:T(8,128)(2,1)}, u32[]{:S(2)}, u32[]{:S(2)}) collective-permute-start(bf16[9,256,256]{1,2,0:T(8,128)(2,1)} %fusion.23), channel_id=1, source_target_pairs={{0,2},{2,4},{4,6},{1,3},{3,5},{5,7},{8,10},{10,12},{12,14},{9,11},... | collective-permute-start | bytes 3538952 | tf_op jit(solution)/shard_map/ppermute | solution.py:60
  86.4 29.8 %collective-permute-start.8 = (bf16[9,256,256]{1,2,0:T(8,128)(2,1)}, bf16[9,256,256]{1,2,0:T(8,128)(2,1)}, u32[]{:S(2)}, u32[]{:S(2)}) collective-permute-start(bf16[9,256,256]{1,2,0:T(8,128)(2,1)} %fusion.16), channel_id=1, source_target_pairs={{0,2},{2,6},{6,4},{4,0},{1,3},{3,7},{7,5},{5,1},{8,10},{10,14},{14... | collective-permute-start | bytes 3538952 | tf_op jit(solution)/shard_map/ppermute | solution.py:85
  93.5 22.7 %copy-start.2 = (f32[256,256]{0,1:T(8,128)S(1)}, f32[256,256]{0,1:T(8,128)}, u32[]{:S(2)}) copy-start(f32[256,256]{0,1:T(8,128)} %get-tuple-element.52) | copy-start | bytes 786436
  120.1 2.9 %collective-permute-start.9 = (bf16[9,256,256]{1,2,0:T(8,128)(2,1)S(1)}, bf16[9,256,256]{1,2,0:T(8,128)(2,1)S(1)}, u32[]{:S(2)}, u32[]{:S(2)}) collective-permute-start(bf16[9,256,256]{1,2,0:T(8,128)(2,1)S(1)} %fusion.13), channel_id=1, source_target_pairs={{0,1},{1,0},{2,3},{3,2},{4,5},{5,4},{6,7},{7,6},{8,9},{9,8},{10,11... | collective-permute-start | bytes 3538952 | tf_op jit(solution)/shard_map/ppermute | solution.py:19
  134.0 30.3 %collective-permute-start.12 = (bf16[9,256,256]{1,2,0:T(8,128)(2,1)}, bf16[9,256,256]{1,2,0:T(8,128)(2,1)}, u32[]{:S(2)}, u32[]{:S(2)}) collective-permute-start(bf16[9,256,256]{1,2,0:T(8,128)(2,1)} %fusion.27), channel_id=1, source_target_pairs={{0,4},{1,5},{8,12},{9,13},{16,20},{17,21},{24,28},{25,29}} | collective-permute-start | bytes 3538952 | tf_op jit(solution)/shard_map/ppermute | solution.py:64
  138.7 29.9 %collective-permute-start.11 = (bf16[9,256,256]{1,2,0:T(8,128)(2,1)}, bf16[9,256,256]{1,2,0:T(8,128)(2,1)}, u32[]{:S(2)}, u32[]{:S(2)}) collective-permute-start(bf16[9,256,256]{1,2,0:T(8,128)(2,1)} %fusion.27), channel_id=1, source_target_pairs={{6,4},{4,2},{2,0},{7,5},{5,3},{3,1},{14,12},{12,10},{10,8},{15,13}... | collective-permute-start | bytes 3538952 | tf_op jit(solution)/shard_map/ppermute | solution.py:63
  145.7 22.9 %collective-permute-start.13 = (bf16[9,256,256]{1,2,0:T(8,128)(2,1)}, bf16[9,256,256]{1,2,0:T(8,128)(2,1)}, u32[]{:S(2)}, u32[]{:S(2)}) collective-permute-start(bf16[9,256,256]{1,2,0:T(8,128)(2,1)} %fusion.26), channel_id=1, source_target_pairs={{6,2},{7,3},{14,10},{15,11},{22,18},{23,19},{30,26},{31,27}} | collective-permute-start | bytes 3538952 | tf_op jit(solution)/shard_map/ppermute | solution.py:61
  147.4 41.4 %collective-permute-start.10 = (bf16[9,256,256]{1,2,0:T(8,128)(2,1)}, bf16[9,256,256]{1,2,0:T(8,128)(2,1)}, u32[]{:S(2)}, u32[]{:S(2)}) collective-permute-start(bf16[9,256,256]{1,2,0:T(8,128)(2,1)} %fusion.26), channel_id=1, source_target_pairs={{0,2},{2,4},{4,6},{1,3},{3,5},{5,7},{8,10},{10,12},{12,14},{9,11},... | collective-permute-start | bytes 3538952 | tf_op jit(solution)/shard_map/ppermute | solution.py:60
  192.3 15.8 %collective-permute-start.14 = (bf16[4,256,256]{1,2,0:T(8,128)(2,1)}, bf16[4,256,256]{1,2,0:T(8,128)(2,1)}, u32[]{:S(2)}, u32[]{:S(2)}) collective-permute-start(bf16[4,256,256]{1,2,0:T(8,128)(2,1)} %slice.49), channel_id=1, source_target_pairs={{0,2},{2,6},{6,4},{4,0},{1,3},{3,7},{7,5},{5,1},{8,10},{10,14},{14... | collective-permute-start | bytes 1572872 | tf_op jit(solution)/shard_map/ppermute | solution.py:85
  198.2 9.9 %copy-start.3 = (f32[256,256]{0,1:T(8,128)S(1)}, f32[256,256]{0,1:T(8,128)}, u32[]{:S(2)}) copy-start(f32[256,256]{0,1:T(8,128)} %get-tuple-element.52) | copy-start | bytes 786436
  202.6 6.6 %copy-start.1 = (bf16[9,256,256]{1,2,0:T(8,128)(2,1)S(1)}, bf16[9,256,256]{1,2,0:T(8,128)(2,1)}, u32[]{:S(2)}) copy-start(bf16[9,256,256]{1,2,0:T(8,128)(2,1)} %copy-done) | copy-start | bytes 3538948
  209.3 17.1 %collective-permute-start.16 = (bf16[5,256,256]{1,2,0:T(8,128)(2,1)S(1)}, bf16[5,256,256]{1,2,0:T(8,128)(2,1)S(1)}, u32[]{:S(2)}, u32[]{:S(2)}) collective-permute-start(bf16[5,256,256]{1,2,0:T(8,128)(2,1)S(1)} %slice.40), channel_id=1, source_target_pairs={{0,2},{2,6},{6,4},{4,0},{1,3},{3,7},{7,5},{5,1},{8,10},{10,14},{14... | collective-permute-start | bytes 1966088 | tf_op jit(solution)/shard_map/ppermute | solution.py:85
  210.8 12.0 %collective-permute-start.15 = (bf16[1,4,1,256,256]{3,4,1,2,0:T(8,128)(2,1)S(1)}, bf16[1,4,1,256,256]{3,4,1,2,0:T(8,128)(2,1)S(1)}, u32[]{:S(2)}, u32[]{:S(2)}) collective-permute-start(bf16[1,4,1,256,256]{3,4,1,2,0:T(8,128)(2,1)S(1)} %bitcast.123), channel_id=1, source_target_pairs={{0,16},{8,24},{16,0},{24,8},{1,17},{9,25},{17,1},{25,9},{2,18},{10... | collective-permute-start | bytes 1572872 | tf_op jit(solution)/shard_map/ppermute | solution.py:19
  226.6 15.3 %collective-permute-start.17 = (bf16[1,5,1,256,256]{3,4,1,2,0:T(8,128)(2,1)S(1)}, bf16[1,5,1,256,256]{3,4,1,2,0:T(8,128)(2,1)S(1)}, u32[]{:S(2)}, u32[]{:S(2)}) collective-permute-start(bf16[1,5,1,256,256]{3,4,1,2,0:T(8,128)(2,1)S(1)} %fusion.33), channel_id=1, source_target_pairs={{0,16},{8,24},{16,0},{24,8},{1,17},{9,25},{17,1},{25,9},{2,18},{10... | collective-permute-start | bytes 1966088 | tf_op jit(solution)/shard_map/ppermute | solution.py:19
  (4 other events, 17.5 us)

commit v8 on v7

--- a/solution.py
+++ b/solution.py
@@ -41,28 +41,23 @@
     return jnp.concatenate(held, axis=0), jnp.take(mpo, order, axis=0)
 
 
-def pick(table, sector, ket, bra, mpo):
-    p = jnp.asarray(table, jnp.int32)[sector]
-    return (
-        lax.dynamic_index_in_dim(ket, p, 0, keepdims=False),
-        lax.dynamic_index_in_dim(bra, p, 0, keepdims=False),
-        lax.dynamic_index_in_dim(mpo, p, 2, keepdims=False),
-    )
-
-
 def advance_line(current, ket, bra, mpo, live_mask, sector, held, pieces, finish):
     gathered, mpo = chan_gathered(current, mpo)
     f32 = jnp.float32
     one = jnp.ones((), f32)
     zero = jnp.zeros((), f32)
-    slot_a = term(gathered, *pick(SLOT_A, sector, ket, bra, mpo))
+    order = jnp.asarray(list(zip(SLOT_A, SLOT_B, LAST_P, (0,) * 4)), jnp.int32)[sector]
+    ket = jnp.take(ket, order, axis=0)
+    bra = jnp.take(bra, order, axis=0)
+    mpo = jnp.take(mpo, order, axis=2)
+    slot_a = term(gathered, ket[0], bra[0], mpo[:, :, 0])
     held, slot_a = lax.optimization_barrier((held, slot_a))
     got_right = lax.ppermute(slot_a, "sector", RIGHT)
     middle_left = lax.ppermute(slot_a, "sector", ((3, 1),))
-    slot_b = term(gathered, *pick(SLOT_B, sector, ket, bra, mpo))
+    slot_b = term(gathered, ket[1], bra[1], mpo[:, :, 1])
     got_left = lax.ppermute(slot_b, "sector", LEFT)
     middle_right = lax.ppermute(slot_b, "sector", ((0, 2),))
-    third = term(gathered, *pick(LAST_P, sector, ket, bra, mpo))
+    third = term(gathered, ket[2], bra[2], mpo[:, :, 2])
     got = (got_right, got_left, middle_right, middle_left, third)
     got_right, got_left, middle_right, middle_left, third = lax.optimization_barrier(got)
     got_middle = middle_right + middle_left
@@ -71,7 +66,7 @@
     send = third.astype(f32) + (1 - keep_right) * got_right.astype(f32)
     send = send + (1 - keep_left) * got_left.astype(f32)
     send = send.astype(jnp.bfloat16)
-    own = term(gathered, ket[0], bra[0], mpo[:, :, 0])
+    own = term(gathered, ket[3], bra[3], mpo[:, :, 3])
     total = own.astype(f32) + keep_right * got_right.astype(f32)
     total = total + keep_left * got_left.astype(f32) + got_middle.astype(f32)
     width = send.shape[0]

time: 245 us -> 245 us (level)
  between operations: 6.6 us -> 0.98 us
  local copies, waits for them, and re-layouts: 12.2 us -> 15.9 us
  matrix products: 53.1 us -> 49.6 us
  other arithmetic: 16.7 us -> 19.8 us
    gather x0 -> x6, local copies, waits for them, and re-layouts: none -> 5.91 us  [the longest x2 2.32 us: advance_line(): bra = jnp.take(bra, order, axis=0)]
    ppermute x3, waiting for transfers between devices: 28.1 us -> 33.6 us  [advance_line(): got_last = lax.ppermute(send[low:high], 'sector', LAST)]
    ppermute x2, waiting for transfers between devices: 8.25 us -> 4.76 us  [advance_line(): middle_right = lax.ppermute(slot_b, 'sector', ((0, 2),))]
  transfers between devices with their start and end apart: 18 -> 18, of which waited for: 12 -> 11; matrix products, arithmetic and copies ran while one was open for 23% -> 25% of each run, Pallas kernels for 0% -> 0%
where the time goes in v8:
time: 245 us; the launch traced here: 244 us
  waiting for transfers between devices  112 us (46%)
  matrix products  49.6 us (20%)
  starting transfers between devices  45.6 us (19%)
  other arithmetic  19.8 us (8%)
  local copies, waits for them, and re-layouts  15.9 us (6%)
    ppermute x2, waiting for transfers between devices, advance_line(): got_right = lax.ppermute(slot_a, 'sector', RIGHT)  40.5 us
    ppermute x3, waiting for transfers between devices, advance_line(): got_last = lax.ppermute(send[low:high], 'sector', LAST)  33.6 us
    dot_general x8, matrix products, term(): jnp.einsum('bd,vbc->vdc', bra_p, rotated, preferred_element_type=jnp.floa...  28.1 us
    ppermute x7, waiting for transfers between devices, shifted(): return lax.ppermute(value, axis, pairs)  24.1 us
    dot_general x8, matrix products, term(): jnp.einsum('wv,wba->vba', mpo_p, gathered, preferred_element_type=jnp.flo...  21.5 us
    ppermute x2, starting transfers between devices, advance_line(): got_right = lax.ppermute(slot_a, 'sector', RIGHT)  10.3 us
    ppermute x2, starting transfers between devices, advance_line(): middle_right = lax.ppermute(slot_b, 'sector', ((0, 2),))  10.2 us
    ppermute x3, starting transfers between devices, advance_line(): got_last = lax.ppermute(send[low:high], 'sector', LAST)  9.92 us
  transfers between devices with their start and end apart: 18, of which 11 were waited for; matrix products, arithmetic and copies ran while one was open for 25% of the time, Pallas kernels for 0%

profile of v8, /device:TPU:0, one launch (start us, length us, event | category | flops | bytes accessed | tf_op | source)
XLA Modules:
  0.0 244.2 jit_solution(1550535622263443511)
XLA Ops:
  1.5 3.9 %collective-permute-start.2 = (bf16[18,9,4]{1,2,0:T(4,128)(2,1)}, bf16[18,9,4]{1,2,0:T(4,128)(2,1)}, u32[]{:S(2)}, u32[]{:S(2)}) collective-permute-start(bf16[18,9,4]{1,2,0:T(4,128)(2,1)} %bitcast.3), channel_id=1, source_target_pairs={{0,24},{8,0},{16,8},{24,16},{1,25},{9,1},{17,9},{25,17},{2,26},{10... | collective-permute-start | bytes 3896 | tf_op jit(solution)/shard_map/ppermute | solution.py:19
  20.7 3.6 %fusion.24 = bf16[9,256,256]{1,2,0:T(8,128)(2,1)} fusion(bf16[9,256,256]{2,0,1:T(8,128)(2,1)} %fusion.2, bf16[4,256,256]{2,1,0:T(8,128)(2,1)} %get-tuple-element.55, bf16[4,256,256]{2,1,0:T(8,128)(2,1)} %get-tuple-element.54), kind=kOutput, calls=%fused_computation.66 | convolution fusion | flops 605159424 | bytes 3538944 | tf_op jit(solution)/shard_map/bd,vbc->vdc/dot_general | solution.py:29
  24.3 5.5 %collective-permute-start.6 = (bf16[9,256,256]{1,2,0:T(8,128)(2,1)}, bf16[9,256,256]{1,2,0:T(8,128)(2,1)}, u32[]{:S(2)}, u32[]{:S(2)}) collective-permute-start(bf16[9,256,256]{1,2,0:T(8,128)(2,1)} %fusion.24), channel_id=1, source_target_pairs={{0,4},{1,5},{8,12},{9,13},{16,20},{17,21},{24,28},{25,29}} | collective-permute-start | bytes 3538952 | tf_op jit(solution)/shard_map/ppermute | solution.py:59
  34.4 3.6 %fusion.23 = bf16[9,256,256]{1,2,0:T(8,128)(2,1)} fusion(bf16[9,256,256]{2,0,1:T(8,128)(2,1)} %fusion.6, bf16[4,256,256]{2,1,0:T(8,128)(2,1)} %get-tuple-element.55, bf16[4,256,256]{2,1,0:T(8,128)(2,1)} %get-tuple-element.54), kind=kOutput, calls=%fused_computation.65 | convolution fusion | flops 605159424 | bytes 3538944 | tf_op jit(solution)/shard_map/bd,vbc->vdc/dot_general | solution.py:29
  39.8 5.2 %collective-permute-start.4 = (bf16[9,256,256]{1,2,0:T(8,128)(2,1)}, bf16[9,256,256]{1,2,0:T(8,128)(2,1)}, u32[]{:S(2)}, u32[]{:S(2)}) collective-permute-start(bf16[9,256,256]{1,2,0:T(8,128)(2,1)} %fusion.23), channel_id=1, source_target_pairs={{0,2},{2,4},{4,6},{1,3},{3,5},{5,7},{8,10},{10,12},{12,14},{9,11},... | collective-permute-start | bytes 3538952 | tf_op jit(solution)/shard_map/ppermute | solution.py:55
  48.3 3.6 %fusion.25 = bf16[9,256,256]{1,2,0:T(8,128)(2,1)} fusion(bf16[9,256,256]{2,0,1:T(8,128)(2,1)} %fusion, bf16[4,256,256]{2,1,0:T(8,128)(2,1)} %get-tuple-element.55, bf16[4,256,256]{2,1,0:T(8,128)(2,1)} %get-tuple-element.54), kind=kOutput, calls=%fused_computation.67 | convolution fusion | flops 605159424 | bytes 3538944 | tf_op jit(solution)/shard_map/bd,vbc->vdc/dot_general | solution.py:29
  55.4 4.6 %collective-permute-done.5 = bf16[9,256,256]{1,2,0:T(8,128)(2,1)S(1)} collective-permute-done((bf16[9,256,256]{1,2,0:T(8,128)(2,1)}, bf16[9,256,256]{1,2,0:T(8,128)(2,1)S(1)}, u32[]{:S(2)}, u32[]{:S(2)}) %collective-permute-start.5) | collective-permute-done | bytes 1179680 | tf_op jit(solution)/shard_map/ppermute | solution.py:58
  60.0 20.3 %collective-permute-done.4 = bf16[9,256,256]{1,2,0:T(8,128)(2,1)} collective-permute-done((bf16[9,256,256]{1,2,0:T(8,128)(2,1)}, bf16[9,256,256]{1,2,0:T(8,128)(2,1)}, u32[]{:S(2)}, u32[]{:S(2)}) %collective-permute-start.4) | collective-permute-done | bytes 1179680 | tf_op jit(solution)/shard_map/ppermute | solution.py:55
  83.5 3.7 %collective-permute-start.8 = (bf16[9,256,256]{1,2,0:T(8,128)(2,1)}, bf16[9,256,256]{1,2,0:T(8,128)(2,1)}, u32[]{:S(2)}, u32[]{:S(2)}) collective-permute-start(bf16[9,256,256]{1,2,0:T(8,128)(2,1)} %fusion.16), channel_id=1, source_target_pairs={{0,2},{2,6},{6,4},{4,0},{1,3},{3,7},{7,5},{5,1},{8,10},{10,14},{14... | collective-permute-start | bytes 3538952 | tf_op jit(solution)/shard_map/ppermute | solution.py:80
  90.6 3.6 %convolution_convert_fusion.12 = bf16[9,256,256]{2,1,0:T(8,128)(2,1)} fusion(bf16[9,256,256]{2,0,1:T(8,128)(2,1)} %fusion.4, bf16[4,256,256]{2,1,0:T(8,128)(2,1)} %get-tuple-element.55, bf16[4,256,256]{2,1,0:T(8,128)(2,1)} %get-tuple-element.54), kind=kOutput, calls=%fused_computation.61 | convolution fusion | flops 605159424 | bytes 3538944 | tf_op jit(solution)/shard_map/bd,vbc->vdc/dot_general | solution.py:29
  94.2 19.1 %collective-permute-done.8 = bf16[9,256,256]{1,2,0:T(8,128)(2,1)} collective-permute-done((bf16[9,256,256]{1,2,0:T(8,128)(2,1)}, bf16[9,256,256]{1,2,0:T(8,128)(2,1)}, u32[]{:S(2)}, u32[]{:S(2)}) %collective-permute-start.8) | collective-permute-done | bytes 1179680 | tf_op jit(solution)/shard_map/ppermute | solution.py:80
  113.3 3.9 %fusion.13 = bf16[9,256,256]{1,2,0:T(8,128)(2,1)S(1)} fusion(bf16[9,256,256]{1,2,0:T(8,128)(2,1)} %collective-permute-done.4, bf16[9,256,256]{1,2,0:T(8,128)(2,1)S(1)} %collective-permute-done.5, bf16[9,256,256]{2,1,0:T(8,128)(2,1)} %convolution_convert_fusion.12, bf16[9,256,256]{1,2,0:T(8,128)(2,1)} %collective-permute-done.8, f32[256,256]{0,1:T(8,128)S(1)} %copy-done, ...), kind=kLoop, calls=%fused_computation.29 | loop fusion | flops 8257536 | bytes 8519688 | tf_op jit(solution)/shard_map/convert_element_type | solution.py:84
  126.0 3.7 %copy.20 = bf16[18,256,256]{2,0,1:T(8,128)(2,1)S(1)} copy(bf16[18,256,256]{1,2,0:T(8,128)(2,1)} %pad_maximum_fusion.1) | data formatting | bytes 4718592 | tf_op jit(solution)/shard_map/concatenate | solution.py:41
  131.7 3.6 %fusion.27 = bf16[9,256,256]{1,2,0:T(8,128)(2,1)} fusion(bf16[9,256,256]{2,0,1:T(8,128)(2,1)} %fusion.37, bf16[4,256,256]{2,1,0:T(8,128)(2,1)} %get-tuple-element.51, bf16[4,256,256]{2,1,0:T(8,128)(2,1)} %get-tuple-element.50), kind=kOutput, calls=%fused_computation.69 | convolution fusion | flops 605159424 | bytes 3538944 | tf_op jit(solution)/shard_map/bd,vbc->vdc/dot_general | solution.py:29
  135.4 4.7 %collective-permute-start.12 = (bf16[9,256,256]{1,2,0:T(8,128)(2,1)}, bf16[9,256,256]{1,2,0:T(8,128)(2,1)}, u32[]{:S(2)}, u32[]{:S(2)}) collective-permute-start(bf16[9,256,256]{1,2,0:T(8,128)(2,1)} %fusion.27), channel_id=1, source_target_pairs={{0,4},{1,5},{8,12},{9,13},{16,20},{17,21},{24,28},{25,29}} | collective-permute-start | bytes 3538952 | tf_op jit(solution)/shard_map/ppermute | solution.py:59
  143.4 3.6 %fusion.26 = bf16[9,256,256]{1,2,0:T(8,128)(2,1)} fusion(bf16[9,256,256]{2,0,1:T(8,128)(2,1)} %fusion.39, bf16[4,256,256]{2,1,0:T(8,128)(2,1)} %get-tuple-element.51, bf16[4,256,256]{2,1,0:T(8,128)(2,1)} %get-tuple-element.50), kind=kOutput, calls=%fused_computation.68 | convolution fusion | flops 605159424 | bytes 3538944 | tf_op jit(solution)/shard_map/bd,vbc->vdc/dot_general | solution.py:29
  148.7 5.2 %collective-permute-start.10 = (bf16[9,256,256]{1,2,0:T(8,128)(2,1)}, bf16[9,256,256]{1,2,0:T(8,128)(2,1)}, u32[]{:S(2)}, u32[]{:S(2)}) collective-permute-start(bf16[9,256,256]{1,2,0:T(8,128)(2,1)} %fusion.26), channel_id=1, source_target_pairs={{0,2},{2,4},{4,6},{1,3},{3,5},{5,7},{8,10},{10,12},{12,14},{9,11},... | collective-permute-start | bytes 3538952 | tf_op jit(solution)/shard_map/ppermute | solution.py:55
  155.9 3.7 %fusion.28 = bf16[9,256,256]{1,2,0:T(8,128)(2,1)} fusion(bf16[9,256,256]{2,0,1:T(8,128)(2,1)} %fusion.35, bf16[4,256,256]{2,1,0:T(8,128)(2,1)} %get-tuple-element.51, bf16[4,256,256]{2,1,0:T(8,128)(2,1)} %get-tuple-element.50), kind=kOutput, calls=%fused_computation.70 | convolution fusion | flops 605159424 | bytes 3538944 | tf_op jit(solution)/shard_map/bd,vbc->vdc/dot_general | solution.py:29
  165.6 4.7 %collective-permute-done.11 = bf16[9,256,256]{1,2,0:T(8,128)(2,1)} collective-permute-done((bf16[9,256,256]{1,2,0:T(8,128)(2,1)}, bf16[9,256,256]{1,2,0:T(8,128)(2,1)}, u32[]{:S(2)}, u32[]{:S(2)}) %collective-permute-start.11) | collective-permute-done | bytes 1179680 | tf_op jit(solution)/shard_map/ppermute | solution.py:58
  170.3 20.2 %collective-permute-done.10 = bf16[9,256,256]{1,2,0:T(8,128)(2,1)} collective-permute-done((bf16[9,256,256]{1,2,0:T(8,128)(2,1)}, bf16[9,256,256]{1,2,0:T(8,128)(2,1)}, u32[]{:S(2)}, u32[]{:S(2)}) %collective-permute-start.10) | collective-permute-done | bytes 1179680 | tf_op jit(solution)/shard_map/ppermute | solution.py:55
  194.2 4.3 %collective-permute-start.14 = (bf16[4,256,256]{1,2,0:T(8,128)(2,1)S(1)}, bf16[4,256,256]{1,2,0:T(8,128)(2,1)S(1)}, u32[]{:S(2)}, u32[]{:S(2)}) collective-permute-start(bf16[4,256,256]{1,2,0:T(8,128)(2,1)S(1)} %slice.153), channel_id=1, source_target_pairs={{0,2},{2,6},{6,4},{4,0},{1,3},{3,7},{7,5},{5,1},{8,10},{10,14},{14... | collective-permute-start | bytes 1572872 | tf_op jit(solution)/shard_map/ppermute | solution.py:80
  198.4 11.3 %collective-permute-done.14 = bf16[4,256,256]{1,2,0:T(8,128)(2,1)S(1)} collective-permute-done((bf16[4,256,256]{1,2,0:T(8,128)(2,1)S(1)}, bf16[4,256,256]{1,2,0:T(8,128)(2,1)S(1)}, u32[]{:S(2)}, u32[]{:S(2)}) %collective-permute-start.14) | collective-permute-done | bytes 524320 | tf_op jit(solution)/shard_map/ppermute | solution.py:80
  213.4 10.4 %collective-permute-done.15 = bf16[1,4,1,256,256]{3,4,1,2,0:T(8,128)(2,1)S(1)} collective-permute-done((bf16[1,4,1,256,256]{3,4,1,2,0:T(8,128)(2,1)S(1)}, bf16[1,4,1,256,256]{3,4,1,2,0:T(8,128)(2,1)S(1)}, u32[]{:S(2)}, u32[]{:S(2)}) %collective-permute-start.15) | collective-permute-done | bytes 524320 | tf_op jit(solution)/shard_map/ppermute | solution.py:19
  228.8 13.7 %collective-permute-done.17 = bf16[1,5,1,256,256]{3,4,1,2,0:T(8,128)(2,1)S(1)} collective-permute-done((bf16[1,5,1,256,256]{3,4,1,2,0:T(8,128)(2,1)S(1)}, bf16[1,5,1,256,256]{3,4,1,2,0:T(8,128)(2,1)S(1)}, u32[]{:S(2)}, u32[]{:S(2)}) %collective-permute-start.17) | collective-permute-done | bytes 655392 | tf_op jit(solution)/shard_map/ppermute | solution.py:19
  (88 shorter events, 73.5 us)
Async XLA Ops:
  0.0 11.8 %copy-start.3 = (bf16[1,1,4,256,256]{4,3,2,1,0:T(8,128)(2,1)S(1)}, bf16[1,1,4,256,256]{4,3,2,1,0:T(8,128)(2,1)}, u32[]{:S(2)}) copy-start(bf16[1,1,4,256,256]{4,3,2,1,0:T(8,128)(2,1)} %param.14) | copy-start | bytes 1572868
  0.0 11.2 %copy-start.4 = (bf16[1,1,4,256,256]{4,3,2,1,0:T(8,128)(2,1)S(1)}, bf16[1,1,4,256,256]{4,3,2,1,0:T(8,128)(2,1)}, u32[]{:S(2)}) copy-start(bf16[1,1,4,256,256]{4,3,2,1,0:T(8,128)(2,1)} %param.15) | copy-start | bytes 1572868
  1.5 36.5 %collective-permute-start.2 = (bf16[18,9,4]{1,2,0:T(4,128)(2,1)}, bf16[18,9,4]{1,2,0:T(4,128)(2,1)}, u32[]{:S(2)}, u32[]{:S(2)}) collective-permute-start(bf16[18,9,4]{1,2,0:T(4,128)(2,1)} %bitcast.3), channel_id=1, source_target_pairs={{0,24},{8,0},{16,8},{24,16},{1,25},{9,1},{17,9},{25,17},{2,26},{10... | collective-permute-start | bytes 3896 | tf_op jit(solution)/shard_map/ppermute | solution.py:19
  5.4 32.6 %collective-permute-start = (bf16[4,256,256]{2,1,0:T(8,128)(2,1)}, bf16[4,256,256]{2,1,0:T(8,128)(2,1)}, u32[]{:S(2)}, u32[]{:S(2)}) collective-permute-start(bf16[4,256,256]{2,1,0:T(8,128)(2,1)} %bitcast.117), channel_id=1, source_target_pairs={{0,24},{8,0},{16,8},{24,16},{1,25},{9,1},{17,9},{25,17},{2,26},{10... | collective-permute-start | bytes 1572872 | tf_op jit(solution)/shard_map/ppermute | solution.py:19
  5.9 32.1 %collective-permute-start.1 = (bf16[4,256,256]{2,1,0:T(8,128)(2,1)}, bf16[4,256,256]{2,1,0:T(8,128)(2,1)}, u32[]{:S(2)}, u32[]{:S(2)}) collective-permute-start(bf16[4,256,256]{2,1,0:T(8,128)(2,1)} %bitcast.119), channel_id=1, source_target_pairs={{0,24},{8,0},{16,8},{24,16},{1,25},{9,1},{17,9},{25,17},{2,26},{10... | collective-permute-start | bytes 1572872 | tf_op jit(solution)/shard_map/ppermute | solution.py:19
  10.4 5.5 %collective-permute-start.3 = (bf16[9,256,256]{2,1,0:T(8,128)(2,1)S(1)}, bf16[9,256,256]{2,1,0:T(8,128)(2,1)}, u32[]{:S(2)}, u32[]{:S(2)}) collective-permute-start(bf16[9,256,256]{2,1,0:T(8,128)(2,1)S(1)} %bitcast_select_fusion), channel_id=1, source_target_pairs={{0,1},{1,0},{2,3},{3,2},{4,5},{5,4},{6,7},{7,6},{8,9},{9,8},{10,11... | collective-permute-start | bytes 3538952 | tf_op jit(solution)/shard_map/ppermute | solution.py:19
  24.3 31.1 %collective-permute-start.6 = (bf16[9,256,256]{1,2,0:T(8,128)(2,1)}, bf16[9,256,256]{1,2,0:T(8,128)(2,1)}, u32[]{:S(2)}, u32[]{:S(2)}) collective-permute-start(bf16[9,256,256]{1,2,0:T(8,128)(2,1)} %fusion.24), channel_id=1, source_target_pairs={{0,4},{1,5},{8,12},{9,13},{16,20},{17,21},{24,28},{25,29}} | collective-permute-start | bytes 3538952 | tf_op jit(solution)/shard_map/ppermute | solution.py:59
  29.8 30.2 %collective-permute-start.5 = (bf16[9,256,256]{1,2,0:T(8,128)(2,1)}, bf16[9,256,256]{1,2,0:T(8,128)(2,1)S(1)}, u32[]{:S(2)}, u32[]{:S(2)}) collective-permute-start(bf16[9,256,256]{1,2,0:T(8,128)(2,1)} %fusion.24), channel_id=1, source_target_pairs={{6,4},{4,2},{2,0},{7,5},{5,3},{3,1},{14,12},{12,10},{10,8},{15,13}... | collective-permute-start | bytes 3538952 | tf_op jit(solution)/shard_map/ppermute | solution.py:58
  38.0 21.9 %collective-permute-start.7 = (bf16[9,256,256]{1,2,0:T(8,128)(2,1)}, bf16[9,256,256]{1,2,0:T(8,128)(2,1)}, u32[]{:S(2)}, u32[]{:S(2)}) collective-permute-start(bf16[9,256,256]{1,2,0:T(8,128)(2,1)} %fusion.23), channel_id=1, source_target_pairs={{6,2},{7,3},{14,10},{15,11},{22,18},{23,19},{30,26},{31,27}} | collective-permute-start | bytes 3538952 | tf_op jit(solution)/shard_map/ppermute | solution.py:56
  39.8 40.5 %collective-permute-start.4 = (bf16[9,256,256]{1,2,0:T(8,128)(2,1)}, bf16[9,256,256]{1,2,0:T(8,128)(2,1)}, u32[]{:S(2)}, u32[]{:S(2)}) collective-permute-start(bf16[9,256,256]{1,2,0:T(8,128)(2,1)} %fusion.23), channel_id=1, source_target_pairs={{0,2},{2,4},{4,6},{1,3},{3,5},{5,7},{8,10},{10,12},{12,14},{9,11},... | collective-permute-start | bytes 3538952 | tf_op jit(solution)/shard_map/ppermute | solution.py:55
  83.5 29.8 %collective-permute-start.8 = (bf16[9,256,256]{1,2,0:T(8,128)(2,1)}, bf16[9,256,256]{1,2,0:T(8,128)(2,1)}, u32[]{:S(2)}, u32[]{:S(2)}) collective-permute-start(bf16[9,256,256]{1,2,0:T(8,128)(2,1)} %fusion.16), channel_id=1, source_target_pairs={{0,2},{2,6},{6,4},{4,0},{1,3},{3,7},{7,5},{5,1},{8,10},{10,14},{14... | collective-permute-start | bytes 3538952 | tf_op jit(solution)/shard_map/ppermute | solution.py:80
  90.6 22.8 %copy-start = (f32[256,256]{0,1:T(8,128)S(1)}, f32[256,256]{0,1:T(8,128)}, u32[]{:S(2)}) copy-start(f32[256,256]{0,1:T(8,128)} %get-tuple-element.52) | copy-start | bytes 786436
  117.2 5.9 %copy-start.6 = (pred[4]{0:T(512)(128)(4,1)S(1)}, pred[4]{0:T(512)(128)(4,1)}, u32[]{:S(2)}) copy-start(pred[4]{0:T(512)(128)(4,1)} %copy-done.5) | copy-start | bytes 16
  117.2 7.2 %collective-permute-start.9 = (bf16[9,256,256]{1,2,0:T(8,128)(2,1)S(1)}, bf16[9,256,256]{1,2,0:T(8,128)(2,1)S(1)}, u32[]{:S(2)}, u32[]{:S(2)}) collective-permute-start(bf16[9,256,256]{1,2,0:T(8,128)(2,1)S(1)} %fusion.13), channel_id=1, source_target_pairs={{0,1},{1,0},{2,3},{3,2},{4,5},{5,4},{6,7},{7,6},{8,9},{9,8},{10,11... | collective-permute-start | bytes 3538952 | tf_op jit(solution)/shard_map/ppermute | solution.py:19
  135.4 30.3 %collective-permute-start.12 = (bf16[9,256,256]{1,2,0:T(8,128)(2,1)}, bf16[9,256,256]{1,2,0:T(8,128)(2,1)}, u32[]{:S(2)}, u32[]{:S(2)}) collective-permute-start(bf16[9,256,256]{1,2,0:T(8,128)(2,1)} %fusion.27), channel_id=1, source_target_pairs={{0,4},{1,5},{8,12},{9,13},{16,20},{17,21},{24,28},{25,29}} | collective-permute-start | bytes 3538952 | tf_op jit(solution)/shard_map/ppermute | solution.py:59
  140.1 30.3 %collective-permute-start.11 = (bf16[9,256,256]{1,2,0:T(8,128)(2,1)}, bf16[9,256,256]{1,2,0:T(8,128)(2,1)}, u32[]{:S(2)}, u32[]{:S(2)}) collective-permute-start(bf16[9,256,256]{1,2,0:T(8,128)(2,1)} %fusion.27), channel_id=1, source_target_pairs={{6,4},{4,2},{2,0},{7,5},{5,3},{3,1},{14,12},{12,10},{10,8},{15,13}... | collective-permute-start | bytes 3538952 | tf_op jit(solution)/shard_map/ppermute | solution.py:58
  147.0 23.3 %collective-permute-start.13 = (bf16[9,256,256]{1,2,0:T(8,128)(2,1)}, bf16[9,256,256]{1,2,0:T(8,128)(2,1)}, u32[]{:S(2)}, u32[]{:S(2)}) collective-permute-start(bf16[9,256,256]{1,2,0:T(8,128)(2,1)} %fusion.26), channel_id=1, source_target_pairs={{6,2},{7,3},{14,10},{15,11},{22,18},{23,19},{30,26},{31,27}} | collective-permute-start | bytes 3538952 | tf_op jit(solution)/shard_map/ppermute | solution.py:56
  148.7 41.8 %collective-permute-start.10 = (bf16[9,256,256]{1,2,0:T(8,128)(2,1)}, bf16[9,256,256]{1,2,0:T(8,128)(2,1)}, u32[]{:S(2)}, u32[]{:S(2)}) collective-permute-start(bf16[9,256,256]{1,2,0:T(8,128)(2,1)} %fusion.26), channel_id=1, source_target_pairs={{0,2},{2,4},{4,6},{1,3},{3,5},{5,7},{8,10},{10,12},{12,14},{9,11},... | collective-permute-start | bytes 3538952 | tf_op jit(solution)/shard_map/ppermute | solution.py:55
  161.7 28.8 %copy-start.2 = (bf16[9,256,256]{1,2,0:T(8,128)(2,1)S(1)}, bf16[9,256,256]{1,2,0:T(8,128)(2,1)}, u32[]{:S(2)}) copy-start(bf16[9,256,256]{1,2,0:T(8,128)(2,1)} %fusion.28) | copy-start | bytes 3538948
  164.4 45.3 %copy-start.1 = (f32[256,256]{0,1:T(8,128)S(1)}, f32[256,256]{0,1:T(8,128)}, u32[]{:S(2)}) copy-start(f32[256,256]{0,1:T(8,128)} %get-tuple-element.52) | copy-start | bytes 786436
  194.2 15.5 %collective-permute-start.14 = (bf16[4,256,256]{1,2,0:T(8,128)(2,1)S(1)}, bf16[4,256,256]{1,2,0:T(8,128)(2,1)S(1)}, u32[]{:S(2)}, u32[]{:S(2)}) collective-permute-start(bf16[4,256,256]{1,2,0:T(8,128)(2,1)S(1)} %slice.153), channel_id=1, source_target_pairs={{0,2},{2,6},{6,4},{4,0},{1,3},{3,7},{7,5},{5,1},{8,10},{10,14},{14... | collective-permute-start | bytes 1572872 | tf_op jit(solution)/shard_map/ppermute | solution.py:80
  209.9 17.1 %collective-permute-start.16 = (bf16[5,256,256]{1,2,0:T(8,128)(2,1)S(1)}, bf16[5,256,256]{1,2,0:T(8,128)(2,1)S(1)}, u32[]{:S(2)}, u32[]{:S(2)}) collective-permute-start(bf16[5,256,256]{1,2,0:T(8,128)(2,1)S(1)} %slice.110), channel_id=1, source_target_pairs={{0,2},{2,6},{6,4},{4,0},{1,3},{3,7},{7,5},{5,1},{8,10},{10,14},{14... | collective-permute-start | bytes 1966088 | tf_op jit(solution)/shard_map/ppermute | solution.py:80
  211.8 11.9 %collective-permute-start.15 = (bf16[1,4,1,256,256]{3,4,1,2,0:T(8,128)(2,1)S(1)}, bf16[1,4,1,256,256]{3,4,1,2,0:T(8,128)(2,1)S(1)}, u32[]{:S(2)}, u32[]{:S(2)}) collective-permute-start(bf16[1,4,1,256,256]{3,4,1,2,0:T(8,128)(2,1)S(1)} %bitcast.121), channel_id=1, source_target_pairs={{0,16},{8,24},{16,0},{24,8},{1,17},{9,25},{17,1},{25,9},{2,18},{10... | collective-permute-start | bytes 1572872 | tf_op jit(solution)/shard_map/ppermute | solution.py:19
  227.2 15.3 %collective-permute-start.17 = (bf16[1,5,1,256,256]{3,4,1,2,0:T(8,128)(2,1)S(1)}, bf16[1,5,1,256,256]{3,4,1,2,0:T(8,128)(2,1)S(1)}, u32[]{:S(2)}, u32[]{:S(2)}) collective-permute-start(bf16[1,5,1,256,256]{3,4,1,2,0:T(8,128)(2,1)S(1)} %fusion.33), channel_id=1, source_target_pairs={{0,16},{8,24},{16,0},{24,8},{1,17},{9,25},{17,1},{25,9},{2,18},{10... | collective-permute-start | bytes 1966088 | tf_op jit(solution)/shard_map/ppermute | solution.py:19
  (5 other events, 17.4 us)

commit v9 on v8

--- a/solution.py
+++ b/solution.py
@@ -58,8 +58,8 @@
     got_left = lax.ppermute(slot_b, "sector", LEFT)
     middle_right = lax.ppermute(slot_b, "sector", ((0, 2),))
     third = term(gathered, ket[2], bra[2], mpo[:, :, 2])
-    got = (got_right, got_left, middle_right, middle_left, third)
-    got_right, got_left, middle_right, middle_left, third = lax.optimization_barrier(got)
+    got = (got_right, got_left, third)
+    got_right, got_left, third = lax.optimization_barrier(got)
     got_middle = middle_right + middle_left
     keep_right = jnp.where(sector == 1, zero, one)
     keep_left = jnp.where(sector == 2, zero, one)

time: 245 us -> 247 us (level)
  starting transfers between devices: 45.6 us -> 41.3 us
    ppermute x2, waiting for transfers between devices: 40.5 us -> 14.1 us  [advance_line(): got_right = lax.ppermute(slot_a, 'sector', RIGHT)]
    ppermute x2, waiting for transfers between devices: 4.76 us -> 29.9 us  [advance_line(): middle_right = lax.ppermute(slot_b, 'sector', ((0, 2),))]
    ppermute x3, starting transfers between devices: 9.92 us -> 5.02 us  [advance_line(): got_last = lax.ppermute(send[low:high], 'sector', LAST)]
  transfers between devices with their start and end apart: 18 -> 18, of which waited for: 11 -> 11; matrix products, arithmetic and copies ran while one was open for 25% -> 27% of each run, Pallas kernels for 0% -> 0%
where the time goes in v9:
time: 247 us; the launch traced here: 244 us
  waiting for transfers between devices  114 us (46%)
  matrix products  51.4 us (21%)
  starting transfers between devices  41.3 us (17%)
  other arithmetic  19.9 us (8%)
  local copies, waits for them, and re-layouts  16.7 us (7%)
    ppermute x3, waiting for transfers between devices, advance_line(): got_last = lax.ppermute(send[low:high], 'sector', LAST)  35.8 us
    ppermute x2, waiting for transfers between devices, advance_line(): middle_right = lax.ppermute(slot_b, 'sector', ((0, 2),))  29.9 us
    dot_general x8, matrix products, term(): jnp.einsum('bd,vbc->vdc', bra_p, rotated, preferred_element_type=jnp.floa...  29.9 us
    ppermute x7, waiting for transfers between devices, shifted(): return lax.ppermute(value, axis, pairs)  23 us
    dot_general x8, matrix products, term(): jnp.einsum('wv,wba->vba', mpo_p, gathered, preferred_element_type=jnp.flo...  21.5 us
    ppermute x2, waiting for transfers between devices, advance_line(): got_right = lax.ppermute(slot_a, 'sector', RIGHT)  14.1 us
    ppermute x2, starting transfers between devices, advance_line(): got_right = lax.ppermute(slot_a, 'sector', RIGHT)  11.6 us
    ppermute x2, waiting for transfers between devices, advance_line(): got_left = lax.ppermute(slot_b, 'sector', LEFT)  11.5 us
  transfers between devices with their start and end apart: 18, of which 11 were waited for; matrix products, arithmetic and copies ran while one was open for 27% of the time, Pallas kernels for 0%

profile of v9, /device:TPU:0, one launch (start us, length us, event | category | flops | bytes accessed | tf_op | source)
XLA Modules:
  0.0 244.5 jit_solution(14807124380009462047)
XLA Ops:
  1.5 3.9 %collective-permute-start.2 = (bf16[18,9,4]{1,2,0:T(4,128)(2,1)}, bf16[18,9,4]{1,2,0:T(4,128)(2,1)}, u32[]{:S(2)}, u32[]{:S(2)}) collective-permute-start(bf16[18,9,4]{1,2,0:T(4,128)(2,1)} %bitcast.3), channel_id=1, source_target_pairs={{0,24},{8,0},{16,8},{24,16},{1,25},{9,1},{17,9},{25,17},{2,26},{10... | collective-permute-start | bytes 3896 | tf_op jit(solution)/shard_map/ppermute | solution.py:19
  20.7 3.6 %fusion.24 = bf16[9,256,256]{1,2,0:T(8,128)(2,1)} fusion(bf16[9,256,256]{2,0,1:T(8,128)(2,1)} %fusion.2, bf16[4,256,256]{2,1,0:T(8,128)(2,1)} %get-tuple-element.45, bf16[4,256,256]{2,1,0:T(8,128)(2,1)} %get-tuple-element.44), kind=kOutput, calls=%fused_computation.66 | convolution fusion | flops 605159424 | bytes 3538944 | tf_op jit(solution)/shard_map/bd,vbc->vdc/dot_general | solution.py:29
  29.0 3.6 %fusion.23 = bf16[9,256,256]{1,2,0:T(8,128)(2,1)} fusion(bf16[9,256,256]{2,0,1:T(8,128)(2,1)} %fusion.6, bf16[4,256,256]{2,1,0:T(8,128)(2,1)} %get-tuple-element.45, bf16[4,256,256]{2,1,0:T(8,128)(2,1)} %get-tuple-element.44), kind=kOutput, calls=%fused_computation.65 | convolution fusion | flops 605159424 | bytes 3538944 | tf_op jit(solution)/shard_map/bd,vbc->vdc/dot_general | solution.py:29
  32.6 5.6 %collective-permute-start.4 = (bf16[9,256,256]{1,2,0:T(8,128)(2,1)}, bf16[9,256,256]{1,2,0:T(8,128)(2,1)}, u32[]{:S(2)}, u32[]{:S(2)}) collective-permute-start(bf16[9,256,256]{1,2,0:T(8,128)(2,1)} %fusion.23), channel_id=1, source_target_pairs={{0,2},{2,4},{4,6},{1,3},{3,5},{5,7},{8,10},{10,12},{12,14},{9,11},... | collective-permute-start | bytes 3538952 | tf_op jit(solution)/shard_map/ppermute | solution.py:55
  38.2 4.6 %collective-permute-start.6 = (bf16[9,256,256]{1,2,0:T(8,128)(2,1)}, bf16[9,256,256]{1,2,0:T(8,128)(2,1)}, u32[]{:S(2)}, u32[]{:S(2)}) collective-permute-start(bf16[9,256,256]{1,2,0:T(8,128)(2,1)} %fusion.24), channel_id=1, source_target_pairs={{0,4},{1,5},{8,12},{9,13},{16,20},{17,21},{24,28},{25,29}} | collective-permute-start | bytes 3538952 | tf_op jit(solution)/shard_map/ppermute | solution.py:59
  47.8 3.6 %fusion.25 = bf16[9,256,256]{1,2,0:T(8,128)(2,1)} fusion(bf16[9,256,256]{2,0,1:T(8,128)(2,1)} %fusion, bf16[4,256,256]{2,1,0:T(8,128)(2,1)} %get-tuple-element.45, bf16[4,256,256]{2,1,0:T(8,128)(2,1)} %get-tuple-element.44), kind=kOutput, calls=%fused_computation.67 | convolution fusion | flops 605159424 | bytes 3538944 | tf_op jit(solution)/shard_map/bd,vbc->vdc/dot_general | solution.py:29
  54.8 9.0 %collective-permute-done.4 = bf16[9,256,256]{1,2,0:T(8,128)(2,1)} collective-permute-done((bf16[9,256,256]{1,2,0:T(8,128)(2,1)}, bf16[9,256,256]{1,2,0:T(8,128)(2,1)}, u32[]{:S(2)}, u32[]{:S(2)}) %collective-permute-start.4) | collective-permute-done | bytes 1179680 | tf_op jit(solution)/shard_map/ppermute | solution.py:55
  72.8 3.7 %convolution_convert_fusion.12 = bf16[9,256,256]{2,1,0:T(8,128)(2,1)} fusion(bf16[9,256,256]{2,0,1:T(8,128)(2,1)} %fusion.4, bf16[4,256,256]{2,1,0:T(8,128)(2,1)} %get-tuple-element.45, bf16[4,256,256]{2,1,0:T(8,128)(2,1)} %get-tuple-element.44), kind=kOutput, calls=%fused_computation.61 | convolution fusion | flops 605159424 | bytes 3538944 | tf_op jit(solution)/shard_map/bd,vbc->vdc/dot_general | solution.py:29
  76.5 12.5 %collective-permute-done.6 = bf16[9,256,256]{1,2,0:T(8,128)(2,1)} collective-permute-done((bf16[9,256,256]{1,2,0:T(8,128)(2,1)}, bf16[9,256,256]{1,2,0:T(8,128)(2,1)}, u32[]{:S(2)}, u32[]{:S(2)}) %collective-permute-start.6) | collective-permute-done | bytes 1179680 | tf_op jit(solution)/shard_map/ppermute | solution.py:59
  89.1 24.5 %collective-permute-done.8 = bf16[9,256,256]{1,2,0:T(8,128)(2,1)} collective-permute-done((bf16[9,256,256]{1,2,0:T(8,128)(2,1)}, bf16[9,256,256]{1,2,0:T(8,128)(2,1)}, u32[]{:S(2)}, u32[]{:S(2)}) %collective-permute-start.8) | collective-permute-done | bytes 1179680 | tf_op jit(solution)/shard_map/ppermute | solution.py:80
  113.6 3.9 %fusion.13 = bf16[9,256,256]{1,2,0:T(8,128)(2,1)S(1)} fusion(bf16[9,256,256]{1,2,0:T(8,128)(2,1)} %collective-permute-done.4, bf16[9,256,256]{1,2,0:T(8,128)(2,1)S(1)} %collective-permute-done.5, bf16[9,256,256]{2,1,0:T(8,128)(2,1)} %convolution_convert_fusion.12, bf16[9,256,256]{1,2,0:T(8,128)(2,1)} %collective-permute-done.8, f32[256,256]{0,1:T(8,128)S(1)} %copy-done.2, ...), kind=kLoop, calls=%fused_computation.29 | loop fusion | flops 8257536 | bytes 8519688 | tf_op jit(solution)/shard_map/convert_element_type | solution.py:84
  126.3 3.7 %copy.20 = bf16[18,256,256]{2,0,1:T(8,128)(2,1)S(1)} copy(bf16[18,256,256]{1,2,0:T(8,128)(2,1)} %pad_maximum_fusion.1) | data formatting | bytes 4718592 | tf_op jit(solution)/shard_map/concatenate | solution.py:41
  134.1 3.6 %fusion.27 = bf16[9,256,256]{1,2,0:T(8,128)(2,1)} fusion(bf16[9,256,256]{2,0,1:T(8,128)(2,1)} %fusion.37, bf16[4,256,256]{2,1,0:T(8,128)(2,1)} %get-tuple-element.41, bf16[4,256,256]{2,1,0:T(8,128)(2,1)} %get-tuple-element.40), kind=kOutput, calls=%fused_computation.69 | convolution fusion | flops 605159424 | bytes 3538944 | tf_op jit(solution)/shard_map/bd,vbc->vdc/dot_general | solution.py:29
  139.0 3.6 %fusion.26 = bf16[9,256,256]{1,2,0:T(8,128)(2,1)} fusion(bf16[9,256,256]{2,0,1:T(8,128)(2,1)} %fusion.39, bf16[4,256,256]{2,1,0:T(8,128)(2,1)} %get-tuple-element.41, bf16[4,256,256]{2,1,0:T(8,128)(2,1)} %get-tuple-element.40), kind=kOutput, calls=%fused_computation.68 | convolution fusion | flops 605159424 | bytes 3538944 | tf_op jit(solution)/shard_map/bd,vbc->vdc/dot_general | solution.py:29
  142.6 6.0 %collective-permute-start.10 = (bf16[9,256,256]{1,2,0:T(8,128)(2,1)}, bf16[9,256,256]{1,2,0:T(8,128)(2,1)}, u32[]{:S(2)}, u32[]{:S(2)}) collective-permute-start(bf16[9,256,256]{1,2,0:T(8,128)(2,1)} %fusion.26), channel_id=1, source_target_pairs={{0,2},{2,4},{4,6},{1,3},{3,5},{5,7},{8,10},{10,12},{12,14},{9,11},... | collective-permute-start | bytes 3538952 | tf_op jit(solution)/shard_map/ppermute | solution.py:55
  148.6 4.9 %collective-permute-start.12 = (bf16[9,256,256]{1,2,0:T(8,128)(2,1)}, bf16[9,256,256]{1,2,0:T(8,128)(2,1)}, u32[]{:S(2)}, u32[]{:S(2)}) collective-permute-start(bf16[9,256,256]{1,2,0:T(8,128)(2,1)} %fusion.27), channel_id=1, source_target_pairs={{0,4},{1,5},{8,12},{9,13},{16,20},{17,21},{24,28},{25,29}} | collective-permute-start | bytes 3538952 | tf_op jit(solution)/shard_map/ppermute | solution.py:59
  157.3 3.6 %fusion.28 = bf16[9,256,256]{1,2,0:T(8,128)(2,1)} fusion(bf16[9,256,256]{2,0,1:T(8,128)(2,1)} %fusion.35, bf16[4,256,256]{2,1,0:T(8,128)(2,1)} %get-tuple-element.41, bf16[4,256,256]{2,1,0:T(8,128)(2,1)} %get-tuple-element.40), kind=kOutput, calls=%fused_computation.70 | convolution fusion | flops 605159424 | bytes 3538944 | tf_op jit(solution)/shard_map/bd,vbc->vdc/dot_general | solution.py:29
  160.9 8.1 %collective-permute-done.11 = bf16[9,256,256]{1,2,0:T(8,128)(2,1)} collective-permute-done((bf16[9,256,256]{1,2,0:T(8,128)(2,1)}, bf16[9,256,256]{1,2,0:T(8,128)(2,1)}, u32[]{:S(2)}, u32[]{:S(2)}) %collective-permute-start.11) | collective-permute-done | bytes 1179680 | tf_op jit(solution)/shard_map/ppermute | solution.py:58
  169.0 5.2 %collective-permute-done.10 = bf16[9,256,256]{1,2,0:T(8,128)(2,1)} collective-permute-done((bf16[9,256,256]{1,2,0:T(8,128)(2,1)}, bf16[9,256,256]{1,2,0:T(8,128)(2,1)}, u32[]{:S(2)}, u32[]{:S(2)}) %collective-permute-start.10) | collective-permute-done | bytes 1179680 | tf_op jit(solution)/shard_map/ppermute | solution.py:55
  182.2 17.3 %collective-permute-done.12 = bf16[9,256,256]{1,2,0:T(8,128)(2,1)} collective-permute-done((bf16[9,256,256]{1,2,0:T(8,128)(2,1)}, bf16[9,256,256]{1,2,0:T(8,128)(2,1)}, u32[]{:S(2)}, u32[]{:S(2)}) %collective-permute-start.12) | collective-permute-done | bytes 1179680 | tf_op jit(solution)/shard_map/ppermute | solution.py:59
  199.5 4.4 %fusion.19 = f32[9,256,256]{1,2,0:T(8,128)S(1)} fusion(bf16[9,256,256]{1,2,0:T(8,128)(2,1)} %collective-permute-done.10, bf16[9,256,256]{1,2,0:T(8,128)(2,1)} %collective-permute-done.11, bf16[9,256,256]{1,2,0:T(8,128)(2,1)} %collective-permute-done.12, bf16[9,256,256]{1,2,0:T(8,128)(2,1)} %collective-permute-done.13, f32[]{:T(128)S(6)} %select_n.57, ...), kind=kOutput, calls=%fused_computation.35 | convolution fusion | flops 612237312 | bytes 9437192 | tf_op jit(solution)/shard_map/bd,vbc->vdc/dot_general | solution.py:29
  203.9 9.8 %collective-permute-done.14 = bf16[4,256,256]{1,2,0:T(8,128)(2,1)} collective-permute-done((bf16[4,256,256]{1,2,0:T(8,128)(2,1)}, bf16[4,256,256]{1,2,0:T(8,128)(2,1)}, u32[]{:S(2)}, u32[]{:S(2)}) %collective-permute-start.14) | collective-permute-done | bytes 524320 | tf_op jit(solution)/shard_map/ppermute | solution.py:80
  216.6 10.8 %collective-permute-done.15 = bf16[1,4,1,256,256]{3,4,1,2,0:T(8,128)(2,1)S(1)} collective-permute-done((bf16[1,4,1,256,256]{3,4,1,2,0:T(8,128)(2,1)S(1)}, bf16[1,4,1,256,256]{3,4,1,2,0:T(8,128)(2,1)S(1)}, u32[]{:S(2)}, u32[]{:S(2)}) %collective-permute-start.15) | collective-permute-done | bytes 524320 | tf_op jit(solution)/shard_map/ppermute | solution.py:19
  230.7 12.1 %collective-permute-done.17 = bf16[1,5,1,256,256]{3,4,1,2,0:T(8,128)(2,1)S(1)} collective-permute-done((bf16[1,5,1,256,256]{3,4,1,2,0:T(8,128)(2,1)S(1)}, bf16[1,5,1,256,256]{3,4,1,2,0:T(8,128)(2,1)S(1)}, u32[]{:S(2)}, u32[]{:S(2)}) %collective-permute-start.17) | collective-permute-done | bytes 655392 | tf_op jit(solution)/shard_map/ppermute | solution.py:19
  (90 shorter events, 71.8 us)
Async XLA Ops:
  0.0 11.8 %copy-start.4 = (bf16[1,1,4,256,256]{4,3,2,1,0:T(8,128)(2,1)S(1)}, bf16[1,1,4,256,256]{4,3,2,1,0:T(8,128)(2,1)}, u32[]{:S(2)}) copy-start(bf16[1,1,4,256,256]{4,3,2,1,0:T(8,128)(2,1)} %param.14) | copy-start | bytes 1572868
  0.0 11.2 %copy-start.5 = (bf16[1,1,4,256,256]{4,3,2,1,0:T(8,128)(2,1)S(1)}, bf16[1,1,4,256,256]{4,3,2,1,0:T(8,128)(2,1)}, u32[]{:S(2)}) copy-start(bf16[1,1,4,256,256]{4,3,2,1,0:T(8,128)(2,1)} %param.15) | copy-start | bytes 1572868
  1.5 31.1 %collective-permute-start.2 = (bf16[18,9,4]{1,2,0:T(4,128)(2,1)}, bf16[18,9,4]{1,2,0:T(4,128)(2,1)}, u32[]{:S(2)}, u32[]{:S(2)}) collective-permute-start(bf16[18,9,4]{1,2,0:T(4,128)(2,1)} %bitcast.3), channel_id=1, source_target_pairs={{0,24},{8,0},{16,8},{24,16},{1,25},{9,1},{17,9},{25,17},{2,26},{10... | collective-permute-start | bytes 3896 | tf_op jit(solution)/shard_map/ppermute | solution.py:19
  5.4 27.2 %collective-permute-start = (bf16[4,256,256]{2,1,0:T(8,128)(2,1)}, bf16[4,256,256]{2,1,0:T(8,128)(2,1)}, u32[]{:S(2)}, u32[]{:S(2)}) collective-permute-start(bf16[4,256,256]{2,1,0:T(8,128)(2,1)} %bitcast.119), channel_id=1, source_target_pairs={{0,24},{8,0},{16,8},{24,16},{1,25},{9,1},{17,9},{25,17},{2,26},{10... | collective-permute-start | bytes 1572872 | tf_op jit(solution)/shard_map/ppermute | solution.py:19
  5.9 26.6 %collective-permute-start.1 = (bf16[4,256,256]{2,1,0:T(8,128)(2,1)}, bf16[4,256,256]{2,1,0:T(8,128)(2,1)}, u32[]{:S(2)}, u32[]{:S(2)}) collective-permute-start(bf16[4,256,256]{2,1,0:T(8,128)(2,1)} %bitcast.121), channel_id=1, source_target_pairs={{0,24},{8,0},{16,8},{24,16},{1,25},{9,1},{17,9},{25,17},{2,26},{10... | collective-permute-start | bytes 1572872 | tf_op jit(solution)/shard_map/ppermute | solution.py:19
  10.4 5.5 %collective-permute-start.3 = (bf16[9,256,256]{2,1,0:T(8,128)(2,1)S(1)}, bf16[9,256,256]{2,1,0:T(8,128)(2,1)}, u32[]{:S(2)}, u32[]{:S(2)}) collective-permute-start(bf16[9,256,256]{2,1,0:T(8,128)(2,1)S(1)} %bitcast_select_fusion), channel_id=1, source_target_pairs={{0,1},{1,0},{2,3},{3,2},{4,5},{5,4},{6,7},{7,6},{8,9},{9,8},{10,11... | collective-permute-start | bytes 3538952 | tf_op jit(solution)/shard_map/ppermute | solution.py:19
  24.4 30.4 %collective-permute-start.5 = (bf16[9,256,256]{1,2,0:T(8,128)(2,1)}, bf16[9,256,256]{1,2,0:T(8,128)(2,1)S(1)}, u32[]{:S(2)}, u32[]{:S(2)}) collective-permute-start(bf16[9,256,256]{1,2,0:T(8,128)(2,1)} %fusion.24), channel_id=1, source_target_pairs={{6,4},{4,2},{2,0},{7,5},{5,3},{3,1},{14,12},{12,10},{10,8},{15,13}... | collective-permute-start | bytes 3538952 | tf_op jit(solution)/shard_map/ppermute | solution.py:58
  32.6 31.2 %collective-permute-start.4 = (bf16[9,256,256]{1,2,0:T(8,128)(2,1)}, bf16[9,256,256]{1,2,0:T(8,128)(2,1)}, u32[]{:S(2)}, u32[]{:S(2)}) collective-permute-start(bf16[9,256,256]{1,2,0:T(8,128)(2,1)} %fusion.23), channel_id=1, source_target_pairs={{0,2},{2,4},{4,6},{1,3},{3,5},{5,7},{8,10},{10,12},{12,14},{9,11},... | collective-permute-start | bytes 3538952 | tf_op jit(solution)/shard_map/ppermute | solution.py:55
  38.2 50.9 %collective-permute-start.6 = (bf16[9,256,256]{1,2,0:T(8,128)(2,1)}, bf16[9,256,256]{1,2,0:T(8,128)(2,1)}, u32[]{:S(2)}, u32[]{:S(2)}) collective-permute-start(bf16[9,256,256]{1,2,0:T(8,128)(2,1)} %fusion.24), channel_id=1, source_target_pairs={{0,4},{1,5},{8,12},{9,13},{16,20},{17,21},{24,28},{25,29}} | collective-permute-start | bytes 3538952 | tf_op jit(solution)/shard_map/ppermute | solution.py:59
  42.8 46.3 %collective-permute-start.7 = (bf16[9,256,256]{1,2,0:T(8,128)(2,1)}, bf16[9,256,256]{1,2,0:T(8,128)(2,1)}, u32[]{:S(2)}, u32[]{:S(2)}) collective-permute-start(bf16[9,256,256]{1,2,0:T(8,128)(2,1)} %fusion.23), channel_id=1, source_target_pairs={{6,2},{7,3},{14,10},{15,11},{22,18},{23,19},{30,26},{31,27}} | collective-permute-start | bytes 3538952 | tf_op jit(solution)/shard_map/ppermute | solution.py:56
  67.0 46.6 %collective-permute-start.8 = (bf16[9,256,256]{1,2,0:T(8,128)(2,1)}, bf16[9,256,256]{1,2,0:T(8,128)(2,1)}, u32[]{:S(2)}, u32[]{:S(2)}) collective-permute-start(bf16[9,256,256]{1,2,0:T(8,128)(2,1)} %fusion.16), channel_id=1, source_target_pairs={{0,2},{2,6},{6,4},{4,0},{1,3},{3,7},{7,5},{5,1},{8,10},{10,14},{14... | collective-permute-start | bytes 3538952 | tf_op jit(solution)/shard_map/ppermute | solution.py:80
  72.8 40.8 %copy-start.2 = (f32[256,256]{0,1:T(8,128)S(1)}, f32[256,256]{0,1:T(8,128)}, u32[]{:S(2)}) copy-start(f32[256,256]{0,1:T(8,128)} %get-tuple-element.42) | copy-start | bytes 786436
  117.5 5.9 %copy-start.7 = (pred[4]{0:T(512)(128)(4,1)S(1)}, pred[4]{0:T(512)(128)(4,1)}, u32[]{:S(2)}) copy-start(pred[4]{0:T(512)(128)(4,1)} %copy-done.6) | copy-start | bytes 16
  117.5 7.2 %collective-permute-start.9 = (bf16[9,256,256]{1,2,0:T(8,128)(2,1)S(1)}, bf16[9,256,256]{1,2,0:T(8,128)(2,1)S(1)}, u32[]{:S(2)}, u32[]{:S(2)}) collective-permute-start(bf16[9,256,256]{1,2,0:T(8,128)(2,1)S(1)} %fusion.13), channel_id=1, source_target_pairs={{0,1},{1,0},{2,3},{3,2},{4,5},{5,4},{6,7},{7,6},{8,9},{9,8},{10,11... | collective-permute-start | bytes 3538952 | tf_op jit(solution)/shard_map/ppermute | solution.py:19
  137.7 31.3 %collective-permute-start.11 = (bf16[9,256,256]{1,2,0:T(8,128)(2,1)}, bf16[9,256,256]{1,2,0:T(8,128)(2,1)}, u32[]{:S(2)}, u32[]{:S(2)}) collective-permute-start(bf16[9,256,256]{1,2,0:T(8,128)(2,1)} %fusion.27), channel_id=1, source_target_pairs={{6,4},{4,2},{2,0},{7,5},{5,3},{3,1},{14,12},{12,10},{10,8},{15,13}... | collective-permute-start | bytes 3538952 | tf_op jit(solution)/shard_map/ppermute | solution.py:58
  142.6 31.6 %collective-permute-start.10 = (bf16[9,256,256]{1,2,0:T(8,128)(2,1)}, bf16[9,256,256]{1,2,0:T(8,128)(2,1)}, u32[]{:S(2)}, u32[]{:S(2)}) collective-permute-start(bf16[9,256,256]{1,2,0:T(8,128)(2,1)} %fusion.26), channel_id=1, source_target_pairs={{0,2},{2,4},{4,6},{1,3},{3,5},{5,7},{8,10},{10,12},{12,14},{9,11},... | collective-permute-start | bytes 3538952 | tf_op jit(solution)/shard_map/ppermute | solution.py:55
  148.6 50.9 %collective-permute-start.12 = (bf16[9,256,256]{1,2,0:T(8,128)(2,1)}, bf16[9,256,256]{1,2,0:T(8,128)(2,1)}, u32[]{:S(2)}, u32[]{:S(2)}) collective-permute-start(bf16[9,256,256]{1,2,0:T(8,128)(2,1)} %fusion.27), channel_id=1, source_target_pairs={{0,4},{1,5},{8,12},{9,13},{16,20},{17,21},{24,28},{25,29}} | collective-permute-start | bytes 3538952 | tf_op jit(solution)/shard_map/ppermute | solution.py:59
  153.5 46.0 %collective-permute-start.13 = (bf16[9,256,256]{1,2,0:T(8,128)(2,1)}, bf16[9,256,256]{1,2,0:T(8,128)(2,1)}, u32[]{:S(2)}, u32[]{:S(2)}) collective-permute-start(bf16[9,256,256]{1,2,0:T(8,128)(2,1)} %fusion.26), channel_id=1, source_target_pairs={{6,2},{7,3},{14,10},{15,11},{22,18},{23,19},{30,26},{31,27}} | collective-permute-start | bytes 3538952 | tf_op jit(solution)/shard_map/ppermute | solution.py:56
  177.6 36.0 %collective-permute-start.14 = (bf16[4,256,256]{1,2,0:T(8,128)(2,1)}, bf16[4,256,256]{1,2,0:T(8,128)(2,1)}, u32[]{:S(2)}, u32[]{:S(2)}) collective-permute-start(bf16[4,256,256]{1,2,0:T(8,128)(2,1)} %slice.153), channel_id=1, source_target_pairs={{0,2},{2,6},{6,4},{4,0},{1,3},{3,7},{7,5},{5,1},{8,10},{10,14},{14... | collective-permute-start | bytes 1572872 | tf_op jit(solution)/shard_map/ppermute | solution.py:80
  182.2 31.5 %copy-start.3 = (f32[256,256]{0,1:T(8,128)S(1)}, f32[256,256]{0,1:T(8,128)}, u32[]{:S(2)}) copy-start(f32[256,256]{0,1:T(8,128)} %get-tuple-element.42) | copy-start | bytes 786436
  203.9 11.0 %copy-start.1 = (bf16[9,256,256]{1,2,0:T(8,128)(2,1)S(1)}, bf16[9,256,256]{1,2,0:T(8,128)(2,1)}, u32[]{:S(2)}) copy-start(bf16[9,256,256]{1,2,0:T(8,128)(2,1)} %copy-done) | copy-start | bytes 3538948
  214.9 14.0 %collective-permute-start.16 = (bf16[5,256,256]{1,2,0:T(8,128)(2,1)S(1)}, bf16[5,256,256]{1,2,0:T(8,128)(2,1)S(1)}, u32[]{:S(2)}, u32[]{:S(2)}) collective-permute-start(bf16[5,256,256]{1,2,0:T(8,128)(2,1)S(1)} %slice.110), channel_id=1, source_target_pairs={{0,2},{2,6},{6,4},{4,0},{1,3},{3,7},{7,5},{5,1},{8,10},{10,14},{14... | collective-permute-start | bytes 1966088 | tf_op jit(solution)/shard_map/ppermute | solution.py:80
  215.0 12.4 %collective-permute-start.15 = (bf16[1,4,1,256,256]{3,4,1,2,0:T(8,128)(2,1)S(1)}, bf16[1,4,1,256,256]{3,4,1,2,0:T(8,128)(2,1)S(1)}, u32[]{:S(2)}, u32[]{:S(2)}) collective-permute-start(bf16[1,4,1,256,256]{3,4,1,2,0:T(8,128)(2,1)S(1)} %bitcast.123), channel_id=1, source_target_pairs={{0,16},{8,24},{16,0},{24,8},{1,17},{9,25},{17,1},{25,9},{2,18},{10... | collective-permute-start | bytes 1572872 | tf_op jit(solution)/shard_map/ppermute | solution.py:19
  229.1 13.7 %collective-permute-start.17 = (bf16[1,5,1,256,256]{3,4,1,2,0:T(8,128)(2,1)S(1)}, bf16[1,5,1,256,256]{3,4,1,2,0:T(8,128)(2,1)S(1)}, u32[]{:S(2)}, u32[]{:S(2)}) collective-permute-start(bf16[1,5,1,256,256]{3,4,1,2,0:T(8,128)(2,1)S(1)} %fusion.33), channel_id=1, source_target_pairs={{0,16},{8,24},{16,0},{24,8},{1,17},{9,25},{17,1},{25,9},{2,18},{10... | collective-permute-start | bytes 1966088 | tf_op jit(solution)/shard_map/ppermute | solution.py:19
  (6 other events, 22.9 us)

commit v10 on v7

--- a/solution.py
+++ b/solution.py
@@ -125,7 +125,7 @@
         if line:
             parts, tensors[step + 1 :] = advance_line(
                 current, ket, bra, mpo, live_mask, sector, tensors[step + 1 :],
-                2 if last else 1, onward if last else (lambda part: part),
+                3 if last else 1, onward if last else (lambda part: part),
             )
         else:
             parts = [advance_direct(current, ket, bra, mpo, live_mask)]

time: 245 us -> 236 us (0.963)
  waiting for transfers between devices: 110 us -> 106 us
  local copies, waits for them, and re-layouts: 12.2 us -> 9.7 us
    ppermute x7 -> x8, waiting for transfers between devices: 25.5 us -> 9.26 us  [shifted(): return lax.ppermute(value, axis, pairs)]
    ppermute x3 -> x4, waiting for transfers between devices: 28.1 us -> 41.4 us  [advance_line(): got_last = lax.ppermute(send[low:high], 'sector', LAST)]
    ppermute x7 -> x8, starting transfers between devices: 9.13 us -> 10.7 us  [shifted(): return lax.ppermute(value, axis, pairs)]
    convert_element_type x2 -> x3, other arithmetic: 5.03 us -> 4.06 us  [advance_line(): piece = (piece * live_mask[None]).astype(jnp.bfloat16)]
    ppermute x3 -> x4, starting transfers between devices: 8.97 us -> 9.65 us  [advance_line(): got_last = lax.ppermute(send[low:high], 'sector', LAST)]
  transfers between devices with their start and end apart: 18 -> 20, of which waited for: 12 -> 12; matrix products, arithmetic and copies ran while one was open for 23% -> 21% of each run, Pallas kernels for 0% -> 0%
where the time goes in v10:
time: 236 us; the launch traced here: 235 us
  waiting for transfers between devices  106 us (45%)
  matrix products  50.7 us (21%)
  starting transfers between devices  46.8 us (20%)
  other arithmetic  15.3 us (6%)
  local copies, waits for them, and re-layouts  9.7 us (4%)
  between operations  6.55 us (3%)
    ppermute x4, waiting for transfers between devices, advance_line(): got_last = lax.ppermute(send[low:high], 'sector', LAST)  41.4 us
    ppermute x2, waiting for transfers between devices, advance_line(): got_right = lax.ppermute(slot_a, 'sector', RIGHT)  40.4 us
    dot_general x8, matrix products, term(): jnp.einsum('bd,vbc->vdc', bra_p, rotated, preferred_element_type=jnp.floa...  28.8 us
    dot_general x8, matrix products, term(): jnp.einsum('wv,wba->vba', mpo_p, gathered, preferred_element_type=jnp.flo...  21.9 us
    ppermute x8, starting transfers between devices, shifted(): return lax.ppermute(value, axis, pairs)  10.7 us
    ppermute x2, starting transfers between devices, advance_line(): got_right = lax.ppermute(slot_a, 'sector', RIGHT)  10.3 us
    ppermute x2, starting transfers between devices, advance_line(): middle_right = lax.ppermute(slot_b, 'sector', ((0, 2),))  10.2 us
    ppermute x4, starting transfers between devices, advance_line(): got_last = lax.ppermute(send[low:high], 'sector', LAST)  9.65 us
  transfers between devices with their start and end apart: 20, of which 12 were waited for; matrix products, arithmetic and copies ran while one was open for 21% of the time, Pallas kernels for 0%

profile of v10, /device:TPU:0, one launch (start us, length us, event | category | flops | bytes accessed | tf_op | source)
XLA Modules:
  0.0 235.5 jit_solution(12943231572601237387)
XLA Ops:
  22.0 3.6 %fusion.24 = bf16[9,256,256]{1,2,0:T(8,128)(2,1)} fusion(bf16[9,256,256]{2,0,1:T(8,128)(2,1)} %fusion.2, bf16[1,1,4,256,256]{4,3,2,1,0:T(8,128)(2,1)} %param.15, s32[]{:T(128)S(6)} %select_n.81, bf16[1,1,4,256,256]{4,3,2,1,0:T(8,128)(2,1)} %param.14), kind=kOutput, calls=%fused_computation.60 | convolution fusion | flops 605159424 | bytes 3539968 | tf_op jit(solution)/shard_map/bd,vbc->vdc/dot_general | solution.py:29
  25.7 5.5 %collective-permute-start.6 = (bf16[9,256,256]{1,2,0:T(8,128)(2,1)}, bf16[9,256,256]{1,2,0:T(8,128)(2,1)}, u32[]{:S(2)}, u32[]{:S(2)}) collective-permute-start(bf16[9,256,256]{1,2,0:T(8,128)(2,1)} %fusion.24), channel_id=1, source_target_pairs={{0,4},{1,5},{8,12},{9,13},{16,20},{17,21},{24,28},{25,29}} | collective-permute-start | bytes 3538952 | tf_op jit(solution)/shard_map/ppermute | solution.py:64
  35.8 3.6 %fusion.23 = bf16[9,256,256]{1,2,0:T(8,128)(2,1)} fusion(bf16[9,256,256]{2,0,1:T(8,128)(2,1)} %fusion.6, bf16[1,1,4,256,256]{4,3,2,1,0:T(8,128)(2,1)} %param.15, s32[]{:T(128)S(6)} %select_n.78, bf16[1,1,4,256,256]{4,3,2,1,0:T(8,128)(2,1)} %param.14), kind=kOutput, calls=%fused_computation.59 | convolution fusion | flops 605159424 | bytes 3539968 | tf_op jit(solution)/shard_map/bd,vbc->vdc/dot_general | solution.py:29
  41.2 5.2 %collective-permute-start.4 = (bf16[9,256,256]{1,2,0:T(8,128)(2,1)}, bf16[9,256,256]{1,2,0:T(8,128)(2,1)}, u32[]{:S(2)}, u32[]{:S(2)}) collective-permute-start(bf16[9,256,256]{1,2,0:T(8,128)(2,1)} %fusion.23), channel_id=1, source_target_pairs={{0,2},{2,4},{4,6},{1,3},{3,5},{5,7},{8,10},{10,12},{12,14},{9,11},... | collective-permute-start | bytes 3538952 | tf_op jit(solution)/shard_map/ppermute | solution.py:60
  49.7 3.7 %fusion.25 = bf16[9,256,256]{1,2,0:T(8,128)(2,1)} fusion(bf16[9,256,256]{2,0,1:T(8,128)(2,1)} %fusion, bf16[1,1,4,256,256]{4,3,2,1,0:T(8,128)(2,1)} %param.15, s32[]{:T(128)S(6)} %select_n.82, bf16[1,1,4,256,256]{4,3,2,1,0:T(8,128)(2,1)} %param.14), kind=kOutput, calls=%fused_computation.61 | convolution fusion | flops 605159424 | bytes 3539968 | tf_op jit(solution)/shard_map/bd,vbc->vdc/dot_general | solution.py:29
  56.9 3.7 %collective-permute-done.5 = bf16[9,256,256]{1,2,0:T(8,128)(2,1)} collective-permute-done((bf16[9,256,256]{1,2,0:T(8,128)(2,1)}, bf16[9,256,256]{1,2,0:T(8,128)(2,1)}, u32[]{:S(2)}, u32[]{:S(2)}) %collective-permute-start.5) | collective-permute-done | bytes 1179680 | tf_op jit(solution)/shard_map/ppermute | solution.py:63
  60.6 20.2 %collective-permute-done.4 = bf16[9,256,256]{1,2,0:T(8,128)(2,1)} collective-permute-done((bf16[9,256,256]{1,2,0:T(8,128)(2,1)}, bf16[9,256,256]{1,2,0:T(8,128)(2,1)}, u32[]{:S(2)}, u32[]{:S(2)}) %collective-permute-start.4) | collective-permute-done | bytes 1179680 | tf_op jit(solution)/shard_map/ppermute | solution.py:60
  84.4 3.7 %collective-permute-start.8 = (bf16[9,256,256]{1,2,0:T(8,128)(2,1)}, bf16[9,256,256]{1,2,0:T(8,128)(2,1)}, u32[]{:S(2)}, u32[]{:S(2)}) collective-permute-start(bf16[9,256,256]{1,2,0:T(8,128)(2,1)} %fusion.16), channel_id=1, source_target_pairs={{0,2},{2,6},{6,4},{4,0},{1,3},{3,7},{7,5},{5,1},{8,10},{10,14},{14... | collective-permute-start | bytes 3538952 | tf_op jit(solution)/shard_map/ppermute | solution.py:85
  94.1 20.1 %collective-permute-done.8 = bf16[9,256,256]{1,2,0:T(8,128)(2,1)} collective-permute-done((bf16[9,256,256]{1,2,0:T(8,128)(2,1)}, bf16[9,256,256]{1,2,0:T(8,128)(2,1)}, u32[]{:S(2)}, u32[]{:S(2)}) %collective-permute-start.8) | collective-permute-done | bytes 1179680 | tf_op jit(solution)/shard_map/ppermute | solution.py:85
  114.2 3.9 %fusion.13 = bf16[9,256,256]{1,2,0:T(8,128)(2,1)S(1)} fusion(bf16[9,256,256]{1,2,0:T(8,128)(2,1)} %collective-permute-done.4, bf16[9,256,256]{1,2,0:T(8,128)(2,1)} %collective-permute-done.5, bf16[9,256,256]{2,1,0:T(8,128)(2,1)S(1)} %convolution_convert_fusion.12, bf16[9,256,256]{1,2,0:T(8,128)(2,1)} %collective-permute-done.8, ...), kind=kLoop, calls=%fused_computation.23 | loop fusion | flops 8257536 | bytes 8519688 | tf_op jit(solution)/shard_map/convert_element_type | solution.py:89
  122.6 3.7 %copy.30 = bf16[18,256,256]{2,0,1:T(8,128)(2,1)S(1)} copy(bf16[18,256,256]{1,2,0:T(8,128)(2,1)} %pad_maximum_fusion.1) | data formatting | bytes 4718592 | tf_op jit(solution)/shard_map/concatenate | solution.py:41
  128.4 3.6 %fusion.27 = bf16[9,256,256]{1,2,0:T(8,128)(2,1)} fusion(bf16[9,256,256]{2,0,1:T(8,128)(2,1)} %fusion.88, bf16[4,256,256]{2,1,0:T(8,128)(2,1)} %copy-done.4, s32[]{:T(128)S(6)} %select_n.81, bf16[4,256,256]{2,1,0:T(8,128)(2,1)} %collective-permute-done), kind=kOutput, calls=%fused_computation.63 | convolution fusion | flops 605159424 | bytes 3539968 | tf_op jit(solution)/shard_map/bd,vbc->vdc/dot_general | solution.py:29
  132.0 4.7 %collective-permute-start.12 = (bf16[9,256,256]{1,2,0:T(8,128)(2,1)}, bf16[9,256,256]{1,2,0:T(8,128)(2,1)}, u32[]{:S(2)}, u32[]{:S(2)}) collective-permute-start(bf16[9,256,256]{1,2,0:T(8,128)(2,1)} %fusion.27), channel_id=1, source_target_pairs={{0,4},{1,5},{8,12},{9,13},{16,20},{17,21},{24,28},{25,29}} | collective-permute-start | bytes 3538952 | tf_op jit(solution)/shard_map/ppermute | solution.py:64
  145.4 5.2 %collective-permute-start.10 = (bf16[9,256,256]{1,2,0:T(8,128)(2,1)}, bf16[9,256,256]{1,2,0:T(8,128)(2,1)}, u32[]{:S(2)}, u32[]{:S(2)}) collective-permute-start(bf16[9,256,256]{1,2,0:T(8,128)(2,1)} %fusion.26), channel_id=1, source_target_pairs={{0,2},{2,4},{4,6},{1,3},{3,5},{5,7},{8,10},{10,12},{12,14},{9,11},... | collective-permute-start | bytes 3538952 | tf_op jit(solution)/shard_map/ppermute | solution.py:60
  152.6 3.7 %fusion.28 = bf16[9,256,256]{1,2,0:T(8,128)(2,1)} fusion(bf16[9,256,256]{2,0,1:T(8,128)(2,1)} %fusion.86, bf16[4,256,256]{2,1,0:T(8,128)(2,1)} %copy-done.4, s32[]{:T(128)S(6)} %select_n.82, bf16[4,256,256]{2,1,0:T(8,128)(2,1)} %collective-permute-done), kind=kOutput, calls=%fused_computation.64 | convolution fusion | flops 605159424 | bytes 3539968 | tf_op jit(solution)/shard_map/bd,vbc->vdc/dot_general | solution.py:29
  158.4 3.9 %collective-permute-done.12 = bf16[9,256,256]{1,2,0:T(8,128)(2,1)} collective-permute-done((bf16[9,256,256]{1,2,0:T(8,128)(2,1)}, bf16[9,256,256]{1,2,0:T(8,128)(2,1)}, u32[]{:S(2)}, u32[]{:S(2)}) %collective-permute-start.12) | collective-permute-done | bytes 1179680 | tf_op jit(solution)/shard_map/ppermute | solution.py:64
  162.3 4.3 %collective-permute-done.11 = bf16[9,256,256]{1,2,0:T(8,128)(2,1)} collective-permute-done((bf16[9,256,256]{1,2,0:T(8,128)(2,1)}, bf16[9,256,256]{1,2,0:T(8,128)(2,1)}, u32[]{:S(2)}, u32[]{:S(2)}) %collective-permute-start.11) | collective-permute-done | bytes 1179680 | tf_op jit(solution)/shard_map/ppermute | solution.py:63
  166.6 20.2 %collective-permute-done.10 = bf16[9,256,256]{1,2,0:T(8,128)(2,1)} collective-permute-done((bf16[9,256,256]{1,2,0:T(8,128)(2,1)}, bf16[9,256,256]{1,2,0:T(8,128)(2,1)}, u32[]{:S(2)}, u32[]{:S(2)}) %collective-permute-start.10) | collective-permute-done | bytes 1179680 | tf_op jit(solution)/shard_map/ppermute | solution.py:60
  190.0 3.7 %collective-permute-start.14 = (bf16[3,256,256]{1,2,0:T(8,128)(2,1)S(1)}, bf16[3,256,256]{1,2,0:T(8,128)(2,1)S(1)}, u32[]{:S(2)}, u32[]{:S(2)}) collective-permute-start(bf16[3,256,256]{1,2,0:T(8,128)(2,1)S(1)} %slice.57), channel_id=1, source_target_pairs={{0,2},{2,6},{6,4},{4,0},{1,3},{3,7},{7,5},{5,1},{8,10},{10,14},{14... | collective-permute-start | bytes 1179656 | tf_op jit(solution)/shard_map/ppermute | solution.py:85
  193.8 4.4 %fusion.19 = f32[9,256,256]{1,2,0:T(8,128)S(1)} fusion(bf16[9,256,256]{1,2,0:T(8,128)(2,1)} %collective-permute-done.10, bf16[9,256,256]{1,2,0:T(8,128)(2,1)} %collective-permute-done.11, bf16[9,256,256]{1,2,0:T(8,128)(2,1)} %collective-permute-done.12, bf16[9,256,256]{1,2,0:T(8,128)(2,1)} %collective-permute-done.13, f32[]{:T(128)S(6)} %select_n.83, ...), kind=kOutput, calls=%fused_computation.29 | convolution fusion | flops 612237312 | bytes 9437192 | tf_op jit(solution)/shard_map/bd,vbc->vdc/dot_general | solution.py:29
  198.2 4.5 %collective-permute-done.14 = bf16[3,256,256]{1,2,0:T(8,128)(2,1)S(1)} collective-permute-done((bf16[3,256,256]{1,2,0:T(8,128)(2,1)S(1)}, bf16[3,256,256]{1,2,0:T(8,128)(2,1)S(1)}, u32[]{:S(2)}, u32[]{:S(2)}) %collective-permute-start.14) | collective-permute-done | bytes 393248 | tf_op jit(solution)/shard_map/ppermute | solution.py:85
  205.8 8.5 %collective-permute-done.16 = bf16[3,256,256]{1,2,0:T(8,128)(2,1)S(1)} collective-permute-done((bf16[3,256,256]{1,2,0:T(8,128)(2,1)S(1)}, bf16[3,256,256]{1,2,0:T(8,128)(2,1)S(1)}, u32[]{:S(2)}, u32[]{:S(2)}) %collective-permute-start.16) | collective-permute-done | bytes 393248 | tf_op jit(solution)/shard_map/ppermute | solution.py:85
  216.6 8.3 %collective-permute-done.18 = bf16[3,256,256]{1,2,0:T(8,128)(2,1)S(1)} collective-permute-done((bf16[3,256,256]{1,2,0:T(8,128)(2,1)S(1)}, bf16[3,256,256]{1,2,0:T(8,128)(2,1)S(1)}, u32[]{:S(2)}, u32[]{:S(2)}) %collective-permute-start.18) | collective-permute-done | bytes 393248 | tf_op jit(solution)/shard_map/ppermute | solution.py:85
  226.7 7.1 %collective-permute-done.19 = bf16[1,3,1,256,256]{3,4,1,2,0:T(8,128)(2,1)S(1)} collective-permute-done((bf16[1,3,1,256,256]{3,4,1,2,0:T(8,128)(2,1)S(1)}, bf16[1,3,1,256,256]{3,4,1,2,0:T(8,128)(2,1)S(1)}, u32[]{:S(2)}, u32[]{:S(2)}) %collective-permute-start.19) | collective-permute-done | bytes 393248 | tf_op jit(solution)/shard_map/ppermute | solution.py:19
  (81 shorter events, 70.0 us)
Async XLA Ops:
  0.0 10.5 %copy-start.7 = (s32[4]{0:T(128)S(1)}, s32[4]{0:T(128)}, u32[]{:S(2)}) copy-start(s32[4]{0:T(128)} %constant.106.clone) | copy-start | bytes 52
  0.0 12.2 %copy-start.6 = (s32[4]{0:T(128)S(1)}, s32[4]{0:T(128)}, u32[]{:S(2)}) copy-start(s32[4]{0:T(128)} %constant.105.clone) | copy-start | bytes 52
  2.3 14.5 %copy-start.2 = (bf16[9,256,256]{2,1,0:T(8,128)(2,1)}, bf16[9,256,256]{2,1,0:T(8,128)(2,1)S(1)}, u32[]{:S(2)}) copy-start(bf16[9,256,256]{2,1,0:T(8,128)(2,1)S(1)} %bitcast_select_fusion) | copy-start | bytes 3538948
  2.4 14.5 %collective-permute-start.3 = (bf16[9,256,256]{2,1,0:T(8,128)(2,1)S(1)}, bf16[9,256,256]{2,1,0:T(8,128)(2,1)}, u32[]{:S(2)}, u32[]{:S(2)}) collective-permute-start(bf16[9,256,256]{2,1,0:T(8,128)(2,1)S(1)} %bitcast_select_fusion), channel_id=1, source_target_pairs={{0,1},{1,0},{2,3},{3,2},{4,5},{5,4},{6,7},{7,6},{8,9},{9,8},{10,11... | collective-permute-start | bytes 3538952 | tf_op jit(solution)/shard_map/ppermute | solution.py:19
  3.0 36.4 %collective-permute-start.2 = (bf16[18,9,4]{1,2,0:T(4,128)(2,1)S(1)}, bf16[18,9,4]{1,2,0:T(4,128)(2,1)S(1)}, u32[]{:S(2)}, u32[]{:S(2)}) collective-permute-start(bf16[18,9,4]{1,2,0:T(4,128)(2,1)S(1)} %bitcast.124), channel_id=1, source_target_pairs={{0,24},{8,0},{16,8},{24,16},{1,25},{9,1},{17,9},{25,17},{2,26},{10... | collective-permute-start | bytes 3896 | tf_op jit(solution)/shard_map/ppermute | solution.py:19
  6.5 32.9 %collective-permute-start.1 = (bf16[4,256,256]{2,1,0:T(8,128)(2,1)}, bf16[4,256,256]{2,1,0:T(8,128)(2,1)S(1)}, u32[]{:S(2)}, u32[]{:S(2)}) collective-permute-start(bf16[4,256,256]{2,1,0:T(8,128)(2,1)} %bitcast.1), channel_id=1, source_target_pairs={{0,24},{8,0},{16,8},{24,16},{1,25},{9,1},{17,9},{25,17},{2,26},{10... | collective-permute-start | bytes 1572872 | tf_op jit(solution)/shard_map/ppermute | solution.py:19
  7.1 32.4 %collective-permute-start = (bf16[4,256,256]{2,1,0:T(8,128)(2,1)}, bf16[4,256,256]{2,1,0:T(8,128)(2,1)}, u32[]{:S(2)}, u32[]{:S(2)}) collective-permute-start(bf16[4,256,256]{2,1,0:T(8,128)(2,1)} %bitcast), channel_id=1, source_target_pairs={{0,24},{8,0},{16,8},{24,16},{1,25},{9,1},{17,9},{25,17},{2,26},{10... | collective-permute-start | bytes 1572872 | tf_op jit(solution)/shard_map/ppermute | solution.py:19
  25.7 31.2 %collective-permute-start.6 = (bf16[9,256,256]{1,2,0:T(8,128)(2,1)}, bf16[9,256,256]{1,2,0:T(8,128)(2,1)}, u32[]{:S(2)}, u32[]{:S(2)}) collective-permute-start(bf16[9,256,256]{1,2,0:T(8,128)(2,1)} %fusion.24), channel_id=1, source_target_pairs={{0,4},{1,5},{8,12},{9,13},{16,20},{17,21},{24,28},{25,29}} | collective-permute-start | bytes 3538952 | tf_op jit(solution)/shard_map/ppermute | solution.py:64
  31.2 29.4 %collective-permute-start.5 = (bf16[9,256,256]{1,2,0:T(8,128)(2,1)}, bf16[9,256,256]{1,2,0:T(8,128)(2,1)}, u32[]{:S(2)}, u32[]{:S(2)}) collective-permute-start(bf16[9,256,256]{1,2,0:T(8,128)(2,1)} %fusion.24), channel_id=1, source_target_pairs={{6,4},{4,2},{2,0},{7,5},{5,3},{3,1},{14,12},{12,10},{10,8},{15,13}... | collective-permute-start | bytes 3538952 | tf_op jit(solution)/shard_map/ppermute | solution.py:63
  39.5 21.2 %collective-permute-start.7 = (bf16[9,256,256]{1,2,0:T(8,128)(2,1)}, bf16[9,256,256]{1,2,0:T(8,128)(2,1)}, u32[]{:S(2)}, u32[]{:S(2)}) collective-permute-start(bf16[9,256,256]{1,2,0:T(8,128)(2,1)} %fusion.23), channel_id=1, source_target_pairs={{6,2},{7,3},{14,10},{15,11},{22,18},{23,19},{30,26},{31,27}} | collective-permute-start | bytes 3538952 | tf_op jit(solution)/shard_map/ppermute | solution.py:61
  41.2 39.6 %collective-permute-start.4 = (bf16[9,256,256]{1,2,0:T(8,128)(2,1)}, bf16[9,256,256]{1,2,0:T(8,128)(2,1)}, u32[]{:S(2)}, u32[]{:S(2)}) collective-permute-start(bf16[9,256,256]{1,2,0:T(8,128)(2,1)} %fusion.23), channel_id=1, source_target_pairs={{0,2},{2,4},{4,6},{1,3},{3,5},{5,7},{8,10},{10,12},{12,14},{9,11},... | collective-permute-start | bytes 3538952 | tf_op jit(solution)/shard_map/ppermute | solution.py:60
  84.4 29.8 %collective-permute-start.8 = (bf16[9,256,256]{1,2,0:T(8,128)(2,1)}, bf16[9,256,256]{1,2,0:T(8,128)(2,1)}, u32[]{:S(2)}, u32[]{:S(2)}) collective-permute-start(bf16[9,256,256]{1,2,0:T(8,128)(2,1)} %fusion.16), channel_id=1, source_target_pairs={{0,2},{2,6},{6,4},{4,0},{1,3},{3,7},{7,5},{5,1},{8,10},{10,14},{14... | collective-permute-start | bytes 3538952 | tf_op jit(solution)/shard_map/ppermute | solution.py:85
  118.0 2.9 %collective-permute-start.9 = (bf16[9,256,256]{1,2,0:T(8,128)(2,1)S(1)}, bf16[9,256,256]{1,2,0:T(8,128)(2,1)S(1)}, u32[]{:S(2)}, u32[]{:S(2)}) collective-permute-start(bf16[9,256,256]{1,2,0:T(8,128)(2,1)S(1)} %fusion.13), channel_id=1, source_target_pairs={{0,1},{1,0},{2,3},{3,2},{4,5},{5,4},{6,7},{7,6},{8,9},{9,8},{10,11... | collective-permute-start | bytes 3538952 | tf_op jit(solution)/shard_map/ppermute | solution.py:19
  132.0 30.3 %collective-permute-start.12 = (bf16[9,256,256]{1,2,0:T(8,128)(2,1)}, bf16[9,256,256]{1,2,0:T(8,128)(2,1)}, u32[]{:S(2)}, u32[]{:S(2)}) collective-permute-start(bf16[9,256,256]{1,2,0:T(8,128)(2,1)} %fusion.27), channel_id=1, source_target_pairs={{0,4},{1,5},{8,12},{9,13},{16,20},{17,21},{24,28},{25,29}} | collective-permute-start | bytes 3538952 | tf_op jit(solution)/shard_map/ppermute | solution.py:64
  136.7 29.9 %collective-permute-start.11 = (bf16[9,256,256]{1,2,0:T(8,128)(2,1)}, bf16[9,256,256]{1,2,0:T(8,128)(2,1)}, u32[]{:S(2)}, u32[]{:S(2)}) collective-permute-start(bf16[9,256,256]{1,2,0:T(8,128)(2,1)} %fusion.27), channel_id=1, source_target_pairs={{6,4},{4,2},{2,0},{7,5},{5,3},{3,1},{14,12},{12,10},{10,8},{15,13}... | collective-permute-start | bytes 3538952 | tf_op jit(solution)/shard_map/ppermute | solution.py:63
  143.7 22.9 %collective-permute-start.13 = (bf16[9,256,256]{1,2,0:T(8,128)(2,1)}, bf16[9,256,256]{1,2,0:T(8,128)(2,1)}, u32[]{:S(2)}, u32[]{:S(2)}) collective-permute-start(bf16[9,256,256]{1,2,0:T(8,128)(2,1)} %fusion.26), channel_id=1, source_target_pairs={{6,2},{7,3},{14,10},{15,11},{22,18},{23,19},{30,26},{31,27}} | collective-permute-start | bytes 3538952 | tf_op jit(solution)/shard_map/ppermute | solution.py:61
  145.4 41.4 %collective-permute-start.10 = (bf16[9,256,256]{1,2,0:T(8,128)(2,1)}, bf16[9,256,256]{1,2,0:T(8,128)(2,1)}, u32[]{:S(2)}, u32[]{:S(2)}) collective-permute-start(bf16[9,256,256]{1,2,0:T(8,128)(2,1)} %fusion.26), channel_id=1, source_target_pairs={{0,2},{2,4},{4,6},{1,3},{3,5},{5,7},{8,10},{10,12},{12,14},{9,11},... | collective-permute-start | bytes 3538952 | tf_op jit(solution)/shard_map/ppermute | solution.py:60
  156.3 30.5 %copy-start.3 = (bf16[9,256,256]{1,2,0:T(8,128)(2,1)S(1)}, bf16[9,256,256]{1,2,0:T(8,128)(2,1)}, u32[]{:S(2)}) copy-start(bf16[9,256,256]{1,2,0:T(8,128)(2,1)} %fusion.28) | copy-start | bytes 3538948
  190.0 12.6 %collective-permute-start.14 = (bf16[3,256,256]{1,2,0:T(8,128)(2,1)S(1)}, bf16[3,256,256]{1,2,0:T(8,128)(2,1)S(1)}, u32[]{:S(2)}, u32[]{:S(2)}) collective-permute-start(bf16[3,256,256]{1,2,0:T(8,128)(2,1)S(1)} %slice.57), channel_id=1, source_target_pairs={{0,2},{2,6},{6,4},{4,0},{1,3},{3,7},{7,5},{5,1},{8,10},{10,14},{14... | collective-permute-start | bytes 1179656 | tf_op jit(solution)/shard_map/ppermute | solution.py:85
  202.8 11.5 %collective-permute-start.16 = (bf16[3,256,256]{1,2,0:T(8,128)(2,1)S(1)}, bf16[3,256,256]{1,2,0:T(8,128)(2,1)S(1)}, u32[]{:S(2)}, u32[]{:S(2)}) collective-permute-start(bf16[3,256,256]{1,2,0:T(8,128)(2,1)S(1)} %slice.46), channel_id=1, source_target_pairs={{0,2},{2,6},{6,4},{4,0},{1,3},{3,7},{7,5},{5,1},{8,10},{10,14},{14... | collective-permute-start | bytes 1179656 | tf_op jit(solution)/shard_map/ppermute | solution.py:85
  204.3 10.0 %collective-permute-start.15 = (bf16[1,3,1,256,256]{3,4,1,2,0:T(8,128)(2,1)S(1)}, bf16[1,3,1,256,256]{3,4,1,2,0:T(8,128)(2,1)S(1)}, u32[]{:S(2)}, u32[]{:S(2)}) collective-permute-start(bf16[1,3,1,256,256]{3,4,1,2,0:T(8,128)(2,1)S(1)} %bitcast.127), channel_id=1, source_target_pairs={{0,16},{8,24},{16,0},{24,8},{1,17},{9,25},{17,1},{25,9},{2,18},{10... | collective-permute-start | bytes 1179656 | tf_op jit(solution)/shard_map/ppermute | solution.py:19
  214.4 10.5 %collective-permute-start.18 = (bf16[3,256,256]{1,2,0:T(8,128)(2,1)S(1)}, bf16[3,256,256]{1,2,0:T(8,128)(2,1)S(1)}, u32[]{:S(2)}, u32[]{:S(2)}) collective-permute-start(bf16[3,256,256]{1,2,0:T(8,128)(2,1)S(1)} %slice.48), channel_id=1, source_target_pairs={{0,2},{2,6},{6,4},{4,0},{1,3},{3,7},{7,5},{5,1},{8,10},{10,14},{14... | collective-permute-start | bytes 1179656 | tf_op jit(solution)/shard_map/ppermute | solution.py:85
  215.1 9.9 %collective-permute-start.17 = (bf16[1,3,1,256,256]{3,4,1,2,0:T(8,128)(2,1)S(1)}, bf16[1,3,1,256,256]{3,4,1,2,0:T(8,128)(2,1)S(1)}, u32[]{:S(2)}, u32[]{:S(2)}) collective-permute-start(bf16[1,3,1,256,256]{3,4,1,2,0:T(8,128)(2,1)S(1)} %bitcast.126), channel_id=1, source_target_pairs={{0,16},{8,24},{16,0},{24,8},{1,17},{9,25},{17,1},{25,9},{2,18},{10... | collective-permute-start | bytes 1179656 | tf_op jit(solution)/shard_map/ppermute | solution.py:19
  225.1 8.7 %collective-permute-start.19 = (bf16[1,3,1,256,256]{3,4,1,2,0:T(8,128)(2,1)S(1)}, bf16[1,3,1,256,256]{3,4,1,2,0:T(8,128)(2,1)S(1)}, u32[]{:S(2)}, u32[]{:S(2)}) collective-permute-start(bf16[1,3,1,256,256]{3,4,1,2,0:T(8,128)(2,1)S(1)} %fusion.35), channel_id=1, source_target_pairs={{0,16},{8,24},{16,0},{24,8},{1,17},{9,25},{17,1},{25,9},{2,18},{10... | collective-permute-start | bytes 1179656 | tf_op jit(solution)/shard_map/ppermute | solution.py:19
  (5 other events, 27.2 us)

commit v11 on v10

--- a/solution.py
+++ b/solution.py
@@ -125,7 +125,7 @@
         if line:
             parts, tensors[step + 1 :] = advance_line(
                 current, ket, bra, mpo, live_mask, sector, tensors[step + 1 :],
-                3 if last else 1, onward if last else (lambda part: part),
+                5 if last else 1, onward if last else (lambda part: part),
             )
         else:
             parts = [advance_direct(current, ket, bra, mpo, live_mask)]

time: 236 us -> 243 us (1.030)
  local copies, waits for them, and re-layouts: 9.7 us -> 15.2 us
  starting transfers between devices: 46.8 us -> 51.5 us
  waiting for transfers between devices: 106 us -> 103 us
    ppermute x4 -> x6, waiting for transfers between devices: 41.4 us -> 36.3 us  [advance_line(): got_last = lax.ppermute(send[low:high], 'sector', LAST)]
    ppermute x8 -> x10, starting transfers between devices: 10.7 us -> 13.8 us  [shifted(): return lax.ppermute(value, axis, pairs)]
    unnamed x19 -> x23, local copies, waits for them, and re-layouts: 1.14 us -> 3.99 us
    ppermute x8 -> x10, waiting for transfers between devices: 9.26 us -> 11.4 us  [shifted(): return lax.ppermute(value, axis, pairs)]
    ppermute x4 -> x6, starting transfers between devices: 9.65 us -> 11.2 us  [advance_line(): got_last = lax.ppermute(send[low:high], 'sector', LAST)]
  transfers between devices with their start and end apart: 20 -> 24, of which waited for: 12 -> 16; matrix products, arithmetic and copies ran while one was open for 21% -> 22% of each run, Pallas kernels for 0% -> 0%
where the time goes in v11:
time: 243 us
  waiting for transfers between devices  103 us (42%)
  starting transfers between devices  51.5 us (21%)
  matrix products  50.7 us (21%)
  local copies, waits for them, and re-layouts  15.2 us (6%)
  other arithmetic  15.2 us (6%)
  between operations  6.52 us (3%)
    ppermute x2, waiting for transfers between devices, advance_line(): got_right = lax.ppermute(slot_a, 'sector', RIGHT)  40.4 us
    ppermute x6, waiting for transfers between devices, advance_line(): got_last = lax.ppermute(send[low:high], 'sector', LAST)  36.3 us
    dot_general x8, matrix products, term(): jnp.einsum('bd,vbc->vdc', bra_p, rotated, preferred_element_type=jnp.floa...  28.8 us
    dot_general x8, matrix products, term(): jnp.einsum('wv,wba->vba', mpo_p, gathered, preferred_element_type=jnp.flo...  21.9 us
    ppermute x10, starting transfers between devices, shifted(): return lax.ppermute(value, axis, pairs)  13.8 us
    ppermute x10, waiting for transfers between devices, shifted(): return lax.ppermute(value, axis, pairs)  11.4 us
    ppermute x6, starting transfers between devices, advance_line(): got_last = lax.ppermute(send[low:high], 'sector', LAST)  11.2 us
    ppermute x2, starting transfers between devices, advance_line(): got_right = lax.ppermute(slot_a, 'sector', RIGHT)  10.4 us
  transfers between devices with their start and end apart: 24, of which 16 were waited for; matrix products, arithmetic and copies ran while one was open for 22% of the time, Pallas kernels for 0%

profile of v11, /device:TPU:0, one launch (start us, length us, event | category | flops | bytes accessed | tf_op | source)
XLA Modules:
  0.0 242.5 jit_solution(18436119966775472129)
XLA Ops:
  22.0 3.6 %fusion.24 = bf16[9,256,256]{1,2,0:T(8,128)(2,1)} fusion(bf16[9,256,256]{2,0,1:T(8,128)(2,1)} %fusion.2, bf16[1,1,4,256,256]{4,3,2,1,0:T(8,128)(2,1)} %param.15, s32[]{:T(128)S(6)} %select_n.81, bf16[1,1,4,256,256]{4,3,2,1,0:T(8,128)(2,1)} %param.14), kind=kOutput, calls=%fused_computation.60 | convolution fusion | flops 605159424 | bytes 3539968 | tf_op jit(solution)/shard_map/bd,vbc->vdc/dot_general | solution.py:29
  25.6 5.5 %collective-permute-start.6 = (bf16[9,256,256]{1,2,0:T(8,128)(2,1)}, bf16[9,256,256]{1,2,0:T(8,128)(2,1)}, u32[]{:S(2)}, u32[]{:S(2)}) collective-permute-start(bf16[9,256,256]{1,2,0:T(8,128)(2,1)} %fusion.24), channel_id=1, source_target_pairs={{0,4},{1,5},{8,12},{9,13},{16,20},{17,21},{24,28},{25,29}} | collective-permute-start | bytes 3538952 | tf_op jit(solution)/shard_map/ppermute | solution.py:64
  35.8 3.6 %fusion.23 = bf16[9,256,256]{1,2,0:T(8,128)(2,1)} fusion(bf16[9,256,256]{2,0,1:T(8,128)(2,1)} %fusion.6, bf16[1,1,4,256,256]{4,3,2,1,0:T(8,128)(2,1)} %param.15, s32[]{:T(128)S(6)} %select_n.78, bf16[1,1,4,256,256]{4,3,2,1,0:T(8,128)(2,1)} %param.14), kind=kOutput, calls=%fused_computation.59 | convolution fusion | flops 605159424 | bytes 3539968 | tf_op jit(solution)/shard_map/bd,vbc->vdc/dot_general | solution.py:29
  41.1 5.2 %collective-permute-start.4 = (bf16[9,256,256]{1,2,0:T(8,128)(2,1)}, bf16[9,256,256]{1,2,0:T(8,128)(2,1)}, u32[]{:S(2)}, u32[]{:S(2)}) collective-permute-start(bf16[9,256,256]{1,2,0:T(8,128)(2,1)} %fusion.23), channel_id=1, source_target_pairs={{0,2},{2,4},{4,6},{1,3},{3,5},{5,7},{8,10},{10,12},{12,14},{9,11},... | collective-permute-start | bytes 3538952 | tf_op jit(solution)/shard_map/ppermute | solution.py:60
  49.7 3.7 %fusion.25 = bf16[9,256,256]{1,2,0:T(8,128)(2,1)} fusion(bf16[9,256,256]{2,0,1:T(8,128)(2,1)} %fusion, bf16[1,1,4,256,256]{4,3,2,1,0:T(8,128)(2,1)} %param.15, s32[]{:T(128)S(6)} %select_n.82, bf16[1,1,4,256,256]{4,3,2,1,0:T(8,128)(2,1)} %param.14), kind=kOutput, calls=%fused_computation.61 | convolution fusion | flops 605159424 | bytes 3539968 | tf_op jit(solution)/shard_map/bd,vbc->vdc/dot_general | solution.py:29
  56.8 3.7 %collective-permute-done.5 = bf16[9,256,256]{1,2,0:T(8,128)(2,1)} collective-permute-done((bf16[9,256,256]{1,2,0:T(8,128)(2,1)}, bf16[9,256,256]{1,2,0:T(8,128)(2,1)}, u32[]{:S(2)}, u32[]{:S(2)}) %collective-permute-start.5) | collective-permute-done | bytes 1179680 | tf_op jit(solution)/shard_map/ppermute | solution.py:63
  60.6 20.2 %collective-permute-done.4 = bf16[9,256,256]{1,2,0:T(8,128)(2,1)} collective-permute-done((bf16[9,256,256]{1,2,0:T(8,128)(2,1)}, bf16[9,256,256]{1,2,0:T(8,128)(2,1)}, u32[]{:S(2)}, u32[]{:S(2)}) %collective-permute-start.4) | collective-permute-done | bytes 1179680 | tf_op jit(solution)/shard_map/ppermute | solution.py:60
  84.3 3.7 %collective-permute-start.8 = (bf16[9,256,256]{1,2,0:T(8,128)(2,1)}, bf16[9,256,256]{1,2,0:T(8,128)(2,1)}, u32[]{:S(2)}, u32[]{:S(2)}) collective-permute-start(bf16[9,256,256]{1,2,0:T(8,128)(2,1)} %fusion.16), channel_id=1, source_target_pairs={{0,2},{2,6},{6,4},{4,0},{1,3},{3,7},{7,5},{5,1},{8,10},{10,14},{14... | collective-permute-start | bytes 3538952 | tf_op jit(solution)/shard_map/ppermute | solution.py:85
  94.0 20.1 %collective-permute-done.8 = bf16[9,256,256]{1,2,0:T(8,128)(2,1)} collective-permute-done((bf16[9,256,256]{1,2,0:T(8,128)(2,1)}, bf16[9,256,256]{1,2,0:T(8,128)(2,1)}, u32[]{:S(2)}, u32[]{:S(2)}) %collective-permute-start.8) | collective-permute-done | bytes 1179680 | tf_op jit(solution)/shard_map/ppermute | solution.py:85
  114.1 3.9 %fusion.13 = bf16[9,256,256]{1,2,0:T(8,128)(2,1)S(1)} fusion(bf16[9,256,256]{1,2,0:T(8,128)(2,1)} %collective-permute-done.4, bf16[9,256,256]{1,2,0:T(8,128)(2,1)} %collective-permute-done.5, bf16[9,256,256]{2,1,0:T(8,128)(2,1)S(1)} %convolution_convert_fusion.12, bf16[9,256,256]{1,2,0:T(8,128)(2,1)} %collective-permute-done.8, ...), kind=kLoop, calls=%fused_computation.23 | loop fusion | flops 8257536 | bytes 8519688 | tf_op jit(solution)/shard_map/convert_element_type | solution.py:89
  122.5 3.7 %copy.32 = bf16[18,256,256]{2,0,1:T(8,128)(2,1)S(1)} copy(bf16[18,256,256]{1,2,0:T(8,128)(2,1)} %pad_maximum_fusion.1) | data formatting | bytes 4718592 | tf_op jit(solution)/shard_map/concatenate | solution.py:41
  128.3 3.6 %fusion.27 = bf16[9,256,256]{1,2,0:T(8,128)(2,1)} fusion(bf16[9,256,256]{2,0,1:T(8,128)(2,1)} %fusion.92, bf16[4,256,256]{2,1,0:T(8,128)(2,1)} %copy-done.4, s32[]{:T(128)S(6)} %select_n.81, bf16[4,256,256]{2,1,0:T(8,128)(2,1)} %collective-permute-done), kind=kOutput, calls=%fused_computation.63 | convolution fusion | flops 605159424 | bytes 3539968 | tf_op jit(solution)/shard_map/bd,vbc->vdc/dot_general | solution.py:29
  131.9 4.7 %collective-permute-start.12 = (bf16[9,256,256]{1,2,0:T(8,128)(2,1)}, bf16[9,256,256]{1,2,0:T(8,128)(2,1)}, u32[]{:S(2)}, u32[]{:S(2)}) collective-permute-start(bf16[9,256,256]{1,2,0:T(8,128)(2,1)} %fusion.27), channel_id=1, source_target_pairs={{0,4},{1,5},{8,12},{9,13},{16,20},{17,21},{24,28},{25,29}} | collective-permute-start | bytes 3538952 | tf_op jit(solution)/shard_map/ppermute | solution.py:64
  140.0 3.6 %fusion.26 = bf16[9,256,256]{1,2,0:T(8,128)(2,1)} fusion(bf16[9,256,256]{2,0,1:T(8,128)(2,1)} %fusion.94, bf16[4,256,256]{2,1,0:T(8,128)(2,1)} %copy-done.4, s32[]{:T(128)S(6)} %select_n.78, bf16[4,256,256]{2,1,0:T(8,128)(2,1)} %collective-permute-done), kind=kOutput, calls=%fused_computation.62 | convolution fusion | flops 605159424 | bytes 3539968 | tf_op jit(solution)/shard_map/bd,vbc->vdc/dot_general | solution.py:29
  145.3 5.2 %collective-permute-start.10 = (bf16[9,256,256]{1,2,0:T(8,128)(2,1)}, bf16[9,256,256]{1,2,0:T(8,128)(2,1)}, u32[]{:S(2)}, u32[]{:S(2)}) collective-permute-start(bf16[9,256,256]{1,2,0:T(8,128)(2,1)} %fusion.26), channel_id=1, source_target_pairs={{0,2},{2,4},{4,6},{1,3},{3,5},{5,7},{8,10},{10,12},{12,14},{9,11},... | collective-permute-start | bytes 3538952 | tf_op jit(solution)/shard_map/ppermute | solution.py:60
  152.6 3.7 %fusion.28 = bf16[9,256,256]{1,2,0:T(8,128)(2,1)} fusion(bf16[9,256,256]{2,0,1:T(8,128)(2,1)} %fusion.90, bf16[4,256,256]{2,1,0:T(8,128)(2,1)} %copy-done.4, s32[]{:T(128)S(6)} %select_n.82, bf16[4,256,256]{2,1,0:T(8,128)(2,1)} %collective-permute-done), kind=kOutput, calls=%fused_computation.64 | convolution fusion | flops 605159424 | bytes 3539968 | tf_op jit(solution)/shard_map/bd,vbc->vdc/dot_general | solution.py:29
  158.4 3.8 %collective-permute-done.12 = bf16[9,256,256]{1,2,0:T(8,128)(2,1)} collective-permute-done((bf16[9,256,256]{1,2,0:T(8,128)(2,1)}, bf16[9,256,256]{1,2,0:T(8,128)(2,1)}, u32[]{:S(2)}, u32[]{:S(2)}) %collective-permute-start.12) | collective-permute-done | bytes 1179680 | tf_op jit(solution)/shard_map/ppermute | solution.py:64
  162.2 4.3 %collective-permute-done.11 = bf16[9,256,256]{1,2,0:T(8,128)(2,1)} collective-permute-done((bf16[9,256,256]{1,2,0:T(8,128)(2,1)}, bf16[9,256,256]{1,2,0:T(8,128)(2,1)}, u32[]{:S(2)}, u32[]{:S(2)}) %collective-permute-start.11) | collective-permute-done | bytes 1179680 | tf_op jit(solution)/shard_map/ppermute | solution.py:63
  166.5 20.2 %collective-permute-done.10 = bf16[9,256,256]{1,2,0:T(8,128)(2,1)} collective-permute-done((bf16[9,256,256]{1,2,0:T(8,128)(2,1)}, bf16[9,256,256]{1,2,0:T(8,128)(2,1)}, u32[]{:S(2)}, u32[]{:S(2)}) %collective-permute-start.10) | collective-permute-done | bytes 1179680 | tf_op jit(solution)/shard_map/ppermute | solution.py:60
  190.0 3.7 %collective-permute-start.14 = (bf16[1,256,256]{1,2,0:T(8,128)(2,1)S(1)}, bf16[1,256,256]{1,2,0:T(8,128)(2,1)S(1)}, u32[]{:S(2)}, u32[]{:S(2)}) collective-permute-start(bf16[1,256,256]{1,2,0:T(8,128)(2,1)S(1)} %slice.73), channel_id=1, source_target_pairs={{0,2},{2,6},{6,4},{4,0},{1,3},{3,7},{7,5},{5,1},{8,10},{10,14},{14... | collective-permute-start | bytes 393224 | tf_op jit(solution)/shard_map/ppermute | solution.py:85
  193.7 4.4 %fusion.19 = f32[9,256,256]{1,2,0:T(8,128)S(1)} fusion(bf16[9,256,256]{1,2,0:T(8,128)(2,1)} %collective-permute-done.10, bf16[9,256,256]{1,2,0:T(8,128)(2,1)} %collective-permute-done.11, bf16[9,256,256]{1,2,0:T(8,128)(2,1)} %collective-permute-done.12, bf16[9,256,256]{1,2,0:T(8,128)(2,1)} %collective-permute-done.13, f32[]{:T(128)S(6)} %select_n.83, ...), kind=kOutput, calls=%fused_computation.29 | convolution fusion | flops 612237312 | bytes 9437192 | tf_op jit(solution)/shard_map/bd,vbc->vdc/dot_general | solution.py:29
  209.3 5.7 %collective-permute-done.18 = bf16[2,256,256]{1,2,0:T(8,128)(2,1)S(1)} collective-permute-done((bf16[2,256,256]{1,2,0:T(8,128)(2,1)S(1)}, bf16[2,256,256]{1,2,0:T(8,128)(2,1)S(1)}, u32[]{:S(2)}, u32[]{:S(2)}) %collective-permute-start.18) | collective-permute-done | bytes 262176 | tf_op jit(solution)/shard_map/ppermute | solution.py:85
  218.4 3.9 %collective-permute-done.20 = bf16[2,256,256]{1,2,0:T(8,128)(2,1)S(1)} collective-permute-done((bf16[2,256,256]{1,2,0:T(8,128)(2,1)S(1)}, bf16[2,256,256]{1,2,0:T(8,128)(2,1)S(1)}, u32[]{:S(2)}, u32[]{:S(2)}) %collective-permute-start.20) | collective-permute-done | bytes 262176 | tf_op jit(solution)/shard_map/ppermute | solution.py:85
  226.8 3.9 %collective-permute-done.22 = bf16[2,256,256]{1,2,0:T(8,128)(2,1)S(1)} collective-permute-done((bf16[2,256,256]{1,2,0:T(8,128)(2,1)S(1)}, bf16[2,256,256]{1,2,0:T(8,128)(2,1)S(1)}, u32[]{:S(2)}, u32[]{:S(2)}) %collective-permute-start.22) | collective-permute-done | bytes 262176 | tf_op jit(solution)/shard_map/ppermute | solution.py:85
  (97 shorter events, 88.3 us)
Async XLA Ops:
  2.4 14.4 %collective-permute-start.3 = (bf16[9,256,256]{2,1,0:T(8,128)(2,1)S(1)}, bf16[9,256,256]{2,1,0:T(8,128)(2,1)}, u32[]{:S(2)}, u32[]{:S(2)}) collective-permute-start(bf16[9,256,256]{2,1,0:T(8,128)(2,1)S(1)} %bitcast_select_fusion), channel_id=1, source_target_pairs={{0,1},{1,0},{2,3},{3,2},{4,5},{5,4},{6,7},{7,6},{8,9},{9,8},{10,11... | collective-permute-start | bytes 3538952 | tf_op jit(solution)/shard_map/ppermute | solution.py:19
  3.0 36.4 %collective-permute-start.2 = (bf16[18,9,4]{1,2,0:T(4,128)(2,1)S(1)}, bf16[18,9,4]{1,2,0:T(4,128)(2,1)S(1)}, u32[]{:S(2)}, u32[]{:S(2)}) collective-permute-start(bf16[18,9,4]{1,2,0:T(4,128)(2,1)S(1)} %bitcast.128), channel_id=1, source_target_pairs={{0,24},{8,0},{16,8},{24,16},{1,25},{9,1},{17,9},{25,17},{2,26},{10... | collective-permute-start | bytes 3896 | tf_op jit(solution)/shard_map/ppermute | solution.py:19
  6.5 32.9 %collective-permute-start.1 = (bf16[4,256,256]{2,1,0:T(8,128)(2,1)}, bf16[4,256,256]{2,1,0:T(8,128)(2,1)S(1)}, u32[]{:S(2)}, u32[]{:S(2)}) collective-permute-start(bf16[4,256,256]{2,1,0:T(8,128)(2,1)} %bitcast.2), channel_id=1, source_target_pairs={{0,24},{8,0},{16,8},{24,16},{1,25},{9,1},{17,9},{25,17},{2,26},{10... | collective-permute-start | bytes 1572872 | tf_op jit(solution)/shard_map/ppermute | solution.py:19
  7.1 32.3 %collective-permute-start = (bf16[4,256,256]{2,1,0:T(8,128)(2,1)}, bf16[4,256,256]{2,1,0:T(8,128)(2,1)}, u32[]{:S(2)}, u32[]{:S(2)}) collective-permute-start(bf16[4,256,256]{2,1,0:T(8,128)(2,1)} %bitcast.1), channel_id=1, source_target_pairs={{0,24},{8,0},{16,8},{24,16},{1,25},{9,1},{17,9},{25,17},{2,26},{10... | collective-permute-start | bytes 1572872 | tf_op jit(solution)/shard_map/ppermute | solution.py:19
  25.6 31.2 %collective-permute-start.6 = (bf16[9,256,256]{1,2,0:T(8,128)(2,1)}, bf16[9,256,256]{1,2,0:T(8,128)(2,1)}, u32[]{:S(2)}, u32[]{:S(2)}) collective-permute-start(bf16[9,256,256]{1,2,0:T(8,128)(2,1)} %fusion.24), channel_id=1, source_target_pairs={{0,4},{1,5},{8,12},{9,13},{16,20},{17,21},{24,28},{25,29}} | collective-permute-start | bytes 3538952 | tf_op jit(solution)/shard_map/ppermute | solution.py:64
  31.1 29.4 %collective-permute-start.5 = (bf16[9,256,256]{1,2,0:T(8,128)(2,1)}, bf16[9,256,256]{1,2,0:T(8,128)(2,1)}, u32[]{:S(2)}, u32[]{:S(2)}) collective-permute-start(bf16[9,256,256]{1,2,0:T(8,128)(2,1)} %fusion.24), channel_id=1, source_target_pairs={{6,4},{4,2},{2,0},{7,5},{5,3},{3,1},{14,12},{12,10},{10,8},{15,13}... | collective-permute-start | bytes 3538952 | tf_op jit(solution)/shard_map/ppermute | solution.py:63
  39.4 21.2 %collective-permute-start.7 = (bf16[9,256,256]{1,2,0:T(8,128)(2,1)}, bf16[9,256,256]{1,2,0:T(8,128)(2,1)}, u32[]{:S(2)}, u32[]{:S(2)}) collective-permute-start(bf16[9,256,256]{1,2,0:T(8,128)(2,1)} %fusion.23), channel_id=1, source_target_pairs={{6,2},{7,3},{14,10},{15,11},{22,18},{23,19},{30,26},{31,27}} | collective-permute-start | bytes 3538952 | tf_op jit(solution)/shard_map/ppermute | solution.py:61
  41.1 39.6 %collective-permute-start.4 = (bf16[9,256,256]{1,2,0:T(8,128)(2,1)}, bf16[9,256,256]{1,2,0:T(8,128)(2,1)}, u32[]{:S(2)}, u32[]{:S(2)}) collective-permute-start(bf16[9,256,256]{1,2,0:T(8,128)(2,1)} %fusion.23), channel_id=1, source_target_pairs={{0,2},{2,4},{4,6},{1,3},{3,5},{5,7},{8,10},{10,12},{12,14},{9,11},... | collective-permute-start | bytes 3538952 | tf_op jit(solution)/shard_map/ppermute | solution.py:60
  84.3 29.8 %collective-permute-start.8 = (bf16[9,256,256]{1,2,0:T(8,128)(2,1)}, bf16[9,256,256]{1,2,0:T(8,128)(2,1)}, u32[]{:S(2)}, u32[]{:S(2)}) collective-permute-start(bf16[9,256,256]{1,2,0:T(8,128)(2,1)} %fusion.16), channel_id=1, source_target_pairs={{0,2},{2,6},{6,4},{4,0},{1,3},{3,7},{7,5},{5,1},{8,10},{10,14},{14... | collective-permute-start | bytes 3538952 | tf_op jit(solution)/shard_map/ppermute | solution.py:85
  118.0 2.9 %collective-permute-start.9 = (bf16[9,256,256]{1,2,0:T(8,128)(2,1)S(1)}, bf16[9,256,256]{1,2,0:T(8,128)(2,1)S(1)}, u32[]{:S(2)}, u32[]{:S(2)}) collective-permute-start(bf16[9,256,256]{1,2,0:T(8,128)(2,1)S(1)} %fusion.13), channel_id=1, source_target_pairs={{0,1},{1,0},{2,3},{3,2},{4,5},{5,4},{6,7},{7,6},{8,9},{9,8},{10,11... | collective-permute-start | bytes 3538952 | tf_op jit(solution)/shard_map/ppermute | solution.py:19
  131.9 30.3 %collective-permute-start.12 = (bf16[9,256,256]{1,2,0:T(8,128)(2,1)}, bf16[9,256,256]{1,2,0:T(8,128)(2,1)}, u32[]{:S(2)}, u32[]{:S(2)}) collective-permute-start(bf16[9,256,256]{1,2,0:T(8,128)(2,1)} %fusion.27), channel_id=1, source_target_pairs={{0,4},{1,5},{8,12},{9,13},{16,20},{17,21},{24,28},{25,29}} | collective-permute-start | bytes 3538952 | tf_op jit(solution)/shard_map/ppermute | solution.py:64
  136.6 29.9 %collective-permute-start.11 = (bf16[9,256,256]{1,2,0:T(8,128)(2,1)}, bf16[9,256,256]{1,2,0:T(8,128)(2,1)}, u32[]{:S(2)}, u32[]{:S(2)}) collective-permute-start(bf16[9,256,256]{1,2,0:T(8,128)(2,1)} %fusion.27), channel_id=1, source_target_pairs={{6,4},{4,2},{2,0},{7,5},{5,3},{3,1},{14,12},{12,10},{10,8},{15,13}... | collective-permute-start | bytes 3538952 | tf_op jit(solution)/shard_map/ppermute | solution.py:63
  143.6 22.9 %collective-permute-start.13 = (bf16[9,256,256]{1,2,0:T(8,128)(2,1)}, bf16[9,256,256]{1,2,0:T(8,128)(2,1)}, u32[]{:S(2)}, u32[]{:S(2)}) collective-permute-start(bf16[9,256,256]{1,2,0:T(8,128)(2,1)} %fusion.26), channel_id=1, source_target_pairs={{6,2},{7,3},{14,10},{15,11},{22,18},{23,19},{30,26},{31,27}} | collective-permute-start | bytes 3538952 | tf_op jit(solution)/shard_map/ppermute | solution.py:61
  145.3 41.4 %collective-permute-start.10 = (bf16[9,256,256]{1,2,0:T(8,128)(2,1)}, bf16[9,256,256]{1,2,0:T(8,128)(2,1)}, u32[]{:S(2)}, u32[]{:S(2)}) collective-permute-start(bf16[9,256,256]{1,2,0:T(8,128)(2,1)} %fusion.26), channel_id=1, source_target_pairs={{0,2},{2,4},{4,6},{1,3},{3,5},{5,7},{8,10},{10,12},{12,14},{9,11},... | collective-permute-start | bytes 3538952 | tf_op jit(solution)/shard_map/ppermute | solution.py:60
  190.0 8.2 %collective-permute-start.14 = (bf16[1,256,256]{1,2,0:T(8,128)(2,1)S(1)}, bf16[1,256,256]{1,2,0:T(8,128)(2,1)S(1)}, u32[]{:S(2)}, u32[]{:S(2)}) collective-permute-start(bf16[1,256,256]{1,2,0:T(8,128)(2,1)S(1)} %slice.73), channel_id=1, source_target_pairs={{0,2},{2,6},{6,4},{4,0},{1,3},{3,7},{7,5},{5,1},{8,10},{10,14},{14... | collective-permute-start | bytes 393224 | tf_op jit(solution)/shard_map/ppermute | solution.py:85
  199.3 8.2 %collective-permute-start.16 = (bf16[2,256,256]{1,2,0:T(8,128)(2,1)S(1)}, bf16[2,256,256]{1,2,0:T(8,128)(2,1)S(1)}, u32[]{:S(2)}, u32[]{:S(2)}) collective-permute-start(bf16[2,256,256]{1,2,0:T(8,128)(2,1)S(1)} %slice.58), channel_id=1, source_target_pairs={{0,2},{2,6},{6,4},{4,0},{1,3},{3,7},{7,5},{5,1},{8,10},{10,14},{14... | collective-permute-start | bytes 786440 | tf_op jit(solution)/shard_map/ppermute | solution.py:85
  199.8 5.0 %collective-permute-start.15 = (bf16[1,1,1,256,256]{3,4,2,1,0:T(8,128)(2,1)S(1)}, bf16[1,1,1,256,256]{3,4,2,1,0:T(8,128)(2,1)S(1)}, u32[]{:S(2)}, u32[]{:S(2)}) collective-permute-start(bf16[1,1,1,256,256]{3,4,2,1,0:T(8,128)(2,1)S(1)} %bitcast.133), channel_id=1, source_target_pairs={{0,16},{8,24},{16,0},{24,8},{1,17},{9,25},{17,1},{25,9},{2,18},{10... | collective-permute-start | bytes 393224 | tf_op jit(solution)/shard_map/ppermute | solution.py:19
  207.6 7.3 %collective-permute-start.18 = (bf16[2,256,256]{1,2,0:T(8,128)(2,1)S(1)}, bf16[2,256,256]{1,2,0:T(8,128)(2,1)S(1)}, u32[]{:S(2)}, u32[]{:S(2)}) collective-permute-start(bf16[2,256,256]{1,2,0:T(8,128)(2,1)S(1)} %slice.60), channel_id=1, source_target_pairs={{0,2},{2,6},{6,4},{4,0},{1,3},{3,7},{7,5},{5,1},{8,10},{10,14},{14... | collective-permute-start | bytes 786440 | tf_op jit(solution)/shard_map/ppermute | solution.py:85
  207.7 7.3 %collective-permute-start.17 = (bf16[1,2,1,256,256]{3,4,1,2,0:T(8,128)(2,1)S(1)}, bf16[1,2,1,256,256]{3,4,1,2,0:T(8,128)(2,1)S(1)}, u32[]{:S(2)}, u32[]{:S(2)}) collective-permute-start(bf16[1,2,1,256,256]{3,4,1,2,0:T(8,128)(2,1)S(1)} %bitcast.131), channel_id=1, source_target_pairs={{0,16},{8,24},{16,0},{24,8},{1,17},{9,25},{17,1},{25,9},{2,18},{10... | collective-permute-start | bytes 786440 | tf_op jit(solution)/shard_map/ppermute | solution.py:19
  215.0 7.3 %collective-permute-start.20 = (bf16[2,256,256]{1,2,0:T(8,128)(2,1)S(1)}, bf16[2,256,256]{1,2,0:T(8,128)(2,1)S(1)}, u32[]{:S(2)}, u32[]{:S(2)}) collective-permute-start(bf16[2,256,256]{1,2,0:T(8,128)(2,1)S(1)} %slice.62), channel_id=1, source_target_pairs={{0,2},{2,6},{6,4},{4,0},{1,3},{3,7},{7,5},{5,1},{8,10},{10,14},{14... | collective-permute-start | bytes 786440 | tf_op jit(solution)/shard_map/ppermute | solution.py:85
  216.9 6.4 %collective-permute-start.19 = (bf16[1,2,1,256,256]{3,4,1,2,0:T(8,128)(2,1)S(1)}, bf16[1,2,1,256,256]{3,4,1,2,0:T(8,128)(2,1)S(1)}, u32[]{:S(2)}, u32[]{:S(2)}) collective-permute-start(bf16[1,2,1,256,256]{3,4,1,2,0:T(8,128)(2,1)S(1)} %bitcast.132), channel_id=1, source_target_pairs={{0,16},{8,24},{16,0},{24,8},{1,17},{9,25},{17,1},{25,9},{2,18},{10... | collective-permute-start | bytes 786440 | tf_op jit(solution)/shard_map/ppermute | solution.py:19
  223.4 7.3 %collective-permute-start.22 = (bf16[2,256,256]{1,2,0:T(8,128)(2,1)S(1)}, bf16[2,256,256]{1,2,0:T(8,128)(2,1)S(1)}, u32[]{:S(2)}, u32[]{:S(2)}) collective-permute-start(bf16[2,256,256]{1,2,0:T(8,128)(2,1)S(1)} %slice.64), channel_id=1, source_target_pairs={{0,2},{2,6},{6,4},{4,0},{1,3},{3,7},{7,5},{5,1},{8,10},{10,14},{14... | collective-permute-start | bytes 786440 | tf_op jit(solution)/shard_map/ppermute | solution.py:85
  224.6 8.3 %collective-permute-start.21 = (bf16[1,2,1,256,256]{3,4,1,2,0:T(8,128)(2,1)S(1)}, bf16[1,2,1,256,256]{3,4,1,2,0:T(8,128)(2,1)S(1)}, u32[]{:S(2)}, u32[]{:S(2)}) collective-permute-start(bf16[1,2,1,256,256]{3,4,1,2,0:T(8,128)(2,1)S(1)} %bitcast.130), channel_id=1, source_target_pairs={{0,16},{8,24},{16,0},{24,8},{1,17},{9,25},{17,1},{25,9},{2,18},{10... | collective-permute-start | bytes 786440 | tf_op jit(solution)/shard_map/ppermute | solution.py:19
  233.0 6.4 %collective-permute-start.23 = (bf16[1,2,1,256,256]{3,4,1,2,0:T(8,128)(2,1)S(1)}, bf16[1,2,1,256,256]{3,4,1,2,0:T(8,128)(2,1)S(1)}, u32[]{:S(2)}, u32[]{:S(2)}) collective-permute-start(bf16[1,2,1,256,256]{3,4,1,2,0:T(8,128)(2,1)S(1)} %fusion.37), channel_id=1, source_target_pairs={{0,16},{8,24},{16,0},{24,8},{1,17},{9,25},{17,1},{25,9},{2,18},{10... | collective-permute-start | bytes 786440 | tf_op jit(solution)/shard_map/ppermute | solution.py:19
  (9 other events, 99.8 us)

commit v12 on v11

--- a/solution.py
+++ b/solution.py
@@ -31,11 +31,15 @@
     ).astype(jnp.bfloat16)
 
 
-def chan_gathered(current, mpo):
+def chan_copies(piece):
+    return [piece] + [shifted(piece, "chan", k) for k in range(1, lax.axis_size("chan"))]
+
+
+def chan_gathered(pieces, mpo):
     count = lax.axis_size("chan")
     me = lax.axis_index("chan")
-    width = current.shape[0]
-    held = [current] + [shifted(current, "chan", k) for k in range(1, count)]
+    held = [jnp.concatenate([p[k] for p in pieces], axis=0) for k in range(count)]
+    width = held[0].shape[0]
     rows = [(me - k) % count for k in range(count)]
     order = jnp.concatenate([jnp.arange(width) + r * width for r in rows])
     return jnp.concatenate(held, axis=0), jnp.take(mpo, order, axis=0)
@@ -119,20 +123,22 @@
     def onward(part):
         return shifted(part[None, :, None], "site", STEPS)
 
+    pieces = [chan_copies(current)]
+    current = None
     for step in range(STEPS):
         ket, bra, mpo = tensors[step]
         last = step == STEPS - 1
         if line:
             parts, tensors[step + 1 :] = advance_line(
-                current, ket, bra, mpo, live_mask, sector, tensors[step + 1 :],
-                5 if last else 1, onward if last else (lambda part: part),
+                pieces, ket, bra, mpo, live_mask, sector, tensors[step + 1 :],
+                3 if last else 2, onward if last else chan_copies,
             )
         else:
-            parts = [advance_direct(current, ket, bra, mpo, live_mask)]
-            parts = [onward(parts[0])] if last else parts
-        if not last:
-            current = jnp.concatenate(parts, axis=0)
-    return jnp.concatenate(parts, axis=1)
+            parts = [advance_direct(pieces, ket, bra, mpo, live_mask)]
+            current = parts[0]
+            parts = [onward(current)] if last else [chan_copies(current)]
+        pieces = parts
+    return jnp.concatenate(pieces, axis=1)
 
 
 def solution(mesh):

time: 243 us -> 234 us (0.963)
  local copies, waits for them, and re-layouts: 15.2 us -> 9.81 us
  starting transfers between devices: 51.5 us -> 46.7 us
  waiting for transfers between devices: 103 us -> 107 us
  other arithmetic: 15.2 us -> 11.9 us
    ppermute x6 -> x5, waiting for transfers between devices: 36.3 us -> 47.2 us  [advance_line(): got_last = lax.ppermute(send[low:high], 'sector', LAST)]
    convert_element_type x5 -> x4, other arithmetic: 4.17 us -> 0.58 us  [advance_line(): piece = (piece * live_mask[None]).astype(jnp.bfloat16)]
    ppermute x2, waiting for transfers between devices: 7.29 us -> 3.84 us  [advance_line(): middle_right = lax.ppermute(slot_b, 'sector', ((0, 2),))]
    ppermute x10 -> x9, starting transfers between devices: 13.8 us -> 10.7 us  [shifted(): return lax.ppermute(value, axis, pairs)]
    unnamed x23 -> x21, local copies, waits for them, and re-layouts: 3.99 us -> 1.14 us
    ppermute x2, waiting for transfers between devices: 8.02 us -> 5.42 us  [advance_line(): got_left = lax.ppermute(slot_b, 'sector', LEFT)]
    ppermute x10 -> x9, waiting for transfers between devices: 11.4 us -> 10.4 us  [shifted(): return lax.ppermute(value, axis, pairs)]
    ppermute x6 -> x5, starting transfers between devices: 11.2 us -> 10.6 us  [advance_line(): got_last = lax.ppermute(send[low:high], 'sector', LAST)]
  transfers between devices with their start and end apart: 24 -> 22, of which waited for: 16 -> 13; matrix products, arithmetic and copies ran while one was open for 22% -> 22% of each run, Pallas kernels for 0% -> 0%
where the time goes in v12:
time: 234 us; the launch traced here: 233 us
  waiting for transfers between devices  107 us (46%)
  matrix products  50.8 us (22%)
  starting transfers between devices  46.7 us (20%)
  other arithmetic  11.9 us (5%)
  local copies, waits for them, and re-layouts  9.81 us (4%)
  between operations  6.53 us (3%)
    ppermute x5, waiting for transfers between devices, advance_line(): got_last = lax.ppermute(send[low:high], 'sector', LAST)  47.2 us
    ppermute x2, waiting for transfers between devices, advance_line(): got_right = lax.ppermute(slot_a, 'sector', RIGHT)  40.4 us
    dot_general x8, matrix products, term(): jnp.einsum('bd,vbc->vdc', bra_p, rotated, preferred_element_type=jnp.floa...  28.9 us
    dot_general x8, matrix products, term(): jnp.einsum('wv,wba->vba', mpo_p, gathered, preferred_element_type=jnp.flo...  21.9 us
    ppermute x9, starting transfers between devices, shifted(): return lax.ppermute(value, axis, pairs)  10.7 us
    ppermute x5, starting transfers between devices, advance_line(): got_last = lax.ppermute(send[low:high], 'sector', LAST)  10.6 us
    ppermute x9, waiting for transfers between devices, shifted(): return lax.ppermute(value, axis, pairs)  10.4 us
    ppermute x2, starting transfers between devices, advance_line(): got_right = lax.ppermute(slot_a, 'sector', RIGHT)  10.4 us
  transfers between devices with their start and end apart: 22, of which 13 were waited for; matrix products, arithmetic and copies ran while one was open for 22% of the time, Pallas kernels for 0%

profile of v12, /device:TPU:0, one launch (start us, length us, event | category | flops | bytes accessed | tf_op | source)
XLA Modules:
  0.0 233.0 jit_solution(16449683947200840745)
XLA Ops:
  22.0 3.6 %fusion.21 = bf16[9,256,256]{1,2,0:T(8,128)(2,1)} fusion(bf16[9,256,256]{2,0,1:T(8,128)(2,1)} %fusion.2, bf16[1,1,4,256,256]{4,3,2,1,0:T(8,128)(2,1)} %param.15, s32[]{:T(128)S(6)} %select_n.81, bf16[1,1,4,256,256]{4,3,2,1,0:T(8,128)(2,1)} %param.14), kind=kOutput, calls=%fused_computation.57 | convolution fusion | flops 605159424 | bytes 3539968 | tf_op jit(solution)/shard_map/bd,vbc->vdc/dot_general | solution.py:29
  25.6 5.5 %collective-permute-start.6 = (bf16[9,256,256]{1,2,0:T(8,128)(2,1)}, bf16[9,256,256]{1,2,0:T(8,128)(2,1)}, u32[]{:S(2)}, u32[]{:S(2)}) collective-permute-start(bf16[9,256,256]{1,2,0:T(8,128)(2,1)} %fusion.21), channel_id=1, source_target_pairs={{0,4},{1,5},{8,12},{9,13},{16,20},{17,21},{24,28},{25,29}} | collective-permute-start | bytes 3538952 | tf_op jit(solution)/shard_map/ppermute | solution.py:68
  35.8 3.6 %fusion.20 = bf16[9,256,256]{1,2,0:T(8,128)(2,1)} fusion(bf16[9,256,256]{2,0,1:T(8,128)(2,1)} %fusion.6, bf16[1,1,4,256,256]{4,3,2,1,0:T(8,128)(2,1)} %param.15, s32[]{:T(128)S(6)} %select_n.78, bf16[1,1,4,256,256]{4,3,2,1,0:T(8,128)(2,1)} %param.14), kind=kOutput, calls=%fused_computation.56 | convolution fusion | flops 605159424 | bytes 3539968 | tf_op jit(solution)/shard_map/bd,vbc->vdc/dot_general | solution.py:29
  41.2 5.2 %collective-permute-start.4 = (bf16[9,256,256]{1,2,0:T(8,128)(2,1)}, bf16[9,256,256]{1,2,0:T(8,128)(2,1)}, u32[]{:S(2)}, u32[]{:S(2)}) collective-permute-start(bf16[9,256,256]{1,2,0:T(8,128)(2,1)} %fusion.20), channel_id=1, source_target_pairs={{0,2},{2,4},{4,6},{1,3},{3,5},{5,7},{8,10},{10,12},{12,14},{9,11},... | collective-permute-start | bytes 3538952 | tf_op jit(solution)/shard_map/ppermute | solution.py:64
  49.7 3.7 %fusion.22 = bf16[9,256,256]{1,2,0:T(8,128)(2,1)} fusion(bf16[9,256,256]{2,0,1:T(8,128)(2,1)} %fusion, bf16[1,1,4,256,256]{4,3,2,1,0:T(8,128)(2,1)} %param.15, s32[]{:T(128)S(6)} %select_n.82, bf16[1,1,4,256,256]{4,3,2,1,0:T(8,128)(2,1)} %param.14), kind=kOutput, calls=%fused_computation.58 | convolution fusion | flops 605159424 | bytes 3539968 | tf_op jit(solution)/shard_map/bd,vbc->vdc/dot_general | solution.py:29
  60.6 20.2 %collective-permute-done.4 = bf16[9,256,256]{1,2,0:T(8,128)(2,1)} collective-permute-done((bf16[9,256,256]{1,2,0:T(8,128)(2,1)}, bf16[9,256,256]{1,2,0:T(8,128)(2,1)}, u32[]{:S(2)}, u32[]{:S(2)}) %collective-permute-start.4) | collective-permute-done | bytes 1179680 | tf_op jit(solution)/shard_map/ppermute | solution.py:64
  80.8 3.6 %fusion.13 = (bf16[9,256,256]{1,2,0:T(8,128)(2,1)S(1)}, f32[9,256,256]{1,2,0:T(8,128)S(1)}) fusion(bf16[9,256,256]{1,2,0:T(8,128)(2,1)} %collective-permute-done.4, bf16[9,256,256]{1,2,0:T(8,128)(2,1)} %collective-permute-done.5, bf16[9,256,256]{1,2,0:T(8,128)(2,1)S(1)} %copy-done.4, f32[]{:T(128)S(6)} %sub.14, f32[]{:T(128)S(6)} %sub.13, ...), kind=kLoop, calls=%fused_computation.23 | loop fusion | flops 9437184 | bytes 10616848 | tf_op jit(solution)/shard_map/convert_element_type | solution.py:77
  84.4 3.8 %collective-permute-start.8 = (bf16[4,256,256]{1,2,0:T(8,128)(2,1)S(1)}, bf16[4,256,256]{1,2,0:T(8,128)(2,1)S(1)}, u32[]{:S(2)}, u32[]{:S(2)}) collective-permute-start(bf16[4,256,256]{1,2,0:T(8,128)(2,1)S(1)} %slice.73), channel_id=1, source_target_pairs={{0,2},{2,6},{6,4},{4,0},{1,3},{3,7},{7,5},{5,1},{8,10},{10,14},{14... | collective-permute-start | bytes 1572872 | tf_op jit(solution)/shard_map/ppermute | solution.py:89
  88.2 11.7 %collective-permute-done.8 = bf16[4,256,256]{1,2,0:T(8,128)(2,1)S(1)} collective-permute-done((bf16[4,256,256]{1,2,0:T(8,128)(2,1)S(1)}, bf16[4,256,256]{1,2,0:T(8,128)(2,1)S(1)}, u32[]{:S(2)}, u32[]{:S(2)}) %collective-permute-start.8) | collective-permute-done | bytes 524320 | tf_op jit(solution)/shard_map/ppermute | solution.py:89
  103.0 14.2 %collective-permute-done.10 = bf16[5,256,256]{1,2,0:T(8,128)(2,1)S(1)} collective-permute-done((bf16[5,256,256]{1,2,0:T(8,128)(2,1)S(1)}, bf16[5,256,256]{1,2,0:T(8,128)(2,1)S(1)}, u32[]{:S(2)}, u32[]{:S(2)}) %collective-permute-start.10) | collective-permute-done | bytes 655392 | tf_op jit(solution)/shard_map/ppermute | solution.py:89
  121.3 3.7 %copy.30 = bf16[18,256,256]{2,0,1:T(8,128)(2,1)S(1)} copy(bf16[18,256,256]{1,2,0:T(8,128)(2,1)} %pad_maximum_fusion.1) | data formatting | bytes 4718592 | tf_op jit(solution)/shard_map/concatenate | solution.py:45
  127.1 3.6 %fusion.24 = bf16[9,256,256]{1,2,0:T(8,128)(2,1)} fusion(bf16[9,256,256]{2,0,1:T(8,128)(2,1)} %fusion.89, bf16[4,256,256]{2,1,0:T(8,128)(2,1)} %copy-done.5, s32[]{:T(128)S(6)} %select_n.81, bf16[4,256,256]{2,1,0:T(8,128)(2,1)} %collective-permute-done), kind=kOutput, calls=%fused_computation.60 | convolution fusion | flops 605159424 | bytes 3539968 | tf_op jit(solution)/shard_map/bd,vbc->vdc/dot_general | solution.py:29
  137.6 3.6 %fusion.23 = bf16[9,256,256]{1,2,0:T(8,128)(2,1)} fusion(bf16[9,256,256]{2,0,1:T(8,128)(2,1)} %fusion.91, bf16[4,256,256]{2,1,0:T(8,128)(2,1)} %copy-done.5, s32[]{:T(128)S(6)} %select_n.78, bf16[4,256,256]{2,1,0:T(8,128)(2,1)} %collective-permute-done), kind=kOutput, calls=%fused_computation.59 | convolution fusion | flops 605159424 | bytes 3539968 | tf_op jit(solution)/shard_map/bd,vbc->vdc/dot_general | solution.py:29
  142.9 5.2 %collective-permute-start.12 = (bf16[9,256,256]{1,2,0:T(8,128)(2,1)}, bf16[9,256,256]{1,2,0:T(8,128)(2,1)}, u32[]{:S(2)}, u32[]{:S(2)}) collective-permute-start(bf16[9,256,256]{1,2,0:T(8,128)(2,1)} %fusion.23), channel_id=1, source_target_pairs={{0,2},{2,4},{4,6},{1,3},{3,5},{5,7},{8,10},{10,12},{12,14},{9,11},... | collective-permute-start | bytes 3538952 | tf_op jit(solution)/shard_map/ppermute | solution.py:64
  150.2 3.7 %fusion.25 = bf16[9,256,256]{1,2,0:T(8,128)(2,1)} fusion(bf16[9,256,256]{2,0,1:T(8,128)(2,1)} %fusion.87, bf16[4,256,256]{2,1,0:T(8,128)(2,1)} %copy-done.5, s32[]{:T(128)S(6)} %select_n.82, bf16[4,256,256]{2,1,0:T(8,128)(2,1)} %collective-permute-done), kind=kOutput, calls=%fused_computation.61 | convolution fusion | flops 605159424 | bytes 3539968 | tf_op jit(solution)/shard_map/bd,vbc->vdc/dot_general | solution.py:29
  156.0 3.8 %collective-permute-done.14 = bf16[9,256,256]{1,2,0:T(8,128)(2,1)} collective-permute-done((bf16[9,256,256]{1,2,0:T(8,128)(2,1)}, bf16[9,256,256]{1,2,0:T(8,128)(2,1)}, u32[]{:S(2)}, u32[]{:S(2)}) %collective-permute-start.14) | collective-permute-done | bytes 1179680 | tf_op jit(solution)/shard_map/ppermute | solution.py:68
  159.8 4.3 %collective-permute-done.13 = bf16[9,256,256]{1,2,0:T(8,128)(2,1)} collective-permute-done((bf16[9,256,256]{1,2,0:T(8,128)(2,1)}, bf16[9,256,256]{1,2,0:T(8,128)(2,1)}, u32[]{:S(2)}, u32[]{:S(2)}) %collective-permute-start.13) | collective-permute-done | bytes 1179680 | tf_op jit(solution)/shard_map/ppermute | solution.py:67
  164.1 20.2 %collective-permute-done.12 = bf16[9,256,256]{1,2,0:T(8,128)(2,1)} collective-permute-done((bf16[9,256,256]{1,2,0:T(8,128)(2,1)}, bf16[9,256,256]{1,2,0:T(8,128)(2,1)}, u32[]{:S(2)}, u32[]{:S(2)}) %collective-permute-start.12) | collective-permute-done | bytes 1179680 | tf_op jit(solution)/shard_map/ppermute | solution.py:64
  187.5 3.7 %collective-permute-start.16 = (bf16[3,256,256]{1,2,0:T(8,128)(2,1)S(1)}, bf16[3,256,256]{1,2,0:T(8,128)(2,1)S(1)}, u32[]{:S(2)}, u32[]{:S(2)}) collective-permute-start(bf16[3,256,256]{1,2,0:T(8,128)(2,1)S(1)} %slice.76), channel_id=1, source_target_pairs={{0,2},{2,6},{6,4},{4,0},{1,3},{3,7},{7,5},{5,1},{8,10},{10,14},{14... | collective-permute-start | bytes 1179656 | tf_op jit(solution)/shard_map/ppermute | solution.py:89
  191.3 4.4 %fusion.16 = f32[9,256,256]{1,2,0:T(8,128)S(1)} fusion(bf16[9,256,256]{1,2,0:T(8,128)(2,1)} %collective-permute-done.12, bf16[9,256,256]{1,2,0:T(8,128)(2,1)} %collective-permute-done.13, bf16[9,256,256]{1,2,0:T(8,128)(2,1)} %collective-permute-done.14, bf16[9,256,256]{1,2,0:T(8,128)(2,1)} %collective-permute-done.15, f32[]{:T(128)S(6)} %select_n.83, ...), kind=kOutput, calls=%fused_computation.26 | convolution fusion | flops 612237312 | bytes 9437192 | tf_op jit(solution)/shard_map/bd,vbc->vdc/dot_general | solution.py:29
  195.7 4.5 %collective-permute-done.16 = bf16[3,256,256]{1,2,0:T(8,128)(2,1)S(1)} collective-permute-done((bf16[3,256,256]{1,2,0:T(8,128)(2,1)S(1)}, bf16[3,256,256]{1,2,0:T(8,128)(2,1)S(1)}, u32[]{:S(2)}, u32[]{:S(2)}) %collective-permute-start.16) | collective-permute-done | bytes 393248 | tf_op jit(solution)/shard_map/ppermute | solution.py:89
  203.3 8.5 %collective-permute-done.18 = bf16[3,256,256]{1,2,0:T(8,128)(2,1)S(1)} collective-permute-done((bf16[3,256,256]{1,2,0:T(8,128)(2,1)S(1)}, bf16[3,256,256]{1,2,0:T(8,128)(2,1)S(1)}, u32[]{:S(2)}, u32[]{:S(2)}) %collective-permute-start.18) | collective-permute-done | bytes 393248 | tf_op jit(solution)/shard_map/ppermute | solution.py:89
  214.1 8.3 %collective-permute-done.20 = bf16[3,256,256]{1,2,0:T(8,128)(2,1)S(1)} collective-permute-done((bf16[3,256,256]{1,2,0:T(8,128)(2,1)S(1)}, bf16[3,256,256]{1,2,0:T(8,128)(2,1)S(1)}, u32[]{:S(2)}, u32[]{:S(2)}) %collective-permute-start.20) | collective-permute-done | bytes 393248 | tf_op jit(solution)/shard_map/ppermute | solution.py:89
  224.2 7.1 %collective-permute-done.21 = bf16[1,3,1,256,256]{3,4,1,2,0:T(8,128)(2,1)S(1)} collective-permute-done((bf16[1,3,1,256,256]{3,4,1,2,0:T(8,128)(2,1)S(1)}, bf16[1,3,1,256,256]{3,4,1,2,0:T(8,128)(2,1)S(1)}, u32[]{:S(2)}, u32[]{:S(2)}) %collective-permute-start.21) | collective-permute-done | bytes 393248 | tf_op jit(solution)/shard_map/ppermute | solution.py:19
  (90 shorter events, 66.7 us)
Async XLA Ops:
  2.4 14.4 %collective-permute-start.3 = (bf16[9,256,256]{2,1,0:T(8,128)(2,1)S(1)}, bf16[9,256,256]{2,1,0:T(8,128)(2,1)}, u32[]{:S(2)}, u32[]{:S(2)}) collective-permute-start(bf16[9,256,256]{2,1,0:T(8,128)(2,1)S(1)} %bitcast_select_fusion), channel_id=1, source_target_pairs={{0,1},{1,0},{2,3},{3,2},{4,5},{5,4},{6,7},{7,6},{8,9},{9,8},{10,11... | collective-permute-start | bytes 3538952 | tf_op jit(solution)/shard_map/ppermute | solution.py:19
  3.0 36.4 %collective-permute-start.2 = (bf16[18,9,4]{1,2,0:T(4,128)(2,1)S(1)}, bf16[18,9,4]{1,2,0:T(4,128)(2,1)S(1)}, u32[]{:S(2)}, u32[]{:S(2)}) collective-permute-start(bf16[18,9,4]{1,2,0:T(4,128)(2,1)S(1)} %bitcast.124), channel_id=1, source_target_pairs={{0,24},{8,0},{16,8},{24,16},{1,25},{9,1},{17,9},{25,17},{2,26},{10... | collective-permute-start | bytes 3896 | tf_op jit(solution)/shard_map/ppermute | solution.py:19
  6.5 32.9 %collective-permute-start.1 = (bf16[4,256,256]{2,1,0:T(8,128)(2,1)}, bf16[4,256,256]{2,1,0:T(8,128)(2,1)S(1)}, u32[]{:S(2)}, u32[]{:S(2)}) collective-permute-start(bf16[4,256,256]{2,1,0:T(8,128)(2,1)} %bitcast.1), channel_id=1, source_target_pairs={{0,24},{8,0},{16,8},{24,16},{1,25},{9,1},{17,9},{25,17},{2,26},{10... | collective-permute-start | bytes 1572872 | tf_op jit(solution)/shard_map/ppermute | solution.py:19
  7.1 32.4 %collective-permute-start = (bf16[4,256,256]{2,1,0:T(8,128)(2,1)}, bf16[4,256,256]{2,1,0:T(8,128)(2,1)}, u32[]{:S(2)}, u32[]{:S(2)}) collective-permute-start(bf16[4,256,256]{2,1,0:T(8,128)(2,1)} %bitcast), channel_id=1, source_target_pairs={{0,24},{8,0},{16,8},{24,16},{1,25},{9,1},{17,9},{25,17},{2,26},{10... | collective-permute-start | bytes 1572872 | tf_op jit(solution)/shard_map/ppermute | solution.py:19
  25.6 33.8 %collective-permute-start.6 = (bf16[9,256,256]{1,2,0:T(8,128)(2,1)}, bf16[9,256,256]{1,2,0:T(8,128)(2,1)}, u32[]{:S(2)}, u32[]{:S(2)}) collective-permute-start(bf16[9,256,256]{1,2,0:T(8,128)(2,1)} %fusion.21), channel_id=1, source_target_pairs={{0,4},{1,5},{8,12},{9,13},{16,20},{17,21},{24,28},{25,29}} | collective-permute-start | bytes 3538952 | tf_op jit(solution)/shard_map/ppermute | solution.py:68
  31.2 29.4 %collective-permute-start.5 = (bf16[9,256,256]{1,2,0:T(8,128)(2,1)}, bf16[9,256,256]{1,2,0:T(8,128)(2,1)}, u32[]{:S(2)}, u32[]{:S(2)}) collective-permute-start(bf16[9,256,256]{1,2,0:T(8,128)(2,1)} %fusion.21), channel_id=1, source_target_pairs={{6,4},{4,2},{2,0},{7,5},{5,3},{3,1},{14,12},{12,10},{10,8},{15,13}... | collective-permute-start | bytes 3538952 | tf_op jit(solution)/shard_map/ppermute | solution.py:67
  39.5 21.2 %collective-permute-start.7 = (bf16[9,256,256]{1,2,0:T(8,128)(2,1)}, bf16[9,256,256]{1,2,0:T(8,128)(2,1)}, u32[]{:S(2)}, u32[]{:S(2)}) collective-permute-start(bf16[9,256,256]{1,2,0:T(8,128)(2,1)} %fusion.20), channel_id=1, source_target_pairs={{6,2},{7,3},{14,10},{15,11},{22,18},{23,19},{30,26},{31,27}} | collective-permute-start | bytes 3538952 | tf_op jit(solution)/shard_map/ppermute | solution.py:65
  41.2 39.6 %collective-permute-start.4 = (bf16[9,256,256]{1,2,0:T(8,128)(2,1)}, bf16[9,256,256]{1,2,0:T(8,128)(2,1)}, u32[]{:S(2)}, u32[]{:S(2)}) collective-permute-start(bf16[9,256,256]{1,2,0:T(8,128)(2,1)} %fusion.20), channel_id=1, source_target_pairs={{0,2},{2,4},{4,6},{1,3},{3,5},{5,7},{8,10},{10,12},{12,14},{9,11},... | collective-permute-start | bytes 3538952 | tf_op jit(solution)/shard_map/ppermute | solution.py:64
  56.8 24.0 %copy-start.4 = (bf16[9,256,256]{1,2,0:T(8,128)(2,1)S(1)}, bf16[9,256,256]{1,2,0:T(8,128)(2,1)}, u32[]{:S(2)}) copy-start(bf16[9,256,256]{1,2,0:T(8,128)(2,1)} %fusion.22) | copy-start | bytes 3538948
  84.4 15.5 %collective-permute-start.8 = (bf16[4,256,256]{1,2,0:T(8,128)(2,1)S(1)}, bf16[4,256,256]{1,2,0:T(8,128)(2,1)S(1)}, u32[]{:S(2)}, u32[]{:S(2)}) collective-permute-start(bf16[4,256,256]{1,2,0:T(8,128)(2,1)S(1)} %slice.73), channel_id=1, source_target_pairs={{0,2},{2,6},{6,4},{4,0},{1,3},{3,7},{7,5},{5,1},{8,10},{10,14},{14... | collective-permute-start | bytes 1572872 | tf_op jit(solution)/shard_map/ppermute | solution.py:89
  100.2 17.1 %collective-permute-start.10 = (bf16[5,256,256]{1,2,0:T(8,128)(2,1)S(1)}, bf16[5,256,256]{1,2,0:T(8,128)(2,1)S(1)}, u32[]{:S(2)}, u32[]{:S(2)}) collective-permute-start(bf16[5,256,256]{1,2,0:T(8,128)(2,1)S(1)} %slice.56), channel_id=1, source_target_pairs={{0,2},{2,6},{6,4},{4,0},{1,3},{3,7},{7,5},{5,1},{8,10},{10,14},{14... | collective-permute-start | bytes 1966088 | tf_op jit(solution)/shard_map/ppermute | solution.py:89
  101.1 1.9 collective-permute-start.9
  117.4 2.2 collective-permute-start.11
  130.7 29.1 %collective-permute-start.14 = (bf16[9,256,256]{1,2,0:T(8,128)(2,1)}, bf16[9,256,256]{1,2,0:T(8,128)(2,1)}, u32[]{:S(2)}, u32[]{:S(2)}) collective-permute-start(bf16[9,256,256]{1,2,0:T(8,128)(2,1)} %fusion.24), channel_id=1, source_target_pairs={{0,4},{1,5},{8,12},{9,13},{16,20},{17,21},{24,28},{25,29}} | collective-permute-start | bytes 3538952 | tf_op jit(solution)/shard_map/ppermute | solution.py:68
  134.2 29.9 %collective-permute-start.13 = (bf16[9,256,256]{1,2,0:T(8,128)(2,1)}, bf16[9,256,256]{1,2,0:T(8,128)(2,1)}, u32[]{:S(2)}, u32[]{:S(2)}) collective-permute-start(bf16[9,256,256]{1,2,0:T(8,128)(2,1)} %fusion.24), channel_id=1, source_target_pairs={{6,4},{4,2},{2,0},{7,5},{5,3},{3,1},{14,12},{12,10},{10,8},{15,13}... | collective-permute-start | bytes 3538952 | tf_op jit(solution)/shard_map/ppermute | solution.py:67
  141.2 22.9 %collective-permute-start.15 = (bf16[9,256,256]{1,2,0:T(8,128)(2,1)}, bf16[9,256,256]{1,2,0:T(8,128)(2,1)}, u32[]{:S(2)}, u32[]{:S(2)}) collective-permute-start(bf16[9,256,256]{1,2,0:T(8,128)(2,1)} %fusion.23), channel_id=1, source_target_pairs={{6,2},{7,3},{14,10},{15,11},{22,18},{23,19},{30,26},{31,27}} | collective-permute-start | bytes 3538952 | tf_op jit(solution)/shard_map/ppermute | solution.py:65
  142.9 41.4 %collective-permute-start.12 = (bf16[9,256,256]{1,2,0:T(8,128)(2,1)}, bf16[9,256,256]{1,2,0:T(8,128)(2,1)}, u32[]{:S(2)}, u32[]{:S(2)}) collective-permute-start(bf16[9,256,256]{1,2,0:T(8,128)(2,1)} %fusion.23), channel_id=1, source_target_pairs={{0,2},{2,4},{4,6},{1,3},{3,5},{5,7},{8,10},{10,12},{12,14},{9,11},... | collective-permute-start | bytes 3538952 | tf_op jit(solution)/shard_map/ppermute | solution.py:64
  153.9 30.4 %copy-start.3 = (bf16[9,256,256]{1,2,0:T(8,128)(2,1)S(1)}, bf16[9,256,256]{1,2,0:T(8,128)(2,1)}, u32[]{:S(2)}) copy-start(bf16[9,256,256]{1,2,0:T(8,128)(2,1)} %fusion.25) | copy-start | bytes 3538948
  187.5 12.6 %collective-permute-start.16 = (bf16[3,256,256]{1,2,0:T(8,128)(2,1)S(1)}, bf16[3,256,256]{1,2,0:T(8,128)(2,1)S(1)}, u32[]{:S(2)}, u32[]{:S(2)}) collective-permute-start(bf16[3,256,256]{1,2,0:T(8,128)(2,1)S(1)} %slice.76), channel_id=1, source_target_pairs={{0,2},{2,6},{6,4},{4,0},{1,3},{3,7},{7,5},{5,1},{8,10},{10,14},{14... | collective-permute-start | bytes 1179656 | tf_op jit(solution)/shard_map/ppermute | solution.py:89
  200.3 11.5 %collective-permute-start.18 = (bf16[3,256,256]{1,2,0:T(8,128)(2,1)S(1)}, bf16[3,256,256]{1,2,0:T(8,128)(2,1)S(1)}, u32[]{:S(2)}, u32[]{:S(2)}) collective-permute-start(bf16[3,256,256]{1,2,0:T(8,128)(2,1)S(1)} %slice.62), channel_id=1, source_target_pairs={{0,2},{2,6},{6,4},{4,0},{1,3},{3,7},{7,5},{5,1},{8,10},{10,14},{14... | collective-permute-start | bytes 1179656 | tf_op jit(solution)/shard_map/ppermute | solution.py:89
  201.8 10.0 %collective-permute-start.17 = (bf16[1,3,1,256,256]{3,4,1,2,0:T(8,128)(2,1)S(1)}, bf16[1,3,1,256,256]{3,4,1,2,0:T(8,128)(2,1)S(1)}, u32[]{:S(2)}, u32[]{:S(2)}) collective-permute-start(bf16[1,3,1,256,256]{3,4,1,2,0:T(8,128)(2,1)S(1)} %bitcast.127), channel_id=1, source_target_pairs={{0,16},{8,24},{16,0},{24,8},{1,17},{9,25},{17,1},{25,9},{2,18},{10... | collective-permute-start | bytes 1179656 | tf_op jit(solution)/shard_map/ppermute | solution.py:19
  211.9 10.5 %collective-permute-start.20 = (bf16[3,256,256]{1,2,0:T(8,128)(2,1)S(1)}, bf16[3,256,256]{1,2,0:T(8,128)(2,1)S(1)}, u32[]{:S(2)}, u32[]{:S(2)}) collective-permute-start(bf16[3,256,256]{1,2,0:T(8,128)(2,1)S(1)} %slice.64), channel_id=1, source_target_pairs={{0,2},{2,6},{6,4},{4,0},{1,3},{3,7},{7,5},{5,1},{8,10},{10,14},{14... | collective-permute-start | bytes 1179656 | tf_op jit(solution)/shard_map/ppermute | solution.py:89
  212.6 9.9 %collective-permute-start.19 = (bf16[1,3,1,256,256]{3,4,1,2,0:T(8,128)(2,1)S(1)}, bf16[1,3,1,256,256]{3,4,1,2,0:T(8,128)(2,1)S(1)}, u32[]{:S(2)}, u32[]{:S(2)}) collective-permute-start(bf16[1,3,1,256,256]{3,4,1,2,0:T(8,128)(2,1)S(1)} %bitcast.126), channel_id=1, source_target_pairs={{0,16},{8,24},{16,0},{24,8},{1,17},{9,25},{17,1},{25,9},{2,18},{10... | collective-permute-start | bytes 1179656 | tf_op jit(solution)/shard_map/ppermute | solution.py:19
  222.6 8.7 %collective-permute-start.21 = (bf16[1,3,1,256,256]{3,4,1,2,0:T(8,128)(2,1)S(1)}, bf16[1,3,1,256,256]{3,4,1,2,0:T(8,128)(2,1)S(1)}, u32[]{:S(2)}, u32[]{:S(2)}) collective-permute-start(bf16[1,3,1,256,256]{3,4,1,2,0:T(8,128)(2,1)S(1)} %fusion.36), channel_id=1, source_target_pairs={{0,16},{8,24},{16,0},{24,8},{1,17},{9,25},{17,1},{25,9},{2,18},{10... | collective-permute-start | bytes 1179656 | tf_op jit(solution)/shard_map/ppermute | solution.py:19
  (8 other events, 64.5 us)

commit v13 on v12

--- a/solution.py
+++ b/solution.py
@@ -131,7 +131,7 @@
         if line:
             parts, tensors[step + 1 :] = advance_line(
                 pieces, ket, bra, mpo, live_mask, sector, tensors[step + 1 :],
-                3 if last else 2, onward if last else chan_copies,
+                3 if last else 3, onward if last else chan_copies,
             )
         else:
             parts = [advance_direct(pieces, ket, bra, mpo, live_mask)]

time: 234 us -> 241 us (1.030)
  local copies, waits for them, and re-layouts: 9.81 us -> 16.5 us
    unnamed x21 -> x23, local copies, waits for them, and re-layouts: 1.14 us -> 6.22 us
    ppermute x9 -> x10, waiting for transfers between devices: 10.4 us -> 7.22 us  [shifted(): return lax.ppermute(value, axis, pairs)]
    ppermute x5 -> x6, waiting for transfers between devices: 47.2 us -> 49.2 us  [advance_line(): got_last = lax.ppermute(send[low:high], 'sector', LAST)]
    ppermute x5 -> x6, starting transfers between devices: 10.6 us -> 11.6 us  [advance_line(): got_last = lax.ppermute(send[low:high], 'sector', LAST)]
    ppermute x9 -> x10, starting transfers between devices: 10.7 us -> 10.6 us  [shifted(): return lax.ppermute(value, axis, pairs)]
  transfers between devices with their start and end apart: 22 -> 24, of which waited for: 13 -> 12; matrix products, arithmetic and copies ran while one was open for 22% -> 23% of each run, Pallas kernels for 0% -> 0%
where the time goes in v13:
time: 241 us; the launch traced here: 240 us
  waiting for transfers between devices  105 us (44%)
  matrix products  51.8 us (21%)
  starting transfers between devices  46.8 us (19%)
  local copies, waits for them, and re-layouts  16.5 us (7%)
  other arithmetic  12.6 us (5%)
  between operations  6.85 us (3%)
    ppermute x6, waiting for transfers between devices, advance_line(): got_last = lax.ppermute(send[low:high], 'sector', LAST)  49.2 us
    ppermute x2, waiting for transfers between devices, advance_line(): got_right = lax.ppermute(slot_a, 'sector', RIGHT)  40.3 us
    dot_general x8, matrix products, term(): jnp.einsum('bd,vbc->vdc', bra_p, rotated, preferred_element_type=jnp.floa...  29.9 us
    dot_general x8, matrix products, term(): jnp.einsum('wv,wba->vba', mpo_p, gathered, preferred_element_type=jnp.flo...  22 us
    ppermute x6, starting transfers between devices, advance_line(): got_last = lax.ppermute(send[low:high], 'sector', LAST)  11.6 us
    ppermute x10, starting transfers between devices, shifted(): return lax.ppermute(value, axis, pairs)  10.6 us
    ppermute x2, starting transfers between devices, advance_line(): got_right = lax.ppermute(slot_a, 'sector', RIGHT)  10.6 us
    ppermute x2, starting transfers between devices, advance_line(): middle_right = lax.ppermute(slot_b, 'sector', ((0, 2),))  8.03 us
  transfers between devices with their start and end apart: 24, of which 12 were waited for; matrix products, arithmetic and copies ran while one was open for 23% of the time, Pallas kernels for 0%

profile of v13, /device:TPU:0, one launch (start us, length us, event | category | flops | bytes accessed | tf_op | source)
XLA Modules:
  0.0 239.9 jit_solution(1828611656666182394)
XLA Ops:
  22.4 3.6 %fusion.21 = bf16[9,256,256]{1,2,0:T(8,128)(2,1)} fusion(bf16[9,256,256]{2,0,1:T(8,128)(2,1)} %fusion.2, bf16[1,1,4,256,256]{4,3,2,1,0:T(8,128)(2,1)} %param.15, s32[]{:T(128)S(6)} %select_n.81, bf16[1,1,4,256,256]{4,3,2,1,0:T(8,128)(2,1)} %param.14), kind=kOutput, calls=%fused_computation.56 | convolution fusion | flops 605159424 | bytes 3539968 | tf_op jit(solution)/shard_map/bd,vbc->vdc/dot_general | solution.py:29
  26.0 5.5 %collective-permute-start.6 = (bf16[9,256,256]{1,2,0:T(8,128)(2,1)}, bf16[9,256,256]{1,2,0:T(8,128)(2,1)}, u32[]{:S(2)}, u32[]{:S(2)}) collective-permute-start(bf16[9,256,256]{1,2,0:T(8,128)(2,1)} %fusion.21), channel_id=1, source_target_pairs={{0,4},{1,5},{8,12},{9,13},{16,20},{17,21},{24,28},{25,29}} | collective-permute-start | bytes 3538952 | tf_op jit(solution)/shard_map/ppermute | solution.py:68
  41.6 5.2 %collective-permute-start.4 = (bf16[9,256,256]{1,2,0:T(8,128)(2,1)}, bf16[9,256,256]{1,2,0:T(8,128)(2,1)}, u32[]{:S(2)}, u32[]{:S(2)}) collective-permute-start(bf16[9,256,256]{1,2,0:T(8,128)(2,1)} %fusion.20), channel_id=1, source_target_pairs={{0,2},{2,4},{4,6},{1,3},{3,5},{5,7},{8,10},{10,12},{12,14},{9,11},... | collective-permute-start | bytes 3538952 | tf_op jit(solution)/shard_map/ppermute | solution.py:64
  50.1 3.7 %fusion.22 = bf16[9,256,256]{1,2,0:T(8,128)(2,1)} fusion(bf16[9,256,256]{2,0,1:T(8,128)(2,1)} %fusion, bf16[1,1,4,256,256]{4,3,2,1,0:T(8,128)(2,1)} %param.15, s32[]{:T(128)S(6)} %select_n.82, bf16[1,1,4,256,256]{4,3,2,1,0:T(8,128)(2,1)} %param.14), kind=kOutput, calls=%fused_computation.57 | convolution fusion | flops 605159424 | bytes 3539968 | tf_op jit(solution)/shard_map/bd,vbc->vdc/dot_general | solution.py:29
  57.2 3.6 %convolution_convert_fusion.12 = bf16[9,256,256]{2,1,0:T(8,128)(2,1)} fusion(bf16[9,256,256]{2,0,1:T(8,128)(2,1)} %fusion.4, bf16[1,1,4,256,256]{4,3,2,1,0:T(8,128)(2,1)} %param.15, bf16[1,1,4,256,256]{4,3,2,1,0:T(8,128)(2,1)} %param.14), kind=kOutput, calls=%fused_computation.51 | convolution fusion | flops 605159424 | bytes 3538944 | tf_op jit(solution)/shard_map/bd,vbc->vdc/dot_general | solution.py:29
  61.0 20.2 %collective-permute-done.4 = bf16[9,256,256]{1,2,0:T(8,128)(2,1)} collective-permute-done((bf16[9,256,256]{1,2,0:T(8,128)(2,1)}, bf16[9,256,256]{1,2,0:T(8,128)(2,1)}, u32[]{:S(2)}, u32[]{:S(2)}) %collective-permute-start.4) | collective-permute-done | bytes 1179680 | tf_op jit(solution)/shard_map/ppermute | solution.py:64
  81.2 4.3 %fusion.13 = (bf16[9,256,256]{1,2,0:T(8,128)(2,1)S(1)}, f32[9,256,256]{1,2,0:T(8,128)S(1)}) fusion(bf16[9,256,256]{1,2,0:T(8,128)(2,1)} %collective-permute-done.4, bf16[9,256,256]{1,2,0:T(8,128)(2,1)} %collective-permute-done.5, bf16[9,256,256]{1,2,0:T(8,128)(2,1)} %fusion.22, f32[]{:T(128)S(6)} %sub.14, f32[]{:T(128)S(6)} %sub.13, ...), kind=kLoop, calls=%fused_computation.23 | loop fusion | flops 9437184 | bytes 10616848 | tf_op jit(solution)/shard_map/convert_element_type | solution.py:77
  85.5 3.8 %collective-permute-start.8 = (bf16[3,256,256]{1,2,0:T(8,128)(2,1)S(1)}, bf16[3,256,256]{1,2,0:T(8,128)(2,1)S(1)}, u32[]{:S(2)}, u32[]{:S(2)}) collective-permute-start(bf16[3,256,256]{1,2,0:T(8,128)(2,1)S(1)} %slice.81), channel_id=1, source_target_pairs={{0,2},{2,6},{6,4},{4,0},{1,3},{3,7},{7,5},{5,1},{8,10},{10,14},{14... | collective-permute-start | bytes 1179656 | tf_op jit(solution)/shard_map/ppermute | solution.py:89
  89.3 8.9 %collective-permute-done.8 = bf16[3,256,256]{1,2,0:T(8,128)(2,1)S(1)} collective-permute-done((bf16[3,256,256]{1,2,0:T(8,128)(2,1)S(1)}, bf16[3,256,256]{1,2,0:T(8,128)(2,1)S(1)}, u32[]{:S(2)}, u32[]{:S(2)}) %collective-permute-start.8) | collective-permute-done | bytes 393248 | tf_op jit(solution)/shard_map/ppermute | solution.py:89
  99.3 10.5 %collective-permute-done.10 = bf16[3,256,256]{1,2,0:T(8,128)(2,1)S(1)} collective-permute-done((bf16[3,256,256]{1,2,0:T(8,128)(2,1)S(1)}, bf16[3,256,256]{1,2,0:T(8,128)(2,1)S(1)}, u32[]{:S(2)}, u32[]{:S(2)}) %collective-permute-start.10) | collective-permute-done | bytes 393248 | tf_op jit(solution)/shard_map/ppermute | solution.py:89
  112.2 9.3 %collective-permute-done.12 = bf16[3,256,256]{1,2,0:T(8,128)(2,1)} collective-permute-done((bf16[3,256,256]{1,2,0:T(8,128)(2,1)}, bf16[3,256,256]{1,2,0:T(8,128)(2,1)}, u32[]{:S(2)}, u32[]{:S(2)}) %collective-permute-start.12) | collective-permute-done | bytes 393248 | tf_op jit(solution)/shard_map/ppermute | solution.py:89
  128.5 3.7 %copy.30 = bf16[18,256,256]{2,0,1:T(8,128)(2,1)S(1)} copy(bf16[18,256,256]{1,2,0:T(8,128)(2,1)} %constant_dynamic-update-slice_fusion) | data formatting | bytes 4718592 | tf_op jit(solution)/shard_map/concatenate | solution.py:45
  134.3 3.6 %fusion.24 = bf16[9,256,256]{1,2,0:T(8,128)(2,1)} fusion(bf16[9,256,256]{2,0,1:T(8,128)(2,1)} %fusion.91, bf16[4,256,256]{2,1,0:T(8,128)(2,1)} %copy-done.4, s32[]{:T(128)S(6)} %select_n.81, bf16[4,256,256]{2,1,0:T(8,128)(2,1)} %collective-permute-done), kind=kOutput, calls=%fused_computation.59 | convolution fusion | flops 605159424 | bytes 3539968 | tf_op jit(solution)/shard_map/bd,vbc->vdc/dot_general | solution.py:29
  149.2 5.4 %collective-permute-start.14 = (bf16[9,256,256]{1,2,0:T(8,128)(2,1)}, bf16[9,256,256]{1,2,0:T(8,128)(2,1)}, u32[]{:S(2)}, u32[]{:S(2)}) collective-permute-start(bf16[9,256,256]{1,2,0:T(8,128)(2,1)} %fusion.23), channel_id=1, source_target_pairs={{0,2},{2,4},{4,6},{1,3},{3,5},{5,7},{8,10},{10,12},{12,14},{9,11},... | collective-permute-start | bytes 3538952 | tf_op jit(solution)/shard_map/ppermute | solution.py:64
  156.7 3.7 %fusion.25 = bf16[9,256,256]{1,2,0:T(8,128)(2,1)} fusion(bf16[9,256,256]{2,0,1:T(8,128)(2,1)} %fusion.89, bf16[4,256,256]{2,1,0:T(8,128)(2,1)} %copy-done.4, s32[]{:T(128)S(6)} %select_n.82, bf16[4,256,256]{2,1,0:T(8,128)(2,1)} %collective-permute-done), kind=kOutput, calls=%fused_computation.60 | convolution fusion | flops 605159424 | bytes 3539968 | tf_op jit(solution)/shard_map/bd,vbc->vdc/dot_general | solution.py:29
  162.5 3.6 %collective-permute-done.16 = bf16[9,256,256]{1,2,0:T(8,128)(2,1)} collective-permute-done((bf16[9,256,256]{1,2,0:T(8,128)(2,1)}, bf16[9,256,256]{1,2,0:T(8,128)(2,1)}, u32[]{:S(2)}, u32[]{:S(2)}) %collective-permute-start.16) | collective-permute-done | bytes 1179680 | tf_op jit(solution)/shard_map/ppermute | solution.py:68
  166.1 4.8 %collective-permute-done.15 = bf16[9,256,256]{1,2,0:T(8,128)(2,1)} collective-permute-done((bf16[9,256,256]{1,2,0:T(8,128)(2,1)}, bf16[9,256,256]{1,2,0:T(8,128)(2,1)}, u32[]{:S(2)}, u32[]{:S(2)}) %collective-permute-start.15) | collective-permute-done | bytes 1179680 | tf_op jit(solution)/shard_map/ppermute | solution.py:67
  170.9 20.2 %collective-permute-done.14 = bf16[9,256,256]{1,2,0:T(8,128)(2,1)} collective-permute-done((bf16[9,256,256]{1,2,0:T(8,128)(2,1)}, bf16[9,256,256]{1,2,0:T(8,128)(2,1)}, u32[]{:S(2)}, u32[]{:S(2)}) %collective-permute-start.14) | collective-permute-done | bytes 1179680 | tf_op jit(solution)/shard_map/ppermute | solution.py:64
  194.3 3.9 %collective-permute-start.18 = (bf16[3,256,256]{1,2,0:T(8,128)(2,1)S(1)}, bf16[3,256,256]{1,2,0:T(8,128)(2,1)S(1)}, u32[]{:S(2)}, u32[]{:S(2)}) collective-permute-start(bf16[3,256,256]{1,2,0:T(8,128)(2,1)S(1)} %slice.85), channel_id=1, source_target_pairs={{0,2},{2,6},{6,4},{4,0},{1,3},{3,7},{7,5},{5,1},{8,10},{10,14},{14... | collective-permute-start | bytes 1179656 | tf_op jit(solution)/shard_map/ppermute | solution.py:89
  198.1 4.4 %fusion.16 = f32[9,256,256]{1,2,0:T(8,128)S(1)} fusion(bf16[9,256,256]{1,2,0:T(8,128)(2,1)} %collective-permute-done.14, bf16[9,256,256]{1,2,0:T(8,128)(2,1)} %collective-permute-done.15, bf16[9,256,256]{1,2,0:T(8,128)(2,1)} %collective-permute-done.16, bf16[9,256,256]{1,2,0:T(8,128)(2,1)} %collective-permute-done.17, f32[]{:T(128)S(6)} %select_n.83, ...), kind=kOutput, calls=%fused_computation.26 | convolution fusion | flops 612237312 | bytes 9437192 | tf_op jit(solution)/shard_map/bd,vbc->vdc/dot_general | solution.py:29
  202.6 4.4 %collective-permute-done.18 = bf16[3,256,256]{1,2,0:T(8,128)(2,1)S(1)} collective-permute-done((bf16[3,256,256]{1,2,0:T(8,128)(2,1)S(1)}, bf16[3,256,256]{1,2,0:T(8,128)(2,1)S(1)}, u32[]{:S(2)}, u32[]{:S(2)}) %collective-permute-start.18) | collective-permute-done | bytes 393248 | tf_op jit(solution)/shard_map/ppermute | solution.py:89
  210.4 8.2 %collective-permute-done.20 = bf16[3,256,256]{1,2,0:T(8,128)(2,1)S(1)} collective-permute-done((bf16[3,256,256]{1,2,0:T(8,128)(2,1)S(1)}, bf16[3,256,256]{1,2,0:T(8,128)(2,1)S(1)}, u32[]{:S(2)}, u32[]{:S(2)}) %collective-permute-start.20) | collective-permute-done | bytes 393248 | tf_op jit(solution)/shard_map/ppermute | solution.py:89
  221.5 7.9 %collective-permute-done.22 = bf16[3,256,256]{1,2,0:T(8,128)(2,1)S(1)} collective-permute-done((bf16[3,256,256]{1,2,0:T(8,128)(2,1)S(1)}, bf16[3,256,256]{1,2,0:T(8,128)(2,1)S(1)}, u32[]{:S(2)}, u32[]{:S(2)}) %collective-permute-start.22) | collective-permute-done | bytes 393248 | tf_op jit(solution)/shard_map/ppermute | solution.py:89
  231.0 7.2 %collective-permute-done.23 = bf16[1,3,1,256,256]{3,4,1,2,0:T(8,128)(2,1)S(1)} collective-permute-done((bf16[1,3,1,256,256]{3,4,1,2,0:T(8,128)(2,1)S(1)}, bf16[1,3,1,256,256]{3,4,1,2,0:T(8,128)(2,1)S(1)}, u32[]{:S(2)}, u32[]{:S(2)}) %collective-permute-start.23) | collective-permute-done | bytes 393248 | tf_op jit(solution)/shard_map/ppermute | solution.py:19
  (98 shorter events, 73.5 us)
Async XLA Ops:
  2.4 14.8 %collective-permute-start.3 = (bf16[9,256,256]{2,1,0:T(8,128)(2,1)S(1)}, bf16[9,256,256]{2,1,0:T(8,128)(2,1)}, u32[]{:S(2)}, u32[]{:S(2)}) collective-permute-start(bf16[9,256,256]{2,1,0:T(8,128)(2,1)S(1)} %bitcast_select_fusion), channel_id=1, source_target_pairs={{0,1},{1,0},{2,3},{3,2},{4,5},{5,4},{6,7},{7,6},{8,9},{9,8},{10,11... | collective-permute-start | bytes 3538952 | tf_op jit(solution)/shard_map/ppermute | solution.py:19
  3.0 36.9 %collective-permute-start.2 = (bf16[18,9,4]{1,2,0:T(4,128)(2,1)S(1)}, bf16[18,9,4]{1,2,0:T(4,128)(2,1)S(1)}, u32[]{:S(2)}, u32[]{:S(2)}) collective-permute-start(bf16[18,9,4]{1,2,0:T(4,128)(2,1)S(1)} %bitcast.124), channel_id=1, source_target_pairs={{0,24},{8,0},{16,8},{24,16},{1,25},{9,1},{17,9},{25,17},{2,26},{10... | collective-permute-start | bytes 3896 | tf_op jit(solution)/shard_map/ppermute | solution.py:19
  6.5 33.3 %collective-permute-start.1 = (bf16[4,256,256]{2,1,0:T(8,128)(2,1)}, bf16[4,256,256]{2,1,0:T(8,128)(2,1)S(1)}, u32[]{:S(2)}, u32[]{:S(2)}) collective-permute-start(bf16[4,256,256]{2,1,0:T(8,128)(2,1)} %bitcast.1), channel_id=1, source_target_pairs={{0,24},{8,0},{16,8},{24,16},{1,25},{9,1},{17,9},{25,17},{2,26},{10... | collective-permute-start | bytes 1572872 | tf_op jit(solution)/shard_map/ppermute | solution.py:19
  7.1 32.8 %collective-permute-start = (bf16[4,256,256]{2,1,0:T(8,128)(2,1)}, bf16[4,256,256]{2,1,0:T(8,128)(2,1)}, u32[]{:S(2)}, u32[]{:S(2)}) collective-permute-start(bf16[4,256,256]{2,1,0:T(8,128)(2,1)} %bitcast), channel_id=1, source_target_pairs={{0,24},{8,0},{16,8},{24,16},{1,25},{9,1},{17,9},{25,17},{2,26},{10... | collective-permute-start | bytes 1572872 | tf_op jit(solution)/shard_map/ppermute | solution.py:19
  26.0 34.8 %collective-permute-start.6 = (bf16[9,256,256]{1,2,0:T(8,128)(2,1)}, bf16[9,256,256]{1,2,0:T(8,128)(2,1)}, u32[]{:S(2)}, u32[]{:S(2)}) collective-permute-start(bf16[9,256,256]{1,2,0:T(8,128)(2,1)} %fusion.21), channel_id=1, source_target_pairs={{0,4},{1,5},{8,12},{9,13},{16,20},{17,21},{24,28},{25,29}} | collective-permute-start | bytes 3538952 | tf_op jit(solution)/shard_map/ppermute | solution.py:68
  31.6 29.4 %collective-permute-start.5 = (bf16[9,256,256]{1,2,0:T(8,128)(2,1)}, bf16[9,256,256]{1,2,0:T(8,128)(2,1)}, u32[]{:S(2)}, u32[]{:S(2)}) collective-permute-start(bf16[9,256,256]{1,2,0:T(8,128)(2,1)} %fusion.21), channel_id=1, source_target_pairs={{6,4},{4,2},{2,0},{7,5},{5,3},{3,1},{14,12},{12,10},{10,8},{15,13}... | collective-permute-start | bytes 3538952 | tf_op jit(solution)/shard_map/ppermute | solution.py:67
  39.9 21.2 %collective-permute-start.7 = (bf16[9,256,256]{1,2,0:T(8,128)(2,1)}, bf16[9,256,256]{1,2,0:T(8,128)(2,1)}, u32[]{:S(2)}, u32[]{:S(2)}) collective-permute-start(bf16[9,256,256]{1,2,0:T(8,128)(2,1)} %fusion.20), channel_id=1, source_target_pairs={{6,2},{7,3},{14,10},{15,11},{22,18},{23,19},{30,26},{31,27}} | collective-permute-start | bytes 3538952 | tf_op jit(solution)/shard_map/ppermute | solution.py:65
  41.6 39.6 %collective-permute-start.4 = (bf16[9,256,256]{1,2,0:T(8,128)(2,1)}, bf16[9,256,256]{1,2,0:T(8,128)(2,1)}, u32[]{:S(2)}, u32[]{:S(2)}) collective-permute-start(bf16[9,256,256]{1,2,0:T(8,128)(2,1)} %fusion.20), channel_id=1, source_target_pairs={{0,2},{2,4},{4,6},{1,3},{3,5},{5,7},{8,10},{10,12},{12,14},{9,11},... | collective-permute-start | bytes 3538952 | tf_op jit(solution)/shard_map/ppermute | solution.py:64
  85.5 12.7 %collective-permute-start.8 = (bf16[3,256,256]{1,2,0:T(8,128)(2,1)S(1)}, bf16[3,256,256]{1,2,0:T(8,128)(2,1)S(1)}, u32[]{:S(2)}, u32[]{:S(2)}) collective-permute-start(bf16[3,256,256]{1,2,0:T(8,128)(2,1)S(1)} %slice.81), channel_id=1, source_target_pairs={{0,2},{2,6},{6,4},{4,0},{1,3},{3,7},{7,5},{5,1},{8,10},{10,14},{14... | collective-permute-start | bytes 1179656 | tf_op jit(solution)/shard_map/ppermute | solution.py:89
  98.4 11.5 %collective-permute-start.10 = (bf16[3,256,256]{1,2,0:T(8,128)(2,1)S(1)}, bf16[3,256,256]{1,2,0:T(8,128)(2,1)S(1)}, u32[]{:S(2)}, u32[]{:S(2)}) collective-permute-start(bf16[3,256,256]{1,2,0:T(8,128)(2,1)S(1)} %slice.62), channel_id=1, source_target_pairs={{0,2},{2,6},{6,4},{4,0},{1,3},{3,7},{7,5},{5,1},{8,10},{10,14},{14... | collective-permute-start | bytes 1179656 | tf_op jit(solution)/shard_map/ppermute | solution.py:89
  99.3 10.5 %collective-permute-start.9 = (bf16[3,256,256]{1,2,0:T(8,128)(2,1)S(1)}, bf16[3,256,256]{1,2,0:T(8,128)(2,1)}, u32[]{:S(2)}, u32[]{:S(2)}) collective-permute-start(bf16[3,256,256]{1,2,0:T(8,128)(2,1)S(1)} %fusion.37), channel_id=1, source_target_pairs={{0,1},{1,0},{2,3},{3,2},{4,5},{5,4},{6,7},{7,6},{8,9},{9,8},{10,11... | collective-permute-start | bytes 1179656 | tf_op jit(solution)/shard_map/ppermute | solution.py:19
  110.7 10.8 %collective-permute-start.12 = (bf16[3,256,256]{1,2,0:T(8,128)(2,1)}, bf16[3,256,256]{1,2,0:T(8,128)(2,1)}, u32[]{:S(2)}, u32[]{:S(2)}) collective-permute-start(bf16[3,256,256]{1,2,0:T(8,128)(2,1)} %slice.64), channel_id=1, source_target_pairs={{0,2},{2,6},{6,4},{4,0},{1,3},{3,7},{7,5},{5,1},{8,10},{10,14},{14... | collective-permute-start | bytes 1179656 | tf_op jit(solution)/shard_map/ppermute | solution.py:89
  110.7 10.8 %collective-permute-start.11 = (bf16[3,256,256]{1,2,0:T(8,128)(2,1)S(1)}, bf16[3,256,256]{1,2,0:T(8,128)(2,1)}, u32[]{:S(2)}, u32[]{:S(2)}) collective-permute-start(bf16[3,256,256]{1,2,0:T(8,128)(2,1)S(1)} %fusion.35), channel_id=1, source_target_pairs={{0,1},{1,0},{2,3},{3,2},{4,5},{5,4},{6,7},{7,6},{8,9},{9,8},{10,11... | collective-permute-start | bytes 1179656 | tf_op jit(solution)/shard_map/ppermute | solution.py:19
  124.2 3.6 %collective-permute-start.13 = (bf16[3,256,256]{1,2,0:T(8,128)(2,1)S(1)}, bf16[3,256,256]{1,2,0:T(8,128)(2,1)S(1)}, u32[]{:S(2)}, u32[]{:S(2)}) collective-permute-start(bf16[3,256,256]{1,2,0:T(8,128)(2,1)S(1)} %get-tuple-element.71), channel_id=1, source_target_pairs={{0,1},{1,0},{2,3},{3,2},{4,5},{5,4},{6,7},{7,6},{8,9},{9,8},{10,11... | collective-permute-start | bytes 1179656 | tf_op jit(solution)/shard_map/ppermute | solution.py:19
  137.9 28.1 %collective-permute-start.16 = (bf16[9,256,256]{1,2,0:T(8,128)(2,1)}, bf16[9,256,256]{1,2,0:T(8,128)(2,1)}, u32[]{:S(2)}, u32[]{:S(2)}) collective-permute-start(bf16[9,256,256]{1,2,0:T(8,128)(2,1)} %fusion.24), channel_id=1, source_target_pairs={{0,4},{1,5},{8,12},{9,13},{16,20},{17,21},{24,28},{25,29}} | collective-permute-start | bytes 3538952 | tf_op jit(solution)/shard_map/ppermute | solution.py:68
  140.4 30.4 %collective-permute-start.15 = (bf16[9,256,256]{1,2,0:T(8,128)(2,1)}, bf16[9,256,256]{1,2,0:T(8,128)(2,1)}, u32[]{:S(2)}, u32[]{:S(2)}) collective-permute-start(bf16[9,256,256]{1,2,0:T(8,128)(2,1)} %fusion.24), channel_id=1, source_target_pairs={{6,4},{4,2},{2,0},{7,5},{5,3},{3,1},{14,12},{12,10},{10,8},{15,13}... | collective-permute-start | bytes 3538952 | tf_op jit(solution)/shard_map/ppermute | solution.py:67
  147.4 23.4 %collective-permute-start.17 = (bf16[9,256,256]{1,2,0:T(8,128)(2,1)}, bf16[9,256,256]{1,2,0:T(8,128)(2,1)}, u32[]{:S(2)}, u32[]{:S(2)}) collective-permute-start(bf16[9,256,256]{1,2,0:T(8,128)(2,1)} %fusion.23), channel_id=1, source_target_pairs={{6,2},{7,3},{14,10},{15,11},{22,18},{23,19},{30,26},{31,27}} | collective-permute-start | bytes 3538952 | tf_op jit(solution)/shard_map/ppermute | solution.py:65
  149.2 41.9 %collective-permute-start.14 = (bf16[9,256,256]{1,2,0:T(8,128)(2,1)}, bf16[9,256,256]{1,2,0:T(8,128)(2,1)}, u32[]{:S(2)}, u32[]{:S(2)}) collective-permute-start(bf16[9,256,256]{1,2,0:T(8,128)(2,1)} %fusion.23), channel_id=1, source_target_pairs={{0,2},{2,4},{4,6},{1,3},{3,5},{5,7},{8,10},{10,12},{12,14},{9,11},... | collective-permute-start | bytes 3538952 | tf_op jit(solution)/shard_map/ppermute | solution.py:64
  194.3 12.7 %collective-permute-start.18 = (bf16[3,256,256]{1,2,0:T(8,128)(2,1)S(1)}, bf16[3,256,256]{1,2,0:T(8,128)(2,1)S(1)}, u32[]{:S(2)}, u32[]{:S(2)}) collective-permute-start(bf16[3,256,256]{1,2,0:T(8,128)(2,1)S(1)} %slice.85), channel_id=1, source_target_pairs={{0,2},{2,6},{6,4},{4,0},{1,3},{3,7},{7,5},{5,1},{8,10},{10,14},{14... | collective-permute-start | bytes 1179656 | tf_op jit(solution)/shard_map/ppermute | solution.py:89
  207.1 11.5 %collective-permute-start.20 = (bf16[3,256,256]{1,2,0:T(8,128)(2,1)S(1)}, bf16[3,256,256]{1,2,0:T(8,128)(2,1)S(1)}, u32[]{:S(2)}, u32[]{:S(2)}) collective-permute-start(bf16[3,256,256]{1,2,0:T(8,128)(2,1)S(1)} %slice.70), channel_id=1, source_target_pairs={{0,2},{2,6},{6,4},{4,0},{1,3},{3,7},{7,5},{5,1},{8,10},{10,14},{14... | collective-permute-start | bytes 1179656 | tf_op jit(solution)/shard_map/ppermute | solution.py:89
  208.9 9.7 %collective-permute-start.19 = (bf16[1,3,1,256,256]{3,4,1,2,0:T(8,128)(2,1)S(1)}, bf16[1,3,1,256,256]{3,4,1,2,0:T(8,128)(2,1)S(1)}, u32[]{:S(2)}, u32[]{:S(2)}) collective-permute-start(bf16[1,3,1,256,256]{3,4,1,2,0:T(8,128)(2,1)S(1)} %bitcast.127), channel_id=1, source_target_pairs={{0,16},{8,24},{16,0},{24,8},{1,17},{9,25},{17,1},{25,9},{2,18},{10... | collective-permute-start | bytes 1179656 | tf_op jit(solution)/shard_map/ppermute | solution.py:19
  218.8 10.6 %collective-permute-start.22 = (bf16[3,256,256]{1,2,0:T(8,128)(2,1)S(1)}, bf16[3,256,256]{1,2,0:T(8,128)(2,1)S(1)}, u32[]{:S(2)}, u32[]{:S(2)}) collective-permute-start(bf16[3,256,256]{1,2,0:T(8,128)(2,1)S(1)} %slice.72), channel_id=1, source_target_pairs={{0,2},{2,6},{6,4},{4,0},{1,3},{3,7},{7,5},{5,1},{8,10},{10,14},{14... | collective-permute-start | bytes 1179656 | tf_op jit(solution)/shard_map/ppermute | solution.py:89
  219.9 9.4 %collective-permute-start.21 = (bf16[1,3,1,256,256]{3,4,1,2,0:T(8,128)(2,1)S(1)}, bf16[1,3,1,256,256]{3,4,1,2,0:T(8,128)(2,1)S(1)}, u32[]{:S(2)}, u32[]{:S(2)}) collective-permute-start(bf16[1,3,1,256,256]{3,4,1,2,0:T(8,128)(2,1)S(1)} %bitcast.126), channel_id=1, source_target_pairs={{0,16},{8,24},{16,0},{24,8},{1,17},{9,25},{17,1},{25,9},{2,18},{10... | collective-permute-start | bytes 1179656 | tf_op jit(solution)/shard_map/ppermute | solution.py:19
  229.5 8.8 %collective-permute-start.23 = (bf16[1,3,1,256,256]{3,4,1,2,0:T(8,128)(2,1)S(1)}, bf16[1,3,1,256,256]{3,4,1,2,0:T(8,128)(2,1)S(1)}, u32[]{:S(2)}, u32[]{:S(2)}) collective-permute-start(bf16[1,3,1,256,256]{3,4,1,2,0:T(8,128)(2,1)S(1)} %fusion.38), channel_id=1, source_target_pairs={{0,16},{8,24},{16,0},{24,8},{1,17},{9,25},{17,1},{25,9},{2,18},{10... | collective-permute-start | bytes 1179656 | tf_op jit(solution)/shard_map/ppermute | solution.py:19
  (9 other events, 95.2 us)

commit v14 on v13

--- a/solution.py
+++ b/solution.py
@@ -131,7 +131,7 @@
         if line:
             parts, tensors[step + 1 :] = advance_line(
                 pieces, ket, bra, mpo, live_mask, sector, tensors[step + 1 :],
-                3 if last else 3, onward if last else chan_copies,
+                4 if last else 2, onward if last else chan_copies,
             )
         else:
             parts = [advance_direct(pieces, ket, bra, mpo, live_mask)]

time: 241 us -> 235 us (0.975)
  local copies, waits for them, and re-layouts: 16.5 us -> 10.8 us
    ppermute x6, waiting for transfers between devices: 49.2 us -> 41 us  [advance_line(): got_last = lax.ppermute(send[low:high], 'sector', LAST)]
    ppermute x10, waiting for transfers between devices: 7.22 us -> 14.4 us  [shifted(): return lax.ppermute(value, axis, pairs)]
    unnamed x23 -> x21, local copies, waits for them, and re-layouts: 6.22 us -> 1.15 us
  transfers between devices with their start and end apart: 24 -> 24, of which waited for: 12 -> 15; matrix products, arithmetic and copies ran while one was open for 23% -> 22% of each run, Pallas kernels for 0% -> 0%
where the time goes in v14:
time: 235 us
  waiting for transfers between devices  105 us (45%)
  matrix products  50.9 us (22%)
  starting transfers between devices  49.2 us (21%)
  other arithmetic  11.9 us (5%)
  local copies, waits for them, and re-layouts  10.8 us (5%)
  between operations  6.88 us (3%)
    ppermute x6, waiting for transfers between devices, advance_line(): got_last = lax.ppermute(send[low:high], 'sector', LAST)  41 us
    ppermute x2, waiting for transfers between devices, advance_line(): got_right = lax.ppermute(slot_a, 'sector', RIGHT)  40.3 us
    dot_general x8, matrix products, term(): jnp.einsum('bd,vbc->vdc', bra_p, rotated, preferred_element_type=jnp.floa...  28.9 us
    dot_general x8, matrix products, term(): jnp.einsum('wv,wba->vba', mpo_p, gathered, preferred_element_type=jnp.flo...  22 us
    ppermute x10, waiting for transfers between devices, shifted(): return lax.ppermute(value, axis, pairs)  14.4 us
    ppermute x10, starting transfers between devices, shifted(): return lax.ppermute(value, axis, pairs)  12.2 us
    ppermute x6, starting transfers between devices, advance_line(): got_last = lax.ppermute(send[low:high], 'sector', LAST)  11.6 us
    ppermute x2, starting transfers between devices, advance_line(): got_right = lax.ppermute(slot_a, 'sector', RIGHT)  10.4 us
  transfers between devices with their start and end apart: 24, of which 15 were waited for; matrix products, arithmetic and copies ran while one was open for 22% of the time, Pallas kernels for 0%

profile of v14, /device:TPU:0, one launch (start us, length us, event | category | flops | bytes accessed | tf_op | source)
XLA Modules:
  0.0 234.7 jit_solution(1178437502211282735)
XLA Ops:
  22.4 3.6 %fusion.21 = bf16[9,256,256]{1,2,0:T(8,128)(2,1)} fusion(bf16[9,256,256]{2,0,1:T(8,128)(2,1)} %fusion.2, bf16[1,1,4,256,256]{4,3,2,1,0:T(8,128)(2,1)} %param.15, s32[]{:T(128)S(6)} %select_n.81, bf16[1,1,4,256,256]{4,3,2,1,0:T(8,128)(2,1)} %param.14), kind=kOutput, calls=%fused_computation.57 | convolution fusion | flops 605159424 | bytes 3539968 | tf_op jit(solution)/shard_map/bd,vbc->vdc/dot_general | solution.py:29
  26.0 5.5 %collective-permute-start.6 = (bf16[9,256,256]{1,2,0:T(8,128)(2,1)}, bf16[9,256,256]{1,2,0:T(8,128)(2,1)}, u32[]{:S(2)}, u32[]{:S(2)}) collective-permute-start(bf16[9,256,256]{1,2,0:T(8,128)(2,1)} %fusion.21), channel_id=1, source_target_pairs={{0,4},{1,5},{8,12},{9,13},{16,20},{17,21},{24,28},{25,29}} | collective-permute-start | bytes 3538952 | tf_op jit(solution)/shard_map/ppermute | solution.py:68
  36.3 3.6 %fusion.20 = bf16[9,256,256]{1,2,0:T(8,128)(2,1)} fusion(bf16[9,256,256]{2,0,1:T(8,128)(2,1)} %fusion.6, bf16[1,1,4,256,256]{4,3,2,1,0:T(8,128)(2,1)} %param.15, s32[]{:T(128)S(6)} %select_n.78, bf16[1,1,4,256,256]{4,3,2,1,0:T(8,128)(2,1)} %param.14), kind=kOutput, calls=%fused_computation.56 | convolution fusion | flops 605159424 | bytes 3539968 | tf_op jit(solution)/shard_map/bd,vbc->vdc/dot_general | solution.py:29
  41.6 5.2 %collective-permute-start.4 = (bf16[9,256,256]{1,2,0:T(8,128)(2,1)}, bf16[9,256,256]{1,2,0:T(8,128)(2,1)}, u32[]{:S(2)}, u32[]{:S(2)}) collective-permute-start(bf16[9,256,256]{1,2,0:T(8,128)(2,1)} %fusion.20), channel_id=1, source_target_pairs={{0,2},{2,4},{4,6},{1,3},{3,5},{5,7},{8,10},{10,12},{12,14},{9,11},... | collective-permute-start | bytes 3538952 | tf_op jit(solution)/shard_map/ppermute | solution.py:64
  50.1 3.7 %fusion.22 = bf16[9,256,256]{1,2,0:T(8,128)(2,1)} fusion(bf16[9,256,256]{2,0,1:T(8,128)(2,1)} %fusion, bf16[1,1,4,256,256]{4,3,2,1,0:T(8,128)(2,1)} %param.15, s32[]{:T(128)S(6)} %select_n.82, bf16[1,1,4,256,256]{4,3,2,1,0:T(8,128)(2,1)} %param.14), kind=kOutput, calls=%fused_computation.58 | convolution fusion | flops 605159424 | bytes 3539968 | tf_op jit(solution)/shard_map/bd,vbc->vdc/dot_general | solution.py:29
  61.0 20.2 %collective-permute-done.4 = bf16[9,256,256]{1,2,0:T(8,128)(2,1)} collective-permute-done((bf16[9,256,256]{1,2,0:T(8,128)(2,1)}, bf16[9,256,256]{1,2,0:T(8,128)(2,1)}, u32[]{:S(2)}, u32[]{:S(2)}) %collective-permute-start.4) | collective-permute-done | bytes 1179680 | tf_op jit(solution)/shard_map/ppermute | solution.py:64
  81.2 3.6 %fusion.13 = (bf16[9,256,256]{1,2,0:T(8,128)(2,1)S(1)}, f32[9,256,256]{1,2,0:T(8,128)S(1)}) fusion(bf16[9,256,256]{1,2,0:T(8,128)(2,1)} %collective-permute-done.4, bf16[9,256,256]{1,2,0:T(8,128)(2,1)} %collective-permute-done.5, bf16[9,256,256]{1,2,0:T(8,128)(2,1)S(1)} %copy-done.4, f32[]{:T(128)S(6)} %sub.14, f32[]{:T(128)S(6)} %sub.13, ...), kind=kLoop, calls=%fused_computation.23 | loop fusion | flops 9437184 | bytes 10616848 | tf_op jit(solution)/shard_map/convert_element_type | solution.py:77
  84.8 3.8 %collective-permute-start.8 = (bf16[4,256,256]{1,2,0:T(8,128)(2,1)S(1)}, bf16[4,256,256]{1,2,0:T(8,128)(2,1)S(1)}, u32[]{:S(2)}, u32[]{:S(2)}) collective-permute-start(bf16[4,256,256]{1,2,0:T(8,128)(2,1)S(1)} %slice.81), channel_id=1, source_target_pairs={{0,2},{2,6},{6,4},{4,0},{1,3},{3,7},{7,5},{5,1},{8,10},{10,14},{14... | collective-permute-start | bytes 1572872 | tf_op jit(solution)/shard_map/ppermute | solution.py:89
  88.6 11.7 %collective-permute-done.8 = bf16[4,256,256]{1,2,0:T(8,128)(2,1)S(1)} collective-permute-done((bf16[4,256,256]{1,2,0:T(8,128)(2,1)S(1)}, bf16[4,256,256]{1,2,0:T(8,128)(2,1)S(1)}, u32[]{:S(2)}, u32[]{:S(2)}) %collective-permute-start.8) | collective-permute-done | bytes 524320 | tf_op jit(solution)/shard_map/ppermute | solution.py:89
  103.4 14.2 %collective-permute-done.10 = bf16[5,256,256]{1,2,0:T(8,128)(2,1)S(1)} collective-permute-done((bf16[5,256,256]{1,2,0:T(8,128)(2,1)S(1)}, bf16[5,256,256]{1,2,0:T(8,128)(2,1)S(1)}, u32[]{:S(2)}, u32[]{:S(2)}) %collective-permute-start.10) | collective-permute-done | bytes 655392 | tf_op jit(solution)/shard_map/ppermute | solution.py:89
  121.7 3.7 %copy.30 = bf16[18,256,256]{2,0,1:T(8,128)(2,1)S(1)} copy(bf16[18,256,256]{1,2,0:T(8,128)(2,1)} %pad_maximum_fusion.1) | data formatting | bytes 4718592 | tf_op jit(solution)/shard_map/concatenate | solution.py:45
  127.5 3.6 %fusion.24 = bf16[9,256,256]{1,2,0:T(8,128)(2,1)} fusion(bf16[9,256,256]{2,0,1:T(8,128)(2,1)} %fusion.91, bf16[4,256,256]{2,1,0:T(8,128)(2,1)} %copy-done.5, s32[]{:T(128)S(6)} %select_n.81, bf16[4,256,256]{2,1,0:T(8,128)(2,1)} %collective-permute-done), kind=kOutput, calls=%fused_computation.60 | convolution fusion | flops 605159424 | bytes 3539968 | tf_op jit(solution)/shard_map/bd,vbc->vdc/dot_general | solution.py:29
  138.0 3.6 %fusion.23 = bf16[9,256,256]{1,2,0:T(8,128)(2,1)} fusion(bf16[9,256,256]{2,0,1:T(8,128)(2,1)} %fusion.93, bf16[4,256,256]{2,1,0:T(8,128)(2,1)} %copy-done.5, s32[]{:T(128)S(6)} %select_n.78, bf16[4,256,256]{2,1,0:T(8,128)(2,1)} %collective-permute-done), kind=kOutput, calls=%fused_computation.59 | convolution fusion | flops 605159424 | bytes 3539968 | tf_op jit(solution)/shard_map/bd,vbc->vdc/dot_general | solution.py:29
  143.3 5.2 %collective-permute-start.12 = (bf16[9,256,256]{1,2,0:T(8,128)(2,1)}, bf16[9,256,256]{1,2,0:T(8,128)(2,1)}, u32[]{:S(2)}, u32[]{:S(2)}) collective-permute-start(bf16[9,256,256]{1,2,0:T(8,128)(2,1)} %fusion.23), channel_id=1, source_target_pairs={{0,2},{2,4},{4,6},{1,3},{3,5},{5,7},{8,10},{10,12},{12,14},{9,11},... | collective-permute-start | bytes 3538952 | tf_op jit(solution)/shard_map/ppermute | solution.py:64
  150.6 3.7 %fusion.25 = bf16[9,256,256]{1,2,0:T(8,128)(2,1)} fusion(bf16[9,256,256]{2,0,1:T(8,128)(2,1)} %fusion.89, bf16[4,256,256]{2,1,0:T(8,128)(2,1)} %copy-done.5, s32[]{:T(128)S(6)} %select_n.82, bf16[4,256,256]{2,1,0:T(8,128)(2,1)} %collective-permute-done), kind=kOutput, calls=%fused_computation.61 | convolution fusion | flops 605159424 | bytes 3539968 | tf_op jit(solution)/shard_map/bd,vbc->vdc/dot_general | solution.py:29
  156.4 3.8 %collective-permute-done.14 = bf16[9,256,256]{1,2,0:T(8,128)(2,1)} collective-permute-done((bf16[9,256,256]{1,2,0:T(8,128)(2,1)}, bf16[9,256,256]{1,2,0:T(8,128)(2,1)}, u32[]{:S(2)}, u32[]{:S(2)}) %collective-permute-start.14) | collective-permute-done | bytes 1179680 | tf_op jit(solution)/shard_map/ppermute | solution.py:68
  160.2 4.3 %collective-permute-done.13 = bf16[9,256,256]{1,2,0:T(8,128)(2,1)} collective-permute-done((bf16[9,256,256]{1,2,0:T(8,128)(2,1)}, bf16[9,256,256]{1,2,0:T(8,128)(2,1)}, u32[]{:S(2)}, u32[]{:S(2)}) %collective-permute-start.13) | collective-permute-done | bytes 1179680 | tf_op jit(solution)/shard_map/ppermute | solution.py:67
  164.5 20.2 %collective-permute-done.12 = bf16[9,256,256]{1,2,0:T(8,128)(2,1)} collective-permute-done((bf16[9,256,256]{1,2,0:T(8,128)(2,1)}, bf16[9,256,256]{1,2,0:T(8,128)(2,1)}, u32[]{:S(2)}, u32[]{:S(2)}) %collective-permute-start.12) | collective-permute-done | bytes 1179680 | tf_op jit(solution)/shard_map/ppermute | solution.py:64
  188.0 3.7 %collective-permute-start.16 = (bf16[2,256,256]{1,2,0:T(8,128)(2,1)S(1)}, bf16[2,256,256]{1,2,0:T(8,128)(2,1)S(1)}, u32[]{:S(2)}, u32[]{:S(2)}) collective-permute-start(bf16[2,256,256]{1,2,0:T(8,128)(2,1)S(1)} %slice.84), channel_id=1, source_target_pairs={{0,2},{2,6},{6,4},{4,0},{1,3},{3,7},{7,5},{5,1},{8,10},{10,14},{14... | collective-permute-start | bytes 786440 | tf_op jit(solution)/shard_map/ppermute | solution.py:89
  191.7 4.4 %fusion.16 = f32[9,256,256]{1,2,0:T(8,128)S(1)} fusion(bf16[9,256,256]{1,2,0:T(8,128)(2,1)} %collective-permute-done.12, bf16[9,256,256]{1,2,0:T(8,128)(2,1)} %collective-permute-done.13, bf16[9,256,256]{1,2,0:T(8,128)(2,1)} %collective-permute-done.14, bf16[9,256,256]{1,2,0:T(8,128)(2,1)} %collective-permute-done.15, f32[]{:T(128)S(6)} %select_n.83, ...), kind=kOutput, calls=%fused_computation.26 | convolution fusion | flops 612237312 | bytes 9437192 | tf_op jit(solution)/shard_map/bd,vbc->vdc/dot_general | solution.py:29
  201.8 5.6 %collective-permute-done.18 = bf16[2,256,256]{1,2,0:T(8,128)(2,1)S(1)} collective-permute-done((bf16[2,256,256]{1,2,0:T(8,128)(2,1)S(1)}, bf16[2,256,256]{1,2,0:T(8,128)(2,1)S(1)}, u32[]{:S(2)}, u32[]{:S(2)}) %collective-permute-start.18) | collective-permute-done | bytes 262176 | tf_op jit(solution)/shard_map/ppermute | solution.py:89
  209.8 5.5 %collective-permute-done.20 = bf16[2,256,256]{1,2,0:T(8,128)(2,1)S(1)} collective-permute-done((bf16[2,256,256]{1,2,0:T(8,128)(2,1)S(1)}, bf16[2,256,256]{1,2,0:T(8,128)(2,1)S(1)}, u32[]{:S(2)}, u32[]{:S(2)}) %collective-permute-start.20) | collective-permute-done | bytes 262176 | tf_op jit(solution)/shard_map/ppermute | solution.py:89
  218.0 4.9 %collective-permute-done.21 = bf16[1,2,1,256,256]{3,4,1,2,0:T(8,128)(2,1)S(1)} collective-permute-done((bf16[1,2,1,256,256]{3,4,1,2,0:T(8,128)(2,1)S(1)}, bf16[1,2,1,256,256]{3,4,1,2,0:T(8,128)(2,1)S(1)}, u32[]{:S(2)}, u32[]{:S(2)}) %collective-permute-start.21) | collective-permute-done | bytes 262176 | tf_op jit(solution)/shard_map/ppermute | solution.py:19
  226.8 6.3 %collective-permute-done.23 = bf16[1,3,1,256,256]{3,4,1,2,0:T(8,128)(2,1)S(1)} collective-permute-done((bf16[1,3,1,256,256]{3,4,1,2,0:T(8,128)(2,1)S(1)}, bf16[1,3,1,256,256]{3,4,1,2,0:T(8,128)(2,1)S(1)}, u32[]{:S(2)}, u32[]{:S(2)}) %collective-permute-start.23) | collective-permute-done | bytes 393248 | tf_op jit(solution)/shard_map/ppermute | solution.py:19
  (96 shorter events, 74.2 us)
Async XLA Ops:
  2.4 14.8 %collective-permute-start.3 = (bf16[9,256,256]{2,1,0:T(8,128)(2,1)S(1)}, bf16[9,256,256]{2,1,0:T(8,128)(2,1)}, u32[]{:S(2)}, u32[]{:S(2)}) collective-permute-start(bf16[9,256,256]{2,1,0:T(8,128)(2,1)S(1)} %bitcast_select_fusion), channel_id=1, source_target_pairs={{0,1},{1,0},{2,3},{3,2},{4,5},{5,4},{6,7},{7,6},{8,9},{9,8},{10,11... | collective-permute-start | bytes 3538952 | tf_op jit(solution)/shard_map/ppermute | solution.py:19
  3.0 36.9 %collective-permute-start.2 = (bf16[18,9,4]{1,2,0:T(4,128)(2,1)S(1)}, bf16[18,9,4]{1,2,0:T(4,128)(2,1)S(1)}, u32[]{:S(2)}, u32[]{:S(2)}) collective-permute-start(bf16[18,9,4]{1,2,0:T(4,128)(2,1)S(1)} %bitcast.125), channel_id=1, source_target_pairs={{0,24},{8,0},{16,8},{24,16},{1,25},{9,1},{17,9},{25,17},{2,26},{10... | collective-permute-start | bytes 3896 | tf_op jit(solution)/shard_map/ppermute | solution.py:19
  6.5 33.3 %collective-permute-start.1 = (bf16[4,256,256]{2,1,0:T(8,128)(2,1)}, bf16[4,256,256]{2,1,0:T(8,128)(2,1)S(1)}, u32[]{:S(2)}, u32[]{:S(2)}) collective-permute-start(bf16[4,256,256]{2,1,0:T(8,128)(2,1)} %bitcast.1), channel_id=1, source_target_pairs={{0,24},{8,0},{16,8},{24,16},{1,25},{9,1},{17,9},{25,17},{2,26},{10... | collective-permute-start | bytes 1572872 | tf_op jit(solution)/shard_map/ppermute | solution.py:19
  7.1 32.8 %collective-permute-start = (bf16[4,256,256]{2,1,0:T(8,128)(2,1)}, bf16[4,256,256]{2,1,0:T(8,128)(2,1)}, u32[]{:S(2)}, u32[]{:S(2)}) collective-permute-start(bf16[4,256,256]{2,1,0:T(8,128)(2,1)} %bitcast), channel_id=1, source_target_pairs={{0,24},{8,0},{16,8},{24,16},{1,25},{9,1},{17,9},{25,17},{2,26},{10... | collective-permute-start | bytes 1572872 | tf_op jit(solution)/shard_map/ppermute | solution.py:19
  26.0 33.9 %collective-permute-start.6 = (bf16[9,256,256]{1,2,0:T(8,128)(2,1)}, bf16[9,256,256]{1,2,0:T(8,128)(2,1)}, u32[]{:S(2)}, u32[]{:S(2)}) collective-permute-start(bf16[9,256,256]{1,2,0:T(8,128)(2,1)} %fusion.21), channel_id=1, source_target_pairs={{0,4},{1,5},{8,12},{9,13},{16,20},{17,21},{24,28},{25,29}} | collective-permute-start | bytes 3538952 | tf_op jit(solution)/shard_map/ppermute | solution.py:68
  31.6 29.4 %collective-permute-start.5 = (bf16[9,256,256]{1,2,0:T(8,128)(2,1)}, bf16[9,256,256]{1,2,0:T(8,128)(2,1)}, u32[]{:S(2)}, u32[]{:S(2)}) collective-permute-start(bf16[9,256,256]{1,2,0:T(8,128)(2,1)} %fusion.21), channel_id=1, source_target_pairs={{6,4},{4,2},{2,0},{7,5},{5,3},{3,1},{14,12},{12,10},{10,8},{15,13}... | collective-permute-start | bytes 3538952 | tf_op jit(solution)/shard_map/ppermute | solution.py:67
  39.9 21.2 %collective-permute-start.7 = (bf16[9,256,256]{1,2,0:T(8,128)(2,1)}, bf16[9,256,256]{1,2,0:T(8,128)(2,1)}, u32[]{:S(2)}, u32[]{:S(2)}) collective-permute-start(bf16[9,256,256]{1,2,0:T(8,128)(2,1)} %fusion.20), channel_id=1, source_target_pairs={{6,2},{7,3},{14,10},{15,11},{22,18},{23,19},{30,26},{31,27}} | collective-permute-start | bytes 3538952 | tf_op jit(solution)/shard_map/ppermute | solution.py:65
  41.6 39.6 %collective-permute-start.4 = (bf16[9,256,256]{1,2,0:T(8,128)(2,1)}, bf16[9,256,256]{1,2,0:T(8,128)(2,1)}, u32[]{:S(2)}, u32[]{:S(2)}) collective-permute-start(bf16[9,256,256]{1,2,0:T(8,128)(2,1)} %fusion.20), channel_id=1, source_target_pairs={{0,2},{2,4},{4,6},{1,3},{3,5},{5,7},{8,10},{10,12},{12,14},{9,11},... | collective-permute-start | bytes 3538952 | tf_op jit(solution)/shard_map/ppermute | solution.py:64
  84.8 15.5 %collective-permute-start.8 = (bf16[4,256,256]{1,2,0:T(8,128)(2,1)S(1)}, bf16[4,256,256]{1,2,0:T(8,128)(2,1)S(1)}, u32[]{:S(2)}, u32[]{:S(2)}) collective-permute-start(bf16[4,256,256]{1,2,0:T(8,128)(2,1)S(1)} %slice.81), channel_id=1, source_target_pairs={{0,2},{2,6},{6,4},{4,0},{1,3},{3,7},{7,5},{5,1},{8,10},{10,14},{14... | collective-permute-start | bytes 1572872 | tf_op jit(solution)/shard_map/ppermute | solution.py:89
  100.6 17.1 %collective-permute-start.10 = (bf16[5,256,256]{1,2,0:T(8,128)(2,1)S(1)}, bf16[5,256,256]{1,2,0:T(8,128)(2,1)S(1)}, u32[]{:S(2)}, u32[]{:S(2)}) collective-permute-start(bf16[5,256,256]{1,2,0:T(8,128)(2,1)S(1)} %slice.62), channel_id=1, source_target_pairs={{0,2},{2,6},{6,4},{4,0},{1,3},{3,7},{7,5},{5,1},{8,10},{10,14},{14... | collective-permute-start | bytes 1966088 | tf_op jit(solution)/shard_map/ppermute | solution.py:89
  101.5 1.9 collective-permute-start.9
  117.8 2.2 collective-permute-start.11
  131.1 29.1 %collective-permute-start.14 = (bf16[9,256,256]{1,2,0:T(8,128)(2,1)}, bf16[9,256,256]{1,2,0:T(8,128)(2,1)}, u32[]{:S(2)}, u32[]{:S(2)}) collective-permute-start(bf16[9,256,256]{1,2,0:T(8,128)(2,1)} %fusion.24), channel_id=1, source_target_pairs={{0,4},{1,5},{8,12},{9,13},{16,20},{17,21},{24,28},{25,29}} | collective-permute-start | bytes 3538952 | tf_op jit(solution)/shard_map/ppermute | solution.py:68
  134.6 29.9 %collective-permute-start.13 = (bf16[9,256,256]{1,2,0:T(8,128)(2,1)}, bf16[9,256,256]{1,2,0:T(8,128)(2,1)}, u32[]{:S(2)}, u32[]{:S(2)}) collective-permute-start(bf16[9,256,256]{1,2,0:T(8,128)(2,1)} %fusion.24), channel_id=1, source_target_pairs={{6,4},{4,2},{2,0},{7,5},{5,3},{3,1},{14,12},{12,10},{10,8},{15,13}... | collective-permute-start | bytes 3538952 | tf_op jit(solution)/shard_map/ppermute | solution.py:67
  141.6 22.9 %collective-permute-start.15 = (bf16[9,256,256]{1,2,0:T(8,128)(2,1)}, bf16[9,256,256]{1,2,0:T(8,128)(2,1)}, u32[]{:S(2)}, u32[]{:S(2)}) collective-permute-start(bf16[9,256,256]{1,2,0:T(8,128)(2,1)} %fusion.23), channel_id=1, source_target_pairs={{6,2},{7,3},{14,10},{15,11},{22,18},{23,19},{30,26},{31,27}} | collective-permute-start | bytes 3538952 | tf_op jit(solution)/shard_map/ppermute | solution.py:65
  143.3 41.4 %collective-permute-start.12 = (bf16[9,256,256]{1,2,0:T(8,128)(2,1)}, bf16[9,256,256]{1,2,0:T(8,128)(2,1)}, u32[]{:S(2)}, u32[]{:S(2)}) collective-permute-start(bf16[9,256,256]{1,2,0:T(8,128)(2,1)} %fusion.23), channel_id=1, source_target_pairs={{0,2},{2,4},{4,6},{1,3},{3,5},{5,7},{8,10},{10,12},{12,14},{9,11},... | collective-permute-start | bytes 3538952 | tf_op jit(solution)/shard_map/ppermute | solution.py:64
  188.0 9.8 %collective-permute-start.16 = (bf16[2,256,256]{1,2,0:T(8,128)(2,1)S(1)}, bf16[2,256,256]{1,2,0:T(8,128)(2,1)S(1)}, u32[]{:S(2)}, u32[]{:S(2)}) collective-permute-start(bf16[2,256,256]{1,2,0:T(8,128)(2,1)S(1)} %slice.84), channel_id=1, source_target_pairs={{0,2},{2,6},{6,4},{4,0},{1,3},{3,7},{7,5},{5,1},{8,10},{10,14},{14... | collective-permute-start | bytes 786440 | tf_op jit(solution)/shard_map/ppermute | solution.py:89
  198.8 8.7 %collective-permute-start.18 = (bf16[2,256,256]{1,2,0:T(8,128)(2,1)S(1)}, bf16[2,256,256]{1,2,0:T(8,128)(2,1)S(1)}, u32[]{:S(2)}, u32[]{:S(2)}) collective-permute-start(bf16[2,256,256]{1,2,0:T(8,128)(2,1)S(1)} %slice.68), channel_id=1, source_target_pairs={{0,2},{2,6},{6,4},{4,0},{1,3},{3,7},{7,5},{5,1},{8,10},{10,14},{14... | collective-permute-start | bytes 786440 | tf_op jit(solution)/shard_map/ppermute | solution.py:89
  200.3 7.2 %collective-permute-start.17 = (bf16[1,2,1,256,256]{3,4,1,2,0:T(8,128)(2,1)S(1)}, bf16[1,2,1,256,256]{3,4,1,2,0:T(8,128)(2,1)S(1)}, u32[]{:S(2)}, u32[]{:S(2)}) collective-permute-start(bf16[1,2,1,256,256]{3,4,1,2,0:T(8,128)(2,1)S(1)} %bitcast.127), channel_id=1, source_target_pairs={{0,16},{8,24},{16,0},{24,8},{1,17},{9,25},{17,1},{25,9},{2,18},{10... | collective-permute-start | bytes 786440 | tf_op jit(solution)/shard_map/ppermute | solution.py:19
  207.6 7.7 %collective-permute-start.20 = (bf16[2,256,256]{1,2,0:T(8,128)(2,1)S(1)}, bf16[2,256,256]{1,2,0:T(8,128)(2,1)S(1)}, u32[]{:S(2)}, u32[]{:S(2)}) collective-permute-start(bf16[2,256,256]{1,2,0:T(8,128)(2,1)S(1)} %slice.70), channel_id=1, source_target_pairs={{0,2},{2,6},{6,4},{4,0},{1,3},{3,7},{7,5},{5,1},{8,10},{10,14},{14... | collective-permute-start | bytes 786440 | tf_op jit(solution)/shard_map/ppermute | solution.py:89
  208.3 7.1 %collective-permute-start.19 = (bf16[1,2,1,256,256]{3,4,1,2,0:T(8,128)(2,1)S(1)}, bf16[1,2,1,256,256]{3,4,1,2,0:T(8,128)(2,1)S(1)}, u32[]{:S(2)}, u32[]{:S(2)}) collective-permute-start(bf16[1,2,1,256,256]{3,4,1,2,0:T(8,128)(2,1)S(1)} %bitcast.128), channel_id=1, source_target_pairs={{0,16},{8,24},{16,0},{24,8},{1,17},{9,25},{17,1},{25,9},{2,18},{10... | collective-permute-start | bytes 786440 | tf_op jit(solution)/shard_map/ppermute | solution.py:19
  215.4 9.6 %collective-permute-start.22 = (bf16[3,256,256]{1,2,0:T(8,128)(2,1)S(1)}, bf16[3,256,256]{1,2,0:T(8,128)(2,1)S(1)}, u32[]{:S(2)}, u32[]{:S(2)}) collective-permute-start(bf16[3,256,256]{1,2,0:T(8,128)(2,1)S(1)} %slice.72), channel_id=1, source_target_pairs={{0,2},{2,6},{6,4},{4,0},{1,3},{3,7},{7,5},{5,1},{8,10},{10,14},{14... | collective-permute-start | bytes 1179656 | tf_op jit(solution)/shard_map/ppermute | solution.py:89
  216.5 6.4 %collective-permute-start.21 = (bf16[1,2,1,256,256]{3,4,1,2,0:T(8,128)(2,1)S(1)}, bf16[1,2,1,256,256]{3,4,1,2,0:T(8,128)(2,1)S(1)}, u32[]{:S(2)}, u32[]{:S(2)}) collective-permute-start(bf16[1,2,1,256,256]{3,4,1,2,0:T(8,128)(2,1)S(1)} %bitcast.129), channel_id=1, source_target_pairs={{0,16},{8,24},{16,0},{24,8},{1,17},{9,25},{17,1},{25,9},{2,18},{10... | collective-permute-start | bytes 786440 | tf_op jit(solution)/shard_map/ppermute | solution.py:19
  225.2 7.8 %collective-permute-start.23 = (bf16[1,3,1,256,256]{3,4,1,2,0:T(8,128)(2,1)S(1)}, bf16[1,3,1,256,256]{3,4,1,2,0:T(8,128)(2,1)S(1)}, u32[]{:S(2)}, u32[]{:S(2)}) collective-permute-start(bf16[1,3,1,256,256]{3,4,1,2,0:T(8,128)(2,1)S(1)} %fusion.38), channel_id=1, source_target_pairs={{0,16},{8,24},{16,0},{24,8},{1,17},{9,25},{17,1},{25,9},{2,18},{10... | collective-permute-start | bytes 1179656 | tf_op jit(solution)/shard_map/ppermute | solution.py:19
  (10 other events, 125.9 us)

commit v15 on v12

--- a/solution.py
+++ b/solution.py
@@ -72,21 +72,22 @@
     got_middle = middle_right + middle_left
     keep_right = jnp.where(sector == 1, zero, one)
     keep_left = jnp.where(sector == 2, zero, one)
-    send = third.astype(f32) + (1 - keep_right) * got_right.astype(f32)
-    send = send + (1 - keep_left) * got_left.astype(f32)
-    send = send.astype(jnp.bfloat16)
     own = term(gathered, ket[0], bra[0], mpo[:, :, 0])
     total = own.astype(f32) + keep_right * got_right.astype(f32)
     total = total + keep_left * got_left.astype(f32) + got_middle.astype(f32)
-    width = send.shape[0]
+    width = third.shape[0]
     bounds = [width * k // pieces for k in range(pieces + 1)]
     results = []
     piece = None
     for low, high in zip(bounds[:-1], bounds[1:]):
+        send = third[low:high].astype(f32)
+        send = send + (1 - keep_right) * got_right[low:high].astype(f32)
+        send = send + (1 - keep_left) * got_left[low:high].astype(f32)
+        send = send.astype(jnp.bfloat16)
         if results:
             piece, send = lax.optimization_barrier((piece, send))
             results[-1] = finish(piece)
-        got_last = lax.ppermute(send[low:high], "sector", LAST)
+        got_last = lax.ppermute(send, "sector", LAST)
         if results:
             results[-1], got_last = lax.optimization_barrier((results[-1], got_last))
         piece = total[low:high] + got_last.astype(f32)

time: 234 us -> 233 us (level)
  other arithmetic: 11.9 us -> 16.2 us
    ppermute x5, waiting for transfers between devices: 47.2 us -> 29.2 us  [advance_line(): got_last = lax.ppermute(send, 'sector', LAST)]
    ppermute x9, waiting for transfers between devices: 10.4 us -> 26.2 us  [shifted(): return lax.ppermute(value, axis, pairs)]
    add x0 -> x1, other arithmetic: none -> 3.18 us  [advance_line(): total = total + keep_left * got_left.astype(f32) + got_middle.astype(f32)]
    convert_element_type x2 -> x3, other arithmetic: 5.82 us -> 5.99 us  [advance_line(): send = send.astype(jnp.bfloat16)]
  transfers between devices with their start and end apart: 22 -> 22, of which waited for: 13 -> 15; matrix products, arithmetic and copies ran while one was open for 22% -> 24% of each run, Pallas kernels for 0% -> 0%
where the time goes in v15:
time: 233 us
  waiting for transfers between devices  105 us (45%)
  matrix products  50.8 us (22%)
  starting transfers between devices  45.3 us (19%)
  other arithmetic  16.2 us (7%)
  local copies, waits for them, and re-layouts  8.72 us (4%)
  between operations  6.77 us (3%)
    ppermute x2, waiting for transfers between devices, advance_line(): got_right = lax.ppermute(slot_a, 'sector', RIGHT)  40.4 us
    ppermute x5, waiting for transfers between devices, advance_line(): got_last = lax.ppermute(send, 'sector', LAST)  29.2 us
    dot_general x8, matrix products, term(): jnp.einsum('bd,vbc->vdc', bra_p, rotated, preferred_element_type=jnp.floa...  28.9 us
    ppermute x9, waiting for transfers between devices, shifted(): return lax.ppermute(value, axis, pairs)  26.2 us
    dot_general x8, matrix products, term(): jnp.einsum('wv,wba->vba', mpo_p, gathered, preferred_element_type=jnp.flo...  21.8 us
    ppermute x2, starting transfers between devices, advance_line(): got_right = lax.ppermute(slot_a, 'sector', RIGHT)  10.6 us
    ppermute x5, starting transfers between devices, advance_line(): got_last = lax.ppermute(send, 'sector', LAST)  9.9 us
    ppermute x9, starting transfers between devices, shifted(): return lax.ppermute(value, axis, pairs)  9.81 us
  transfers between devices with their start and end apart: 22, of which 15 were waited for; matrix products, arithmetic and copies ran while one was open for 24% of the time, Pallas kernels for 0%

profile of v15, /device:TPU:0, one launch (start us, length us, event | category | flops | bytes accessed | tf_op | source)
XLA Modules:
  0.0 232.6 jit_solution(7358192483909776597)
XLA Ops:
  3.0 3.5 %collective-permute-start.2 = (bf16[18,9,4]{1,2,0:T(4,128)(2,1)S(1)}, bf16[18,9,4]{1,2,0:T(4,128)(2,1)S(1)}, u32[]{:S(2)}, u32[]{:S(2)}) collective-permute-start(bf16[18,9,4]{1,2,0:T(4,128)(2,1)S(1)} %bitcast.132), channel_id=1, source_target_pairs={{0,24},{8,0},{16,8},{24,16},{1,25},{9,1},{17,9},{25,17},{2,26},{10... | collective-permute-start | bytes 3896 | tf_op jit(solution)/shard_map/ppermute | solution.py:19
  22.3 3.6 %fusion.13 = bf16[9,256,256]{1,2,0:T(8,128)(2,1)} fusion(bf16[9,256,256]{2,0,1:T(8,128)(2,1)} %fusion.2, bf16[1,1,4,256,256]{4,3,2,1,0:T(8,128)(2,1)} %param.15, s32[]{:T(128)S(6)} %select_n.81, bf16[1,1,4,256,256]{4,3,2,1,0:T(8,128)(2,1)} %param.14), kind=kOutput, calls=%fused_computation.43 | convolution fusion | flops 605159424 | bytes 3539968 | tf_op jit(solution)/shard_map/bd,vbc->vdc/dot_general | solution.py:29
  25.9 5.5 %collective-permute-start.6 = (bf16[9,256,256]{1,2,0:T(8,128)(2,1)}, bf16[9,256,256]{1,2,0:T(8,128)(2,1)}, u32[]{:S(2)}, u32[]{:S(2)}) collective-permute-start(bf16[9,256,256]{1,2,0:T(8,128)(2,1)} %fusion.13), channel_id=1, source_target_pairs={{0,4},{1,5},{8,12},{9,13},{16,20},{17,21},{24,28},{25,29}} | collective-permute-start | bytes 3538952 | tf_op jit(solution)/shard_map/ppermute | solution.py:68
  36.1 3.6 %fusion.12 = bf16[9,256,256]{1,2,0:T(8,128)(2,1)} fusion(bf16[9,256,256]{2,0,1:T(8,128)(2,1)} %fusion.6, bf16[1,1,4,256,256]{4,3,2,1,0:T(8,128)(2,1)} %param.15, s32[]{:T(128)S(6)} %select_n.78, bf16[1,1,4,256,256]{4,3,2,1,0:T(8,128)(2,1)} %param.14), kind=kOutput, calls=%fused_computation.42 | convolution fusion | flops 605159424 | bytes 3539968 | tf_op jit(solution)/shard_map/bd,vbc->vdc/dot_general | solution.py:29
  41.5 5.2 %collective-permute-start.4 = (bf16[9,256,256]{1,2,0:T(8,128)(2,1)}, bf16[9,256,256]{1,2,0:T(8,128)(2,1)}, u32[]{:S(2)}, u32[]{:S(2)}) collective-permute-start(bf16[9,256,256]{1,2,0:T(8,128)(2,1)} %fusion.12), channel_id=1, source_target_pairs={{0,2},{2,4},{4,6},{1,3},{3,5},{5,7},{8,10},{10,12},{12,14},{9,11},... | collective-permute-start | bytes 3538952 | tf_op jit(solution)/shard_map/ppermute | solution.py:64
  50.0 3.7 %fusion.14 = bf16[9,256,256]{1,2,0:T(8,128)(2,1)} fusion(bf16[9,256,256]{2,0,1:T(8,128)(2,1)} %fusion, bf16[1,1,4,256,256]{4,3,2,1,0:T(8,128)(2,1)} %param.15, s32[]{:T(128)S(6)} %select_n.82, bf16[1,1,4,256,256]{4,3,2,1,0:T(8,128)(2,1)} %param.14), kind=kOutput, calls=%fused_computation.44 | convolution fusion | flops 605159424 | bytes 3539968 | tf_op jit(solution)/shard_map/bd,vbc->vdc/dot_general | solution.py:29
  60.9 20.2 %collective-permute-done.4 = bf16[9,256,256]{1,2,0:T(8,128)(2,1)} collective-permute-done((bf16[9,256,256]{1,2,0:T(8,128)(2,1)}, bf16[9,256,256]{1,2,0:T(8,128)(2,1)}, u32[]{:S(2)}, u32[]{:S(2)}) %collective-permute-start.4) | collective-permute-done | bytes 1179680 | tf_op jit(solution)/shard_map/ppermute | solution.py:64
  82.6 3.8 %collective-permute-start.8 = (bf16[4,256,256]{1,2,0:T(8,128)(2,1)S(1)}, bf16[4,256,256]{1,2,0:T(8,128)(2,1)S(1)}, u32[]{:S(2)}, u32[]{:S(2)}) collective-permute-start(bf16[4,256,256]{1,2,0:T(8,128)(2,1)S(1)} %add_convert_fusion.1), channel_id=1, source_target_pairs={{0,2},{2,6},{6,4},{4,0},{1,3},{3,7},{7,5},{5,1},{8,10},{10,14},{14... | collective-permute-start | bytes 1572872 | tf_op jit(solution)/shard_map/ppermute | solution.py:90
  91.2 6.9 %collective-permute-done.8 = bf16[4,256,256]{1,2,0:T(8,128)(2,1)S(1)} collective-permute-done((bf16[4,256,256]{1,2,0:T(8,128)(2,1)S(1)}, bf16[4,256,256]{1,2,0:T(8,128)(2,1)S(1)}, u32[]{:S(2)}, u32[]{:S(2)}) %collective-permute-start.8) | collective-permute-done | bytes 524320 | tf_op jit(solution)/shard_map/ppermute | solution.py:90
  101.0 14.2 %collective-permute-done.10 = bf16[5,256,256]{1,2,0:T(8,128)(2,1)S(1)} collective-permute-done((bf16[5,256,256]{1,2,0:T(8,128)(2,1)S(1)}, bf16[5,256,256]{1,2,0:T(8,128)(2,1)S(1)}, u32[]{:S(2)}, u32[]{:S(2)}) %collective-permute-start.10) | collective-permute-done | bytes 655392 | tf_op jit(solution)/shard_map/ppermute | solution.py:90
  119.4 3.7 %copy.30 = bf16[18,256,256]{2,0,1:T(8,128)(2,1)S(1)} copy(bf16[18,256,256]{1,2,0:T(8,128)(2,1)} %pad_maximum_fusion.1) | data formatting | bytes 4718592 | tf_op jit(solution)/shard_map/concatenate | solution.py:45
  125.1 3.6 %fusion.16 = bf16[9,256,256]{1,2,0:T(8,128)(2,1)} fusion(bf16[9,256,256]{2,0,1:T(8,128)(2,1)} %fusion.81, bf16[4,256,256]{2,1,0:T(8,128)(2,1)} %copy-done.3, s32[]{:T(128)S(6)} %select_n.81, bf16[4,256,256]{2,1,0:T(8,128)(2,1)} %collective-permute-done), kind=kOutput, calls=%fused_computation.46 | convolution fusion | flops 605159424 | bytes 3539968 | tf_op jit(solution)/shard_map/bd,vbc->vdc/dot_general | solution.py:29
  135.6 3.6 %fusion.15 = bf16[9,256,256]{1,2,0:T(8,128)(2,1)} fusion(bf16[9,256,256]{2,0,1:T(8,128)(2,1)} %fusion.83, bf16[4,256,256]{2,1,0:T(8,128)(2,1)} %copy-done.3, s32[]{:T(128)S(6)} %select_n.78, bf16[4,256,256]{2,1,0:T(8,128)(2,1)} %collective-permute-done), kind=kOutput, calls=%fused_computation.45 | convolution fusion | flops 605159424 | bytes 3539968 | tf_op jit(solution)/shard_map/bd,vbc->vdc/dot_general | solution.py:29
  140.9 5.4 %collective-permute-start.12 = (bf16[9,256,256]{1,2,0:T(8,128)(2,1)}, bf16[9,256,256]{1,2,0:T(8,128)(2,1)}, u32[]{:S(2)}, u32[]{:S(2)}) collective-permute-start(bf16[9,256,256]{1,2,0:T(8,128)(2,1)} %fusion.15), channel_id=1, source_target_pairs={{0,2},{2,4},{4,6},{1,3},{3,5},{5,7},{8,10},{10,12},{12,14},{9,11},... | collective-permute-start | bytes 3538952 | tf_op jit(solution)/shard_map/ppermute | solution.py:64
  148.4 3.7 %fusion.17 = bf16[9,256,256]{1,2,0:T(8,128)(2,1)} fusion(bf16[9,256,256]{2,0,1:T(8,128)(2,1)} %fusion.79, bf16[4,256,256]{2,1,0:T(8,128)(2,1)} %copy-done.3, s32[]{:T(128)S(6)} %select_n.82, bf16[4,256,256]{2,1,0:T(8,128)(2,1)} %collective-permute-done), kind=kOutput, calls=%fused_computation.47 | convolution fusion | flops 605159424 | bytes 3539968 | tf_op jit(solution)/shard_map/bd,vbc->vdc/dot_general | solution.py:29
  154.2 3.6 %collective-permute-done.14 = bf16[9,256,256]{1,2,0:T(8,128)(2,1)} collective-permute-done((bf16[9,256,256]{1,2,0:T(8,128)(2,1)}, bf16[9,256,256]{1,2,0:T(8,128)(2,1)}, u32[]{:S(2)}, u32[]{:S(2)}) %collective-permute-start.14) | collective-permute-done | bytes 1179680 | tf_op jit(solution)/shard_map/ppermute | solution.py:68
  157.9 4.3 %collective-permute-done.13 = bf16[9,256,256]{1,2,0:T(8,128)(2,1)} collective-permute-done((bf16[9,256,256]{1,2,0:T(8,128)(2,1)}, bf16[9,256,256]{1,2,0:T(8,128)(2,1)}, u32[]{:S(2)}, u32[]{:S(2)}) %collective-permute-start.13) | collective-permute-done | bytes 1179680 | tf_op jit(solution)/shard_map/ppermute | solution.py:67
  162.1 20.2 %collective-permute-done.12 = bf16[9,256,256]{1,2,0:T(8,128)(2,1)} collective-permute-done((bf16[9,256,256]{1,2,0:T(8,128)(2,1)}, bf16[9,256,256]{1,2,0:T(8,128)(2,1)}, u32[]{:S(2)}, u32[]{:S(2)}) %collective-permute-start.12) | collective-permute-done | bytes 1179680 | tf_op jit(solution)/shard_map/ppermute | solution.py:64
  185.3 3.7 %collective-permute-start.16 = (bf16[3,256,256]{1,2,0:T(8,128)(2,1)}, bf16[3,256,256]{1,2,0:T(8,128)(2,1)}, u32[]{:S(2)}, u32[]{:S(2)}) collective-permute-start(bf16[3,256,256]{1,2,0:T(8,128)(2,1)} %get-tuple-element.64), channel_id=1, source_target_pairs={{0,2},{2,6},{6,4},{4,0},{1,3},{3,7},{7,5},{5,1},{8,10},{10,14},{14... | collective-permute-start | bytes 1179656 | tf_op jit(solution)/shard_map/ppermute | solution.py:90
  189.0 4.4 %fusion.9 = f32[9,256,256]{1,2,0:T(8,128)S(1)} fusion(bf16[9,256,256]{1,2,0:T(8,128)(2,1)} %collective-permute-done.13, bf16[9,256,256]{1,2,0:T(8,128)(2,1)} %collective-permute-done.12, bf16[9,256,256]{1,2,0:T(8,128)(2,1)} %collective-permute-done.14, bf16[9,256,256]{1,2,0:T(8,128)(2,1)} %collective-permute-done.15, f32[]{:T(128)S(6)} %select_n.83, ...), kind=kOutput, calls=%fused_computation.14 | convolution fusion | flops 612237312 | bytes 9437192 | tf_op jit(solution)/shard_map/bd,vbc->vdc/dot_general | solution.py:29
  193.4 4.8 %collective-permute-done.16 = bf16[3,256,256]{1,2,0:T(8,128)(2,1)} collective-permute-done((bf16[3,256,256]{1,2,0:T(8,128)(2,1)}, bf16[3,256,256]{1,2,0:T(8,128)(2,1)}, u32[]{:S(2)}, u32[]{:S(2)}) %collective-permute-start.16) | collective-permute-done | bytes 393248 | tf_op jit(solution)/shard_map/ppermute | solution.py:90
  202.3 7.6 %collective-permute-done.17 = bf16[1,3,1,256,256]{3,4,1,2,0:T(8,128)(2,1)S(1)} collective-permute-done((bf16[1,3,1,256,256]{3,4,1,2,0:T(8,128)(2,1)S(1)}, bf16[1,3,1,256,256]{3,4,1,2,0:T(8,128)(2,1)S(1)}, u32[]{:S(2)}, u32[]{:S(2)}) %collective-permute-start.17) | collective-permute-done | bytes 393248 | tf_op jit(solution)/shard_map/ppermute | solution.py:19
  212.7 8.8 %collective-permute-done.19 = bf16[1,3,1,256,256]{3,4,1,2,0:T(8,128)(2,1)S(1)} collective-permute-done((bf16[1,3,1,256,256]{3,4,1,2,0:T(8,128)(2,1)S(1)}, bf16[1,3,1,256,256]{3,4,1,2,0:T(8,128)(2,1)S(1)}, u32[]{:S(2)}, u32[]{:S(2)}) %collective-permute-start.19) | collective-permute-done | bytes 393248 | tf_op jit(solution)/shard_map/ppermute | solution.py:19
  224.3 6.6 %collective-permute-done.21 = bf16[1,3,1,256,256]{3,4,1,2,0:T(8,128)(2,1)S(1)} collective-permute-done((bf16[1,3,1,256,256]{3,4,1,2,0:T(8,128)(2,1)S(1)}, bf16[1,3,1,256,256]{3,4,1,2,0:T(8,128)(2,1)S(1)}, u32[]{:S(2)}, u32[]{:S(2)}) %collective-permute-start.21) | collective-permute-done | bytes 393248 | tf_op jit(solution)/shard_map/ppermute | solution.py:19
  (83 shorter events, 71.5 us)
Async XLA Ops:
  2.4 14.8 %collective-permute-start.3 = (bf16[9,256,256]{2,1,0:T(8,128)(2,1)S(1)}, bf16[9,256,256]{2,1,0:T(8,128)(2,1)}, u32[]{:S(2)}, u32[]{:S(2)}) collective-permute-start(bf16[9,256,256]{2,1,0:T(8,128)(2,1)S(1)} %bitcast_select_fusion), channel_id=1, source_target_pairs={{0,1},{1,0},{2,3},{3,2},{4,5},{5,4},{6,7},{7,6},{8,9},{9,8},{10,11... | collective-permute-start | bytes 3538952 | tf_op jit(solution)/shard_map/ppermute | solution.py:19
  3.0 36.8 %collective-permute-start.2 = (bf16[18,9,4]{1,2,0:T(4,128)(2,1)S(1)}, bf16[18,9,4]{1,2,0:T(4,128)(2,1)S(1)}, u32[]{:S(2)}, u32[]{:S(2)}) collective-permute-start(bf16[18,9,4]{1,2,0:T(4,128)(2,1)S(1)} %bitcast.132), channel_id=1, source_target_pairs={{0,24},{8,0},{16,8},{24,16},{1,25},{9,1},{17,9},{25,17},{2,26},{10... | collective-permute-start | bytes 3896 | tf_op jit(solution)/shard_map/ppermute | solution.py:19
  6.5 33.3 %collective-permute-start.1 = (bf16[4,256,256]{2,1,0:T(8,128)(2,1)}, bf16[4,256,256]{2,1,0:T(8,128)(2,1)S(1)}, u32[]{:S(2)}, u32[]{:S(2)}) collective-permute-start(bf16[4,256,256]{2,1,0:T(8,128)(2,1)} %bitcast.1), channel_id=1, source_target_pairs={{0,24},{8,0},{16,8},{24,16},{1,25},{9,1},{17,9},{25,17},{2,26},{10... | collective-permute-start | bytes 1572872 | tf_op jit(solution)/shard_map/ppermute | solution.py:19
  7.1 32.7 %collective-permute-start = (bf16[4,256,256]{2,1,0:T(8,128)(2,1)}, bf16[4,256,256]{2,1,0:T(8,128)(2,1)}, u32[]{:S(2)}, u32[]{:S(2)}) collective-permute-start(bf16[4,256,256]{2,1,0:T(8,128)(2,1)} %bitcast), channel_id=1, source_target_pairs={{0,24},{8,0},{16,8},{24,16},{1,25},{9,1},{17,9},{25,17},{2,26},{10... | collective-permute-start | bytes 1572872 | tf_op jit(solution)/shard_map/ppermute | solution.py:19
  25.9 33.8 %collective-permute-start.6 = (bf16[9,256,256]{1,2,0:T(8,128)(2,1)}, bf16[9,256,256]{1,2,0:T(8,128)(2,1)}, u32[]{:S(2)}, u32[]{:S(2)}) collective-permute-start(bf16[9,256,256]{1,2,0:T(8,128)(2,1)} %fusion.13), channel_id=1, source_target_pairs={{0,4},{1,5},{8,12},{9,13},{16,20},{17,21},{24,28},{25,29}} | collective-permute-start | bytes 3538952 | tf_op jit(solution)/shard_map/ppermute | solution.py:68
  31.5 29.4 %collective-permute-start.5 = (bf16[9,256,256]{1,2,0:T(8,128)(2,1)}, bf16[9,256,256]{1,2,0:T(8,128)(2,1)}, u32[]{:S(2)}, u32[]{:S(2)}) collective-permute-start(bf16[9,256,256]{1,2,0:T(8,128)(2,1)} %fusion.13), channel_id=1, source_target_pairs={{6,4},{4,2},{2,0},{7,5},{5,3},{3,1},{14,12},{12,10},{10,8},{15,13}... | collective-permute-start | bytes 3538952 | tf_op jit(solution)/shard_map/ppermute | solution.py:67
  39.8 21.1 %collective-permute-start.7 = (bf16[9,256,256]{1,2,0:T(8,128)(2,1)}, bf16[9,256,256]{1,2,0:T(8,128)(2,1)}, u32[]{:S(2)}, u32[]{:S(2)}) collective-permute-start(bf16[9,256,256]{1,2,0:T(8,128)(2,1)} %fusion.12), channel_id=1, source_target_pairs={{6,2},{7,3},{14,10},{15,11},{22,18},{23,19},{30,26},{31,27}} | collective-permute-start | bytes 3538952 | tf_op jit(solution)/shard_map/ppermute | solution.py:65
  41.5 39.6 %collective-permute-start.4 = (bf16[9,256,256]{1,2,0:T(8,128)(2,1)}, bf16[9,256,256]{1,2,0:T(8,128)(2,1)}, u32[]{:S(2)}, u32[]{:S(2)}) collective-permute-start(bf16[9,256,256]{1,2,0:T(8,128)(2,1)} %fusion.12), channel_id=1, source_target_pairs={{0,2},{2,4},{4,6},{1,3},{3,5},{5,7},{8,10},{10,12},{12,14},{9,11},... | collective-permute-start | bytes 3538952 | tf_op jit(solution)/shard_map/ppermute | solution.py:64
  57.1 24.0 %copy-start.2 = (bf16[9,256,256]{1,2,0:T(8,128)(2,1)S(1)}, bf16[9,256,256]{1,2,0:T(8,128)(2,1)}, u32[]{:S(2)}) copy-start(bf16[9,256,256]{1,2,0:T(8,128)(2,1)} %fusion.14) | copy-start | bytes 3538948
  82.6 15.5 %collective-permute-start.8 = (bf16[4,256,256]{1,2,0:T(8,128)(2,1)S(1)}, bf16[4,256,256]{1,2,0:T(8,128)(2,1)S(1)}, u32[]{:S(2)}, u32[]{:S(2)}) collective-permute-start(bf16[4,256,256]{1,2,0:T(8,128)(2,1)S(1)} %add_convert_fusion.1), channel_id=1, source_target_pairs={{0,2},{2,6},{6,4},{4,0},{1,3},{3,7},{7,5},{5,1},{8,10},{10,14},{14... | collective-permute-start | bytes 1572872 | tf_op jit(solution)/shard_map/ppermute | solution.py:90
  98.2 17.1 %collective-permute-start.10 = (bf16[5,256,256]{1,2,0:T(8,128)(2,1)S(1)}, bf16[5,256,256]{1,2,0:T(8,128)(2,1)S(1)}, u32[]{:S(2)}, u32[]{:S(2)}) collective-permute-start(bf16[5,256,256]{1,2,0:T(8,128)(2,1)S(1)} %add_convert_fusion), channel_id=1, source_target_pairs={{0,2},{2,6},{6,4},{4,0},{1,3},{3,7},{7,5},{5,1},{8,10},{10,14},{14... | collective-permute-start | bytes 1966088 | tf_op jit(solution)/shard_map/ppermute | solution.py:90
  99.1 1.9 collective-permute-start.9
  115.5 2.2 collective-permute-start.11
  128.8 29.1 %collective-permute-start.14 = (bf16[9,256,256]{1,2,0:T(8,128)(2,1)}, bf16[9,256,256]{1,2,0:T(8,128)(2,1)}, u32[]{:S(2)}, u32[]{:S(2)}) collective-permute-start(bf16[9,256,256]{1,2,0:T(8,128)(2,1)} %fusion.16), channel_id=1, source_target_pairs={{0,4},{1,5},{8,12},{9,13},{16,20},{17,21},{24,28},{25,29}} | collective-permute-start | bytes 3538952 | tf_op jit(solution)/shard_map/ppermute | solution.py:68
  132.2 29.9 %collective-permute-start.13 = (bf16[9,256,256]{1,2,0:T(8,128)(2,1)}, bf16[9,256,256]{1,2,0:T(8,128)(2,1)}, u32[]{:S(2)}, u32[]{:S(2)}) collective-permute-start(bf16[9,256,256]{1,2,0:T(8,128)(2,1)} %fusion.16), channel_id=1, source_target_pairs={{6,4},{4,2},{2,0},{7,5},{5,3},{3,1},{14,12},{12,10},{10,8},{15,13}... | collective-permute-start | bytes 3538952 | tf_op jit(solution)/shard_map/ppermute | solution.py:67
  139.2 22.9 %collective-permute-start.15 = (bf16[9,256,256]{1,2,0:T(8,128)(2,1)}, bf16[9,256,256]{1,2,0:T(8,128)(2,1)}, u32[]{:S(2)}, u32[]{:S(2)}) collective-permute-start(bf16[9,256,256]{1,2,0:T(8,128)(2,1)} %fusion.15), channel_id=1, source_target_pairs={{6,2},{7,3},{14,10},{15,11},{22,18},{23,19},{30,26},{31,27}} | collective-permute-start | bytes 3538952 | tf_op jit(solution)/shard_map/ppermute | solution.py:65
  140.9 41.4 %collective-permute-start.12 = (bf16[9,256,256]{1,2,0:T(8,128)(2,1)}, bf16[9,256,256]{1,2,0:T(8,128)(2,1)}, u32[]{:S(2)}, u32[]{:S(2)}) collective-permute-start(bf16[9,256,256]{1,2,0:T(8,128)(2,1)} %fusion.15), channel_id=1, source_target_pairs={{0,2},{2,4},{4,6},{1,3},{3,5},{5,7},{8,10},{10,12},{12,14},{9,11},... | collective-permute-start | bytes 3538952 | tf_op jit(solution)/shard_map/ppermute | solution.py:64
  152.1 30.2 %copy-start.1 = (bf16[9,256,256]{1,2,0:T(8,128)(2,1)S(1)}, bf16[9,256,256]{1,2,0:T(8,128)(2,1)}, u32[]{:S(2)}) copy-start(bf16[9,256,256]{1,2,0:T(8,128)(2,1)} %fusion.17) | copy-start | bytes 3538948
  185.3 12.9 %collective-permute-start.16 = (bf16[3,256,256]{1,2,0:T(8,128)(2,1)}, bf16[3,256,256]{1,2,0:T(8,128)(2,1)}, u32[]{:S(2)}, u32[]{:S(2)}) collective-permute-start(bf16[3,256,256]{1,2,0:T(8,128)(2,1)} %get-tuple-element.64), channel_id=1, source_target_pairs={{0,2},{2,6},{6,4},{4,0},{1,3},{3,7},{7,5},{5,1},{8,10},{10,14},{14... | collective-permute-start | bytes 1179656 | tf_op jit(solution)/shard_map/ppermute | solution.py:90
  199.3 10.6 %collective-permute-start.17 = (bf16[1,3,1,256,256]{3,4,1,2,0:T(8,128)(2,1)S(1)}, bf16[1,3,1,256,256]{3,4,1,2,0:T(8,128)(2,1)S(1)}, u32[]{:S(2)}, u32[]{:S(2)}) collective-permute-start(bf16[1,3,1,256,256]{3,4,1,2,0:T(8,128)(2,1)S(1)} %bitcast.135), channel_id=1, source_target_pairs={{0,16},{8,24},{16,0},{24,8},{1,17},{9,25},{17,1},{25,9},{2,18},{10... | collective-permute-start | bytes 1179656 | tf_op jit(solution)/shard_map/ppermute | solution.py:19
  200.9 11.1 %collective-permute-start.18 = (bf16[3,256,256]{1,2,0:T(8,128)(2,1)S(1)}, bf16[3,256,256]{1,2,0:T(8,128)(2,1)S(1)}, u32[]{:S(2)}, u32[]{:S(2)}) collective-permute-start(bf16[3,256,256]{1,2,0:T(8,128)(2,1)S(1)} %get-tuple-element.53), channel_id=1, source_target_pairs={{0,2},{2,6},{6,4},{4,0},{1,3},{3,7},{7,5},{5,1},{8,10},{10,14},{14... | collective-permute-start | bytes 1179656 | tf_op jit(solution)/shard_map/ppermute | solution.py:90
  212.1 9.4 %collective-permute-start.19 = (bf16[1,3,1,256,256]{3,4,1,2,0:T(8,128)(2,1)S(1)}, bf16[1,3,1,256,256]{3,4,1,2,0:T(8,128)(2,1)S(1)}, u32[]{:S(2)}, u32[]{:S(2)}) collective-permute-start(bf16[1,3,1,256,256]{3,4,1,2,0:T(8,128)(2,1)S(1)} %bitcast.134), channel_id=1, source_target_pairs={{0,16},{8,24},{16,0},{24,8},{1,17},{9,25},{17,1},{25,9},{2,18},{10... | collective-permute-start | bytes 1179656 | tf_op jit(solution)/shard_map/ppermute | solution.py:19
  212.7 9.9 %collective-permute-start.20 = (bf16[3,256,256]{1,2,0:T(8,128)(2,1)S(1)}, bf16[3,256,256]{1,2,0:T(8,128)(2,1)S(1)}, u32[]{:S(2)}, u32[]{:S(2)}) collective-permute-start(bf16[3,256,256]{1,2,0:T(8,128)(2,1)S(1)} %get-tuple-element.57), channel_id=1, source_target_pairs={{0,2},{2,6},{6,4},{4,0},{1,3},{3,7},{7,5},{5,1},{8,10},{10,14},{14... | collective-permute-start | bytes 1179656 | tf_op jit(solution)/shard_map/ppermute | solution.py:90
  222.7 8.2 %collective-permute-start.21 = (bf16[1,3,1,256,256]{3,4,1,2,0:T(8,128)(2,1)S(1)}, bf16[1,3,1,256,256]{3,4,1,2,0:T(8,128)(2,1)S(1)}, u32[]{:S(2)}, u32[]{:S(2)}) collective-permute-start(bf16[1,3,1,256,256]{3,4,1,2,0:T(8,128)(2,1)S(1)} %fusion.28), channel_id=1, source_target_pairs={{0,16},{8,24},{16,0},{24,8},{1,17},{9,25},{17,1},{25,9},{2,18},{10... | collective-permute-start | bytes 1179656 | tf_op jit(solution)/shard_map/ppermute | solution.py:19
  (6 other events, 59.0 us)

commit v16 on v15

--- a/solution.py
+++ b/solution.py
@@ -1,6 +1,7 @@
 import jax
 import jax.numpy as jnp
 from jax import lax
+from jax.experimental.layout import Layout, with_layout_constraint
 from jax.sharding import PartitionSpec as P
 
 STEPS = 2
@@ -92,6 +93,8 @@
             results[-1], got_last = lax.optimization_barrier((results[-1], got_last))
         piece = total[low:high] + got_last.astype(f32)
         piece = (piece * live_mask[None]).astype(jnp.bfloat16)
+        if finish is chan_copies:
+            piece = with_layout_constraint(piece, Layout((0, 1, 2)))
         results.append(None)
     results[-1] = finish(piece)
     return results, held

time: 233 us -> 229 us (0.983)
  matrix products: 50.8 us -> 56 us
  local copies, waits for them, and re-layouts: 8.72 us -> 4.08 us
  starting transfers between devices: 45.3 us -> 41.4 us
    ppermute x2, waiting for transfers between devices: 3.62 us -> 24.8 us  [advance_line(): middle_right = lax.ppermute(slot_b, 'sector', ((0, 2),))]
    ppermute x2, waiting for transfers between devices: 40.4 us -> 20.8 us  [advance_line(): got_right = lax.ppermute(slot_a, 'sector', RIGHT)]
    dot_general x8, matrix products: 21.8 us -> 27 us  [term(): jnp.einsum('wv,wba->vba', mpo_p, gathered, preferred_element_type=jnp.flo...]
    concatenate x2 -> x0, local copies, waits for them, and re-layouts: 5.21 us -> none  [the longest x1 3.68 us: chan_gathered(): return (jnp.concatenate(held, axis=0), jnp.take(mpo, order, axis=0))]
    ppermute x2, waiting for transfers between devices: 5.41 us -> 0.95 us  [advance_line(): got_left = lax.ppermute(slot_b, 'sector', LEFT)]
    ppermute x5, starting transfers between devices: 9.9 us -> 6.32 us  [advance_line(): got_last = lax.ppermute(send, 'sector', LAST)]
    ppermute x2, starting transfers between devices: 10.6 us -> 7.52 us  [advance_line(): got_right = lax.ppermute(slot_a, 'sector', RIGHT)]
    ppermute x2, starting transfers between devices: 8.98 us -> 11.8 us  [advance_line(): middle_right = lax.ppermute(slot_b, 'sector', ((0, 2),))]
  transfers between devices with their start and end apart: 22 -> 22, of which waited for: 15 -> 14; matrix products, arithmetic and copies ran while one was open for 24% -> 26% of each run, Pallas kernels for 0% -> 0%
where the time goes in v16:
time: 229 us
  waiting for transfers between devices  103 us (45%)
  matrix products  56 us (24%)
  starting transfers between devices  41.4 us (18%)
  other arithmetic  17.2 us (8%)
  between operations  6.47 us (3%)
  local copies, waits for them, and re-layouts  4.08 us (2%)
    ppermute x5, waiting for transfers between devices, advance_line(): got_last = lax.ppermute(send, 'sector', LAST)  30.3 us
    dot_general x8, matrix products, term(): jnp.einsum('bd,vbc->vdc', bra_p, rotated, preferred_element_type=jnp.floa...  29 us
    dot_general x8, matrix products, term(): jnp.einsum('wv,wba->vba', mpo_p, gathered, preferred_element_type=jnp.flo...  27 us
    ppermute x9, waiting for transfers between devices, shifted(): return lax.ppermute(value, axis, pairs)  26.4 us
    ppermute x2, waiting for transfers between devices, advance_line(): middle_right = lax.ppermute(slot_b, 'sector', ((0, 2),))  24.8 us
    ppermute x2, waiting for transfers between devices, advance_line(): got_right = lax.ppermute(slot_a, 'sector', RIGHT)  20.8 us
    ppermute x2, starting transfers between devices, advance_line(): middle_right = lax.ppermute(slot_b, 'sector', ((0, 2),))  11.8 us
    ppermute x9, starting transfers between devices, shifted(): return lax.ppermute(value, axis, pairs)  9.82 us
  transfers between devices with their start and end apart: 22, of which 14 were waited for; matrix products, arithmetic and copies ran while one was open for 26% of the time, Pallas kernels for 0%

profile of v16, /device:TPU:0, one launch (start us, length us, event | category | flops | bytes accessed | tf_op | source)
XLA Modules:
  0.0 228.5 jit_solution(697826904062445590)
XLA Ops:
  2.8 3.5 %collective-permute-start.2 = (bf16[18,9,4]{1,2,0:T(4,128)(2,1)S(1)}, bf16[18,9,4]{1,2,0:T(4,128)(2,1)S(1)}, u32[]{:S(2)}, u32[]{:S(2)}) collective-permute-start(bf16[18,9,4]{1,2,0:T(4,128)(2,1)S(1)} %bitcast.130), channel_id=1, source_target_pairs={{0,24},{8,0},{16,8},{24,16},{1,25},{9,1},{17,9},{25,17},{2,26},{10... | collective-permute-start | bytes 3896 | tf_op jit(solution)/shard_map/ppermute | solution.py:20
  18.4 3.4 %fusion.10 = bf16[9,256,256]{2,0,1:T(8,128)(2,1)} fusion(bf16[18,256,256]{2,1,0:T(8,128)(2,1)S(1)} %pad_maximum_fusion, bf16[18,9,1]{1,2,0:T(2,128)(2,1)S(1)} %get-tuple-element.70), kind=kOutput, calls=%fused_computation.12 | convolution fusion | flops 21233664 | bytes 3539268 | tf_op jit(solution)/shard_map/wv,wba->vba/dot_general | solution.py:24
  21.8 3.6 %fusion.21 = bf16[9,256,256]{2,1,0:T(8,128)(2,1)} fusion(bf16[9,256,256]{2,0,1:T(8,128)(2,1)} %fusion.10, bf16[1,1,4,256,256]{4,3,2,1,0:T(8,128)(2,1)} %param.15, s32[]{:T(128)S(6)} %select_n.81, bf16[1,1,4,256,256]{4,3,2,1,0:T(8,128)(2,1)} %param.14), kind=kOutput, calls=%fused_computation.51 | convolution fusion | flops 605159424 | bytes 3539968 | tf_op jit(solution)/shard_map/bd,vbc->vdc/dot_general | solution.py:30
  25.5 5.5 %collective-permute-start.6 = (bf16[9,256,256]{2,1,0:T(8,128)(2,1)}, bf16[9,256,256]{2,1,0:T(8,128)(2,1)}, u32[]{:S(2)}, u32[]{:S(2)}) collective-permute-start(bf16[9,256,256]{2,1,0:T(8,128)(2,1)} %fusion.21), channel_id=1, source_target_pairs={{0,4},{1,5},{8,12},{9,13},{16,20},{17,21},{24,28},{25,29}} | collective-permute-start | bytes 3538952 | tf_op jit(solution)/shard_map/ppermute | solution.py:69
  32.3 3.4 %fusion.14 = bf16[9,256,256]{2,0,1:T(8,128)(2,1)} fusion(bf16[18,256,256]{2,1,0:T(8,128)(2,1)S(1)} %pad_maximum_fusion, bf16[18,9,1]{1,2,0:T(2,128)(2,1)S(1)} %get-tuple-element.72), kind=kOutput, calls=%fused_computation.16 | convolution fusion | flops 21233664 | bytes 3539268 | tf_op jit(solution)/shard_map/wv,wba->vba/dot_general | solution.py:24
  35.6 3.7 %fusion.20 = bf16[9,256,256]{2,1,0:T(8,128)(2,1)} fusion(bf16[9,256,256]{2,0,1:T(8,128)(2,1)} %fusion.14, bf16[1,1,4,256,256]{4,3,2,1,0:T(8,128)(2,1)} %param.15, s32[]{:T(128)S(6)} %select_n.78, bf16[1,1,4,256,256]{4,3,2,1,0:T(8,128)(2,1)} %param.14), kind=kOutput, calls=%fused_computation.50 | convolution fusion | flops 605159424 | bytes 3539968 | tf_op jit(solution)/shard_map/bd,vbc->vdc/dot_general | solution.py:30
  41.1 5.2 %collective-permute-start.4 = (bf16[9,256,256]{2,1,0:T(8,128)(2,1)}, bf16[9,256,256]{2,1,0:T(8,128)(2,1)}, u32[]{:S(2)}, u32[]{:S(2)}) collective-permute-start(bf16[9,256,256]{2,1,0:T(8,128)(2,1)} %fusion.20), channel_id=1, source_target_pairs={{0,2},{2,4},{4,6},{1,3},{3,5},{5,7},{8,10},{10,12},{12,14},{9,11},... | collective-permute-start | bytes 3538952 | tf_op jit(solution)/shard_map/ppermute | solution.py:65
  49.6 3.7 %fusion.22 = bf16[9,256,256]{2,1,0:T(8,128)(2,1)} fusion(bf16[9,256,256]{2,0,1:T(8,128)(2,1)} %fusion.8, bf16[1,1,4,256,256]{4,3,2,1,0:T(8,128)(2,1)} %param.15, s32[]{:T(128)S(6)} %select_n.82, bf16[1,1,4,256,256]{4,3,2,1,0:T(8,128)(2,1)} %param.14), kind=kOutput, calls=%fused_computation.52 | convolution fusion | flops 605159424 | bytes 3539968 | tf_op jit(solution)/shard_map/bd,vbc->vdc/dot_general | solution.py:30
  60.4 20.2 %collective-permute-done.4 = bf16[9,256,256]{2,1,0:T(8,128)(2,1)} collective-permute-done((bf16[9,256,256]{2,1,0:T(8,128)(2,1)}, bf16[9,256,256]{2,1,0:T(8,128)(2,1)}, u32[]{:S(2)}, u32[]{:S(2)}) %collective-permute-start.4) | collective-permute-done | bytes 1179680 | tf_op jit(solution)/shard_map/ppermute | solution.py:65
  82.1 3.8 %collective-permute-start.8 = (bf16[4,256,256]{2,1,0:T(8,128)(2,1)S(1)}, bf16[4,256,256]{2,1,0:T(8,128)(2,1)S(1)}, u32[]{:S(2)}, u32[]{:S(2)}) collective-permute-start(bf16[4,256,256]{2,1,0:T(8,128)(2,1)S(1)} %add_convert_fusion.1), channel_id=1, source_target_pairs={{0,2},{2,6},{6,4},{4,0},{1,3},{3,7},{7,5},{5,1},{8,10},{10,14},{14... | collective-permute-start | bytes 1572872 | tf_op jit(solution)/shard_map/ppermute | solution.py:91
  90.7 6.9 %collective-permute-done.8 = bf16[4,256,256]{2,1,0:T(8,128)(2,1)S(1)} collective-permute-done((bf16[4,256,256]{2,1,0:T(8,128)(2,1)S(1)}, bf16[4,256,256]{2,1,0:T(8,128)(2,1)S(1)}, u32[]{:S(2)}, u32[]{:S(2)}) %collective-permute-start.8) | collective-permute-done | bytes 524320 | tf_op jit(solution)/shard_map/ppermute | solution.py:91
  101.4 13.4 %collective-permute-done.10 = bf16[5,256,256]{2,1,0:T(8,128)(2,1)S(1)} collective-permute-done((bf16[5,256,256]{2,1,0:T(8,128)(2,1)S(1)}, bf16[5,256,256]{2,1,0:T(8,128)(2,1)S(1)}, u32[]{:S(2)}, u32[]{:S(2)}) %collective-permute-start.10) | collective-permute-done | bytes 655392 | tf_op jit(solution)/shard_map/ppermute | solution.py:91
  119.0 3.4 %fusion.4 = bf16[9,256,256]{2,0,1:T(8,128)(2,1)} fusion(bf16[18,256,256]{2,1,0:T(8,128)(2,1)S(1)} %pad_maximum_fusion.1, bf16[18,9,1]{1,2,0:T(2,128)(2,1)S(1)} %get-tuple-element.68), kind=kOutput, calls=%fused_computation.6 | convolution fusion | flops 21233664 | bytes 3539268 | tf_op jit(solution)/shard_map/wv,wba->vba/dot_general | solution.py:24
  122.4 3.6 %fusion.23 = bf16[9,256,256]{2,1,0:T(8,128)(2,1)} fusion(bf16[9,256,256]{2,0,1:T(8,128)(2,1)} %fusion.4, bf16[4,256,256]{2,1,0:T(8,128)(2,1)S(1)} %copy-done.6, s32[]{:T(128)S(6)} %select_n.78, bf16[4,256,256]{2,1,0:T(8,128)(2,1)} %collective-permute-done), kind=kOutput, calls=%fused_computation.53 | convolution fusion | flops 605159424 | bytes 3539968 | tf_op jit(solution)/shard_map/bd,vbc->vdc/dot_general | solution.py:30
  133.4 3.6 %fusion.24 = bf16[9,256,256]{2,1,0:T(8,128)(2,1)} fusion(bf16[9,256,256]{2,0,1:T(8,128)(2,1)} %fusion.2, bf16[4,256,256]{2,1,0:T(8,128)(2,1)S(1)} %copy-done.6, s32[]{:T(128)S(6)} %select_n.81, bf16[4,256,256]{2,1,0:T(8,128)(2,1)} %collective-permute-done), kind=kOutput, calls=%fused_computation.54 | convolution fusion | flops 605159424 | bytes 3539968 | tf_op jit(solution)/shard_map/bd,vbc->vdc/dot_general | solution.py:30
  136.9 6.3 %collective-permute-start.14 = (bf16[9,256,256]{2,1,0:T(8,128)(2,1)}, bf16[9,256,256]{2,1,0:T(8,128)(2,1)}, u32[]{:S(2)}, u32[]{:S(2)}) collective-permute-start(bf16[9,256,256]{2,1,0:T(8,128)(2,1)} %fusion.24), channel_id=1, source_target_pairs={{0,4},{1,5},{8,12},{9,13},{16,20},{17,21},{24,28},{25,29}} | collective-permute-start | bytes 3538952 | tf_op jit(solution)/shard_map/ppermute | solution.py:69
  144.5 3.4 %fusion = bf16[9,256,256]{2,0,1:T(8,128)(2,1)} fusion(bf16[18,256,256]{2,1,0:T(8,128)(2,1)S(1)} %pad_maximum_fusion.1, bf16[18,9,1]{1,2,0:T(2,128)(2,1)S(1)} %get-tuple-element.66), kind=kOutput, calls=%fused_computation.2 | convolution fusion | flops 21233664 | bytes 3539268 | tf_op jit(solution)/shard_map/wv,wba->vba/dot_general | solution.py:24
  147.9 3.6 %fusion.25 = bf16[9,256,256]{2,1,0:T(8,128)(2,1)} fusion(bf16[9,256,256]{2,0,1:T(8,128)(2,1)} %fusion, bf16[4,256,256]{2,1,0:T(8,128)(2,1)S(1)} %copy-done.6, s32[]{:T(128)S(6)} %select_n.82, bf16[4,256,256]{2,1,0:T(8,128)(2,1)} %collective-permute-done), kind=kOutput, calls=%fused_computation.55 | convolution fusion | flops 605159424 | bytes 3539968 | tf_op jit(solution)/shard_map/bd,vbc->vdc/dot_general | solution.py:30
  155.5 24.8 %collective-permute-done.14 = bf16[9,256,256]{2,1,0:T(8,128)(2,1)} collective-permute-done((bf16[9,256,256]{2,1,0:T(8,128)(2,1)}, bf16[9,256,256]{2,1,0:T(8,128)(2,1)}, u32[]{:S(2)}, u32[]{:S(2)}) %collective-permute-start.14) | collective-permute-done | bytes 1179680 | tf_op jit(solution)/shard_map/ppermute | solution.py:69
  184.7 4.5 %fusion.17 = f32[9,256,256]{2,1,0:T(8,128)S(1)} fusion(bf16[9,256,256]{2,1,0:T(8,128)(2,1)} %collective-permute-done.13, bf16[9,256,256]{2,1,0:T(8,128)(2,1)} %collective-permute-done.12, bf16[9,256,256]{2,1,0:T(8,128)(2,1)} %collective-permute-done.14, bf16[9,256,256]{2,1,0:T(8,128)(2,1)} %collective-permute-done.15, f32[]{:T(128)S(6)} %select_n.83, ...), kind=kOutput, calls=%fused_computation.22 | convolution fusion | flops 612237312 | bytes 9437192 | tf_op jit(solution)/shard_map/bd,vbc->vdc/dot_general | solution.py:30
  189.2 6.7 %collective-permute-done.16 = bf16[3,256,256]{2,1,0:T(8,128)(2,1)} collective-permute-done((bf16[3,256,256]{2,1,0:T(8,128)(2,1)}, bf16[3,256,256]{2,1,0:T(8,128)(2,1)}, u32[]{:S(2)}, u32[]{:S(2)}) %collective-permute-start.16) | collective-permute-done | bytes 393248 | tf_op jit(solution)/shard_map/ppermute | solution.py:91
  198.7 8.4 %collective-permute-done.17 = bf16[1,3,1,256,256]{4,3,1,2,0:T(8,128)(2,1)S(1)} collective-permute-done((bf16[1,3,1,256,256]{4,3,1,2,0:T(8,128)(2,1)S(1)}, bf16[1,3,1,256,256]{4,3,1,2,0:T(8,128)(2,1)S(1)}, u32[]{:S(2)}, u32[]{:S(2)}) %collective-permute-start.17) | collective-permute-done | bytes 393248 | tf_op jit(solution)/shard_map/ppermute | solution.py:20
  209.9 8.4 %collective-permute-done.19 = bf16[1,3,1,256,256]{4,3,1,2,0:T(8,128)(2,1)S(1)} collective-permute-done((bf16[1,3,1,256,256]{4,3,1,2,0:T(8,128)(2,1)S(1)}, bf16[1,3,1,256,256]{4,3,1,2,0:T(8,128)(2,1)S(1)}, u32[]{:S(2)}, u32[]{:S(2)}) %collective-permute-start.19) | collective-permute-done | bytes 393248 | tf_op jit(solution)/shard_map/ppermute | solution.py:20
  221.1 6.3 %collective-permute-done.21 = bf16[1,3,1,256,256]{4,3,1,2,0:T(8,128)(2,1)S(1)} collective-permute-done((bf16[1,3,1,256,256]{4,3,1,2,0:T(8,128)(2,1)S(1)}, bf16[1,3,1,256,256]{4,3,1,2,0:T(8,128)(2,1)S(1)}, u32[]{:S(2)}, u32[]{:S(2)}) %collective-permute-start.21) | collective-permute-done | bytes 393248 | tf_op jit(solution)/shard_map/ppermute | solution.py:20
  (86 shorter events, 62.9 us)
Async XLA Ops:
  2.2 14.4 %collective-permute-start.3 = (bf16[9,256,256]{2,1,0:T(8,128)(2,1)S(1)}, bf16[9,256,256]{2,1,0:T(8,128)(2,1)}, u32[]{:S(2)}, u32[]{:S(2)}) collective-permute-start(bf16[9,256,256]{2,1,0:T(8,128)(2,1)S(1)} %bitcast_select_fusion), channel_id=1, source_target_pairs={{0,1},{1,0},{2,3},{3,2},{4,5},{5,4},{6,7},{7,6},{8,9},{9,8},{10,11... | collective-permute-start | bytes 3538952 | tf_op jit(solution)/shard_map/ppermute | solution.py:20
  2.8 36.5 %collective-permute-start.2 = (bf16[18,9,4]{1,2,0:T(4,128)(2,1)S(1)}, bf16[18,9,4]{1,2,0:T(4,128)(2,1)S(1)}, u32[]{:S(2)}, u32[]{:S(2)}) collective-permute-start(bf16[18,9,4]{1,2,0:T(4,128)(2,1)S(1)} %bitcast.130), channel_id=1, source_target_pairs={{0,24},{8,0},{16,8},{24,16},{1,25},{9,1},{17,9},{25,17},{2,26},{10... | collective-permute-start | bytes 3896 | tf_op jit(solution)/shard_map/ppermute | solution.py:20
  6.3 33.0 %collective-permute-start.1 = (bf16[4,256,256]{2,1,0:T(8,128)(2,1)}, bf16[4,256,256]{2,1,0:T(8,128)(2,1)S(1)}, u32[]{:S(2)}, u32[]{:S(2)}) collective-permute-start(bf16[4,256,256]{2,1,0:T(8,128)(2,1)} %bitcast.1), channel_id=1, source_target_pairs={{0,24},{8,0},{16,8},{24,16},{1,25},{9,1},{17,9},{25,17},{2,26},{10... | collective-permute-start | bytes 1572872 | tf_op jit(solution)/shard_map/ppermute | solution.py:20
  6.9 32.5 %collective-permute-start = (bf16[4,256,256]{2,1,0:T(8,128)(2,1)}, bf16[4,256,256]{2,1,0:T(8,128)(2,1)}, u32[]{:S(2)}, u32[]{:S(2)}) collective-permute-start(bf16[4,256,256]{2,1,0:T(8,128)(2,1)} %bitcast), channel_id=1, source_target_pairs={{0,24},{8,0},{16,8},{24,16},{1,25},{9,1},{17,9},{25,17},{2,26},{10... | collective-permute-start | bytes 1572872 | tf_op jit(solution)/shard_map/ppermute | solution.py:20
  25.5 34.0 %collective-permute-start.6 = (bf16[9,256,256]{2,1,0:T(8,128)(2,1)}, bf16[9,256,256]{2,1,0:T(8,128)(2,1)}, u32[]{:S(2)}, u32[]{:S(2)}) collective-permute-start(bf16[9,256,256]{2,1,0:T(8,128)(2,1)} %fusion.21), channel_id=1, source_target_pairs={{0,4},{1,5},{8,12},{9,13},{16,20},{17,21},{24,28},{25,29}} | collective-permute-start | bytes 3538952 | tf_op jit(solution)/shard_map/ppermute | solution.py:69
  31.0 29.4 %collective-permute-start.5 = (bf16[9,256,256]{2,1,0:T(8,128)(2,1)}, bf16[9,256,256]{2,1,0:T(8,128)(2,1)}, u32[]{:S(2)}, u32[]{:S(2)}) collective-permute-start(bf16[9,256,256]{2,1,0:T(8,128)(2,1)} %fusion.21), channel_id=1, source_target_pairs={{6,4},{4,2},{2,0},{7,5},{5,3},{3,1},{14,12},{12,10},{10,8},{15,13}... | collective-permute-start | bytes 3538952 | tf_op jit(solution)/shard_map/ppermute | solution.py:68
  39.3 21.1 %collective-permute-start.7 = (bf16[9,256,256]{2,1,0:T(8,128)(2,1)}, bf16[9,256,256]{2,1,0:T(8,128)(2,1)}, u32[]{:S(2)}, u32[]{:S(2)}) collective-permute-start(bf16[9,256,256]{2,1,0:T(8,128)(2,1)} %fusion.20), channel_id=1, source_target_pairs={{6,2},{7,3},{14,10},{15,11},{22,18},{23,19},{30,26},{31,27}} | collective-permute-start | bytes 3538952 | tf_op jit(solution)/shard_map/ppermute | solution.py:66
  41.1 39.6 %collective-permute-start.4 = (bf16[9,256,256]{2,1,0:T(8,128)(2,1)}, bf16[9,256,256]{2,1,0:T(8,128)(2,1)}, u32[]{:S(2)}, u32[]{:S(2)}) collective-permute-start(bf16[9,256,256]{2,1,0:T(8,128)(2,1)} %fusion.20), channel_id=1, source_target_pairs={{0,2},{2,4},{4,6},{1,3},{3,5},{5,7},{8,10},{10,12},{12,14},{9,11},... | collective-permute-start | bytes 3538952 | tf_op jit(solution)/shard_map/ppermute | solution.py:65
  56.7 23.9 %copy-start.3 = (bf16[9,256,256]{2,1,0:T(8,128)(2,1)S(1)}, bf16[9,256,256]{2,1,0:T(8,128)(2,1)}, u32[]{:S(2)}) copy-start(bf16[9,256,256]{2,1,0:T(8,128)(2,1)} %fusion.22) | copy-start | bytes 3538948
  82.1 15.5 %collective-permute-start.8 = (bf16[4,256,256]{2,1,0:T(8,128)(2,1)S(1)}, bf16[4,256,256]{2,1,0:T(8,128)(2,1)S(1)}, u32[]{:S(2)}, u32[]{:S(2)}) collective-permute-start(bf16[4,256,256]{2,1,0:T(8,128)(2,1)S(1)} %add_convert_fusion.1), channel_id=1, source_target_pairs={{0,2},{2,6},{6,4},{4,0},{1,3},{3,7},{7,5},{5,1},{8,10},{10,14},{14... | collective-permute-start | bytes 1572872 | tf_op jit(solution)/shard_map/ppermute | solution.py:91
  97.7 17.1 %collective-permute-start.10 = (bf16[5,256,256]{2,1,0:T(8,128)(2,1)S(1)}, bf16[5,256,256]{2,1,0:T(8,128)(2,1)S(1)}, u32[]{:S(2)}, u32[]{:S(2)}) collective-permute-start(bf16[5,256,256]{2,1,0:T(8,128)(2,1)S(1)} %add_convert_fusion), channel_id=1, source_target_pairs={{0,2},{2,6},{6,4},{4,0},{1,3},{3,7},{7,5},{5,1},{8,10},{10,14},{14... | collective-permute-start | bytes 1966088 | tf_op jit(solution)/shard_map/ppermute | solution.py:91
  98.7 1.9 collective-permute-start.9
  115.0 2.3 %collective-permute-start.11 = (bf16[5,256,256]{2,1,0:T(8,128)(2,1)S(1)}, bf16[5,256,256]{2,1,0:T(8,128)(2,1)}, u32[]{:S(2)}, u32[]{:S(2)}) collective-permute-start(bf16[5,256,256]{2,1,0:T(8,128)(2,1)S(1)} %fusion.27), channel_id=1, source_target_pairs={{0,1},{1,0},{2,3},{3,2},{4,5},{5,4},{6,7},{7,6},{8,9},{9,8},{10,11... | collective-permute-start | bytes 1966088 | tf_op jit(solution)/shard_map/ppermute | solution.py:20
  126.0 28.9 %collective-permute-start.15 = (bf16[9,256,256]{2,1,0:T(8,128)(2,1)}, bf16[9,256,256]{2,1,0:T(8,128)(2,1)}, u32[]{:S(2)}, u32[]{:S(2)}) collective-permute-start(bf16[9,256,256]{2,1,0:T(8,128)(2,1)} %fusion.23), channel_id=1, source_target_pairs={{6,2},{7,3},{14,10},{15,11},{22,18},{23,19},{30,26},{31,27}} | collective-permute-start | bytes 3538952 | tf_op jit(solution)/shard_map/ppermute | solution.py:66
  127.7 27.9 %collective-permute-start.12 = (bf16[9,256,256]{2,1,0:T(8,128)(2,1)}, bf16[9,256,256]{2,1,0:T(8,128)(2,1)}, u32[]{:S(2)}, u32[]{:S(2)}) collective-permute-start(bf16[9,256,256]{2,1,0:T(8,128)(2,1)} %fusion.23), channel_id=1, source_target_pairs={{0,2},{2,4},{4,6},{1,3},{3,5},{5,7},{8,10},{10,12},{12,14},{9,11},... | collective-permute-start | bytes 3538952 | tf_op jit(solution)/shard_map/ppermute | solution.py:65
  136.9 43.4 %collective-permute-start.14 = (bf16[9,256,256]{2,1,0:T(8,128)(2,1)}, bf16[9,256,256]{2,1,0:T(8,128)(2,1)}, u32[]{:S(2)}, u32[]{:S(2)}) collective-permute-start(bf16[9,256,256]{2,1,0:T(8,128)(2,1)} %fusion.24), channel_id=1, source_target_pairs={{0,4},{1,5},{8,12},{9,13},{16,20},{17,21},{24,28},{25,29}} | collective-permute-start | bytes 3538952 | tf_op jit(solution)/shard_map/ppermute | solution.py:69
  143.2 37.1 %collective-permute-start.13 = (bf16[9,256,256]{2,1,0:T(8,128)(2,1)}, bf16[9,256,256]{2,1,0:T(8,128)(2,1)}, u32[]{:S(2)}, u32[]{:S(2)}) collective-permute-start(bf16[9,256,256]{2,1,0:T(8,128)(2,1)} %fusion.24), channel_id=1, source_target_pairs={{6,4},{4,2},{2,0},{7,5},{5,3},{3,1},{14,12},{12,10},{10,8},{15,13}... | collective-permute-start | bytes 3538952 | tf_op jit(solution)/shard_map/ppermute | solution.py:68
  151.5 28.8 %copy-start.2 = (bf16[9,256,256]{2,1,0:T(8,128)(2,1)S(1)}, bf16[9,256,256]{2,1,0:T(8,128)(2,1)}, u32[]{:S(2)}) copy-start(bf16[9,256,256]{2,1,0:T(8,128)(2,1)} %fusion.25) | copy-start | bytes 3538948
  183.3 12.6 %collective-permute-start.16 = (bf16[3,256,256]{2,1,0:T(8,128)(2,1)}, bf16[3,256,256]{2,1,0:T(8,128)(2,1)}, u32[]{:S(2)}, u32[]{:S(2)}) collective-permute-start(bf16[3,256,256]{2,1,0:T(8,128)(2,1)} %get-tuple-element.64), channel_id=1, source_target_pairs={{0,2},{2,6},{6,4},{4,0},{1,3},{3,7},{7,5},{5,1},{8,10},{10,14},{14... | collective-permute-start | bytes 1179656 | tf_op jit(solution)/shard_map/ppermute | solution.py:91
  197.0 10.1 %collective-permute-start.17 = (bf16[1,3,1,256,256]{4,3,1,2,0:T(8,128)(2,1)S(1)}, bf16[1,3,1,256,256]{4,3,1,2,0:T(8,128)(2,1)S(1)}, u32[]{:S(2)}, u32[]{:S(2)}) collective-permute-start(bf16[1,3,1,256,256]{4,3,1,2,0:T(8,128)(2,1)S(1)} %bitcast.133), channel_id=1, source_target_pairs={{0,16},{8,24},{16,0},{24,8},{1,17},{9,25},{17,1},{25,9},{2,18},{10... | collective-permute-start | bytes 1179656 | tf_op jit(solution)/shard_map/ppermute | solution.py:20
  198.6 10.7 %collective-permute-start.18 = (bf16[3,256,256]{2,1,0:T(8,128)(2,1)S(1)}, bf16[3,256,256]{2,1,0:T(8,128)(2,1)S(1)}, u32[]{:S(2)}, u32[]{:S(2)}) collective-permute-start(bf16[3,256,256]{2,1,0:T(8,128)(2,1)S(1)} %get-tuple-element.53), channel_id=1, source_target_pairs={{0,2},{2,6},{6,4},{4,0},{1,3},{3,7},{7,5},{5,1},{8,10},{10,14},{14... | collective-permute-start | bytes 1179656 | tf_op jit(solution)/shard_map/ppermute | solution.py:91
  209.4 8.9 %collective-permute-start.19 = (bf16[1,3,1,256,256]{4,3,1,2,0:T(8,128)(2,1)S(1)}, bf16[1,3,1,256,256]{4,3,1,2,0:T(8,128)(2,1)S(1)}, u32[]{:S(2)}, u32[]{:S(2)}) collective-permute-start(bf16[1,3,1,256,256]{4,3,1,2,0:T(8,128)(2,1)S(1)} %bitcast.132), channel_id=1, source_target_pairs={{0,16},{8,24},{16,0},{24,8},{1,17},{9,25},{17,1},{25,9},{2,18},{10... | collective-permute-start | bytes 1179656 | tf_op jit(solution)/shard_map/ppermute | solution.py:20
  209.9 9.5 %collective-permute-start.20 = (bf16[3,256,256]{2,1,0:T(8,128)(2,1)S(1)}, bf16[3,256,256]{2,1,0:T(8,128)(2,1)S(1)}, u32[]{:S(2)}, u32[]{:S(2)}) collective-permute-start(bf16[3,256,256]{2,1,0:T(8,128)(2,1)S(1)} %get-tuple-element.57), channel_id=1, source_target_pairs={{0,2},{2,6},{6,4},{4,0},{1,3},{3,7},{7,5},{5,1},{8,10},{10,14},{14... | collective-permute-start | bytes 1179656 | tf_op jit(solution)/shard_map/ppermute | solution.py:91
  219.5 7.8 %collective-permute-start.21 = (bf16[1,3,1,256,256]{4,3,1,2,0:T(8,128)(2,1)S(1)}, bf16[1,3,1,256,256]{4,3,1,2,0:T(8,128)(2,1)S(1)}, u32[]{:S(2)}, u32[]{:S(2)}) collective-permute-start(bf16[1,3,1,256,256]{4,3,1,2,0:T(8,128)(2,1)S(1)} %fusion.36), channel_id=1, source_target_pairs={{0,16},{8,24},{16,0},{24,8},{1,17},{9,25},{17,1},{25,9},{2,18},{10... | collective-permute-start | bytes 1179656 | tf_op jit(solution)/shard_map/ppermute | solution.py:20
  (9 other events, 64.6 us)

commit v17 on v16

--- a/solution.py
+++ b/solution.py
@@ -123,11 +123,11 @@
     for _ in range(1, STEPS):
         ket, bra, mpo = tensors[-1]
         tensors.append(tuple(shifted(t, "site", -1) for t in (ket, bra, mpo)))
-    current = jnp.where(live_both, environment[0, :, 0], jnp.zeros((), jnp.bfloat16))
     def onward(part):
         return shifted(part[None, :, None], "site", STEPS)
 
-    pieces = [chan_copies(current)]
+    zero = jnp.zeros((), jnp.bfloat16)
+    pieces = [[jnp.where(live_both, p, zero) for p in chan_copies(environment[0, :, 0])]]
     current = None
     for step in range(STEPS):
         ket, bra, mpo = tensors[step]

time: 229 us -> 230 us (level)
  local copies, waits for them, and re-layouts: 4.08 us -> 6.72 us
  transfers between devices with their start and end apart: 22 -> 22, of which waited for: 14 -> 14; matrix products, arithmetic and copies ran while one was open for 26% -> 27% of each run, Pallas kernels for 0% -> 0%
where the time goes in v17:
time: 230 us; the launch traced here: 229 us
  waiting for transfers between devices  103 us (45%)
  matrix products  55.8 us (24%)
  starting transfers between devices  41.3 us (18%)
  other arithmetic  15.6 us (7%)
  local copies, waits for them, and re-layouts  6.72 us (3%)
  between operations  6.43 us (3%)
    ppermute x5, waiting for transfers between devices, advance_line(): got_last = lax.ppermute(send, 'sector', LAST)  30.3 us
    dot_general x8, matrix products, term(): jnp.einsum('bd,vbc->vdc', bra_p, rotated, preferred_element_type=jnp.floa...  28.9 us
    dot_general x8, matrix products, term(): jnp.einsum('wv,wba->vba', mpo_p, gathered, preferred_element_type=jnp.flo...  26.9 us
    ppermute x9, waiting for transfers between devices, shifted(): return lax.ppermute(value, axis, pairs)  26.4 us
    ppermute x2, waiting for transfers between devices, advance_line(): middle_right = lax.ppermute(slot_b, 'sector', ((0, 2),))  24.8 us
    ppermute x2, waiting for transfers between devices, advance_line(): got_right = lax.ppermute(slot_a, 'sector', RIGHT)  20.9 us
    ppermute x2, starting transfers between devices, advance_line(): middle_right = lax.ppermute(slot_b, 'sector', ((0, 2),))  11.8 us
    ppermute x9, starting transfers between devices, shifted(): return lax.ppermute(value, axis, pairs)  9.72 us
  transfers between devices with their start and end apart: 22, of which 14 were waited for; matrix products, arithmetic and copies ran while one was open for 27% of the time, Pallas kernels for 0%

profile of v17, /device:TPU:0, one launch (start us, length us, event | category | flops | bytes accessed | tf_op | source)
XLA Modules:
  0.0 229.4 jit_solution(10164289246560123197)
XLA Ops:
  1.3 3.5 %collective-permute-start.2 = (bf16[18,9,4]{1,2,0:T(4,128)(2,1)S(1)}, bf16[18,9,4]{1,2,0:T(4,128)(2,1)S(1)}, u32[]{:S(2)}, u32[]{:S(2)}) collective-permute-start(bf16[18,9,4]{1,2,0:T(4,128)(2,1)S(1)} %bitcast.131), channel_id=1, source_target_pairs={{0,24},{8,0},{16,8},{24,16},{1,25},{9,1},{17,9},{25,17},{2,26},{10... | collective-permute-start | bytes 3896 | tf_op jit(solution)/shard_map/ppermute | solution.py:20
  19.4 3.4 %fusion.10 = bf16[9,256,256]{2,0,1:T(8,128)(2,1)} fusion(bf16[18,256,256]{2,1,0:T(8,128)(2,1)S(1)} %pad_maximum_fusion, bf16[18,9,1]{1,2,0:T(2,128)(2,1)S(1)} %get-tuple-element.72), kind=kOutput, calls=%fused_computation.12 | convolution fusion | flops 21233664 | bytes 3539268 | tf_op jit(solution)/shard_map/wv,wba->vba/dot_general | solution.py:24
  22.8 3.6 %fusion.21 = bf16[9,256,256]{2,1,0:T(8,128)(2,1)} fusion(bf16[9,256,256]{2,0,1:T(8,128)(2,1)} %fusion.10, bf16[1,1,4,256,256]{4,3,2,1,0:T(8,128)(2,1)} %param.15, s32[]{:T(128)S(6)} %select_n.85, bf16[1,1,4,256,256]{4,3,2,1,0:T(8,128)(2,1)} %param.14), kind=kOutput, calls=%fused_computation.51 | convolution fusion | flops 605159424 | bytes 3539968 | tf_op jit(solution)/shard_map/bd,vbc->vdc/dot_general | solution.py:30
  26.4 5.5 %collective-permute-start.6 = (bf16[9,256,256]{2,1,0:T(8,128)(2,1)}, bf16[9,256,256]{2,1,0:T(8,128)(2,1)}, u32[]{:S(2)}, u32[]{:S(2)}) collective-permute-start(bf16[9,256,256]{2,1,0:T(8,128)(2,1)} %fusion.21), channel_id=1, source_target_pairs={{0,4},{1,5},{8,12},{9,13},{16,20},{17,21},{24,28},{25,29}} | collective-permute-start | bytes 3538952 | tf_op jit(solution)/shard_map/ppermute | solution.py:69
  33.2 3.4 %fusion.14 = bf16[9,256,256]{2,0,1:T(8,128)(2,1)} fusion(bf16[18,256,256]{2,1,0:T(8,128)(2,1)S(1)} %pad_maximum_fusion, bf16[18,9,1]{1,2,0:T(2,128)(2,1)S(1)} %get-tuple-element.74), kind=kOutput, calls=%fused_computation.16 | convolution fusion | flops 21233664 | bytes 3539268 | tf_op jit(solution)/shard_map/wv,wba->vba/dot_general | solution.py:24
  36.6 3.7 %fusion.20 = bf16[9,256,256]{2,1,0:T(8,128)(2,1)} fusion(bf16[9,256,256]{2,0,1:T(8,128)(2,1)} %fusion.14, bf16[1,1,4,256,256]{4,3,2,1,0:T(8,128)(2,1)} %param.15, s32[]{:T(128)S(6)} %select_n.81, bf16[1,1,4,256,256]{4,3,2,1,0:T(8,128)(2,1)} %param.14), kind=kOutput, calls=%fused_computation.50 | convolution fusion | flops 605159424 | bytes 3539968 | tf_op jit(solution)/shard_map/bd,vbc->vdc/dot_general | solution.py:30
  42.0 5.2 %collective-permute-start.4 = (bf16[9,256,256]{2,1,0:T(8,128)(2,1)}, bf16[9,256,256]{2,1,0:T(8,128)(2,1)}, u32[]{:S(2)}, u32[]{:S(2)}) collective-permute-start(bf16[9,256,256]{2,1,0:T(8,128)(2,1)} %fusion.20), channel_id=1, source_target_pairs={{0,2},{2,4},{4,6},{1,3},{3,5},{5,7},{8,10},{10,12},{12,14},{9,11},... | collective-permute-start | bytes 3538952 | tf_op jit(solution)/shard_map/ppermute | solution.py:65
  50.5 3.7 %fusion.22 = bf16[9,256,256]{2,1,0:T(8,128)(2,1)} fusion(bf16[9,256,256]{2,0,1:T(8,128)(2,1)} %fusion.8, bf16[1,1,4,256,256]{4,3,2,1,0:T(8,128)(2,1)} %param.15, s32[]{:T(128)S(6)} %select_n.86, bf16[1,1,4,256,256]{4,3,2,1,0:T(8,128)(2,1)} %param.14), kind=kOutput, calls=%fused_computation.52 | convolution fusion | flops 605159424 | bytes 3539968 | tf_op jit(solution)/shard_map/bd,vbc->vdc/dot_general | solution.py:30
  61.4 20.2 %collective-permute-done.4 = bf16[9,256,256]{2,1,0:T(8,128)(2,1)} collective-permute-done((bf16[9,256,256]{2,1,0:T(8,128)(2,1)}, bf16[9,256,256]{2,1,0:T(8,128)(2,1)}, u32[]{:S(2)}, u32[]{:S(2)}) %collective-permute-start.4) | collective-permute-done | bytes 1179680 | tf_op jit(solution)/shard_map/ppermute | solution.py:65
  83.0 3.8 %collective-permute-start.8 = (bf16[4,256,256]{2,1,0:T(8,128)(2,1)S(1)}, bf16[4,256,256]{2,1,0:T(8,128)(2,1)S(1)}, u32[]{:S(2)}, u32[]{:S(2)}) collective-permute-start(bf16[4,256,256]{2,1,0:T(8,128)(2,1)S(1)} %add_convert_fusion.1), channel_id=1, source_target_pairs={{0,2},{2,6},{6,4},{4,0},{1,3},{3,7},{7,5},{5,1},{8,10},{10,14},{14... | collective-permute-start | bytes 1572872 | tf_op jit(solution)/shard_map/ppermute | solution.py:91
  91.6 6.9 %collective-permute-done.8 = bf16[4,256,256]{2,1,0:T(8,128)(2,1)S(1)} collective-permute-done((bf16[4,256,256]{2,1,0:T(8,128)(2,1)S(1)}, bf16[4,256,256]{2,1,0:T(8,128)(2,1)S(1)}, u32[]{:S(2)}, u32[]{:S(2)}) %collective-permute-start.8) | collective-permute-done | bytes 524320 | tf_op jit(solution)/shard_map/ppermute | solution.py:91
  102.4 13.4 %collective-permute-done.10 = bf16[5,256,256]{2,1,0:T(8,128)(2,1)S(1)} collective-permute-done((bf16[5,256,256]{2,1,0:T(8,128)(2,1)S(1)}, bf16[5,256,256]{2,1,0:T(8,128)(2,1)S(1)}, u32[]{:S(2)}, u32[]{:S(2)}) %collective-permute-start.10) | collective-permute-done | bytes 655392 | tf_op jit(solution)/shard_map/ppermute | solution.py:91
  119.9 3.4 %fusion.4 = bf16[9,256,256]{2,0,1:T(8,128)(2,1)} fusion(bf16[18,256,256]{2,1,0:T(8,128)(2,1)S(1)} %pad_maximum_fusion.1, bf16[18,9,1]{1,2,0:T(2,128)(2,1)S(1)} %get-tuple-element.70), kind=kOutput, calls=%fused_computation.6 | convolution fusion | flops 21233664 | bytes 3539268 | tf_op jit(solution)/shard_map/wv,wba->vba/dot_general | solution.py:24
  123.3 3.6 %fusion.23 = bf16[9,256,256]{2,1,0:T(8,128)(2,1)} fusion(bf16[9,256,256]{2,0,1:T(8,128)(2,1)} %fusion.4, bf16[4,256,256]{2,1,0:T(8,128)(2,1)S(1)} %copy-done.5, s32[]{:T(128)S(6)} %select_n.81, bf16[4,256,256]{2,1,0:T(8,128)(2,1)} %collective-permute-done), kind=kOutput, calls=%fused_computation.53 | convolution fusion | flops 605159424 | bytes 3539968 | tf_op jit(solution)/shard_map/bd,vbc->vdc/dot_general | solution.py:30
  134.3 3.6 %fusion.24 = bf16[9,256,256]{2,1,0:T(8,128)(2,1)} fusion(bf16[9,256,256]{2,0,1:T(8,128)(2,1)} %fusion.2, bf16[4,256,256]{2,1,0:T(8,128)(2,1)S(1)} %copy-done.5, s32[]{:T(128)S(6)} %select_n.85, bf16[4,256,256]{2,1,0:T(8,128)(2,1)} %collective-permute-done), kind=kOutput, calls=%fused_computation.54 | convolution fusion | flops 605159424 | bytes 3539968 | tf_op jit(solution)/shard_map/bd,vbc->vdc/dot_general | solution.py:30
  137.9 6.3 %collective-permute-start.14 = (bf16[9,256,256]{2,1,0:T(8,128)(2,1)}, bf16[9,256,256]{2,1,0:T(8,128)(2,1)}, u32[]{:S(2)}, u32[]{:S(2)}) collective-permute-start(bf16[9,256,256]{2,1,0:T(8,128)(2,1)} %fusion.24), channel_id=1, source_target_pairs={{0,4},{1,5},{8,12},{9,13},{16,20},{17,21},{24,28},{25,29}} | collective-permute-start | bytes 3538952 | tf_op jit(solution)/shard_map/ppermute | solution.py:69
  145.4 3.4 %fusion = bf16[9,256,256]{2,0,1:T(8,128)(2,1)} fusion(bf16[18,256,256]{2,1,0:T(8,128)(2,1)S(1)} %pad_maximum_fusion.1, bf16[18,9,1]{1,2,0:T(2,128)(2,1)S(1)} %get-tuple-element.68), kind=kOutput, calls=%fused_computation.2 | convolution fusion | flops 21233664 | bytes 3539268 | tf_op jit(solution)/shard_map/wv,wba->vba/dot_general | solution.py:24
  148.8 3.6 %fusion.25 = bf16[9,256,256]{2,1,0:T(8,128)(2,1)} fusion(bf16[9,256,256]{2,0,1:T(8,128)(2,1)} %fusion, bf16[4,256,256]{2,1,0:T(8,128)(2,1)S(1)} %copy-done.5, s32[]{:T(128)S(6)} %select_n.86, bf16[4,256,256]{2,1,0:T(8,128)(2,1)} %collective-permute-done), kind=kOutput, calls=%fused_computation.55 | convolution fusion | flops 605159424 | bytes 3539968 | tf_op jit(solution)/shard_map/bd,vbc->vdc/dot_general | solution.py:30
  156.5 24.8 %collective-permute-done.14 = bf16[9,256,256]{2,1,0:T(8,128)(2,1)} collective-permute-done((bf16[9,256,256]{2,1,0:T(8,128)(2,1)}, bf16[9,256,256]{2,1,0:T(8,128)(2,1)}, u32[]{:S(2)}, u32[]{:S(2)}) %collective-permute-start.14) | collective-permute-done | bytes 1179680 | tf_op jit(solution)/shard_map/ppermute | solution.py:69
  185.6 4.4 %fusion.17 = f32[9,256,256]{2,1,0:T(8,128)S(1)} fusion(bf16[9,256,256]{2,1,0:T(8,128)(2,1)} %collective-permute-done.13, bf16[9,256,256]{2,1,0:T(8,128)(2,1)} %collective-permute-done.12, bf16[9,256,256]{2,1,0:T(8,128)(2,1)} %collective-permute-done.14, bf16[9,256,256]{2,1,0:T(8,128)(2,1)} %collective-permute-done.15, f32[]{:T(128)S(6)} %select_n.87, ...), kind=kOutput, calls=%fused_computation.22 | convolution fusion | flops 612237312 | bytes 9437192 | tf_op jit(solution)/shard_map/bd,vbc->vdc/dot_general | solution.py:30
  190.1 6.7 %collective-permute-done.16 = bf16[3,256,256]{2,1,0:T(8,128)(2,1)} collective-permute-done((bf16[3,256,256]{2,1,0:T(8,128)(2,1)}, bf16[3,256,256]{2,1,0:T(8,128)(2,1)}, u32[]{:S(2)}, u32[]{:S(2)}) %collective-permute-start.16) | collective-permute-done | bytes 393248 | tf_op jit(solution)/shard_map/ppermute | solution.py:91
  199.6 8.4 %collective-permute-done.17 = bf16[1,3,1,256,256]{4,3,1,2,0:T(8,128)(2,1)S(1)} collective-permute-done((bf16[1,3,1,256,256]{4,3,1,2,0:T(8,128)(2,1)S(1)}, bf16[1,3,1,256,256]{4,3,1,2,0:T(8,128)(2,1)S(1)}, u32[]{:S(2)}, u32[]{:S(2)}) %collective-permute-start.17) | collective-permute-done | bytes 393248 | tf_op jit(solution)/shard_map/ppermute | solution.py:20
  210.9 8.3 %collective-permute-done.19 = bf16[1,3,1,256,256]{4,3,1,2,0:T(8,128)(2,1)S(1)} collective-permute-done((bf16[1,3,1,256,256]{4,3,1,2,0:T(8,128)(2,1)S(1)}, bf16[1,3,1,256,256]{4,3,1,2,0:T(8,128)(2,1)S(1)}, u32[]{:S(2)}, u32[]{:S(2)}) %collective-permute-start.19) | collective-permute-done | bytes 393248 | tf_op jit(solution)/shard_map/ppermute | solution.py:20
  222.0 6.3 %collective-permute-done.21 = bf16[1,3,1,256,256]{4,3,1,2,0:T(8,128)(2,1)S(1)} collective-permute-done((bf16[1,3,1,256,256]{4,3,1,2,0:T(8,128)(2,1)S(1)}, bf16[1,3,1,256,256]{4,3,1,2,0:T(8,128)(2,1)S(1)}, u32[]{:S(2)}, u32[]{:S(2)}) %collective-permute-start.21) | collective-permute-done | bytes 393248 | tf_op jit(solution)/shard_map/ppermute | solution.py:20
  (76 shorter events, 64.0 us)
Async XLA Ops:
  0.0 17.7 %collective-permute-start.3 = (bf16[9,256,256]{2,1,0:T(8,128)(2,1)}, bf16[9,256,256]{2,1,0:T(8,128)(2,1)S(1)}, u32[]{:S(2)}, u32[]{:S(2)}) collective-permute-start(bf16[9,256,256]{2,1,0:T(8,128)(2,1)} %bitcast.130), channel_id=1, source_target_pairs={{0,1},{1,0},{2,3},{3,2},{4,5},{5,4},{6,7},{7,6},{8,9},{9,8},{10,11... | collective-permute-start | bytes 3538952 | tf_op jit(solution)/shard_map/ppermute | solution.py:20
  1.3 39.0 %collective-permute-start.2 = (bf16[18,9,4]{1,2,0:T(4,128)(2,1)S(1)}, bf16[18,9,4]{1,2,0:T(4,128)(2,1)S(1)}, u32[]{:S(2)}, u32[]{:S(2)}) collective-permute-start(bf16[18,9,4]{1,2,0:T(4,128)(2,1)S(1)} %bitcast.131), channel_id=1, source_target_pairs={{0,24},{8,0},{16,8},{24,16},{1,25},{9,1},{17,9},{25,17},{2,26},{10... | collective-permute-start | bytes 3896 | tf_op jit(solution)/shard_map/ppermute | solution.py:20
  4.8 35.5 %collective-permute-start.1 = (bf16[4,256,256]{2,1,0:T(8,128)(2,1)}, bf16[4,256,256]{2,1,0:T(8,128)(2,1)S(1)}, u32[]{:S(2)}, u32[]{:S(2)}) collective-permute-start(bf16[4,256,256]{2,1,0:T(8,128)(2,1)} %bitcast.135), channel_id=1, source_target_pairs={{0,24},{8,0},{16,8},{24,16},{1,25},{9,1},{17,9},{25,17},{2,26},{10... | collective-permute-start | bytes 1572872 | tf_op jit(solution)/shard_map/ppermute | solution.py:20
  5.3 35.0 %collective-permute-start = (bf16[4,256,256]{2,1,0:T(8,128)(2,1)}, bf16[4,256,256]{2,1,0:T(8,128)(2,1)}, u32[]{:S(2)}, u32[]{:S(2)}) collective-permute-start(bf16[4,256,256]{2,1,0:T(8,128)(2,1)} %bitcast.136), channel_id=1, source_target_pairs={{0,24},{8,0},{16,8},{24,16},{1,25},{9,1},{17,9},{25,17},{2,26},{10... | collective-permute-start | bytes 1572872 | tf_op jit(solution)/shard_map/ppermute | solution.py:20
  26.4 33.9 %collective-permute-start.6 = (bf16[9,256,256]{2,1,0:T(8,128)(2,1)}, bf16[9,256,256]{2,1,0:T(8,128)(2,1)}, u32[]{:S(2)}, u32[]{:S(2)}) collective-permute-start(bf16[9,256,256]{2,1,0:T(8,128)(2,1)} %fusion.21), channel_id=1, source_target_pairs={{0,4},{1,5},{8,12},{9,13},{16,20},{17,21},{24,28},{25,29}} | collective-permute-start | bytes 3538952 | tf_op jit(solution)/shard_map/ppermute | solution.py:69
  31.9 29.5 %collective-permute-start.5 = (bf16[9,256,256]{2,1,0:T(8,128)(2,1)}, bf16[9,256,256]{2,1,0:T(8,128)(2,1)}, u32[]{:S(2)}, u32[]{:S(2)}) collective-permute-start(bf16[9,256,256]{2,1,0:T(8,128)(2,1)} %fusion.21), channel_id=1, source_target_pairs={{6,4},{4,2},{2,0},{7,5},{5,3},{3,1},{14,12},{12,10},{10,8},{15,13}... | collective-permute-start | bytes 3538952 | tf_op jit(solution)/shard_map/ppermute | solution.py:68
  40.3 21.1 %collective-permute-start.7 = (bf16[9,256,256]{2,1,0:T(8,128)(2,1)}, bf16[9,256,256]{2,1,0:T(8,128)(2,1)}, u32[]{:S(2)}, u32[]{:S(2)}) collective-permute-start(bf16[9,256,256]{2,1,0:T(8,128)(2,1)} %fusion.20), channel_id=1, source_target_pairs={{6,2},{7,3},{14,10},{15,11},{22,18},{23,19},{30,26},{31,27}} | collective-permute-start | bytes 3538952 | tf_op jit(solution)/shard_map/ppermute | solution.py:66
  42.0 39.6 %collective-permute-start.4 = (bf16[9,256,256]{2,1,0:T(8,128)(2,1)}, bf16[9,256,256]{2,1,0:T(8,128)(2,1)}, u32[]{:S(2)}, u32[]{:S(2)}) collective-permute-start(bf16[9,256,256]{2,1,0:T(8,128)(2,1)} %fusion.20), channel_id=1, source_target_pairs={{0,2},{2,4},{4,6},{1,3},{3,5},{5,7},{8,10},{10,12},{12,14},{9,11},... | collective-permute-start | bytes 3538952 | tf_op jit(solution)/shard_map/ppermute | solution.py:65
  57.6 24.0 %copy-start.2 = (bf16[9,256,256]{2,1,0:T(8,128)(2,1)S(1)}, bf16[9,256,256]{2,1,0:T(8,128)(2,1)}, u32[]{:S(2)}) copy-start(bf16[9,256,256]{2,1,0:T(8,128)(2,1)} %fusion.22) | copy-start | bytes 3538948
  83.0 15.5 %collective-permute-start.8 = (bf16[4,256,256]{2,1,0:T(8,128)(2,1)S(1)}, bf16[4,256,256]{2,1,0:T(8,128)(2,1)S(1)}, u32[]{:S(2)}, u32[]{:S(2)}) collective-permute-start(bf16[4,256,256]{2,1,0:T(8,128)(2,1)S(1)} %add_convert_fusion.1), channel_id=1, source_target_pairs={{0,2},{2,6},{6,4},{4,0},{1,3},{3,7},{7,5},{5,1},{8,10},{10,14},{14... | collective-permute-start | bytes 1572872 | tf_op jit(solution)/shard_map/ppermute | solution.py:91
  98.7 17.1 %collective-permute-start.10 = (bf16[5,256,256]{2,1,0:T(8,128)(2,1)S(1)}, bf16[5,256,256]{2,1,0:T(8,128)(2,1)S(1)}, u32[]{:S(2)}, u32[]{:S(2)}) collective-permute-start(bf16[5,256,256]{2,1,0:T(8,128)(2,1)S(1)} %add_convert_fusion), channel_id=1, source_target_pairs={{0,2},{2,6},{6,4},{4,0},{1,3},{3,7},{7,5},{5,1},{8,10},{10,14},{14... | collective-permute-start | bytes 1966088 | tf_op jit(solution)/shard_map/ppermute | solution.py:91
  99.6 1.9 collective-permute-start.9
  115.9 2.3 %collective-permute-start.11 = (bf16[5,256,256]{2,1,0:T(8,128)(2,1)S(1)}, bf16[5,256,256]{2,1,0:T(8,128)(2,1)}, u32[]{:S(2)}, u32[]{:S(2)}) collective-permute-start(bf16[5,256,256]{2,1,0:T(8,128)(2,1)S(1)} %fusion.27), channel_id=1, source_target_pairs={{0,1},{1,0},{2,3},{3,2},{4,5},{5,4},{6,7},{7,6},{8,9},{9,8},{10,11... | collective-permute-start | bytes 1966088 | tf_op jit(solution)/shard_map/ppermute | solution.py:20
  126.9 28.9 %collective-permute-start.15 = (bf16[9,256,256]{2,1,0:T(8,128)(2,1)}, bf16[9,256,256]{2,1,0:T(8,128)(2,1)}, u32[]{:S(2)}, u32[]{:S(2)}) collective-permute-start(bf16[9,256,256]{2,1,0:T(8,128)(2,1)} %fusion.23), channel_id=1, source_target_pairs={{6,2},{7,3},{14,10},{15,11},{22,18},{23,19},{30,26},{31,27}} | collective-permute-start | bytes 3538952 | tf_op jit(solution)/shard_map/ppermute | solution.py:66
  128.6 27.9 %collective-permute-start.12 = (bf16[9,256,256]{2,1,0:T(8,128)(2,1)}, bf16[9,256,256]{2,1,0:T(8,128)(2,1)}, u32[]{:S(2)}, u32[]{:S(2)}) collective-permute-start(bf16[9,256,256]{2,1,0:T(8,128)(2,1)} %fusion.23), channel_id=1, source_target_pairs={{0,2},{2,4},{4,6},{1,3},{3,5},{5,7},{8,10},{10,12},{12,14},{9,11},... | collective-permute-start | bytes 3538952 | tf_op jit(solution)/shard_map/ppermute | solution.py:65
  137.9 43.4 %collective-permute-start.14 = (bf16[9,256,256]{2,1,0:T(8,128)(2,1)}, bf16[9,256,256]{2,1,0:T(8,128)(2,1)}, u32[]{:S(2)}, u32[]{:S(2)}) collective-permute-start(bf16[9,256,256]{2,1,0:T(8,128)(2,1)} %fusion.24), channel_id=1, source_target_pairs={{0,4},{1,5},{8,12},{9,13},{16,20},{17,21},{24,28},{25,29}} | collective-permute-start | bytes 3538952 | tf_op jit(solution)/shard_map/ppermute | solution.py:69
  144.1 37.1 %collective-permute-start.13 = (bf16[9,256,256]{2,1,0:T(8,128)(2,1)}, bf16[9,256,256]{2,1,0:T(8,128)(2,1)}, u32[]{:S(2)}, u32[]{:S(2)}) collective-permute-start(bf16[9,256,256]{2,1,0:T(8,128)(2,1)} %fusion.24), channel_id=1, source_target_pairs={{6,4},{4,2},{2,0},{7,5},{5,3},{3,1},{14,12},{12,10},{10,8},{15,13}... | collective-permute-start | bytes 3538952 | tf_op jit(solution)/shard_map/ppermute | solution.py:68
  152.4 28.9 %copy-start.1 = (bf16[9,256,256]{2,1,0:T(8,128)(2,1)S(1)}, bf16[9,256,256]{2,1,0:T(8,128)(2,1)}, u32[]{:S(2)}) copy-start(bf16[9,256,256]{2,1,0:T(8,128)(2,1)} %fusion.25) | copy-start | bytes 3538948
  184.2 12.6 %collective-permute-start.16 = (bf16[3,256,256]{2,1,0:T(8,128)(2,1)}, bf16[3,256,256]{2,1,0:T(8,128)(2,1)}, u32[]{:S(2)}, u32[]{:S(2)}) collective-permute-start(bf16[3,256,256]{2,1,0:T(8,128)(2,1)} %get-tuple-element.64), channel_id=1, source_target_pairs={{0,2},{2,6},{6,4},{4,0},{1,3},{3,7},{7,5},{5,1},{8,10},{10,14},{14... | collective-permute-start | bytes 1179656 | tf_op jit(solution)/shard_map/ppermute | solution.py:91
  197.9 10.1 %collective-permute-start.17 = (bf16[1,3,1,256,256]{4,3,1,2,0:T(8,128)(2,1)S(1)}, bf16[1,3,1,256,256]{4,3,1,2,0:T(8,128)(2,1)S(1)}, u32[]{:S(2)}, u32[]{:S(2)}) collective-permute-start(bf16[1,3,1,256,256]{4,3,1,2,0:T(8,128)(2,1)S(1)} %bitcast.134), channel_id=1, source_target_pairs={{0,16},{8,24},{16,0},{24,8},{1,17},{9,25},{17,1},{25,9},{2,18},{10... | collective-permute-start | bytes 1179656 | tf_op jit(solution)/shard_map/ppermute | solution.py:20
  199.5 10.7 %collective-permute-start.18 = (bf16[3,256,256]{2,1,0:T(8,128)(2,1)S(1)}, bf16[3,256,256]{2,1,0:T(8,128)(2,1)S(1)}, u32[]{:S(2)}, u32[]{:S(2)}) collective-permute-start(bf16[3,256,256]{2,1,0:T(8,128)(2,1)S(1)} %get-tuple-element.53), channel_id=1, source_target_pairs={{0,2},{2,6},{6,4},{4,0},{1,3},{3,7},{7,5},{5,1},{8,10},{10,14},{14... | collective-permute-start | bytes 1179656 | tf_op jit(solution)/shard_map/ppermute | solution.py:91
  210.3 8.9 %collective-permute-start.19 = (bf16[1,3,1,256,256]{4,3,1,2,0:T(8,128)(2,1)S(1)}, bf16[1,3,1,256,256]{4,3,1,2,0:T(8,128)(2,1)S(1)}, u32[]{:S(2)}, u32[]{:S(2)}) collective-permute-start(bf16[1,3,1,256,256]{4,3,1,2,0:T(8,128)(2,1)S(1)} %bitcast.133), channel_id=1, source_target_pairs={{0,16},{8,24},{16,0},{24,8},{1,17},{9,25},{17,1},{25,9},{2,18},{10... | collective-permute-start | bytes 1179656 | tf_op jit(solution)/shard_map/ppermute | solution.py:20
  210.9 9.5 %collective-permute-start.20 = (bf16[3,256,256]{2,1,0:T(8,128)(2,1)S(1)}, bf16[3,256,256]{2,1,0:T(8,128)(2,1)S(1)}, u32[]{:S(2)}, u32[]{:S(2)}) collective-permute-start(bf16[3,256,256]{2,1,0:T(8,128)(2,1)S(1)} %get-tuple-element.57), channel_id=1, source_target_pairs={{0,2},{2,6},{6,4},{4,0},{1,3},{3,7},{7,5},{5,1},{8,10},{10,14},{14... | collective-permute-start | bytes 1179656 | tf_op jit(solution)/shard_map/ppermute | solution.py:91
  220.4 7.8 %collective-permute-start.21 = (bf16[1,3,1,256,256]{4,3,1,2,0:T(8,128)(2,1)S(1)}, bf16[1,3,1,256,256]{4,3,1,2,0:T(8,128)(2,1)S(1)}, u32[]{:S(2)}, u32[]{:S(2)}) collective-permute-start(bf16[1,3,1,256,256]{4,3,1,2,0:T(8,128)(2,1)S(1)} %fusion.36), channel_id=1, source_target_pairs={{0,16},{8,24},{16,0},{24,8},{1,17},{9,25},{17,1},{25,9},{2,18},{10... | collective-permute-start | bytes 1179656 | tf_op jit(solution)/shard_map/ppermute | solution.py:20
  (4 other events, 17.3 us)

commit v18 on v16

--- a/solution.py
+++ b/solution.py
@@ -122,7 +122,8 @@
     tensors = [(ket_tensor[0, 0], bra_tensor[0, 0], mpo_tensor[0])]
     for _ in range(1, STEPS):
         ket, bra, mpo = tensors[-1]
-        tensors.append(tuple(shifted(t, "site", -1) for t in (ket, bra, mpo)))
+        both = shifted(jnp.concatenate([ket, bra]), "site", -1)
+        tensors.append((both[: ket.shape[0]], both[ket.shape[0] :], shifted(mpo, "site", -1)))
     current = jnp.where(live_both, environment[0, :, 0], jnp.zeros((), jnp.bfloat16))
     def onward(part):
         return shifted(part[None, :, None], "site", STEPS)

time: 229 us -> 241 us (1.052)
  waiting for transfers between devices: 103 us -> 111 us
  local copies, waits for them, and re-layouts: 4.08 us -> 9.85 us
    ppermute x9 -> x8, waiting for transfers between devices: 26.4 us -> 33.5 us  [shifted(): return lax.ppermute(value, axis, pairs)]
    ppermute x9 -> x8, starting transfers between devices: 9.82 us -> 8.44 us  [shifted(): return lax.ppermute(value, axis, pairs)]
  transfers between devices with their start and end apart: 22 -> 21, of which waited for: 14 -> 15; matrix products, arithmetic and copies ran while one was open for 26% -> 27% of each run, Pallas kernels for 0% -> 0%
where the time goes in v18:
time: 241 us; the launch traced here: 240 us
  waiting for transfers between devices  111 us (46%)
  matrix products  55.7 us (23%)
  starting transfers between devices  39.2 us (16%)
  other arithmetic  18.2 us (8%)
  local copies, waits for them, and re-layouts  9.85 us (4%)
  between operations  6.6 us (3%)
    ppermute x8, waiting for transfers between devices, shifted(): return lax.ppermute(value, axis, pairs)  33.5 us
    ppermute x5, waiting for transfers between devices, advance_line(): got_last = lax.ppermute(send, 'sector', LAST)  31.4 us
    dot_general x8, matrix products, term(): jnp.einsum('bd,vbc->vdc', bra_p, rotated, preferred_element_type=jnp.floa...  28.7 us
    dot_general x8, matrix products, term(): jnp.einsum('wv,wba->vba', mpo_p, gathered, preferred_element_type=jnp.flo...  26.9 us
    ppermute x2, waiting for transfers between devices, advance_line(): middle_right = lax.ppermute(slot_b, 'sector', ((0, 2),))  24.8 us
    ppermute x2, waiting for transfers between devices, advance_line(): got_right = lax.ppermute(slot_a, 'sector', RIGHT)  20.9 us
    ppermute x2, starting transfers between devices, advance_line(): middle_right = lax.ppermute(slot_b, 'sector', ((0, 2),))  11.8 us
    ppermute x8, starting transfers between devices, shifted(): return lax.ppermute(value, axis, pairs)  8.44 us
  transfers between devices with their start and end apart: 21, of which 15 were waited for; matrix products, arithmetic and copies ran while one was open for 27% of the time, Pallas kernels for 0%

profile of v18, /device:TPU:0, one launch (start us, length us, event | category | flops | bytes accessed | tf_op | source)
XLA Modules:
  0.0 240.4 jit_solution(8838100956646863730)
XLA Ops:
  1.4 4.0 %collective-permute-start = (bf16[8,256,256]{2,1,0:T(8,128)(2,1)S(1)}, bf16[8,256,256]{2,1,0:T(8,128)(2,1)S(1)}, u32[]{:S(2)}, u32[]{:S(2)}) collective-permute-start(bf16[8,256,256]{2,1,0:T(8,128)(2,1)S(1)} %pad_maximum_fusion.2), channel_id=1, source_target_pairs={{0,24},{8,0},{16,8},{24,16},{1,25},{9,1},{17,9},{25,17},{2,26},{10... | collective-permute-start | bytes 3145736 | tf_op jit(solution)/shard_map/ppermute | solution.py:20
  20.1 7.9 %collective-permute-done = bf16[8,256,256]{2,1,0:T(8,128)(2,1)S(1)} collective-permute-done((bf16[8,256,256]{2,1,0:T(8,128)(2,1)S(1)}, bf16[8,256,256]{2,1,0:T(8,128)(2,1)S(1)}, u32[]{:S(2)}, u32[]{:S(2)}) %collective-permute-start) | collective-permute-done | bytes 1048608 | tf_op jit(solution)/shard_map/ppermute | solution.py:20
  34.2 3.6 %fusion.21 = bf16[9,256,256]{2,1,0:T(8,128)(2,1)} fusion(bf16[9,256,256]{2,0,1:T(8,128)(2,1)} %fusion.10, bf16[1,1,4,256,256]{4,3,2,1,0:T(8,128)(2,1)S(1)} %copy-done.7, s32[]{:T(128)S(6)} %select_n.81, bf16[1,1,4,256,256]{4,3,2,1,0:T(8,128)(2,1)} %param.14), kind=kOutput, calls=%fused_computation.51 | convolution fusion | flops 605159424 | bytes 3539968 | tf_op jit(solution)/shard_map/bd,vbc->vdc/dot_general | solution.py:30
  37.8 5.5 %collective-permute-start.5 = (bf16[9,256,256]{2,1,0:T(8,128)(2,1)}, bf16[9,256,256]{2,1,0:T(8,128)(2,1)}, u32[]{:S(2)}, u32[]{:S(2)}) collective-permute-start(bf16[9,256,256]{2,1,0:T(8,128)(2,1)} %fusion.21), channel_id=1, source_target_pairs={{0,4},{1,5},{8,12},{9,13},{16,20},{17,21},{24,28},{25,29}} | collective-permute-start | bytes 3538952 | tf_op jit(solution)/shard_map/ppermute | solution.py:69
  44.7 3.4 %fusion.14 = bf16[9,256,256]{2,0,1:T(8,128)(2,1)} fusion(bf16[18,256,256]{2,1,0:T(8,128)(2,1)S(1)} %pad_maximum_fusion, bf16[18,9,1]{1,2,0:T(2,128)(2,1)S(1)} %copy-done.9), kind=kOutput, calls=%fused_computation.16 | convolution fusion | flops 21233664 | bytes 3539268 | tf_op jit(solution)/shard_map/wv,wba->vba/dot_general | solution.py:24
  48.0 3.6 %fusion.20 = bf16[9,256,256]{2,1,0:T(8,128)(2,1)} fusion(bf16[9,256,256]{2,0,1:T(8,128)(2,1)} %fusion.14, bf16[1,1,4,256,256]{4,3,2,1,0:T(8,128)(2,1)S(1)} %copy-done.7, s32[]{:T(128)S(6)} %select_n.78, bf16[1,1,4,256,256]{4,3,2,1,0:T(8,128)(2,1)} %param.14), kind=kOutput, calls=%fused_computation.50 | convolution fusion | flops 605159424 | bytes 3539968 | tf_op jit(solution)/shard_map/bd,vbc->vdc/dot_general | solution.py:30
  53.3 5.2 %collective-permute-start.3 = (bf16[9,256,256]{2,1,0:T(8,128)(2,1)}, bf16[9,256,256]{2,1,0:T(8,128)(2,1)}, u32[]{:S(2)}, u32[]{:S(2)}) collective-permute-start(bf16[9,256,256]{2,1,0:T(8,128)(2,1)} %fusion.20), channel_id=1, source_target_pairs={{0,2},{2,4},{4,6},{1,3},{3,5},{5,7},{8,10},{10,12},{12,14},{9,11},... | collective-permute-start | bytes 3538952 | tf_op jit(solution)/shard_map/ppermute | solution.py:65
  61.9 3.7 %fusion.22 = bf16[9,256,256]{2,1,0:T(8,128)(2,1)} fusion(bf16[9,256,256]{2,0,1:T(8,128)(2,1)} %fusion.8, bf16[1,1,4,256,256]{4,3,2,1,0:T(8,128)(2,1)S(1)} %copy-done.7, s32[]{:T(128)S(6)} %select_n.82, bf16[1,1,4,256,256]{4,3,2,1,0:T(8,128)(2,1)} %param.14), kind=kOutput, calls=%fused_computation.52 | convolution fusion | flops 605159424 | bytes 3539968 | tf_op jit(solution)/shard_map/bd,vbc->vdc/dot_general | solution.py:30
  65.6 3.4 %fusion.12 = bf16[9,256,256]{2,0,1:T(8,128)(2,1)} fusion(bf16[18,256,256]{2,1,0:T(8,128)(2,1)S(1)} %pad_maximum_fusion, bf16[18,9,1]{1,2,0:T(2,128)(2,1)S(1)} %get-tuple-element.73), kind=kOutput, calls=%fused_computation.14 | convolution fusion | flops 21233664 | bytes 3539268 | tf_op jit(solution)/shard_map/wv,wba->vba/dot_general | solution.py:24
  71.9 20.2 %collective-permute-done.3 = bf16[9,256,256]{2,1,0:T(8,128)(2,1)} collective-permute-done((bf16[9,256,256]{2,1,0:T(8,128)(2,1)}, bf16[9,256,256]{2,1,0:T(8,128)(2,1)}, u32[]{:S(2)}, u32[]{:S(2)}) %collective-permute-start.3) | collective-permute-done | bytes 1179680 | tf_op jit(solution)/shard_map/ppermute | solution.py:65
  93.6 3.8 %collective-permute-start.7 = (bf16[4,256,256]{2,1,0:T(8,128)(2,1)S(1)}, bf16[4,256,256]{2,1,0:T(8,128)(2,1)S(1)}, u32[]{:S(2)}, u32[]{:S(2)}) collective-permute-start(bf16[4,256,256]{2,1,0:T(8,128)(2,1)S(1)} %add_convert_fusion.1), channel_id=1, source_target_pairs={{0,2},{2,6},{6,4},{4,0},{1,3},{3,7},{7,5},{5,1},{8,10},{10,14},{14... | collective-permute-start | bytes 1572872 | tf_op jit(solution)/shard_map/ppermute | solution.py:91
  102.2 6.9 %collective-permute-done.7 = bf16[4,256,256]{2,1,0:T(8,128)(2,1)S(1)} collective-permute-done((bf16[4,256,256]{2,1,0:T(8,128)(2,1)S(1)}, bf16[4,256,256]{2,1,0:T(8,128)(2,1)S(1)}, u32[]{:S(2)}, u32[]{:S(2)}) %collective-permute-start.7) | collective-permute-done | bytes 524320 | tf_op jit(solution)/shard_map/ppermute | solution.py:91
  112.1 14.2 %collective-permute-done.9 = bf16[5,256,256]{2,1,0:T(8,128)(2,1)S(1)} collective-permute-done((bf16[5,256,256]{2,1,0:T(8,128)(2,1)S(1)}, bf16[5,256,256]{2,1,0:T(8,128)(2,1)S(1)}, u32[]{:S(2)}, u32[]{:S(2)}) %collective-permute-start.9) | collective-permute-done | bytes 655392 | tf_op jit(solution)/shard_map/ppermute | solution.py:91
  133.9 3.6 %fusion.23 = bf16[9,256,256]{2,1,0:T(8,128)(2,1)} fusion(bf16[9,256,256]{2,0,1:T(8,128)(2,1)} %fusion.4, bf16[4,256,256]{2,1,0:T(8,128)(2,1)S(1)} %copy-done.5, s32[]{:T(128)S(6)} %select_n.78, bf16[4,256,256]{2,1,0:T(8,128)(2,1)} %get-tuple-element.45), kind=kOutput, calls=%fused_computation.53 | convolution fusion | flops 605159424 | bytes 3539968 | tf_op jit(solution)/shard_map/bd,vbc->vdc/dot_general | solution.py:30
  141.5 3.4 %fusion.2 = bf16[9,256,256]{2,0,1:T(8,128)(2,1)} fusion(bf16[18,256,256]{2,1,0:T(8,128)(2,1)S(1)} %pad_maximum_fusion.1, bf16[18,9,1]{1,2,0:T(2,128)(2,1)S(1)} %get-tuple-element.69), kind=kOutput, calls=%fused_computation.4 | convolution fusion | flops 21233664 | bytes 3539268 | tf_op jit(solution)/shard_map/wv,wba->vba/dot_general | solution.py:24
  144.9 3.5 %fusion.24 = bf16[9,256,256]{2,1,0:T(8,128)(2,1)} fusion(bf16[9,256,256]{2,0,1:T(8,128)(2,1)} %fusion.2, bf16[4,256,256]{2,1,0:T(8,128)(2,1)S(1)} %copy-done.5, s32[]{:T(128)S(6)} %select_n.81, bf16[4,256,256]{2,1,0:T(8,128)(2,1)} %get-tuple-element.45), kind=kOutput, calls=%fused_computation.54 | convolution fusion | flops 605159424 | bytes 3539968 | tf_op jit(solution)/shard_map/bd,vbc->vdc/dot_general | solution.py:30
  148.4 6.3 %collective-permute-start.13 = (bf16[9,256,256]{2,1,0:T(8,128)(2,1)}, bf16[9,256,256]{2,1,0:T(8,128)(2,1)}, u32[]{:S(2)}, u32[]{:S(2)}) collective-permute-start(bf16[9,256,256]{2,1,0:T(8,128)(2,1)} %fusion.24), channel_id=1, source_target_pairs={{0,4},{1,5},{8,12},{9,13},{16,20},{17,21},{24,28},{25,29}} | collective-permute-start | bytes 3538952 | tf_op jit(solution)/shard_map/ppermute | solution.py:69
  159.4 3.7 %fusion.25 = bf16[9,256,256]{2,1,0:T(8,128)(2,1)} fusion(bf16[9,256,256]{2,0,1:T(8,128)(2,1)} %fusion, bf16[4,256,256]{2,1,0:T(8,128)(2,1)S(1)} %copy-done.5, s32[]{:T(128)S(6)} %select_n.82, bf16[4,256,256]{2,1,0:T(8,128)(2,1)} %get-tuple-element.45), kind=kOutput, calls=%fused_computation.55 | convolution fusion | flops 605159424 | bytes 3539968 | tf_op jit(solution)/shard_map/bd,vbc->vdc/dot_general | solution.py:30
  167.1 24.8 %collective-permute-done.13 = bf16[9,256,256]{2,1,0:T(8,128)(2,1)} collective-permute-done((bf16[9,256,256]{2,1,0:T(8,128)(2,1)}, bf16[9,256,256]{2,1,0:T(8,128)(2,1)}, u32[]{:S(2)}, u32[]{:S(2)}) %collective-permute-start.13) | collective-permute-done | bytes 1179680 | tf_op jit(solution)/shard_map/ppermute | solution.py:69
  196.3 4.4 %fusion.17 = f32[9,256,256]{2,1,0:T(8,128)S(1)} fusion(bf16[9,256,256]{2,1,0:T(8,128)(2,1)} %collective-permute-done.12, bf16[9,256,256]{2,1,0:T(8,128)(2,1)} %collective-permute-done.11, bf16[9,256,256]{2,1,0:T(8,128)(2,1)} %collective-permute-done.13, bf16[9,256,256]{2,1,0:T(8,128)(2,1)} %collective-permute-done.14, f32[]{:T(128)S(6)} %select_n.83, ...), kind=kOutput, calls=%fused_computation.22 | convolution fusion | flops 612237312 | bytes 9437192 | tf_op jit(solution)/shard_map/bd,vbc->vdc/dot_general | solution.py:30
  200.8 6.8 %collective-permute-done.15 = bf16[3,256,256]{2,1,0:T(8,128)(2,1)} collective-permute-done((bf16[3,256,256]{2,1,0:T(8,128)(2,1)}, bf16[3,256,256]{2,1,0:T(8,128)(2,1)}, u32[]{:S(2)}, u32[]{:S(2)}) %collective-permute-start.15) | collective-permute-done | bytes 393248 | tf_op jit(solution)/shard_map/ppermute | solution.py:91
  210.4 8.4 %collective-permute-done.16 = bf16[1,3,1,256,256]{4,3,1,2,0:T(8,128)(2,1)S(1)} collective-permute-done((bf16[1,3,1,256,256]{4,3,1,2,0:T(8,128)(2,1)S(1)}, bf16[1,3,1,256,256]{4,3,1,2,0:T(8,128)(2,1)S(1)}, u32[]{:S(2)}, u32[]{:S(2)}) %collective-permute-start.16) | collective-permute-done | bytes 393248 | tf_op jit(solution)/shard_map/ppermute | solution.py:20
  221.8 8.4 %collective-permute-done.18 = bf16[1,3,1,256,256]{4,3,1,2,0:T(8,128)(2,1)S(1)} collective-permute-done((bf16[1,3,1,256,256]{4,3,1,2,0:T(8,128)(2,1)S(1)}, bf16[1,3,1,256,256]{4,3,1,2,0:T(8,128)(2,1)S(1)}, u32[]{:S(2)}, u32[]{:S(2)}) %collective-permute-start.18) | collective-permute-done | bytes 393248 | tf_op jit(solution)/shard_map/ppermute | solution.py:20
  233.0 6.3 %collective-permute-done.20 = bf16[1,3,1,256,256]{4,3,1,2,0:T(8,128)(2,1)S(1)} collective-permute-done((bf16[1,3,1,256,256]{4,3,1,2,0:T(8,128)(2,1)S(1)}, bf16[1,3,1,256,256]{4,3,1,2,0:T(8,128)(2,1)S(1)}, u32[]{:S(2)}, u32[]{:S(2)}) %collective-permute-start.20) | collective-permute-done | bytes 393248 | tf_op jit(solution)/shard_map/ppermute | solution.py:20
  (92 shorter events, 69.0 us)
Async XLA Ops:
  1.4 26.6 %collective-permute-start = (bf16[8,256,256]{2,1,0:T(8,128)(2,1)S(1)}, bf16[8,256,256]{2,1,0:T(8,128)(2,1)S(1)}, u32[]{:S(2)}, u32[]{:S(2)}) collective-permute-start(bf16[8,256,256]{2,1,0:T(8,128)(2,1)S(1)} %pad_maximum_fusion.2), channel_id=1, source_target_pairs={{0,24},{8,0},{16,8},{24,16},{1,25},{9,1},{17,9},{25,17},{2,26},{10... | collective-permute-start | bytes 3145736 | tf_op jit(solution)/shard_map/ppermute | solution.py:20
  6.2 22.8 %copy-start = (bf16[9,256,256]{2,1,0:T(8,128)(2,1)}, bf16[9,256,256]{2,1,0:T(8,128)(2,1)S(1)}, u32[]{:S(2)}) copy-start(bf16[9,256,256]{2,1,0:T(8,128)(2,1)S(1)} %bitcast_select_fusion) | copy-start | bytes 3538948
  6.2 22.8 %collective-permute-start.2 = (bf16[9,256,256]{2,1,0:T(8,128)(2,1)S(1)}, bf16[9,256,256]{2,1,0:T(8,128)(2,1)}, u32[]{:S(2)}, u32[]{:S(2)}) collective-permute-start(bf16[9,256,256]{2,1,0:T(8,128)(2,1)S(1)} %bitcast_select_fusion), channel_id=1, source_target_pairs={{0,1},{1,0},{2,3},{3,2},{4,5},{5,4},{6,7},{7,6},{8,9},{9,8},{10,11... | collective-permute-start | bytes 3538952 | tf_op jit(solution)/shard_map/ppermute | solution.py:20
  7.2 44.4 %collective-permute-start.1 = (bf16[18,9,4]{1,2,0:T(4,128)(2,1)}, bf16[18,9,4]{1,2,0:T(4,128)(2,1)}, u32[]{:S(2)}, u32[]{:S(2)}) collective-permute-start(bf16[18,9,4]{1,2,0:T(4,128)(2,1)} %bitcast.132), channel_id=1, source_target_pairs={{0,24},{8,0},{16,8},{24,16},{1,25},{9,1},{17,9},{25,17},{2,26},{10... | collective-permute-start | bytes 3896 | tf_op jit(solution)/shard_map/ppermute | solution.py:20
  37.8 33.8 %collective-permute-start.5 = (bf16[9,256,256]{2,1,0:T(8,128)(2,1)}, bf16[9,256,256]{2,1,0:T(8,128)(2,1)}, u32[]{:S(2)}, u32[]{:S(2)}) collective-permute-start(bf16[9,256,256]{2,1,0:T(8,128)(2,1)} %fusion.21), channel_id=1, source_target_pairs={{0,4},{1,5},{8,12},{9,13},{16,20},{17,21},{24,28},{25,29}} | collective-permute-start | bytes 3538952 | tf_op jit(solution)/shard_map/ppermute | solution.py:69
  43.4 28.6 %collective-permute-start.4 = (bf16[9,256,256]{2,1,0:T(8,128)(2,1)}, bf16[9,256,256]{2,1,0:T(8,128)(2,1)}, u32[]{:S(2)}, u32[]{:S(2)}) collective-permute-start(bf16[9,256,256]{2,1,0:T(8,128)(2,1)} %fusion.21), channel_id=1, source_target_pairs={{6,4},{4,2},{2,0},{7,5},{5,3},{3,1},{14,12},{12,10},{10,8},{15,13}... | collective-permute-start | bytes 3538952 | tf_op jit(solution)/shard_map/ppermute | solution.py:68
  51.7 20.3 %collective-permute-start.6 = (bf16[9,256,256]{2,1,0:T(8,128)(2,1)}, bf16[9,256,256]{2,1,0:T(8,128)(2,1)}, u32[]{:S(2)}, u32[]{:S(2)}) collective-permute-start(bf16[9,256,256]{2,1,0:T(8,128)(2,1)} %fusion.20), channel_id=1, source_target_pairs={{6,2},{7,3},{14,10},{15,11},{22,18},{23,19},{30,26},{31,27}} | collective-permute-start | bytes 3538952 | tf_op jit(solution)/shard_map/ppermute | solution.py:66
  53.3 38.8 %collective-permute-start.3 = (bf16[9,256,256]{2,1,0:T(8,128)(2,1)}, bf16[9,256,256]{2,1,0:T(8,128)(2,1)}, u32[]{:S(2)}, u32[]{:S(2)}) collective-permute-start(bf16[9,256,256]{2,1,0:T(8,128)(2,1)} %fusion.20), channel_id=1, source_target_pairs={{0,2},{2,4},{4,6},{1,3},{3,5},{5,7},{8,10},{10,12},{12,14},{9,11},... | collective-permute-start | bytes 3538952 | tf_op jit(solution)/shard_map/ppermute | solution.py:65
  69.0 23.2 %copy-start.4 = (bf16[9,256,256]{2,1,0:T(8,128)(2,1)S(1)}, bf16[9,256,256]{2,1,0:T(8,128)(2,1)}, u32[]{:S(2)}) copy-start(bf16[9,256,256]{2,1,0:T(8,128)(2,1)} %fusion.22) | copy-start | bytes 3538948
  93.6 15.5 %collective-permute-start.7 = (bf16[4,256,256]{2,1,0:T(8,128)(2,1)S(1)}, bf16[4,256,256]{2,1,0:T(8,128)(2,1)S(1)}, u32[]{:S(2)}, u32[]{:S(2)}) collective-permute-start(bf16[4,256,256]{2,1,0:T(8,128)(2,1)S(1)} %add_convert_fusion.1), channel_id=1, source_target_pairs={{0,2},{2,6},{6,4},{4,0},{1,3},{3,7},{7,5},{5,1},{8,10},{10,14},{14... | collective-permute-start | bytes 1572872 | tf_op jit(solution)/shard_map/ppermute | solution.py:91
  109.2 17.1 %collective-permute-start.9 = (bf16[5,256,256]{2,1,0:T(8,128)(2,1)S(1)}, bf16[5,256,256]{2,1,0:T(8,128)(2,1)S(1)}, u32[]{:S(2)}, u32[]{:S(2)}) collective-permute-start(bf16[5,256,256]{2,1,0:T(8,128)(2,1)S(1)} %add_convert_fusion), channel_id=1, source_target_pairs={{0,2},{2,6},{6,4},{4,0},{1,3},{3,7},{7,5},{5,1},{8,10},{10,14},{14... | collective-permute-start | bytes 1966088 | tf_op jit(solution)/shard_map/ppermute | solution.py:91
  109.3 2.0 collective-permute-start.8
  126.5 2.3 collective-permute-start.10
  137.5 28.9 %collective-permute-start.14 = (bf16[9,256,256]{2,1,0:T(8,128)(2,1)}, bf16[9,256,256]{2,1,0:T(8,128)(2,1)}, u32[]{:S(2)}, u32[]{:S(2)}) collective-permute-start(bf16[9,256,256]{2,1,0:T(8,128)(2,1)} %fusion.23), channel_id=1, source_target_pairs={{6,2},{7,3},{14,10},{15,11},{22,18},{23,19},{30,26},{31,27}} | collective-permute-start | bytes 3538952 | tf_op jit(solution)/shard_map/ppermute | solution.py:66
  139.2 27.9 %collective-permute-start.11 = (bf16[9,256,256]{2,1,0:T(8,128)(2,1)}, bf16[9,256,256]{2,1,0:T(8,128)(2,1)}, u32[]{:S(2)}, u32[]{:S(2)}) collective-permute-start(bf16[9,256,256]{2,1,0:T(8,128)(2,1)} %fusion.23), channel_id=1, source_target_pairs={{0,2},{2,4},{4,6},{1,3},{3,5},{5,7},{8,10},{10,12},{12,14},{9,11},... | collective-permute-start | bytes 3538952 | tf_op jit(solution)/shard_map/ppermute | solution.py:65
  148.4 43.4 %collective-permute-start.13 = (bf16[9,256,256]{2,1,0:T(8,128)(2,1)}, bf16[9,256,256]{2,1,0:T(8,128)(2,1)}, u32[]{:S(2)}, u32[]{:S(2)}) collective-permute-start(bf16[9,256,256]{2,1,0:T(8,128)(2,1)} %fusion.24), channel_id=1, source_target_pairs={{0,4},{1,5},{8,12},{9,13},{16,20},{17,21},{24,28},{25,29}} | collective-permute-start | bytes 3538952 | tf_op jit(solution)/shard_map/ppermute | solution.py:69
  154.7 37.1 %collective-permute-start.12 = (bf16[9,256,256]{2,1,0:T(8,128)(2,1)}, bf16[9,256,256]{2,1,0:T(8,128)(2,1)}, u32[]{:S(2)}, u32[]{:S(2)}) collective-permute-start(bf16[9,256,256]{2,1,0:T(8,128)(2,1)} %fusion.24), channel_id=1, source_target_pairs={{6,4},{4,2},{2,0},{7,5},{5,3},{3,1},{14,12},{12,10},{10,8},{15,13}... | collective-permute-start | bytes 3538952 | tf_op jit(solution)/shard_map/ppermute | solution.py:68
  163.0 28.8 %copy-start.2 = (bf16[9,256,256]{2,1,0:T(8,128)(2,1)S(1)}, bf16[9,256,256]{2,1,0:T(8,128)(2,1)}, u32[]{:S(2)}) copy-start(bf16[9,256,256]{2,1,0:T(8,128)(2,1)} %fusion.25) | copy-start | bytes 3538948
  194.9 12.6 %collective-permute-start.15 = (bf16[3,256,256]{2,1,0:T(8,128)(2,1)}, bf16[3,256,256]{2,1,0:T(8,128)(2,1)}, u32[]{:S(2)}, u32[]{:S(2)}) collective-permute-start(bf16[3,256,256]{2,1,0:T(8,128)(2,1)} %get-tuple-element.64), channel_id=1, source_target_pairs={{0,2},{2,6},{6,4},{4,0},{1,3},{3,7},{7,5},{5,1},{8,10},{10,14},{14... | collective-permute-start | bytes 1179656 | tf_op jit(solution)/shard_map/ppermute | solution.py:91
  208.6 10.1 %collective-permute-start.16 = (bf16[1,3,1,256,256]{4,3,1,2,0:T(8,128)(2,1)S(1)}, bf16[1,3,1,256,256]{4,3,1,2,0:T(8,128)(2,1)S(1)}, u32[]{:S(2)}, u32[]{:S(2)}) collective-permute-start(bf16[1,3,1,256,256]{4,3,1,2,0:T(8,128)(2,1)S(1)} %bitcast.135), channel_id=1, source_target_pairs={{0,16},{8,24},{16,0},{24,8},{1,17},{9,25},{17,1},{25,9},{2,18},{10... | collective-permute-start | bytes 1179656 | tf_op jit(solution)/shard_map/ppermute | solution.py:20
  210.2 10.9 %collective-permute-start.17 = (bf16[3,256,256]{2,1,0:T(8,128)(2,1)}, bf16[3,256,256]{2,1,0:T(8,128)(2,1)S(1)}, u32[]{:S(2)}, u32[]{:S(2)}) collective-permute-start(bf16[3,256,256]{2,1,0:T(8,128)(2,1)} %get-tuple-element.53), channel_id=1, source_target_pairs={{0,2},{2,6},{6,4},{4,0},{1,3},{3,7},{7,5},{5,1},{8,10},{10,14},{14... | collective-permute-start | bytes 1179656 | tf_op jit(solution)/shard_map/ppermute | solution.py:91
  221.2 8.9 %collective-permute-start.18 = (bf16[1,3,1,256,256]{4,3,1,2,0:T(8,128)(2,1)S(1)}, bf16[1,3,1,256,256]{4,3,1,2,0:T(8,128)(2,1)S(1)}, u32[]{:S(2)}, u32[]{:S(2)}) collective-permute-start(bf16[1,3,1,256,256]{4,3,1,2,0:T(8,128)(2,1)S(1)} %bitcast.134), channel_id=1, source_target_pairs={{0,16},{8,24},{16,0},{24,8},{1,17},{9,25},{17,1},{25,9},{2,18},{10... | collective-permute-start | bytes 1179656 | tf_op jit(solution)/shard_map/ppermute | solution.py:20
  221.8 9.5 %collective-permute-start.19 = (bf16[3,256,256]{2,1,0:T(8,128)(2,1)S(1)}, bf16[3,256,256]{2,1,0:T(8,128)(2,1)S(1)}, u32[]{:S(2)}, u32[]{:S(2)}) collective-permute-start(bf16[3,256,256]{2,1,0:T(8,128)(2,1)S(1)} %get-tuple-element.57), channel_id=1, source_target_pairs={{0,2},{2,6},{6,4},{4,0},{1,3},{3,7},{7,5},{5,1},{8,10},{10,14},{14... | collective-permute-start | bytes 1179656 | tf_op jit(solution)/shard_map/ppermute | solution.py:91
  231.4 7.8 %collective-permute-start.20 = (bf16[1,3,1,256,256]{4,3,1,2,0:T(8,128)(2,1)S(1)}, bf16[1,3,1,256,256]{4,3,1,2,0:T(8,128)(2,1)S(1)}, u32[]{:S(2)}, u32[]{:S(2)}) collective-permute-start(bf16[1,3,1,256,256]{4,3,1,2,0:T(8,128)(2,1)S(1)} %fusion.36), channel_id=1, source_target_pairs={{0,16},{8,24},{16,0},{24,8},{1,17},{9,25},{17,1},{25,9},{2,18},{10... | collective-permute-start | bytes 1179656 | tf_op jit(solution)/shard_map/ppermute | solution.py:20
  (11 other events, 78.3 us)

commit v19 on v16

--- a/solution.py
+++ b/solution.py
@@ -78,6 +78,9 @@
     total = total + keep_left * got_left.astype(f32) + got_middle.astype(f32)
     width = third.shape[0]
     bounds = [width * k // pieces for k in range(pieces + 1)]
+    if finish is not chan_copies:
+        weights = [sum(range(pieces, pieces - k, -1)) for k in range(pieces + 1)]
+        bounds = [width * w // weights[-1] for w in weights]
     results = []
     piece = None
     for low, high in zip(bounds[:-1], bounds[1:]):

time: 229 us -> 229 us (level)
    ppermute x9, waiting for transfers between devices: 26.4 us -> 9.3 us  [shifted(): return lax.ppermute(value, axis, pairs)]
    ppermute x5, waiting for transfers between devices: 30.3 us -> 44.7 us  [advance_line(): got_last = lax.ppermute(send, 'sector', LAST)]
    convert_element_type x3 -> x5, other arithmetic: 5.99 us -> 7.88 us  [advance_line(): send = send.astype(jnp.bfloat16)]
  transfers between devices with their start and end apart: 22 -> 22, of which waited for: 14 -> 14; matrix products, arithmetic and copies ran while one was open for 26% -> 27% of each run, Pallas kernels for 0% -> 0%
where the time goes in v19:
time: 229 us; the launch traced here: 228 us
  waiting for transfers between devices  101 us (44%)
  matrix products  55.8 us (24%)
  starting transfers between devices  42.8 us (19%)
  other arithmetic  18.1 us (8%)
  between operations  6.48 us (3%)
  local copies, waits for them, and re-layouts  4.09 us (2%)
    ppermute x5, waiting for transfers between devices, advance_line(): got_last = lax.ppermute(send, 'sector', LAST)  44.7 us
    dot_general x8, matrix products, term(): jnp.einsum('bd,vbc->vdc', bra_p, rotated, preferred_element_type=jnp.floa...  28.9 us
    dot_general x8, matrix products, term(): jnp.einsum('wv,wba->vba', mpo_p, gathered, preferred_element_type=jnp.flo...  26.9 us
    ppermute x2, waiting for transfers between devices, advance_line(): middle_right = lax.ppermute(slot_b, 'sector', ((0, 2),))  24.8 us
    ppermute x2, waiting for transfers between devices, advance_line(): got_right = lax.ppermute(slot_a, 'sector', RIGHT)  20.8 us
    ppermute x2, starting transfers between devices, advance_line(): middle_right = lax.ppermute(slot_b, 'sector', ((0, 2),))  11.9 us
    ppermute x9, starting transfers between devices, shifted(): return lax.ppermute(value, axis, pairs)  10.8 us
    ppermute x9, waiting for transfers between devices, shifted(): return lax.ppermute(value, axis, pairs)  9.3 us
  transfers between devices with their start and end apart: 22, of which 14 were waited for; matrix products, arithmetic and copies ran while one was open for 27% of the time, Pallas kernels for 0%

profile of v19, /device:TPU:0, one launch (start us, length us, event | category | flops | bytes accessed | tf_op | source)
XLA Modules:
  0.0 227.9 jit_solution(17444743292238383698)
XLA Ops:
  2.8 3.5 %collective-permute-start.2 = (bf16[18,9,4]{1,2,0:T(4,128)(2,1)S(1)}, bf16[18,9,4]{1,2,0:T(4,128)(2,1)S(1)}, u32[]{:S(2)}, u32[]{:S(2)}) collective-permute-start(bf16[18,9,4]{1,2,0:T(4,128)(2,1)S(1)} %bitcast.131), channel_id=1, source_target_pairs={{0,24},{8,0},{16,8},{24,16},{1,25},{9,1},{17,9},{25,17},{2,26},{10... | collective-permute-start | bytes 3896 | tf_op jit(solution)/shard_map/ppermute | solution.py:20
  18.5 3.4 %fusion.10 = bf16[9,256,256]{2,0,1:T(8,128)(2,1)} fusion(bf16[18,256,256]{2,1,0:T(8,128)(2,1)S(1)} %pad_maximum_fusion, bf16[18,9,1]{1,2,0:T(2,128)(2,1)S(1)} %get-tuple-element.67), kind=kOutput, calls=%fused_computation.12 | convolution fusion | flops 21233664 | bytes 3539268 | tf_op jit(solution)/shard_map/wv,wba->vba/dot_general | solution.py:24
  21.8 3.6 %fusion.21 = bf16[9,256,256]{2,1,0:T(8,128)(2,1)} fusion(bf16[9,256,256]{2,0,1:T(8,128)(2,1)} %fusion.10, bf16[1,1,4,256,256]{4,3,2,1,0:T(8,128)(2,1)} %param.15, s32[]{:T(128)S(6)} %select_n.81, bf16[1,1,4,256,256]{4,3,2,1,0:T(8,128)(2,1)} %param.14), kind=kOutput, calls=%fused_computation.51 | convolution fusion | flops 605159424 | bytes 3539968 | tf_op jit(solution)/shard_map/bd,vbc->vdc/dot_general | solution.py:30
  25.5 5.5 %collective-permute-start.6 = (bf16[9,256,256]{2,1,0:T(8,128)(2,1)}, bf16[9,256,256]{2,1,0:T(8,128)(2,1)}, u32[]{:S(2)}, u32[]{:S(2)}) collective-permute-start(bf16[9,256,256]{2,1,0:T(8,128)(2,1)} %fusion.21), channel_id=1, source_target_pairs={{0,4},{1,5},{8,12},{9,13},{16,20},{17,21},{24,28},{25,29}} | collective-permute-start | bytes 3538952 | tf_op jit(solution)/shard_map/ppermute | solution.py:69
  32.3 3.4 %fusion.14 = bf16[9,256,256]{2,0,1:T(8,128)(2,1)} fusion(bf16[18,256,256]{2,1,0:T(8,128)(2,1)S(1)} %pad_maximum_fusion, bf16[18,9,1]{1,2,0:T(2,128)(2,1)S(1)} %get-tuple-element.69), kind=kOutput, calls=%fused_computation.16 | convolution fusion | flops 21233664 | bytes 3539268 | tf_op jit(solution)/shard_map/wv,wba->vba/dot_general | solution.py:24
  35.6 3.7 %fusion.20 = bf16[9,256,256]{2,1,0:T(8,128)(2,1)} fusion(bf16[9,256,256]{2,0,1:T(8,128)(2,1)} %fusion.14, bf16[1,1,4,256,256]{4,3,2,1,0:T(8,128)(2,1)} %param.15, s32[]{:T(128)S(6)} %select_n.78, bf16[1,1,4,256,256]{4,3,2,1,0:T(8,128)(2,1)} %param.14), kind=kOutput, calls=%fused_computation.50 | convolution fusion | flops 605159424 | bytes 3539968 | tf_op jit(solution)/shard_map/bd,vbc->vdc/dot_general | solution.py:30
  41.0 5.2 %collective-permute-start.4 = (bf16[9,256,256]{2,1,0:T(8,128)(2,1)}, bf16[9,256,256]{2,1,0:T(8,128)(2,1)}, u32[]{:S(2)}, u32[]{:S(2)}) collective-permute-start(bf16[9,256,256]{2,1,0:T(8,128)(2,1)} %fusion.20), channel_id=1, source_target_pairs={{0,2},{2,4},{4,6},{1,3},{3,5},{5,7},{8,10},{10,12},{12,14},{9,11},... | collective-permute-start | bytes 3538952 | tf_op jit(solution)/shard_map/ppermute | solution.py:65
  49.6 3.7 %fusion.22 = bf16[9,256,256]{2,1,0:T(8,128)(2,1)} fusion(bf16[9,256,256]{2,0,1:T(8,128)(2,1)} %fusion.8, bf16[1,1,4,256,256]{4,3,2,1,0:T(8,128)(2,1)} %param.15, s32[]{:T(128)S(6)} %select_n.82, bf16[1,1,4,256,256]{4,3,2,1,0:T(8,128)(2,1)} %param.14), kind=kOutput, calls=%fused_computation.52 | convolution fusion | flops 605159424 | bytes 3539968 | tf_op jit(solution)/shard_map/bd,vbc->vdc/dot_general | solution.py:30
  60.4 20.2 %collective-permute-done.4 = bf16[9,256,256]{2,1,0:T(8,128)(2,1)} collective-permute-done((bf16[9,256,256]{2,1,0:T(8,128)(2,1)}, bf16[9,256,256]{2,1,0:T(8,128)(2,1)}, u32[]{:S(2)}, u32[]{:S(2)}) %collective-permute-start.4) | collective-permute-done | bytes 1179680 | tf_op jit(solution)/shard_map/ppermute | solution.py:65
  82.1 3.8 %collective-permute-start.8 = (bf16[4,256,256]{2,1,0:T(8,128)(2,1)S(1)}, bf16[4,256,256]{2,1,0:T(8,128)(2,1)S(1)}, u32[]{:S(2)}, u32[]{:S(2)}) collective-permute-start(bf16[4,256,256]{2,1,0:T(8,128)(2,1)S(1)} %add_convert_fusion.2), channel_id=1, source_target_pairs={{0,2},{2,6},{6,4},{4,0},{1,3},{3,7},{7,5},{5,1},{8,10},{10,14},{14... | collective-permute-start | bytes 1572872 | tf_op jit(solution)/shard_map/ppermute | solution.py:94
  90.7 6.9 %collective-permute-done.8 = bf16[4,256,256]{2,1,0:T(8,128)(2,1)S(1)} collective-permute-done((bf16[4,256,256]{2,1,0:T(8,128)(2,1)S(1)}, bf16[4,256,256]{2,1,0:T(8,128)(2,1)S(1)}, u32[]{:S(2)}, u32[]{:S(2)}) %collective-permute-start.8) | collective-permute-done | bytes 524320 | tf_op jit(solution)/shard_map/ppermute | solution.py:94
  101.4 13.4 %collective-permute-done.10 = bf16[5,256,256]{2,1,0:T(8,128)(2,1)S(1)} collective-permute-done((bf16[5,256,256]{2,1,0:T(8,128)(2,1)S(1)}, bf16[5,256,256]{2,1,0:T(8,128)(2,1)S(1)}, u32[]{:S(2)}, u32[]{:S(2)}) %collective-permute-start.10) | collective-permute-done | bytes 655392 | tf_op jit(solution)/shard_map/ppermute | solution.py:94
  119.0 3.4 %fusion.4 = bf16[9,256,256]{2,0,1:T(8,128)(2,1)} fusion(bf16[18,256,256]{2,1,0:T(8,128)(2,1)S(1)} %pad_maximum_fusion.1, bf16[18,9,1]{1,2,0:T(2,128)(2,1)S(1)} %get-tuple-element.65), kind=kOutput, calls=%fused_computation.6 | convolution fusion | flops 21233664 | bytes 3539268 | tf_op jit(solution)/shard_map/wv,wba->vba/dot_general | solution.py:24
  122.4 3.6 %fusion.23 = bf16[9,256,256]{2,1,0:T(8,128)(2,1)} fusion(bf16[9,256,256]{2,0,1:T(8,128)(2,1)} %fusion.4, bf16[4,256,256]{2,1,0:T(8,128)(2,1)S(1)} %copy-done.6, s32[]{:T(128)S(6)} %select_n.78, bf16[4,256,256]{2,1,0:T(8,128)(2,1)} %collective-permute-done), kind=kOutput, calls=%fused_computation.53 | convolution fusion | flops 605159424 | bytes 3539968 | tf_op jit(solution)/shard_map/bd,vbc->vdc/dot_general | solution.py:30
  133.3 3.5 %fusion.24 = bf16[9,256,256]{2,1,0:T(8,128)(2,1)} fusion(bf16[9,256,256]{2,0,1:T(8,128)(2,1)} %fusion.2, bf16[4,256,256]{2,1,0:T(8,128)(2,1)S(1)} %copy-done.6, s32[]{:T(128)S(6)} %select_n.81, bf16[4,256,256]{2,1,0:T(8,128)(2,1)} %collective-permute-done), kind=kOutput, calls=%fused_computation.54 | convolution fusion | flops 605159424 | bytes 3539968 | tf_op jit(solution)/shard_map/bd,vbc->vdc/dot_general | solution.py:30
  136.9 6.4 %collective-permute-start.14 = (bf16[9,256,256]{2,1,0:T(8,128)(2,1)}, bf16[9,256,256]{2,1,0:T(8,128)(2,1)}, u32[]{:S(2)}, u32[]{:S(2)}) collective-permute-start(bf16[9,256,256]{2,1,0:T(8,128)(2,1)} %fusion.24), channel_id=1, source_target_pairs={{0,4},{1,5},{8,12},{9,13},{16,20},{17,21},{24,28},{25,29}} | collective-permute-start | bytes 3538952 | tf_op jit(solution)/shard_map/ppermute | solution.py:69
  144.5 3.4 %fusion = bf16[9,256,256]{2,0,1:T(8,128)(2,1)} fusion(bf16[18,256,256]{2,1,0:T(8,128)(2,1)S(1)} %pad_maximum_fusion.1, bf16[18,9,1]{1,2,0:T(2,128)(2,1)S(1)} %get-tuple-element.63), kind=kOutput, calls=%fused_computation.2 | convolution fusion | flops 21233664 | bytes 3539268 | tf_op jit(solution)/shard_map/wv,wba->vba/dot_general | solution.py:24
  147.9 3.6 %fusion.25 = bf16[9,256,256]{2,1,0:T(8,128)(2,1)} fusion(bf16[9,256,256]{2,0,1:T(8,128)(2,1)} %fusion, bf16[4,256,256]{2,1,0:T(8,128)(2,1)S(1)} %copy-done.6, s32[]{:T(128)S(6)} %select_n.82, bf16[4,256,256]{2,1,0:T(8,128)(2,1)} %collective-permute-done), kind=kOutput, calls=%fused_computation.55 | convolution fusion | flops 605159424 | bytes 3539968 | tf_op jit(solution)/shard_map/bd,vbc->vdc/dot_general | solution.py:30
  155.5 24.8 %collective-permute-done.14 = bf16[9,256,256]{2,1,0:T(8,128)(2,1)} collective-permute-done((bf16[9,256,256]{2,1,0:T(8,128)(2,1)}, bf16[9,256,256]{2,1,0:T(8,128)(2,1)}, u32[]{:S(2)}, u32[]{:S(2)}) %collective-permute-start.14) | collective-permute-done | bytes 1179680 | tf_op jit(solution)/shard_map/ppermute | solution.py:69
  185.3 4.5 %fusion.17 = f32[9,256,256]{2,1,0:T(8,128)S(1)} fusion(bf16[9,256,256]{2,1,0:T(8,128)(2,1)} %collective-permute-done.13, bf16[9,256,256]{2,1,0:T(8,128)(2,1)} %collective-permute-done.12, bf16[9,256,256]{2,1,0:T(8,128)(2,1)} %collective-permute-done.14, bf16[9,256,256]{2,1,0:T(8,128)(2,1)} %collective-permute-done.15, f32[]{:T(128)S(6)} %select_n.83, ...), kind=kOutput, calls=%fused_computation.22 | convolution fusion | flops 612237312 | bytes 9437192 | tf_op jit(solution)/shard_map/bd,vbc->vdc/dot_general | solution.py:30
  189.8 8.1 %collective-permute-done.16 = bf16[4,256,256]{2,1,0:T(8,128)(2,1)S(1)} collective-permute-done((bf16[4,256,256]{2,1,0:T(8,128)(2,1)}, bf16[4,256,256]{2,1,0:T(8,128)(2,1)S(1)}, u32[]{:S(2)}, u32[]{:S(2)}) %collective-permute-start.16) | collective-permute-done | bytes 524320 | tf_op jit(solution)/shard_map/ppermute | solution.py:94
  201.0 9.3 %collective-permute-done.18 = bf16[3,256,256]{2,1,0:T(8,128)(2,1)S(1)} collective-permute-done((bf16[3,256,256]{2,1,0:T(8,128)(2,1)S(1)}, bf16[3,256,256]{2,1,0:T(8,128)(2,1)S(1)}, u32[]{:S(2)}, u32[]{:S(2)}) %collective-permute-start.18) | collective-permute-done | bytes 393248 | tf_op jit(solution)/shard_map/ppermute | solution.py:94
  212.9 7.0 %collective-permute-done.20 = bf16[2,256,256]{2,1,0:T(8,128)(2,1)S(1)} collective-permute-done((bf16[2,256,256]{2,1,0:T(8,128)(2,1)S(1)}, bf16[2,256,256]{2,1,0:T(8,128)(2,1)S(1)}, u32[]{:S(2)}, u32[]{:S(2)}) %collective-permute-start.20) | collective-permute-done | bytes 262176 | tf_op jit(solution)/shard_map/ppermute | solution.py:94
  221.9 4.9 %collective-permute-done.21 = bf16[1,2,1,256,256]{4,3,1,2,0:T(8,128)(2,1)S(1)} collective-permute-done((bf16[1,2,1,256,256]{4,3,1,2,0:T(8,128)(2,1)S(1)}, bf16[1,2,1,256,256]{4,3,1,2,0:T(8,128)(2,1)S(1)}, u32[]{:S(2)}, u32[]{:S(2)}) %collective-permute-start.21) | collective-permute-done | bytes 262176 | tf_op jit(solution)/shard_map/ppermute | solution.py:20
  (88 shorter events, 62.9 us)
Async XLA Ops:
  2.2 14.4 %collective-permute-start.3 = (bf16[9,256,256]{2,1,0:T(8,128)(2,1)S(1)}, bf16[9,256,256]{2,1,0:T(8,128)(2,1)}, u32[]{:S(2)}, u32[]{:S(2)}) collective-permute-start(bf16[9,256,256]{2,1,0:T(8,128)(2,1)S(1)} %bitcast_select_fusion), channel_id=1, source_target_pairs={{0,1},{1,0},{2,3},{3,2},{4,5},{5,4},{6,7},{7,6},{8,9},{9,8},{10,11... | collective-permute-start | bytes 3538952 | tf_op jit(solution)/shard_map/ppermute | solution.py:20
  2.8 36.5 %collective-permute-start.2 = (bf16[18,9,4]{1,2,0:T(4,128)(2,1)S(1)}, bf16[18,9,4]{1,2,0:T(4,128)(2,1)S(1)}, u32[]{:S(2)}, u32[]{:S(2)}) collective-permute-start(bf16[18,9,4]{1,2,0:T(4,128)(2,1)S(1)} %bitcast.131), channel_id=1, source_target_pairs={{0,24},{8,0},{16,8},{24,16},{1,25},{9,1},{17,9},{25,17},{2,26},{10... | collective-permute-start | bytes 3896 | tf_op jit(solution)/shard_map/ppermute | solution.py:20
  6.3 33.0 %collective-permute-start.1 = (bf16[4,256,256]{2,1,0:T(8,128)(2,1)}, bf16[4,256,256]{2,1,0:T(8,128)(2,1)S(1)}, u32[]{:S(2)}, u32[]{:S(2)}) collective-permute-start(bf16[4,256,256]{2,1,0:T(8,128)(2,1)} %bitcast.1), channel_id=1, source_target_pairs={{0,24},{8,0},{16,8},{24,16},{1,25},{9,1},{17,9},{25,17},{2,26},{10... | collective-permute-start | bytes 1572872 | tf_op jit(solution)/shard_map/ppermute | solution.py:20
  6.9 32.5 %collective-permute-start = (bf16[4,256,256]{2,1,0:T(8,128)(2,1)}, bf16[4,256,256]{2,1,0:T(8,128)(2,1)}, u32[]{:S(2)}, u32[]{:S(2)}) collective-permute-start(bf16[4,256,256]{2,1,0:T(8,128)(2,1)} %bitcast), channel_id=1, source_target_pairs={{0,24},{8,0},{16,8},{24,16},{1,25},{9,1},{17,9},{25,17},{2,26},{10... | collective-permute-start | bytes 1572872 | tf_op jit(solution)/shard_map/ppermute | solution.py:20
  25.5 34.0 %collective-permute-start.6 = (bf16[9,256,256]{2,1,0:T(8,128)(2,1)}, bf16[9,256,256]{2,1,0:T(8,128)(2,1)}, u32[]{:S(2)}, u32[]{:S(2)}) collective-permute-start(bf16[9,256,256]{2,1,0:T(8,128)(2,1)} %fusion.21), channel_id=1, source_target_pairs={{0,4},{1,5},{8,12},{9,13},{16,20},{17,21},{24,28},{25,29}} | collective-permute-start | bytes 3538952 | tf_op jit(solution)/shard_map/ppermute | solution.py:69
  31.0 29.4 %collective-permute-start.5 = (bf16[9,256,256]{2,1,0:T(8,128)(2,1)}, bf16[9,256,256]{2,1,0:T(8,128)(2,1)}, u32[]{:S(2)}, u32[]{:S(2)}) collective-permute-start(bf16[9,256,256]{2,1,0:T(8,128)(2,1)} %fusion.21), channel_id=1, source_target_pairs={{6,4},{4,2},{2,0},{7,5},{5,3},{3,1},{14,12},{12,10},{10,8},{15,13}... | collective-permute-start | bytes 3538952 | tf_op jit(solution)/shard_map/ppermute | solution.py:68
  39.3 21.1 %collective-permute-start.7 = (bf16[9,256,256]{2,1,0:T(8,128)(2,1)}, bf16[9,256,256]{2,1,0:T(8,128)(2,1)}, u32[]{:S(2)}, u32[]{:S(2)}) collective-permute-start(bf16[9,256,256]{2,1,0:T(8,128)(2,1)} %fusion.20), channel_id=1, source_target_pairs={{6,2},{7,3},{14,10},{15,11},{22,18},{23,19},{30,26},{31,27}} | collective-permute-start | bytes 3538952 | tf_op jit(solution)/shard_map/ppermute | solution.py:66
  41.0 39.6 %collective-permute-start.4 = (bf16[9,256,256]{2,1,0:T(8,128)(2,1)}, bf16[9,256,256]{2,1,0:T(8,128)(2,1)}, u32[]{:S(2)}, u32[]{:S(2)}) collective-permute-start(bf16[9,256,256]{2,1,0:T(8,128)(2,1)} %fusion.20), channel_id=1, source_target_pairs={{0,2},{2,4},{4,6},{1,3},{3,5},{5,7},{8,10},{10,12},{12,14},{9,11},... | collective-permute-start | bytes 3538952 | tf_op jit(solution)/shard_map/ppermute | solution.py:65
  56.7 23.9 %copy-start.3 = (bf16[9,256,256]{2,1,0:T(8,128)(2,1)S(1)}, bf16[9,256,256]{2,1,0:T(8,128)(2,1)}, u32[]{:S(2)}) copy-start(bf16[9,256,256]{2,1,0:T(8,128)(2,1)} %fusion.22) | copy-start | bytes 3538948
  82.1 15.5 %collective-permute-start.8 = (bf16[4,256,256]{2,1,0:T(8,128)(2,1)S(1)}, bf16[4,256,256]{2,1,0:T(8,128)(2,1)S(1)}, u32[]{:S(2)}, u32[]{:S(2)}) collective-permute-start(bf16[4,256,256]{2,1,0:T(8,128)(2,1)S(1)} %add_convert_fusion.2), channel_id=1, source_target_pairs={{0,2},{2,6},{6,4},{4,0},{1,3},{3,7},{7,5},{5,1},{8,10},{10,14},{14... | collective-permute-start | bytes 1572872 | tf_op jit(solution)/shard_map/ppermute | solution.py:94
  97.7 17.1 %collective-permute-start.10 = (bf16[5,256,256]{2,1,0:T(8,128)(2,1)S(1)}, bf16[5,256,256]{2,1,0:T(8,128)(2,1)S(1)}, u32[]{:S(2)}, u32[]{:S(2)}) collective-permute-start(bf16[5,256,256]{2,1,0:T(8,128)(2,1)S(1)} %add_convert_fusion), channel_id=1, source_target_pairs={{0,2},{2,6},{6,4},{4,0},{1,3},{3,7},{7,5},{5,1},{8,10},{10,14},{14... | collective-permute-start | bytes 1966088 | tf_op jit(solution)/shard_map/ppermute | solution.py:94
  98.7 1.9 collective-permute-start.9
  115.0 2.3 %collective-permute-start.11 = (bf16[5,256,256]{2,1,0:T(8,128)(2,1)S(1)}, bf16[5,256,256]{2,1,0:T(8,128)(2,1)}, u32[]{:S(2)}, u32[]{:S(2)}) collective-permute-start(bf16[5,256,256]{2,1,0:T(8,128)(2,1)S(1)} %fusion.27), channel_id=1, source_target_pairs={{0,1},{1,0},{2,3},{3,2},{4,5},{5,4},{6,7},{7,6},{8,9},{9,8},{10,11... | collective-permute-start | bytes 1966088 | tf_op jit(solution)/shard_map/ppermute | solution.py:20
  126.0 28.9 %collective-permute-start.15 = (bf16[9,256,256]{2,1,0:T(8,128)(2,1)}, bf16[9,256,256]{2,1,0:T(8,128)(2,1)}, u32[]{:S(2)}, u32[]{:S(2)}) collective-permute-start(bf16[9,256,256]{2,1,0:T(8,128)(2,1)} %fusion.23), channel_id=1, source_target_pairs={{6,2},{7,3},{14,10},{15,11},{22,18},{23,19},{30,26},{31,27}} | collective-permute-start | bytes 3538952 | tf_op jit(solution)/shard_map/ppermute | solution.py:66
  127.6 27.9 %collective-permute-start.12 = (bf16[9,256,256]{2,1,0:T(8,128)(2,1)}, bf16[9,256,256]{2,1,0:T(8,128)(2,1)}, u32[]{:S(2)}, u32[]{:S(2)}) collective-permute-start(bf16[9,256,256]{2,1,0:T(8,128)(2,1)} %fusion.23), channel_id=1, source_target_pairs={{0,2},{2,4},{4,6},{1,3},{3,5},{5,7},{8,10},{10,12},{12,14},{9,11},... | collective-permute-start | bytes 3538952 | tf_op jit(solution)/shard_map/ppermute | solution.py:65
  136.9 43.4 %collective-permute-start.14 = (bf16[9,256,256]{2,1,0:T(8,128)(2,1)}, bf16[9,256,256]{2,1,0:T(8,128)(2,1)}, u32[]{:S(2)}, u32[]{:S(2)}) collective-permute-start(bf16[9,256,256]{2,1,0:T(8,128)(2,1)} %fusion.24), channel_id=1, source_target_pairs={{0,4},{1,5},{8,12},{9,13},{16,20},{17,21},{24,28},{25,29}} | collective-permute-start | bytes 3538952 | tf_op jit(solution)/shard_map/ppermute | solution.py:69
  143.3 37.1 %collective-permute-start.13 = (bf16[9,256,256]{2,1,0:T(8,128)(2,1)}, bf16[9,256,256]{2,1,0:T(8,128)(2,1)}, u32[]{:S(2)}, u32[]{:S(2)}) collective-permute-start(bf16[9,256,256]{2,1,0:T(8,128)(2,1)} %fusion.24), channel_id=1, source_target_pairs={{6,4},{4,2},{2,0},{7,5},{5,3},{3,1},{14,12},{12,10},{10,8},{15,13}... | collective-permute-start | bytes 3538952 | tf_op jit(solution)/shard_map/ppermute | solution.py:68
  151.5 28.8 %copy-start.2 = (bf16[9,256,256]{2,1,0:T(8,128)(2,1)S(1)}, bf16[9,256,256]{2,1,0:T(8,128)(2,1)}, u32[]{:S(2)}) copy-start(bf16[9,256,256]{2,1,0:T(8,128)(2,1)} %fusion.25) | copy-start | bytes 3538948
  182.6 15.3 %collective-permute-start.16 = (bf16[4,256,256]{2,1,0:T(8,128)(2,1)}, bf16[4,256,256]{2,1,0:T(8,128)(2,1)S(1)}, u32[]{:S(2)}, u32[]{:S(2)}) collective-permute-start(bf16[4,256,256]{2,1,0:T(8,128)(2,1)} %add_convert_fusion.1), channel_id=1, source_target_pairs={{0,2},{2,6},{6,4},{4,0},{1,3},{3,7},{7,5},{5,1},{8,10},{10,14},{14... | collective-permute-start | bytes 1572872 | tf_op jit(solution)/shard_map/ppermute | solution.py:94
  198.0 12.9 %collective-permute-start.17 = (bf16[1,4,1,256,256]{4,3,1,2,0:T(8,128)(2,1)S(1)}, bf16[1,4,1,256,256]{4,3,1,2,0:T(8,128)(2,1)S(1)}, u32[]{:S(2)}, u32[]{:S(2)}) collective-permute-start(bf16[1,4,1,256,256]{4,3,1,2,0:T(8,128)(2,1)S(1)} %bitcast.130), channel_id=1, source_target_pairs={{0,16},{8,24},{16,0},{24,8},{1,17},{9,25},{17,1},{25,9},{2,18},{10... | collective-permute-start | bytes 1572872 | tf_op jit(solution)/shard_map/ppermute | solution.py:20
  199.6 10.7 %collective-permute-start.18 = (bf16[3,256,256]{2,1,0:T(8,128)(2,1)S(1)}, bf16[3,256,256]{2,1,0:T(8,128)(2,1)S(1)}, u32[]{:S(2)}, u32[]{:S(2)}) collective-permute-start(bf16[3,256,256]{2,1,0:T(8,128)(2,1)S(1)} %add_convert_fusion.3), channel_id=1, source_target_pairs={{0,2},{2,6},{6,4},{4,0},{1,3},{3,7},{7,5},{5,1},{8,10},{10,14},{14... | collective-permute-start | bytes 1179656 | tf_op jit(solution)/shard_map/ppermute | solution.py:94
  211.1 9.2 %collective-permute-start.19 = (bf16[1,3,1,256,256]{4,3,1,2,0:T(8,128)(2,1)S(1)}, bf16[1,3,1,256,256]{4,3,1,2,0:T(8,128)(2,1)S(1)}, u32[]{:S(2)}, u32[]{:S(2)}) collective-permute-start(bf16[1,3,1,256,256]{4,3,1,2,0:T(8,128)(2,1)S(1)} %bitcast.133), channel_id=1, source_target_pairs={{0,16},{8,24},{16,0},{24,8},{1,17},{9,25},{17,1},{25,9},{2,18},{10... | collective-permute-start | bytes 1179656 | tf_op jit(solution)/shard_map/ppermute | solution.py:20
  212.6 7.3 %collective-permute-start.20 = (bf16[2,256,256]{2,1,0:T(8,128)(2,1)S(1)}, bf16[2,256,256]{2,1,0:T(8,128)(2,1)S(1)}, u32[]{:S(2)}, u32[]{:S(2)}) collective-permute-start(bf16[2,256,256]{2,1,0:T(8,128)(2,1)S(1)} %add_convert_fusion.4), channel_id=1, source_target_pairs={{0,2},{2,6},{6,4},{4,0},{1,3},{3,7},{7,5},{5,1},{8,10},{10,14},{14... | collective-permute-start | bytes 786440 | tf_op jit(solution)/shard_map/ppermute | solution.py:94
  220.4 6.4 %collective-permute-start.21 = (bf16[1,2,1,256,256]{4,3,1,2,0:T(8,128)(2,1)S(1)}, bf16[1,2,1,256,256]{4,3,1,2,0:T(8,128)(2,1)S(1)}, u32[]{:S(2)}, u32[]{:S(2)}) collective-permute-start(bf16[1,2,1,256,256]{4,3,1,2,0:T(8,128)(2,1)S(1)} %fusion.36), channel_id=1, source_target_pairs={{0,16},{8,24},{16,0},{24,8},{1,17},{9,25},{17,1},{25,9},{2,18},{10... | collective-permute-start | bytes 786440 | tf_op jit(solution)/shard_map/ppermute | solution.py:20
  (9 other events, 65.3 us)

commit v20 on v19

--- a/solution.py
+++ b/solution.py
@@ -77,7 +77,7 @@
     total = own.astype(f32) + keep_right * got_right.astype(f32)
     total = total + keep_left * got_left.astype(f32) + got_middle.astype(f32)
     width = third.shape[0]
-    bounds = [width * k // pieces for k in range(pieces + 1)]
+    bounds = [width - width * (pieces - k) // pieces for k in range(pieces + 1)]
     if finish is not chan_copies:
         weights = [sum(range(pieces, pieces - k, -1)) for k in range(pieces + 1)]
         bounds = [width * w // weights[-1] for w in weights]

time: 229 us -> 229 us (level)
  starting transfers between devices: 42.8 us -> 46.1 us
  waiting for transfers between devices: 101 us -> 98.3 us
    ppermute x5, starting transfers between devices: 6.59 us -> 9.3 us  [advance_line(): got_last = lax.ppermute(send, 'sector', LAST)]
  transfers between devices with their start and end apart: 22 -> 22, of which waited for: 14 -> 13; matrix products, arithmetic and copies ran while one was open for 27% -> 27% of each run, Pallas kernels for 0% -> 0%
where the time goes in v20:
time: 229 us; the launch traced here: 228 us
  waiting for transfers between devices  98.3 us (43%)
  matrix products  55.7 us (24%)
  starting transfers between devices  46.1 us (20%)
  other arithmetic  18.1 us (8%)
  between operations  6.61 us (3%)
  local copies, waits for them, and re-layouts  3.32 us (1%)
    ppermute x5, waiting for transfers between devices, advance_line(): got_last = lax.ppermute(send, 'sector', LAST)  45 us
    dot_general x8, matrix products, term(): jnp.einsum('bd,vbc->vdc', bra_p, rotated, preferred_element_type=jnp.floa...  28.9 us
    dot_general x8, matrix products, term(): jnp.einsum('wv,wba->vba', mpo_p, gathered, preferred_element_type=jnp.flo...  26.8 us
    ppermute x2, waiting for transfers between devices, advance_line(): middle_right = lax.ppermute(slot_b, 'sector', ((0, 2),))  24.6 us
    ppermute x2, waiting for transfers between devices, advance_line(): got_right = lax.ppermute(slot_a, 'sector', RIGHT)  20.5 us
    ppermute x2, starting transfers between devices, advance_line(): middle_right = lax.ppermute(slot_b, 'sector', ((0, 2),))  12.3 us
    ppermute x9, starting transfers between devices, shifted(): return lax.ppermute(value, axis, pairs)  10.9 us
    ppermute x5, starting transfers between devices, advance_line(): got_last = lax.ppermute(send, 'sector', LAST)  9.3 us
  transfers between devices with their start and end apart: 22, of which 13 were waited for; matrix products, arithmetic and copies ran while one was open for 27% of the time, Pallas kernels for 0%

profile of v20, /device:TPU:0, one launch (start us, length us, event | category | flops | bytes accessed | tf_op | source)
XLA Modules:
  0.0 228.3 jit_solution(15169962778794085538)
XLA Ops:
  2.8 3.5 %collective-permute-start.2 = (bf16[18,9,4]{1,2,0:T(4,128)(2,1)S(1)}, bf16[18,9,4]{1,2,0:T(4,128)(2,1)S(1)}, u32[]{:S(2)}, u32[]{:S(2)}) collective-permute-start(bf16[18,9,4]{1,2,0:T(4,128)(2,1)S(1)} %bitcast.131), channel_id=1, source_target_pairs={{0,24},{8,0},{16,8},{24,16},{1,25},{9,1},{17,9},{25,17},{2,26},{10... | collective-permute-start | bytes 3896 | tf_op jit(solution)/shard_map/ppermute | solution.py:20
  18.6 3.4 %fusion.10 = bf16[9,256,256]{2,0,1:T(8,128)(2,1)} fusion(bf16[18,256,256]{2,1,0:T(8,128)(2,1)S(1)} %pad_maximum_fusion, bf16[18,9,1]{1,2,0:T(2,128)(2,1)S(1)} %get-tuple-element.67), kind=kOutput, calls=%fused_computation.12 | convolution fusion | flops 21233664 | bytes 3539268 | tf_op jit(solution)/shard_map/wv,wba->vba/dot_general | solution.py:24
  21.9 3.6 %fusion.21 = bf16[9,256,256]{2,1,0:T(8,128)(2,1)} fusion(bf16[9,256,256]{2,0,1:T(8,128)(2,1)} %fusion.10, bf16[1,1,4,256,256]{4,3,2,1,0:T(8,128)(2,1)} %param.15, s32[]{:T(128)S(6)} %select_n.81, bf16[1,1,4,256,256]{4,3,2,1,0:T(8,128)(2,1)} %param.14), kind=kOutput, calls=%fused_computation.51 | convolution fusion | flops 605159424 | bytes 3539968 | tf_op jit(solution)/shard_map/bd,vbc->vdc/dot_general | solution.py:30
  25.6 5.5 %collective-permute-start.6 = (bf16[9,256,256]{2,1,0:T(8,128)(2,1)}, bf16[9,256,256]{2,1,0:T(8,128)(2,1)}, u32[]{:S(2)}, u32[]{:S(2)}) collective-permute-start(bf16[9,256,256]{2,1,0:T(8,128)(2,1)} %fusion.21), channel_id=1, source_target_pairs={{0,4},{1,5},{8,12},{9,13},{16,20},{17,21},{24,28},{25,29}} | collective-permute-start | bytes 3538952 | tf_op jit(solution)/shard_map/ppermute | solution.py:69
  32.4 3.4 %fusion.14 = bf16[9,256,256]{2,0,1:T(8,128)(2,1)} fusion(bf16[18,256,256]{2,1,0:T(8,128)(2,1)S(1)} %pad_maximum_fusion, bf16[18,9,1]{1,2,0:T(2,128)(2,1)S(1)} %get-tuple-element.69), kind=kOutput, calls=%fused_computation.16 | convolution fusion | flops 21233664 | bytes 3539268 | tf_op jit(solution)/shard_map/wv,wba->vba/dot_general | solution.py:24
  35.7 3.7 %fusion.20 = bf16[9,256,256]{2,1,0:T(8,128)(2,1)} fusion(bf16[9,256,256]{2,0,1:T(8,128)(2,1)} %fusion.14, bf16[1,1,4,256,256]{4,3,2,1,0:T(8,128)(2,1)} %param.15, s32[]{:T(128)S(6)} %select_n.78, bf16[1,1,4,256,256]{4,3,2,1,0:T(8,128)(2,1)} %param.14), kind=kOutput, calls=%fused_computation.50 | convolution fusion | flops 605159424 | bytes 3539968 | tf_op jit(solution)/shard_map/bd,vbc->vdc/dot_general | solution.py:30
  41.1 5.2 %collective-permute-start.4 = (bf16[9,256,256]{2,1,0:T(8,128)(2,1)}, bf16[9,256,256]{2,1,0:T(8,128)(2,1)}, u32[]{:S(2)}, u32[]{:S(2)}) collective-permute-start(bf16[9,256,256]{2,1,0:T(8,128)(2,1)} %fusion.20), channel_id=1, source_target_pairs={{0,2},{2,4},{4,6},{1,3},{3,5},{5,7},{8,10},{10,12},{12,14},{9,11},... | collective-permute-start | bytes 3538952 | tf_op jit(solution)/shard_map/ppermute | solution.py:65
  49.7 3.7 %fusion.22 = bf16[9,256,256]{2,1,0:T(8,128)(2,1)} fusion(bf16[9,256,256]{2,0,1:T(8,128)(2,1)} %fusion.8, bf16[1,1,4,256,256]{4,3,2,1,0:T(8,128)(2,1)} %param.15, s32[]{:T(128)S(6)} %select_n.82, bf16[1,1,4,256,256]{4,3,2,1,0:T(8,128)(2,1)} %param.14), kind=kOutput, calls=%fused_computation.52 | convolution fusion | flops 605159424 | bytes 3539968 | tf_op jit(solution)/shard_map/bd,vbc->vdc/dot_general | solution.py:30
  60.5 20.2 %collective-permute-done.4 = bf16[9,256,256]{2,1,0:T(8,128)(2,1)} collective-permute-done((bf16[9,256,256]{2,1,0:T(8,128)(2,1)}, bf16[9,256,256]{2,1,0:T(8,128)(2,1)}, u32[]{:S(2)}, u32[]{:S(2)}) %collective-permute-start.4) | collective-permute-done | bytes 1179680 | tf_op jit(solution)/shard_map/ppermute | solution.py:65
  82.3 3.8 %collective-permute-start.8 = (bf16[5,256,256]{2,1,0:T(8,128)(2,1)S(1)}, bf16[5,256,256]{2,1,0:T(8,128)(2,1)S(1)}, u32[]{:S(2)}, u32[]{:S(2)}) collective-permute-start(bf16[5,256,256]{2,1,0:T(8,128)(2,1)S(1)} %add_convert_fusion), channel_id=1, source_target_pairs={{0,2},{2,6},{6,4},{4,0},{1,3},{3,7},{7,5},{5,1},{8,10},{10,14},{14... | collective-permute-start | bytes 1966088 | tf_op jit(solution)/shard_map/ppermute | solution.py:94
  90.8 9.9 %collective-permute-done.8 = bf16[5,256,256]{2,1,0:T(8,128)(2,1)S(1)} collective-permute-done((bf16[5,256,256]{2,1,0:T(8,128)(2,1)S(1)}, bf16[5,256,256]{2,1,0:T(8,128)(2,1)S(1)}, u32[]{:S(2)}, u32[]{:S(2)}) %collective-permute-start.8) | collective-permute-done | bytes 655392 | tf_op jit(solution)/shard_map/ppermute | solution.py:94
  101.8 14.3 %collective-permute-done.10 = bf16[4,256,256]{2,1,0:T(8,128)(2,1)S(1)} collective-permute-done((bf16[4,256,256]{2,1,0:T(8,128)(2,1)S(1)}, bf16[4,256,256]{2,1,0:T(8,128)(2,1)S(1)}, u32[]{:S(2)}, u32[]{:S(2)}) %collective-permute-start.10) | collective-permute-done | bytes 524320 | tf_op jit(solution)/shard_map/ppermute | solution.py:94
  120.1 3.4 %fusion.4 = bf16[9,256,256]{2,0,1:T(8,128)(2,1)} fusion(bf16[18,256,256]{2,1,0:T(8,128)(2,1)S(1)} %pad_maximum_fusion.1, bf16[18,9,1]{1,2,0:T(2,128)(2,1)S(1)} %get-tuple-element.65), kind=kOutput, calls=%fused_computation.6 | convolution fusion | flops 21233664 | bytes 3539268 | tf_op jit(solution)/shard_map/wv,wba->vba/dot_general | solution.py:24
  123.5 3.6 %fusion.23 = bf16[9,256,256]{2,1,0:T(8,128)(2,1)} fusion(bf16[9,256,256]{2,0,1:T(8,128)(2,1)} %fusion.4, bf16[4,256,256]{2,1,0:T(8,128)(2,1)S(1)} %copy-done.5, s32[]{:T(128)S(6)} %select_n.78, bf16[4,256,256]{2,1,0:T(8,128)(2,1)} %collective-permute-done), kind=kOutput, calls=%fused_computation.53 | convolution fusion | flops 605159424 | bytes 3539968 | tf_op jit(solution)/shard_map/bd,vbc->vdc/dot_general | solution.py:30
  134.6 3.5 %fusion.24 = bf16[9,256,256]{2,1,0:T(8,128)(2,1)} fusion(bf16[9,256,256]{2,0,1:T(8,128)(2,1)} %fusion.2, bf16[4,256,256]{2,1,0:T(8,128)(2,1)S(1)} %copy-done.5, s32[]{:T(128)S(6)} %select_n.81, bf16[4,256,256]{2,1,0:T(8,128)(2,1)} %collective-permute-done), kind=kOutput, calls=%fused_computation.54 | convolution fusion | flops 605159424 | bytes 3539968 | tf_op jit(solution)/shard_map/bd,vbc->vdc/dot_general | solution.py:30
  138.1 6.7 %collective-permute-start.14 = (bf16[9,256,256]{2,1,0:T(8,128)(2,1)}, bf16[9,256,256]{2,1,0:T(8,128)(2,1)}, u32[]{:S(2)}, u32[]{:S(2)}) collective-permute-start(bf16[9,256,256]{2,1,0:T(8,128)(2,1)} %fusion.24), channel_id=1, source_target_pairs={{0,4},{1,5},{8,12},{9,13},{16,20},{17,21},{24,28},{25,29}} | collective-permute-start | bytes 3538952 | tf_op jit(solution)/shard_map/ppermute | solution.py:69
  146.2 3.4 %fusion = bf16[9,256,256]{2,0,1:T(8,128)(2,1)} fusion(bf16[18,256,256]{2,1,0:T(8,128)(2,1)S(1)} %pad_maximum_fusion.1, bf16[18,9,1]{1,2,0:T(2,128)(2,1)S(1)} %get-tuple-element.63), kind=kOutput, calls=%fused_computation.2 | convolution fusion | flops 21233664 | bytes 3539268 | tf_op jit(solution)/shard_map/wv,wba->vba/dot_general | solution.py:24
  149.5 3.6 %fusion.25 = bf16[9,256,256]{2,1,0:T(8,128)(2,1)} fusion(bf16[9,256,256]{2,0,1:T(8,128)(2,1)} %fusion, bf16[4,256,256]{2,1,0:T(8,128)(2,1)S(1)} %copy-done.5, s32[]{:T(128)S(6)} %select_n.82, bf16[4,256,256]{2,1,0:T(8,128)(2,1)} %collective-permute-done), kind=kOutput, calls=%fused_computation.55 | convolution fusion | flops 605159424 | bytes 3539968 | tf_op jit(solution)/shard_map/bd,vbc->vdc/dot_general | solution.py:30
  156.8 24.6 %collective-permute-done.14 = bf16[9,256,256]{2,1,0:T(8,128)(2,1)} collective-permute-done((bf16[9,256,256]{2,1,0:T(8,128)(2,1)}, bf16[9,256,256]{2,1,0:T(8,128)(2,1)}, u32[]{:S(2)}, u32[]{:S(2)}) %collective-permute-start.14) | collective-permute-done | bytes 1179680 | tf_op jit(solution)/shard_map/ppermute | solution.py:69
  187.0 4.5 %fusion.17 = f32[9,256,256]{2,1,0:T(8,128)S(1)} fusion(bf16[9,256,256]{2,1,0:T(8,128)(2,1)} %collective-permute-done.13, bf16[9,256,256]{2,1,0:T(8,128)(2,1)} %collective-permute-done.12, bf16[9,256,256]{2,1,0:T(8,128)(2,1)} %collective-permute-done.14, bf16[9,256,256]{2,1,0:T(8,128)(2,1)} %collective-permute-done.15, f32[]{:T(128)S(6)} %select_n.83, ...), kind=kOutput, calls=%fused_computation.22 | convolution fusion | flops 612237312 | bytes 9437192 | tf_op jit(solution)/shard_map/bd,vbc->vdc/dot_general | solution.py:30
  191.4 7.3 %collective-permute-done.16 = bf16[4,256,256]{2,1,0:T(8,128)(2,1)S(1)} collective-permute-done((bf16[4,256,256]{2,1,0:T(8,128)(2,1)}, bf16[4,256,256]{2,1,0:T(8,128)(2,1)S(1)}, u32[]{:S(2)}, u32[]{:S(2)}) %collective-permute-start.16) | collective-permute-done | bytes 524320 | tf_op jit(solution)/shard_map/ppermute | solution.py:94
  202.7 7.9 %collective-permute-done.18 = bf16[3,256,256]{2,1,0:T(8,128)(2,1)S(1)} collective-permute-done((bf16[3,256,256]{2,1,0:T(8,128)(2,1)S(1)}, bf16[3,256,256]{2,1,0:T(8,128)(2,1)S(1)}, u32[]{:S(2)}, u32[]{:S(2)}) %collective-permute-start.18) | collective-permute-done | bytes 393248 | tf_op jit(solution)/shard_map/ppermute | solution.py:94
  214.6 5.6 %collective-permute-done.20 = bf16[2,256,256]{2,1,0:T(8,128)(2,1)S(1)} collective-permute-done((bf16[2,256,256]{2,1,0:T(8,128)(2,1)S(1)}, bf16[2,256,256]{2,1,0:T(8,128)(2,1)S(1)}, u32[]{:S(2)}, u32[]{:S(2)}) %collective-permute-start.20) | collective-permute-done | bytes 262176 | tf_op jit(solution)/shard_map/ppermute | solution.py:94
  222.2 4.9 %collective-permute-done.21 = bf16[1,2,1,256,256]{4,3,1,2,0:T(8,128)(2,1)S(1)} collective-permute-done((bf16[1,2,1,256,256]{4,3,1,2,0:T(8,128)(2,1)S(1)}, bf16[1,2,1,256,256]{4,3,1,2,0:T(8,128)(2,1)S(1)}, u32[]{:S(2)}, u32[]{:S(2)}) %collective-permute-start.21) | collective-permute-done | bytes 262176 | tf_op jit(solution)/shard_map/ppermute | solution.py:20
  (86 shorter events, 62.6 us)
Async XLA Ops:
  2.2 14.6 %collective-permute-start.3 = (bf16[9,256,256]{2,1,0:T(8,128)(2,1)S(1)}, bf16[9,256,256]{2,1,0:T(8,128)(2,1)}, u32[]{:S(2)}, u32[]{:S(2)}) collective-permute-start(bf16[9,256,256]{2,1,0:T(8,128)(2,1)S(1)} %bitcast_select_fusion), channel_id=1, source_target_pairs={{0,1},{1,0},{2,3},{3,2},{4,5},{5,4},{6,7},{7,6},{8,9},{9,8},{10,11... | collective-permute-start | bytes 3538952 | tf_op jit(solution)/shard_map/ppermute | solution.py:20
  2.8 36.6 %collective-permute-start.2 = (bf16[18,9,4]{1,2,0:T(4,128)(2,1)S(1)}, bf16[18,9,4]{1,2,0:T(4,128)(2,1)S(1)}, u32[]{:S(2)}, u32[]{:S(2)}) collective-permute-start(bf16[18,9,4]{1,2,0:T(4,128)(2,1)S(1)} %bitcast.131), channel_id=1, source_target_pairs={{0,24},{8,0},{16,8},{24,16},{1,25},{9,1},{17,9},{25,17},{2,26},{10... | collective-permute-start | bytes 3896 | tf_op jit(solution)/shard_map/ppermute | solution.py:20
  6.3 33.1 %collective-permute-start.1 = (bf16[4,256,256]{2,1,0:T(8,128)(2,1)}, bf16[4,256,256]{2,1,0:T(8,128)(2,1)S(1)}, u32[]{:S(2)}, u32[]{:S(2)}) collective-permute-start(bf16[4,256,256]{2,1,0:T(8,128)(2,1)} %bitcast.1), channel_id=1, source_target_pairs={{0,24},{8,0},{16,8},{24,16},{1,25},{9,1},{17,9},{25,17},{2,26},{10... | collective-permute-start | bytes 1572872 | tf_op jit(solution)/shard_map/ppermute | solution.py:20
  6.9 32.5 %collective-permute-start = (bf16[4,256,256]{2,1,0:T(8,128)(2,1)}, bf16[4,256,256]{2,1,0:T(8,128)(2,1)}, u32[]{:S(2)}, u32[]{:S(2)}) collective-permute-start(bf16[4,256,256]{2,1,0:T(8,128)(2,1)} %bitcast), channel_id=1, source_target_pairs={{0,24},{8,0},{16,8},{24,16},{1,25},{9,1},{17,9},{25,17},{2,26},{10... | collective-permute-start | bytes 1572872 | tf_op jit(solution)/shard_map/ppermute | solution.py:20
  25.6 33.9 %collective-permute-start.6 = (bf16[9,256,256]{2,1,0:T(8,128)(2,1)}, bf16[9,256,256]{2,1,0:T(8,128)(2,1)}, u32[]{:S(2)}, u32[]{:S(2)}) collective-permute-start(bf16[9,256,256]{2,1,0:T(8,128)(2,1)} %fusion.21), channel_id=1, source_target_pairs={{0,4},{1,5},{8,12},{9,13},{16,20},{17,21},{24,28},{25,29}} | collective-permute-start | bytes 3538952 | tf_op jit(solution)/shard_map/ppermute | solution.py:69
  31.1 29.4 %collective-permute-start.5 = (bf16[9,256,256]{2,1,0:T(8,128)(2,1)}, bf16[9,256,256]{2,1,0:T(8,128)(2,1)}, u32[]{:S(2)}, u32[]{:S(2)}) collective-permute-start(bf16[9,256,256]{2,1,0:T(8,128)(2,1)} %fusion.21), channel_id=1, source_target_pairs={{6,4},{4,2},{2,0},{7,5},{5,3},{3,1},{14,12},{12,10},{10,8},{15,13}... | collective-permute-start | bytes 3538952 | tf_op jit(solution)/shard_map/ppermute | solution.py:68
  39.4 21.1 %collective-permute-start.7 = (bf16[9,256,256]{2,1,0:T(8,128)(2,1)}, bf16[9,256,256]{2,1,0:T(8,128)(2,1)}, u32[]{:S(2)}, u32[]{:S(2)}) collective-permute-start(bf16[9,256,256]{2,1,0:T(8,128)(2,1)} %fusion.20), channel_id=1, source_target_pairs={{6,2},{7,3},{14,10},{15,11},{22,18},{23,19},{30,26},{31,27}} | collective-permute-start | bytes 3538952 | tf_op jit(solution)/shard_map/ppermute | solution.py:66
  41.1 39.6 %collective-permute-start.4 = (bf16[9,256,256]{2,1,0:T(8,128)(2,1)}, bf16[9,256,256]{2,1,0:T(8,128)(2,1)}, u32[]{:S(2)}, u32[]{:S(2)}) collective-permute-start(bf16[9,256,256]{2,1,0:T(8,128)(2,1)} %fusion.20), channel_id=1, source_target_pairs={{0,2},{2,4},{4,6},{1,3},{3,5},{5,7},{8,10},{10,12},{12,14},{9,11},... | collective-permute-start | bytes 3538952 | tf_op jit(solution)/shard_map/ppermute | solution.py:65
  56.8 23.9 %copy-start.3 = (bf16[9,256,256]{2,1,0:T(8,128)(2,1)S(1)}, bf16[9,256,256]{2,1,0:T(8,128)(2,1)}, u32[]{:S(2)}) copy-start(bf16[9,256,256]{2,1,0:T(8,128)(2,1)} %fusion.22) | copy-start | bytes 3538948
  82.3 18.3 %collective-permute-start.8 = (bf16[5,256,256]{2,1,0:T(8,128)(2,1)S(1)}, bf16[5,256,256]{2,1,0:T(8,128)(2,1)S(1)}, u32[]{:S(2)}, u32[]{:S(2)}) collective-permute-start(bf16[5,256,256]{2,1,0:T(8,128)(2,1)S(1)} %add_convert_fusion), channel_id=1, source_target_pairs={{0,2},{2,6},{6,4},{4,0},{1,3},{3,7},{7,5},{5,1},{8,10},{10,14},{14... | collective-permute-start | bytes 1966088 | tf_op jit(solution)/shard_map/ppermute | solution.py:94
  100.8 15.3 %collective-permute-start.9 = (bf16[5,256,256]{2,1,0:T(8,128)(2,1)S(1)}, bf16[5,256,256]{2,1,0:T(8,128)(2,1)}, u32[]{:S(2)}, u32[]{:S(2)}) collective-permute-start(bf16[5,256,256]{2,1,0:T(8,128)(2,1)S(1)} %fusion.27), channel_id=1, source_target_pairs={{0,1},{1,0},{2,3},{3,2},{4,5},{5,4},{6,7},{7,6},{8,9},{9,8},{10,11... | collective-permute-start | bytes 1966088 | tf_op jit(solution)/shard_map/ppermute | solution.py:20
  100.9 15.2 %collective-permute-start.10 = (bf16[4,256,256]{2,1,0:T(8,128)(2,1)S(1)}, bf16[4,256,256]{2,1,0:T(8,128)(2,1)S(1)}, u32[]{:S(2)}, u32[]{:S(2)}) collective-permute-start(bf16[4,256,256]{2,1,0:T(8,128)(2,1)S(1)} %add_convert_fusion.2), channel_id=1, source_target_pairs={{0,2},{2,6},{6,4},{4,0},{1,3},{3,7},{7,5},{5,1},{8,10},{10,14},{14... | collective-permute-start | bytes 1572872 | tf_op jit(solution)/shard_map/ppermute | solution.py:94
  116.3 2.1 collective-permute-start.11
  127.0 29.5 %collective-permute-start.15 = (bf16[9,256,256]{2,1,0:T(8,128)(2,1)}, bf16[9,256,256]{2,1,0:T(8,128)(2,1)}, u32[]{:S(2)}, u32[]{:S(2)}) collective-permute-start(bf16[9,256,256]{2,1,0:T(8,128)(2,1)} %fusion.23), channel_id=1, source_target_pairs={{6,2},{7,3},{14,10},{15,11},{22,18},{23,19},{30,26},{31,27}} | collective-permute-start | bytes 3538952 | tf_op jit(solution)/shard_map/ppermute | solution.py:66
  128.7 28.1 %collective-permute-start.12 = (bf16[9,256,256]{2,1,0:T(8,128)(2,1)}, bf16[9,256,256]{2,1,0:T(8,128)(2,1)}, u32[]{:S(2)}, u32[]{:S(2)}) collective-permute-start(bf16[9,256,256]{2,1,0:T(8,128)(2,1)} %fusion.23), channel_id=1, source_target_pairs={{0,2},{2,4},{4,6},{1,3},{3,5},{5,7},{8,10},{10,12},{12,14},{9,11},... | collective-permute-start | bytes 3538952 | tf_op jit(solution)/shard_map/ppermute | solution.py:65
  138.1 43.3 %collective-permute-start.14 = (bf16[9,256,256]{2,1,0:T(8,128)(2,1)}, bf16[9,256,256]{2,1,0:T(8,128)(2,1)}, u32[]{:S(2)}, u32[]{:S(2)}) collective-permute-start(bf16[9,256,256]{2,1,0:T(8,128)(2,1)} %fusion.24), channel_id=1, source_target_pairs={{0,4},{1,5},{8,12},{9,13},{16,20},{17,21},{24,28},{25,29}} | collective-permute-start | bytes 3538952 | tf_op jit(solution)/shard_map/ppermute | solution.py:69
  144.9 36.5 %collective-permute-start.13 = (bf16[9,256,256]{2,1,0:T(8,128)(2,1)}, bf16[9,256,256]{2,1,0:T(8,128)(2,1)}, u32[]{:S(2)}, u32[]{:S(2)}) collective-permute-start(bf16[9,256,256]{2,1,0:T(8,128)(2,1)} %fusion.24), channel_id=1, source_target_pairs={{6,4},{4,2},{2,0},{7,5},{5,3},{3,1},{14,12},{12,10},{10,8},{15,13}... | collective-permute-start | bytes 3538952 | tf_op jit(solution)/shard_map/ppermute | solution.py:68
  153.1 28.3 %copy-start.2 = (bf16[9,256,256]{2,1,0:T(8,128)(2,1)S(1)}, bf16[9,256,256]{2,1,0:T(8,128)(2,1)}, u32[]{:S(2)}) copy-start(bf16[9,256,256]{2,1,0:T(8,128)(2,1)} %fusion.25) | copy-start | bytes 3538948
  183.7 15.1 %collective-permute-start.16 = (bf16[4,256,256]{2,1,0:T(8,128)(2,1)}, bf16[4,256,256]{2,1,0:T(8,128)(2,1)S(1)}, u32[]{:S(2)}, u32[]{:S(2)}) collective-permute-start(bf16[4,256,256]{2,1,0:T(8,128)(2,1)} %add_convert_fusion.1), channel_id=1, source_target_pairs={{0,2},{2,6},{6,4},{4,0},{1,3},{3,7},{7,5},{5,1},{8,10},{10,14},{14... | collective-permute-start | bytes 1572872 | tf_op jit(solution)/shard_map/ppermute | solution.py:94
  198.9 12.4 %collective-permute-start.17 = (bf16[1,4,1,256,256]{4,3,1,2,0:T(8,128)(2,1)S(1)}, bf16[1,4,1,256,256]{4,3,1,2,0:T(8,128)(2,1)S(1)}, u32[]{:S(2)}, u32[]{:S(2)}) collective-permute-start(bf16[1,4,1,256,256]{4,3,1,2,0:T(8,128)(2,1)S(1)} %bitcast.130), channel_id=1, source_target_pairs={{0,16},{8,24},{16,0},{24,8},{1,17},{9,25},{17,1},{25,9},{2,18},{10... | collective-permute-start | bytes 1572872 | tf_op jit(solution)/shard_map/ppermute | solution.py:20
  200.5 10.1 %collective-permute-start.18 = (bf16[3,256,256]{2,1,0:T(8,128)(2,1)S(1)}, bf16[3,256,256]{2,1,0:T(8,128)(2,1)S(1)}, u32[]{:S(2)}, u32[]{:S(2)}) collective-permute-start(bf16[3,256,256]{2,1,0:T(8,128)(2,1)S(1)} %add_convert_fusion.3), channel_id=1, source_target_pairs={{0,2},{2,6},{6,4},{4,0},{1,3},{3,7},{7,5},{5,1},{8,10},{10,14},{14... | collective-permute-start | bytes 1179656 | tf_op jit(solution)/shard_map/ppermute | solution.py:94
  211.4 9.2 %collective-permute-start.19 = (bf16[1,3,1,256,256]{4,3,1,2,0:T(8,128)(2,1)S(1)}, bf16[1,3,1,256,256]{4,3,1,2,0:T(8,128)(2,1)S(1)}, u32[]{:S(2)}, u32[]{:S(2)}) collective-permute-start(bf16[1,3,1,256,256]{4,3,1,2,0:T(8,128)(2,1)S(1)} %bitcast.133), channel_id=1, source_target_pairs={{0,16},{8,24},{16,0},{24,8},{1,17},{9,25},{17,1},{25,9},{2,18},{10... | collective-permute-start | bytes 1179656 | tf_op jit(solution)/shard_map/ppermute | solution.py:20
  213.0 7.3 %collective-permute-start.20 = (bf16[2,256,256]{2,1,0:T(8,128)(2,1)S(1)}, bf16[2,256,256]{2,1,0:T(8,128)(2,1)S(1)}, u32[]{:S(2)}, u32[]{:S(2)}) collective-permute-start(bf16[2,256,256]{2,1,0:T(8,128)(2,1)S(1)} %add_convert_fusion.4), channel_id=1, source_target_pairs={{0,2},{2,6},{6,4},{4,0},{1,3},{3,7},{7,5},{5,1},{8,10},{10,14},{14... | collective-permute-start | bytes 786440 | tf_op jit(solution)/shard_map/ppermute | solution.py:94
  220.7 6.4 %collective-permute-start.21 = (bf16[1,2,1,256,256]{4,3,1,2,0:T(8,128)(2,1)S(1)}, bf16[1,2,1,256,256]{4,3,1,2,0:T(8,128)(2,1)S(1)}, u32[]{:S(2)}, u32[]{:S(2)}) collective-permute-start(bf16[1,2,1,256,256]{4,3,1,2,0:T(8,128)(2,1)S(1)} %fusion.36), channel_id=1, source_target_pairs={{0,16},{8,24},{16,0},{24,8},{1,17},{9,25},{17,1},{25,9},{2,18},{10... | collective-permute-start | bytes 786440 | tf_op jit(solution)/shard_map/ppermute | solution.py:20
  (8 other events, 62.5 us)

commit v21 on v19

--- a/solution.py
+++ b/solution.py
@@ -138,7 +138,7 @@
         if line:
             parts, tensors[step + 1 :] = advance_line(
                 pieces, ket, bra, mpo, live_mask, sector, tensors[step + 1 :],
-                3 if last else 2, onward if last else chan_copies,
+                4 if last else 2, onward if last else chan_copies,
             )
         else:
             parts = [advance_direct(pieces, ket, bra, mpo, live_mask)]

time: 229 us -> 233 us (1.017)
  waiting for transfers between devices: 101 us -> 106 us
    ppermute x9 -> x10, waiting for transfers between devices: 9.3 us -> 18 us  [shifted(): return lax.ppermute(value, axis, pairs)]
    ppermute x5 -> x6, waiting for transfers between devices: 44.7 us -> 41.1 us  [advance_line(): got_last = lax.ppermute(send, 'sector', LAST)]
    ppermute x9 -> x10, starting transfers between devices: 10.8 us -> 9.06 us  [shifted(): return lax.ppermute(value, axis, pairs)]
    ppermute x5 -> x6, starting transfers between devices: 6.59 us -> 6.3 us  [advance_line(): got_last = lax.ppermute(send, 'sector', LAST)]
  transfers between devices with their start and end apart: 22 -> 24, of which waited for: 14 -> 16; matrix products, arithmetic and copies ran while one was open for 27% -> 27% of each run, Pallas kernels for 0% -> 0%
where the time goes in v21:
time: 233 us; the launch traced here: 232 us
  waiting for transfers between devices  106 us (45%)
  matrix products  55.9 us (24%)
  starting transfers between devices  40.7 us (17%)
  other arithmetic  18.3 us (8%)
  between operations  6.97 us (3%)
  local copies, waits for them, and re-layouts  4.2 us (2%)
    ppermute x6, waiting for transfers between devices, advance_line(): got_last = lax.ppermute(send, 'sector', LAST)  41.1 us
    dot_general x8, matrix products, term(): jnp.einsum('bd,vbc->vdc', bra_p, rotated, preferred_element_type=jnp.floa...  28.9 us
    dot_general x8, matrix products, term(): jnp.einsum('wv,wba->vba', mpo_p, gathered, preferred_element_type=jnp.flo...  27 us
    ppermute x2, waiting for transfers between devices, advance_line(): middle_right = lax.ppermute(slot_b, 'sector', ((0, 2),))  24.8 us
    ppermute x2, waiting for transfers between devices, advance_line(): got_right = lax.ppermute(slot_a, 'sector', RIGHT)  20.8 us
    ppermute x10, waiting for transfers between devices, shifted(): return lax.ppermute(value, axis, pairs)  18 us
    ppermute x2, starting transfers between devices, advance_line(): middle_right = lax.ppermute(slot_b, 'sector', ((0, 2),))  11.9 us
    ppermute x10, starting transfers between devices, shifted(): return lax.ppermute(value, axis, pairs)  9.06 us
  transfers between devices with their start and end apart: 24, of which 16 were waited for; matrix products, arithmetic and copies ran while one was open for 27% of the time, Pallas kernels for 0%

profile of v21, /device:TPU:0, one launch (start us, length us, event | category | flops | bytes accessed | tf_op | source)
XLA Modules:
  0.0 231.8 jit_solution(2090269352678486744)
XLA Ops:
  2.8 3.5 %collective-permute-start.2 = (bf16[18,9,4]{1,2,0:T(4,128)(2,1)S(1)}, bf16[18,9,4]{1,2,0:T(4,128)(2,1)S(1)}, u32[]{:S(2)}, u32[]{:S(2)}) collective-permute-start(bf16[18,9,4]{1,2,0:T(4,128)(2,1)S(1)} %bitcast.132), channel_id=1, source_target_pairs={{0,24},{8,0},{16,8},{24,16},{1,25},{9,1},{17,9},{25,17},{2,26},{10... | collective-permute-start | bytes 3896 | tf_op jit(solution)/shard_map/ppermute | solution.py:20
  19.0 3.4 %fusion.10 = bf16[9,256,256]{2,0,1:T(8,128)(2,1)} fusion(bf16[18,256,256]{2,1,0:T(8,128)(2,1)S(1)} %pad_maximum_fusion, bf16[18,9,1]{1,2,0:T(2,128)(2,1)S(1)} %get-tuple-element.77), kind=kOutput, calls=%fused_computation.12 | convolution fusion | flops 21233664 | bytes 3539268 | tf_op jit(solution)/shard_map/wv,wba->vba/dot_general | solution.py:24
  22.4 3.6 %fusion.21 = bf16[9,256,256]{2,1,0:T(8,128)(2,1)} fusion(bf16[9,256,256]{2,0,1:T(8,128)(2,1)} %fusion.10, bf16[1,1,4,256,256]{4,3,2,1,0:T(8,128)(2,1)} %param.15, s32[]{:T(128)S(6)} %select_n.81, bf16[1,1,4,256,256]{4,3,2,1,0:T(8,128)(2,1)} %param.14), kind=kOutput, calls=%fused_computation.51 | convolution fusion | flops 605159424 | bytes 3539968 | tf_op jit(solution)/shard_map/bd,vbc->vdc/dot_general | solution.py:30
  26.1 5.5 %collective-permute-start.6 = (bf16[9,256,256]{2,1,0:T(8,128)(2,1)}, bf16[9,256,256]{2,1,0:T(8,128)(2,1)}, u32[]{:S(2)}, u32[]{:S(2)}) collective-permute-start(bf16[9,256,256]{2,1,0:T(8,128)(2,1)} %fusion.21), channel_id=1, source_target_pairs={{0,4},{1,5},{8,12},{9,13},{16,20},{17,21},{24,28},{25,29}} | collective-permute-start | bytes 3538952 | tf_op jit(solution)/shard_map/ppermute | solution.py:69
  36.2 3.7 %fusion.20 = bf16[9,256,256]{2,1,0:T(8,128)(2,1)} fusion(bf16[9,256,256]{2,0,1:T(8,128)(2,1)} %fusion.14, bf16[1,1,4,256,256]{4,3,2,1,0:T(8,128)(2,1)} %param.15, s32[]{:T(128)S(6)} %select_n.78, bf16[1,1,4,256,256]{4,3,2,1,0:T(8,128)(2,1)} %param.14), kind=kOutput, calls=%fused_computation.50 | convolution fusion | flops 605159424 | bytes 3539968 | tf_op jit(solution)/shard_map/bd,vbc->vdc/dot_general | solution.py:30
  41.7 5.2 %collective-permute-start.4 = (bf16[9,256,256]{2,1,0:T(8,128)(2,1)}, bf16[9,256,256]{2,1,0:T(8,128)(2,1)}, u32[]{:S(2)}, u32[]{:S(2)}) collective-permute-start(bf16[9,256,256]{2,1,0:T(8,128)(2,1)} %fusion.20), channel_id=1, source_target_pairs={{0,2},{2,4},{4,6},{1,3},{3,5},{5,7},{8,10},{10,12},{12,14},{9,11},... | collective-permute-start | bytes 3538952 | tf_op jit(solution)/shard_map/ppermute | solution.py:65
  50.2 3.7 %fusion.22 = bf16[9,256,256]{2,1,0:T(8,128)(2,1)} fusion(bf16[9,256,256]{2,0,1:T(8,128)(2,1)} %fusion.8, bf16[1,1,4,256,256]{4,3,2,1,0:T(8,128)(2,1)} %param.15, s32[]{:T(128)S(6)} %select_n.82, bf16[1,1,4,256,256]{4,3,2,1,0:T(8,128)(2,1)} %param.14), kind=kOutput, calls=%fused_computation.52 | convolution fusion | flops 605159424 | bytes 3539968 | tf_op jit(solution)/shard_map/bd,vbc->vdc/dot_general | solution.py:30
  61.0 20.2 %collective-permute-done.4 = bf16[9,256,256]{2,1,0:T(8,128)(2,1)} collective-permute-done((bf16[9,256,256]{2,1,0:T(8,128)(2,1)}, bf16[9,256,256]{2,1,0:T(8,128)(2,1)}, u32[]{:S(2)}, u32[]{:S(2)}) %collective-permute-start.4) | collective-permute-done | bytes 1179680 | tf_op jit(solution)/shard_map/ppermute | solution.py:65
  82.7 3.8 %collective-permute-start.8 = (bf16[4,256,256]{2,1,0:T(8,128)(2,1)S(1)}, bf16[4,256,256]{2,1,0:T(8,128)(2,1)S(1)}, u32[]{:S(2)}, u32[]{:S(2)}) collective-permute-start(bf16[4,256,256]{2,1,0:T(8,128)(2,1)S(1)} %add_convert_fusion.1), channel_id=1, source_target_pairs={{0,2},{2,6},{6,4},{4,0},{1,3},{3,7},{7,5},{5,1},{8,10},{10,14},{14... | collective-permute-start | bytes 1572872 | tf_op jit(solution)/shard_map/ppermute | solution.py:94
  91.3 6.9 %collective-permute-done.8 = bf16[4,256,256]{2,1,0:T(8,128)(2,1)S(1)} collective-permute-done((bf16[4,256,256]{2,1,0:T(8,128)(2,1)S(1)}, bf16[4,256,256]{2,1,0:T(8,128)(2,1)S(1)}, u32[]{:S(2)}, u32[]{:S(2)}) %collective-permute-start.8) | collective-permute-done | bytes 524320 | tf_op jit(solution)/shard_map/ppermute | solution.py:94
  101.9 13.4 %collective-permute-done.10 = bf16[5,256,256]{2,1,0:T(8,128)(2,1)S(1)} collective-permute-done((bf16[5,256,256]{2,1,0:T(8,128)(2,1)S(1)}, bf16[5,256,256]{2,1,0:T(8,128)(2,1)S(1)}, u32[]{:S(2)}, u32[]{:S(2)}) %collective-permute-start.10) | collective-permute-done | bytes 655392 | tf_op jit(solution)/shard_map/ppermute | solution.py:94
  119.6 3.4 %fusion.4 = bf16[9,256,256]{2,0,1:T(8,128)(2,1)} fusion(bf16[18,256,256]{2,1,0:T(8,128)(2,1)S(1)} %pad_maximum_fusion.1, bf16[18,9,1]{1,2,0:T(2,128)(2,1)S(1)} %get-tuple-element.75), kind=kOutput, calls=%fused_computation.6 | convolution fusion | flops 21233664 | bytes 3539268 | tf_op jit(solution)/shard_map/wv,wba->vba/dot_general | solution.py:24
  123.0 3.6 %fusion.23 = bf16[9,256,256]{2,1,0:T(8,128)(2,1)} fusion(bf16[9,256,256]{2,0,1:T(8,128)(2,1)} %fusion.4, bf16[4,256,256]{2,1,0:T(8,128)(2,1)S(1)} %copy-done.6, s32[]{:T(128)S(6)} %select_n.78, bf16[4,256,256]{2,1,0:T(8,128)(2,1)} %collective-permute-done), kind=kOutput, calls=%fused_computation.53 | convolution fusion | flops 605159424 | bytes 3539968 | tf_op jit(solution)/shard_map/bd,vbc->vdc/dot_general | solution.py:30
  133.9 3.5 %fusion.24 = bf16[9,256,256]{2,1,0:T(8,128)(2,1)} fusion(bf16[9,256,256]{2,0,1:T(8,128)(2,1)} %fusion.2, bf16[4,256,256]{2,1,0:T(8,128)(2,1)S(1)} %copy-done.6, s32[]{:T(128)S(6)} %select_n.81, bf16[4,256,256]{2,1,0:T(8,128)(2,1)} %collective-permute-done), kind=kOutput, calls=%fused_computation.54 | convolution fusion | flops 605159424 | bytes 3539968 | tf_op jit(solution)/shard_map/bd,vbc->vdc/dot_general | solution.py:30
  137.5 6.4 %collective-permute-start.14 = (bf16[9,256,256]{2,1,0:T(8,128)(2,1)}, bf16[9,256,256]{2,1,0:T(8,128)(2,1)}, u32[]{:S(2)}, u32[]{:S(2)}) collective-permute-start(bf16[9,256,256]{2,1,0:T(8,128)(2,1)} %fusion.24), channel_id=1, source_target_pairs={{0,4},{1,5},{8,12},{9,13},{16,20},{17,21},{24,28},{25,29}} | collective-permute-start | bytes 3538952 | tf_op jit(solution)/shard_map/ppermute | solution.py:69
  145.1 3.4 %fusion = bf16[9,256,256]{2,0,1:T(8,128)(2,1)} fusion(bf16[18,256,256]{2,1,0:T(8,128)(2,1)S(1)} %pad_maximum_fusion.1, bf16[18,9,1]{1,2,0:T(2,128)(2,1)S(1)} %get-tuple-element.73), kind=kOutput, calls=%fused_computation.2 | convolution fusion | flops 21233664 | bytes 3539268 | tf_op jit(solution)/shard_map/wv,wba->vba/dot_general | solution.py:24
  148.5 3.6 %fusion.25 = bf16[9,256,256]{2,1,0:T(8,128)(2,1)} fusion(bf16[9,256,256]{2,0,1:T(8,128)(2,1)} %fusion, bf16[4,256,256]{2,1,0:T(8,128)(2,1)S(1)} %copy-done.6, s32[]{:T(128)S(6)} %select_n.82, bf16[4,256,256]{2,1,0:T(8,128)(2,1)} %collective-permute-done), kind=kOutput, calls=%fused_computation.55 | convolution fusion | flops 605159424 | bytes 3539968 | tf_op jit(solution)/shard_map/bd,vbc->vdc/dot_general | solution.py:30
  156.1 24.8 %collective-permute-done.14 = bf16[9,256,256]{2,1,0:T(8,128)(2,1)} collective-permute-done((bf16[9,256,256]{2,1,0:T(8,128)(2,1)}, bf16[9,256,256]{2,1,0:T(8,128)(2,1)}, u32[]{:S(2)}, u32[]{:S(2)}) %collective-permute-start.14) | collective-permute-done | bytes 1179680 | tf_op jit(solution)/shard_map/ppermute | solution.py:69
  184.8 4.5 %fusion.17 = f32[9,256,256]{2,1,0:T(8,128)S(1)} fusion(bf16[9,256,256]{2,1,0:T(8,128)(2,1)} %collective-permute-done.13, bf16[9,256,256]{2,1,0:T(8,128)(2,1)} %collective-permute-done.12, bf16[9,256,256]{2,1,0:T(8,128)(2,1)} %collective-permute-done.14, bf16[9,256,256]{2,1,0:T(8,128)(2,1)} %collective-permute-done.15, f32[]{:T(128)S(6)} %select_n.83, ...), kind=kOutput, calls=%fused_computation.22 | convolution fusion | flops 612237312 | bytes 9437192 | tf_op jit(solution)/shard_map/bd,vbc->vdc/dot_general | solution.py:30
  189.3 6.6 %collective-permute-done.16 = bf16[3,256,256]{2,1,0:T(8,128)(2,1)S(1)} collective-permute-done((bf16[3,256,256]{2,1,0:T(8,128)(2,1)}, bf16[3,256,256]{2,1,0:T(8,128)(2,1)S(1)}, u32[]{:S(2)}, u32[]{:S(2)}) %collective-permute-start.16) | collective-permute-done | bytes 393248 | tf_op jit(solution)/shard_map/ppermute | solution.py:94
  199.0 7.1 %collective-permute-done.17 = bf16[1,3,1,256,256]{4,3,1,2,0:T(8,128)(2,1)S(1)} collective-permute-done((bf16[1,3,1,256,256]{4,3,1,2,0:T(8,128)(2,1)S(1)}, bf16[1,3,1,256,256]{4,3,1,2,0:T(8,128)(2,1)S(1)}, u32[]{:S(2)}, u32[]{:S(2)}) %collective-permute-start.17) | collective-permute-done | bytes 393248 | tf_op jit(solution)/shard_map/ppermute | solution.py:20
  210.1 6.2 %collective-permute-done.20 = bf16[2,256,256]{2,1,0:T(8,128)(2,1)S(1)} collective-permute-done((bf16[2,256,256]{2,1,0:T(8,128)(2,1)S(1)}, bf16[2,256,256]{2,1,0:T(8,128)(2,1)S(1)}, u32[]{:S(2)}, u32[]{:S(2)}) %collective-permute-start.20) | collective-permute-done | bytes 262176 | tf_op jit(solution)/shard_map/ppermute | solution.py:94
  218.2 5.9 %collective-permute-done.22 = bf16[1,256,256]{2,1,0:T(8,128)(2,1)S(1)} collective-permute-done((bf16[1,256,256]{2,1,0:T(8,128)(2,1)S(1)}, bf16[1,256,256]{2,1,0:T(8,128)(2,1)S(1)}, u32[]{:S(2)}, u32[]{:S(2)}) %collective-permute-start.22) | collective-permute-done | bytes 131104 | tf_op jit(solution)/shard_map/ppermute | solution.py:94
  225.8 4.8 %collective-permute-done.23 = bf16[1,1,1,256,256]{4,3,2,1,0:T(8,128)(2,1)S(1)} collective-permute-done((bf16[1,1,1,256,256]{4,3,2,1,0:T(8,128)(2,1)S(1)}, bf16[1,1,1,256,256]{4,3,2,1,0:T(8,128)(2,1)S(1)}, u32[]{:S(2)}, u32[]{:S(2)}) %collective-permute-start.23) | collective-permute-done | bytes 131104 | tf_op jit(solution)/shard_map/ppermute | solution.py:20
  (93 shorter events, 68.2 us)
Async XLA Ops:
  2.2 15.0 %collective-permute-start.3 = (bf16[9,256,256]{2,1,0:T(8,128)(2,1)S(1)}, bf16[9,256,256]{2,1,0:T(8,128)(2,1)}, u32[]{:S(2)}, u32[]{:S(2)}) collective-permute-start(bf16[9,256,256]{2,1,0:T(8,128)(2,1)S(1)} %bitcast_select_fusion), channel_id=1, source_target_pairs={{0,1},{1,0},{2,3},{3,2},{4,5},{5,4},{6,7},{7,6},{8,9},{9,8},{10,11... | collective-permute-start | bytes 3538952 | tf_op jit(solution)/shard_map/ppermute | solution.py:20
  2.8 37.1 %collective-permute-start.2 = (bf16[18,9,4]{1,2,0:T(4,128)(2,1)S(1)}, bf16[18,9,4]{1,2,0:T(4,128)(2,1)S(1)}, u32[]{:S(2)}, u32[]{:S(2)}) collective-permute-start(bf16[18,9,4]{1,2,0:T(4,128)(2,1)S(1)} %bitcast.132), channel_id=1, source_target_pairs={{0,24},{8,0},{16,8},{24,16},{1,25},{9,1},{17,9},{25,17},{2,26},{10... | collective-permute-start | bytes 3896 | tf_op jit(solution)/shard_map/ppermute | solution.py:20
  6.3 33.6 %collective-permute-start.1 = (bf16[4,256,256]{2,1,0:T(8,128)(2,1)}, bf16[4,256,256]{2,1,0:T(8,128)(2,1)S(1)}, u32[]{:S(2)}, u32[]{:S(2)}) collective-permute-start(bf16[4,256,256]{2,1,0:T(8,128)(2,1)} %bitcast.1), channel_id=1, source_target_pairs={{0,24},{8,0},{16,8},{24,16},{1,25},{9,1},{17,9},{25,17},{2,26},{10... | collective-permute-start | bytes 1572872 | tf_op jit(solution)/shard_map/ppermute | solution.py:20
  6.9 33.1 %collective-permute-start = (bf16[4,256,256]{2,1,0:T(8,128)(2,1)}, bf16[4,256,256]{2,1,0:T(8,128)(2,1)}, u32[]{:S(2)}, u32[]{:S(2)}) collective-permute-start(bf16[4,256,256]{2,1,0:T(8,128)(2,1)} %bitcast), channel_id=1, source_target_pairs={{0,24},{8,0},{16,8},{24,16},{1,25},{9,1},{17,9},{25,17},{2,26},{10... | collective-permute-start | bytes 1572872 | tf_op jit(solution)/shard_map/ppermute | solution.py:20
  26.1 34.0 %collective-permute-start.6 = (bf16[9,256,256]{2,1,0:T(8,128)(2,1)}, bf16[9,256,256]{2,1,0:T(8,128)(2,1)}, u32[]{:S(2)}, u32[]{:S(2)}) collective-permute-start(bf16[9,256,256]{2,1,0:T(8,128)(2,1)} %fusion.21), channel_id=1, source_target_pairs={{0,4},{1,5},{8,12},{9,13},{16,20},{17,21},{24,28},{25,29}} | collective-permute-start | bytes 3538952 | tf_op jit(solution)/shard_map/ppermute | solution.py:69
  31.6 29.4 %collective-permute-start.5 = (bf16[9,256,256]{2,1,0:T(8,128)(2,1)}, bf16[9,256,256]{2,1,0:T(8,128)(2,1)}, u32[]{:S(2)}, u32[]{:S(2)}) collective-permute-start(bf16[9,256,256]{2,1,0:T(8,128)(2,1)} %fusion.21), channel_id=1, source_target_pairs={{6,4},{4,2},{2,0},{7,5},{5,3},{3,1},{14,12},{12,10},{10,8},{15,13}... | collective-permute-start | bytes 3538952 | tf_op jit(solution)/shard_map/ppermute | solution.py:68
  40.0 21.1 %collective-permute-start.7 = (bf16[9,256,256]{2,1,0:T(8,128)(2,1)}, bf16[9,256,256]{2,1,0:T(8,128)(2,1)}, u32[]{:S(2)}, u32[]{:S(2)}) collective-permute-start(bf16[9,256,256]{2,1,0:T(8,128)(2,1)} %fusion.20), channel_id=1, source_target_pairs={{6,2},{7,3},{14,10},{15,11},{22,18},{23,19},{30,26},{31,27}} | collective-permute-start | bytes 3538952 | tf_op jit(solution)/shard_map/ppermute | solution.py:66
  41.7 39.5 %collective-permute-start.4 = (bf16[9,256,256]{2,1,0:T(8,128)(2,1)}, bf16[9,256,256]{2,1,0:T(8,128)(2,1)}, u32[]{:S(2)}, u32[]{:S(2)}) collective-permute-start(bf16[9,256,256]{2,1,0:T(8,128)(2,1)} %fusion.20), channel_id=1, source_target_pairs={{0,2},{2,4},{4,6},{1,3},{3,5},{5,7},{8,10},{10,12},{12,14},{9,11},... | collective-permute-start | bytes 3538952 | tf_op jit(solution)/shard_map/ppermute | solution.py:65
  82.7 15.5 %collective-permute-start.8 = (bf16[4,256,256]{2,1,0:T(8,128)(2,1)S(1)}, bf16[4,256,256]{2,1,0:T(8,128)(2,1)S(1)}, u32[]{:S(2)}, u32[]{:S(2)}) collective-permute-start(bf16[4,256,256]{2,1,0:T(8,128)(2,1)S(1)} %add_convert_fusion.1), channel_id=1, source_target_pairs={{0,2},{2,6},{6,4},{4,0},{1,3},{3,7},{7,5},{5,1},{8,10},{10,14},{14... | collective-permute-start | bytes 1572872 | tf_op jit(solution)/shard_map/ppermute | solution.py:94
  98.3 17.1 %collective-permute-start.10 = (bf16[5,256,256]{2,1,0:T(8,128)(2,1)S(1)}, bf16[5,256,256]{2,1,0:T(8,128)(2,1)S(1)}, u32[]{:S(2)}, u32[]{:S(2)}) collective-permute-start(bf16[5,256,256]{2,1,0:T(8,128)(2,1)S(1)} %add_convert_fusion), channel_id=1, source_target_pairs={{0,2},{2,6},{6,4},{4,0},{1,3},{3,7},{7,5},{5,1},{8,10},{10,14},{14... | collective-permute-start | bytes 1966088 | tf_op jit(solution)/shard_map/ppermute | solution.py:94
  99.2 1.9 collective-permute-start.9
  115.6 2.3 collective-permute-start.11
  126.5 28.9 %collective-permute-start.15 = (bf16[9,256,256]{2,1,0:T(8,128)(2,1)}, bf16[9,256,256]{2,1,0:T(8,128)(2,1)}, u32[]{:S(2)}, u32[]{:S(2)}) collective-permute-start(bf16[9,256,256]{2,1,0:T(8,128)(2,1)} %fusion.23), channel_id=1, source_target_pairs={{6,2},{7,3},{14,10},{15,11},{22,18},{23,19},{30,26},{31,27}} | collective-permute-start | bytes 3538952 | tf_op jit(solution)/shard_map/ppermute | solution.py:66
  128.2 27.9 %collective-permute-start.12 = (bf16[9,256,256]{2,1,0:T(8,128)(2,1)}, bf16[9,256,256]{2,1,0:T(8,128)(2,1)}, u32[]{:S(2)}, u32[]{:S(2)}) collective-permute-start(bf16[9,256,256]{2,1,0:T(8,128)(2,1)} %fusion.23), channel_id=1, source_target_pairs={{0,2},{2,4},{4,6},{1,3},{3,5},{5,7},{8,10},{10,12},{12,14},{9,11},... | collective-permute-start | bytes 3538952 | tf_op jit(solution)/shard_map/ppermute | solution.py:65
  137.5 43.4 %collective-permute-start.14 = (bf16[9,256,256]{2,1,0:T(8,128)(2,1)}, bf16[9,256,256]{2,1,0:T(8,128)(2,1)}, u32[]{:S(2)}, u32[]{:S(2)}) collective-permute-start(bf16[9,256,256]{2,1,0:T(8,128)(2,1)} %fusion.24), channel_id=1, source_target_pairs={{0,4},{1,5},{8,12},{9,13},{16,20},{17,21},{24,28},{25,29}} | collective-permute-start | bytes 3538952 | tf_op jit(solution)/shard_map/ppermute | solution.py:69
  143.8 37.1 %collective-permute-start.13 = (bf16[9,256,256]{2,1,0:T(8,128)(2,1)}, bf16[9,256,256]{2,1,0:T(8,128)(2,1)}, u32[]{:S(2)}, u32[]{:S(2)}) collective-permute-start(bf16[9,256,256]{2,1,0:T(8,128)(2,1)} %fusion.24), channel_id=1, source_target_pairs={{6,4},{4,2},{2,0},{7,5},{5,3},{3,1},{14,12},{12,10},{10,8},{15,13}... | collective-permute-start | bytes 3538952 | tf_op jit(solution)/shard_map/ppermute | solution.py:68
  183.4 12.5 %collective-permute-start.16 = (bf16[3,256,256]{2,1,0:T(8,128)(2,1)}, bf16[3,256,256]{2,1,0:T(8,128)(2,1)S(1)}, u32[]{:S(2)}, u32[]{:S(2)}) collective-permute-start(bf16[3,256,256]{2,1,0:T(8,128)(2,1)} %get-tuple-element.71), channel_id=1, source_target_pairs={{0,2},{2,6},{6,4},{4,0},{1,3},{3,7},{7,5},{5,1},{8,10},{10,14},{14... | collective-permute-start | bytes 1179656 | tf_op jit(solution)/shard_map/ppermute | solution.py:94
  196.0 10.1 %collective-permute-start.17 = (bf16[1,3,1,256,256]{4,3,1,2,0:T(8,128)(2,1)S(1)}, bf16[1,3,1,256,256]{4,3,1,2,0:T(8,128)(2,1)S(1)}, u32[]{:S(2)}, u32[]{:S(2)}) collective-permute-start(bf16[1,3,1,256,256]{4,3,1,2,0:T(8,128)(2,1)S(1)} %bitcast.135), channel_id=1, source_target_pairs={{0,16},{8,24},{16,0},{24,8},{1,17},{9,25},{17,1},{25,9},{2,18},{10... | collective-permute-start | bytes 1179656 | tf_op jit(solution)/shard_map/ppermute | solution.py:20
  197.6 10.7 %collective-permute-start.18 = (bf16[3,256,256]{2,1,0:T(8,128)(2,1)S(1)}, bf16[3,256,256]{2,1,0:T(8,128)(2,1)S(1)}, u32[]{:S(2)}, u32[]{:S(2)}) collective-permute-start(bf16[3,256,256]{2,1,0:T(8,128)(2,1)S(1)} %get-tuple-element.57), channel_id=1, source_target_pairs={{0,2},{2,6},{6,4},{4,0},{1,3},{3,7},{7,5},{5,1},{8,10},{10,14},{14... | collective-permute-start | bytes 1179656 | tf_op jit(solution)/shard_map/ppermute | solution.py:94
  208.4 9.2 %collective-permute-start.19 = (bf16[1,3,1,256,256]{4,3,1,2,0:T(8,128)(2,1)S(1)}, bf16[1,3,1,256,256]{4,3,1,2,0:T(8,128)(2,1)S(1)}, u32[]{:S(2)}, u32[]{:S(2)}) collective-permute-start(bf16[1,3,1,256,256]{4,3,1,2,0:T(8,128)(2,1)S(1)} %bitcast.134), channel_id=1, source_target_pairs={{0,16},{8,24},{16,0},{24,8},{1,17},{9,25},{17,1},{25,9},{2,18},{10... | collective-permute-start | bytes 1179656 | tf_op jit(solution)/shard_map/ppermute | solution.py:20
  209.0 7.3 %collective-permute-start.20 = (bf16[2,256,256]{2,1,0:T(8,128)(2,1)S(1)}, bf16[2,256,256]{2,1,0:T(8,128)(2,1)S(1)}, u32[]{:S(2)}, u32[]{:S(2)}) collective-permute-start(bf16[2,256,256]{2,1,0:T(8,128)(2,1)S(1)} %add_convert_fusion.4), channel_id=1, source_target_pairs={{0,2},{2,6},{6,4},{4,0},{1,3},{3,7},{7,5},{5,1},{8,10},{10,14},{14... | collective-permute-start | bytes 786440 | tf_op jit(solution)/shard_map/ppermute | solution.py:94
  217.7 7.8 %collective-permute-start.21 = (bf16[1,2,1,256,256]{4,3,1,2,0:T(8,128)(2,1)S(1)}, bf16[1,2,1,256,256]{4,3,1,2,0:T(8,128)(2,1)S(1)}, u32[]{:S(2)}, u32[]{:S(2)}) collective-permute-start(bf16[1,2,1,256,256]{4,3,1,2,0:T(8,128)(2,1)S(1)} %bitcast.136), channel_id=1, source_target_pairs={{0,16},{8,24},{16,0},{24,8},{1,17},{9,25},{17,1},{25,9},{2,18},{10... | collective-permute-start | bytes 786440 | tf_op jit(solution)/shard_map/ppermute | solution.py:20
  218.2 5.9 %collective-permute-start.22 = (bf16[1,256,256]{2,1,0:T(8,128)(2,1)S(1)}, bf16[1,256,256]{2,1,0:T(8,128)(2,1)S(1)}, u32[]{:S(2)}, u32[]{:S(2)}) collective-permute-start(bf16[1,256,256]{2,1,0:T(8,128)(2,1)S(1)} %add_convert_fusion.5), channel_id=1, source_target_pairs={{0,2},{2,6},{6,4},{4,0},{1,3},{3,7},{7,5},{5,1},{8,10},{10,14},{14... | collective-permute-start | bytes 393224 | tf_op jit(solution)/shard_map/ppermute | solution.py:94
  225.6 5.0 %collective-permute-start.23 = (bf16[1,1,1,256,256]{4,3,2,1,0:T(8,128)(2,1)S(1)}, bf16[1,1,1,256,256]{4,3,2,1,0:T(8,128)(2,1)S(1)}, u32[]{:S(2)}, u32[]{:S(2)}) collective-permute-start(bf16[1,1,1,256,256]{4,3,2,1,0:T(8,128)(2,1)S(1)} %fusion.38), channel_id=1, source_target_pairs={{0,16},{8,24},{16,0},{24,8},{1,17},{9,25},{17,1},{25,9},{2,18},{10... | collective-permute-start | bytes 393224 | tf_op jit(solution)/shard_map/ppermute | solution.py:20
  (11 other events, 118.8 us)
